TPU v7x, 32 devices: a whole 2x2x4 slice. The times are simulated.
32 devices in a mesh: grp: 2 (over y), dp: 4 (over x, core), sp: 4 (over z).
Axes of the slice: x: 2, y: 2, z: 4, core: 2. Of those that a mesh axis runs over, the one named last changes fastest.
Arguments:
- rollout_rows: bfloat16 [4096, 5120], P(('grp', 'dp', 'sp')), parts along dimension 0, may hold values from -28 to 28
- routing: int32 [4096], P('grp'), parts along dimension 0, may hold values from 0 to 3, as said below
- segment_labels: int32 [8, 512], P(('grp', 'dp'), 'sp'), parts along dimension 0, may hold values from 0 to 3, never falling along the last dimension, each value on 1 to 256 neighbouring positions
- upstream: bfloat16 [8, 512, 4096], P(('grp', 'dp'), 'sp'), parts along dimension 0, may hold values from -24 to 24
- passes: int32 [32], P('grp'), parts along dimension 0, may hold values from 0 to 10
- group_ids: int32 [32], P('grp'), parts along dimension 0, may hold values from 0 to 1, as said below
Outputs:
- query_gradient: bfloat16 [8, 512, 4096], P(('grp', 'dp'), 'sp'), parts along dimension 0
- kv_grads: bfloat16 [8, 512, 1024], P(('grp', 'dp'), 'sp'), parts along dimension 0
There are 2 independent parts, one for each index of `grp`. A program takes and returns all parts, laid end to end along the dimension named above; each array names one. Nothing has to cross between parts.
Inputs may be any that keep to these rules, and one draw needn't show every extreme that they name: `routing`: among the rows of one column j (rows i with (i // 128) % (4) == j) every owner receives exactly 128 rows; the rows of one device go to each owner in numbers 0, 32 or 64, and every device sends exactly 64 rows to one owner. `group_ids`: every group holds exactly 8 completions.
All inputs are finite; a program needn't handle non-finite values.
Results may differ from a plain program's by a relative error of at most 0.012.
Values may be sent and summed in bfloat16 or wider, within the bound.
No kernel may reach another device: no remote copies, remote signals or barrier semaphores. Data moves between devices by JAX's collectives and lax.ppermute only.
A program may use at most 128 MiB of HBM per device.

v0:
```python
import math

import jax
import jax.numpy as jnp
import numpy as np
from jax import lax
from jax.sharding import PartitionSpec as P

QUERY_HEADS = 32
KEY_VALUE_HEADS = 4
HEAD_SIZE = 128
SEGS = 4
GROUP = 8
TESTS = 10


def slot_layout(row_list, sequence_split_size):
    token_rows = row_list.shape[0]
    per_dev = QUERY_HEADS // sequence_split_size
    query_group = QUERY_HEADS // KEY_VALUE_HEADS
    query_rows = row_list[:, : QUERY_HEADS * HEAD_SIZE].reshape(
        token_rows, sequence_split_size, per_dev * HEAD_SIZE
    )
    key_value_couples = row_list[:, QUERY_HEADS * HEAD_SIZE :].reshape(
        token_rows, 2, KEY_VALUE_HEADS, HEAD_SIZE
    )
    head_table = np.arange(sequence_split_size) * per_dev // query_group
    picked = jnp.transpose(key_value_couples[:, :, head_table, :], (0, 2, 1, 3)).reshape(
        token_rows, sequence_split_size, 2 * HEAD_SIZE
    )
    return jnp.concatenate([query_rows, picked], axis=2)


def group_advantage(passes, group_ids):
    reward = passes.astype(jnp.float32) / TESTS
    labels = jnp.arange(group_ids.shape[0] // GROUP, dtype=jnp.int32)
    member = (group_ids[:, None] == labels[None, :]).astype(jnp.float32)
    group_mean = jnp.sum(member * reward[:, None], axis=0) / jnp.sum(member, axis=0)
    return reward - jnp.sum(member * group_mean[None, :], axis=1)


def body(rollout_rows, routing, segment_labels, upstream, passes, group_ids):
    dp_size = lax.axis_size("dp")
    sequence_split_size = lax.axis_size("sp")
    dp_index = lax.axis_index("dp")
    sp_index = lax.axis_index("sp")
    token_rows = rollout_rows.shape[0]
    row_width = rollout_rows.shape[1]
    capacity = 2 * token_rows // dp_size
    per_dev = QUERY_HEADS // sequence_split_size
    seq_len = sequence_split_size * token_rows
    layout_plan = routing.reshape(dp_size, sequence_split_size, token_rows)
    column_plan = lax.dynamic_index_in_dim(layout_plan, sp_index, axis=1, keepdims=False)
    own_plan = lax.dynamic_index_in_dim(column_plan, dp_index, axis=0, keepdims=False)
    targets = jnp.arange(dp_size, dtype=jnp.int32)
    hit_table = (own_plan[:, None] == targets[None, :]).astype(jnp.int32)
    rank_rows = jnp.sum((jnp.cumsum(hit_table, axis=0) - 1) * hit_table, axis=1)
    slot_ids = own_plan * capacity + rank_rows
    positions = jnp.arange(token_rows, dtype=jnp.int32)
    outgoing = (
        jnp.zeros((dp_size * capacity, row_width), rollout_rows.dtype)
        .at[slot_ids]
        .set(rollout_rows)
    )
    arrived = lax.all_to_all(
        outgoing.reshape(dp_size, capacity, row_width),
        "dp",
        split_axis=0,
        concat_axis=0,
        tiled=True,
    )
    load_table = jnp.sum((column_plan == dp_index).astype(jnp.int32), axis=1)
    end_marks = jnp.cumsum(load_table)
    start_marks = end_marks - load_table
    source = jnp.sum((positions[:, None] >= end_marks[None, :]).astype(jnp.int32), axis=1)
    chosen_start = jnp.sum(
        jnp.where(source[:, None] == targets[None, :], start_marks[None, :], 0), axis=1
    )
    packed_tensor = arrived.reshape(dp_size * capacity, row_width)[
        source * capacity + positions - chosen_start
    ]
    regrouped = lax.all_to_all(
        slot_layout(packed_tensor, sequence_split_size),
        "sp",
        split_axis=1,
        concat_axis=0,
        tiled=True,
    )
    local_rows = regrouped.reshape(seq_len, regrouped.shape[2])
    full_seg = lax.all_gather(segment_labels, "sp", axis=1, tiled=True)[0]
    advantage = group_advantage(passes, group_ids)
    bin_adv = lax.dynamic_slice_in_dim(advantage, dp_index * SEGS, SEGS)
    own_seg = segment_labels[0]
    tok_adv = jnp.sum(
        jnp.where(
            own_seg[:, None] == jnp.arange(SEGS, dtype=jnp.int32)[None, :], bin_adv[None, :], 0.0
        ),
        axis=1,
    )
    weighted_result = (upstream[0].astype(jnp.float32) * tok_adv[:, None]).astype(jnp.bfloat16)
    grads_in = lax.all_to_all(
        weighted_result.reshape(token_rows, sequence_split_size, per_dev * HEAD_SIZE),
        "sp",
        split_axis=1,
        concat_axis=0,
        tiled=True,
    )
    grads_in = grads_in.reshape(seq_len, per_dev, HEAD_SIZE)
    query_rows = local_rows[:, : per_dev * HEAD_SIZE].reshape(seq_len, per_dev, HEAD_SIZE)
    key_matrix = local_rows[:, per_dev * HEAD_SIZE : (per_dev + 1) * HEAD_SIZE]
    value_matrix = local_rows[:, (per_dev + 1) * HEAD_SIZE :]
    block_rows = 512
    inv_root = 1.0 / math.sqrt(HEAD_SIZE)
    key_pos = jnp.arange(seq_len, dtype=jnp.int32)
    key_total = jnp.zeros((seq_len, HEAD_SIZE), jnp.float32)
    value_total = jnp.zeros((seq_len, HEAD_SIZE), jnp.float32)
    query_parts = []
    for block_start in range(0, seq_len, block_rows):
        block_end = block_start + block_rows
        query_block = query_rows[block_start:block_end]
        grad_block = grads_in[block_start:block_end]
        key_part = key_matrix[:block_end]
        value_part = value_matrix[:block_end]
        scores = (
            jnp.einsum("bhd,kd->hbk", query_block, key_part, preferred_element_type=jnp.float32)
            * inv_root
        )
        allowed = (full_seg[block_start:block_end, None] == full_seg[None, :block_end]) & (
            key_pos[None, :block_end] <= key_pos[block_start:block_end, None]
        )
        scores = jnp.where(allowed[None], scores, -1e30)
        row_top = jnp.max(scores, axis=2, keepdims=True)
        scaled_exp = jnp.exp(scores - row_top)
        weights = scaled_exp / jnp.sum(scaled_exp, axis=2, keepdims=True)
        weight_grads = jnp.einsum(
            "bhd,kd->hbk", grad_block, value_part, preferred_element_type=jnp.float32
        )
        row_dot = jnp.sum(weights * weight_grads, axis=2, keepdims=True)
        score_grads = (weights * (weight_grads - row_dot) * inv_root).astype(jnp.bfloat16)
        query_parts.append(
            jnp.einsum(
                "hbk,kd->bhd", score_grads, key_part, preferred_element_type=jnp.float32
            ).astype(jnp.bfloat16)
        )
        key_total = key_total.at[:block_end].add(
            jnp.einsum("hbk,bhd->kd", score_grads, query_block, preferred_element_type=jnp.float32)
        )
        value_total = value_total.at[:block_end].add(
            jnp.einsum(
                "hbk,bhd->kd",
                weights.astype(jnp.bfloat16),
                grad_block,
                preferred_element_type=jnp.float32,
            )
        )
    query_back = jnp.concatenate(query_parts, axis=0).reshape(
        sequence_split_size, token_rows, per_dev * HEAD_SIZE
    )
    query_gradient = lax.all_to_all(query_back, "sp", split_axis=0, concat_axis=2, tiled=True)
    partial_value = jnp.concatenate([key_total, value_total], axis=1).reshape(
        sequence_split_size, token_rows, 2 * HEAD_SIZE
    )
    key_value_pieces = lax.all_to_all(
        partial_value.astype(jnp.bfloat16), "sp", split_axis=0, concat_axis=0, tiled=True
    ).astype(partial_value.dtype)
    summed_total = jnp.sum(
        key_value_pieces.reshape(
            KEY_VALUE_HEADS, sequence_split_size // KEY_VALUE_HEADS, token_rows, 2, HEAD_SIZE
        ),
        axis=1,
    )
    kv_grads = (
        jnp.transpose(summed_total, (1, 2, 0, 3))
        .reshape(1, token_rows, 2 * KEY_VALUE_HEADS * HEAD_SIZE)
        .astype(jnp.bfloat16)
    )
    return (query_gradient, kv_grads)


def solution(mesh):
    return jax.shard_map(
        body,
        mesh=mesh,
        in_specs=(
            P(("grp", "dp", "sp"), None),
            P("grp"),
            P(("grp", "dp"), "sp"),
            P(("grp", "dp"), "sp", None),
            P("grp"),
            P("grp"),
        ),
        out_specs=(P(("grp", "dp"), "sp", None), P(("grp", "dp"), "sp", None)),
        check_vma=False,
    )
```

profile of v0, /device:TPU:0, one launch (start us, length us, event | category | flops | bytes accessed | tf_op | source)
XLA Modules:
  0.0 174.7 jit_solution(5603575321468290316)
XLA Ops:
  2.5 5.0 %scatter_custom_fusion = bf16[256,5120]{1,0:T(8,128)(2,1)} fusion(s32[128]{0:T(128)S(1)} %fusion.32, bf16[128,5120]{1,0:T(8,128)(2,1)} %param.16, bf16[]{:T(256)} %constant.129.clone.1), kind=kCustom, calls=%fused_computation.24 | custom fusion | bytes 2621952 | tf_op jit(solution)/shard_map/scatter | solution.py:63
  7.5 4.2 %all-to-all-start = ((bf16[4,64,5120]{2,1,0:T(8,128)(2,1)}), bf16[4,64,5120]{2,1,0:T(8,128)(2,1)S(1)}, u32[]{:S(2)}, u32[]{:S(2)}) async-start(bf16[4,64,5120]{2,1,0:T(8,128)(2,1)} %bitcast.131), calls=%async_computation | async-start | bytes 5242880 | tf_op jit(solution)/shard_map/all_to_all | solution.py:65
  11.8 3.7 %reshape.279 = f32[128,4,1024]{2,1,0:T(4,128)} reshape(bf16[1,128,4096]{2,1,0:T(8,128)(2,1)} %param.19) | data formatting | bytes 3145728 | tf_op jit(solution)/shard_map/convert_element_type | solution.py:100
  15.9 3.7 %fusion.11 = bf16[128,4,1024]{2,0,1:T(8,128)(2,1)} fusion(f32[128,4,1024]{2,1,0:T(4,128)} %reshape.279, f32[128]{0:T(128)S(1)} %select_reduce_fusion.2), kind=kLoop, calls=%fused_computation.20 | loop fusion | flops 1048576 | bytes 3146240 | tf_op jit(solution)/shard_map/convert_element_type | solution.py:100
  19.6 23.5 %all-to-all-done = bf16[4,64,5120]{2,1,0:T(8,128)(2,1)S(1)} async-done(((bf16[4,64,5120]{2,1,0:T(8,128)(2,1)}), bf16[4,64,5120]{2,1,0:T(8,128)(2,1)S(1)}, u32[]{:S(2)}, u32[]{:S(2)}) %all-to-all-start) | async-done | bytes 2621472 | tf_op jit(solution)/shard_map/all_to_all | solution.py:65
  43.1 5.7 %all-to-all-start.2 = ((bf16[128,4,1024]{2,0,1:T(8,128)(2,1)}), bf16[128,4,1024]{2,0,1:T(8,128)(2,1)}, u32[]{:S(2)}, u32[]{:S(2)}) async-start(bf16[128,4,1024]{2,0,1:T(8,128)(2,1)} %fusion.11), calls=%async_computation.2 | async-start | bytes 2097152 | tf_op jit(solution)/shard_map/all_to_all | solution.py:101
  50.1 2.4 %gather_fusion = bf16[128,5120]{1,0:T(8,128)(2,1)} fusion(bf16[256,5120]{1,0:T(8,128)(2,1)S(1)} %bitcast.129, s32[1024]{0:T(1024)S(1)} %pad_clamp_fusion.1), kind=kCustom, calls=%fused_computation | custom fusion | bytes 2621952 | tf_op jit(solution)/shard_map/gather | solution.py:79
  53.5 1.3 slice.52
  57.2 17.1 %all-to-all-done.2 = bf16[128,4,1024]{2,0,1:T(8,128)(2,1)} async-done(((bf16[128,4,1024]{2,0,1:T(8,128)(2,1)}), bf16[128,4,1024]{2,0,1:T(8,128)(2,1)}, u32[]{:S(2)}, u32[]{:S(2)}) %all-to-all-start.2) | async-done | bytes 1048608 | tf_op jit(solution)/shard_map/all_to_all | solution.py:101
  74.3 3.5 %all-to-all-start.1 = ((bf16[128,4,1280]{2,0,1:T(8,128)(2,1)}), bf16[128,4,1280]{2,0,1:T(8,128)(2,1)S(1)}, u32[]{:S(2)}, u32[]{:S(2)}) async-start(bf16[128,4,1280]{2,0,1:T(8,128)(2,1)} %pad_maximum_fusion), calls=%async_computation.1 | async-start | bytes 2621440 | tf_op jit(solution)/shard_map/all_to_all | solution.py:82
  77.9 26.7 %all_gather.3 = s32[1,512]{1,0:T(1,128)S(1)} all-gather(s32[1,128]{1,0:T(1,128)S(1)} %copy-done.3), channel_id=1, replica_groups=mesh['grp'=2,'dp'=4,'sp'=4] {'sp'}, dimensions={1}, use_global_device_ids=true | all-gather | bytes 2560 | tf_op jit(solution)/shard_map/all_gather | solution.py:90
  104.8 2.6 %copy.83 = bf16[64,8,8,128]{3,2,1,0:T(8,128)(2,1)} copy(bf16[64,8,8,128]{3,1,2,0:T(8,128)(2,1)} %bitcast.57) | data formatting | bytes 2097152
  107.4 1.4 all-to-all-done.1
  109.9 1.5 copy.64
  111.4 1.5 fusion.4
  112.9 1.7 fusion.6
  114.7 3.0 %fusion = (f32[8,512]{1,0:T(8,128)S(1)}, f32[512,512,8]{1,0,2:T(8,128)S(1)}) fusion(f32[8,512]{1,0:T(8,128)S(1)} %fusion.6, f32[8,512]{1,0:T(8,128)S(1)} %get-tuple-element.52, f32[512,512,8]{1,0,2:T(8,128)S(1)} %get-tuple-element.53, pred[512,512]{0,1:T(8,128)(4,1)S(1)} %get-tuple-element.51, bf16[512,8,128]{2,1,0:T(8,128)(2,1)S(1)} %bitcast.141, ...), kind=kOutput, calls=%fused_computation.5 | convolution fusion | flops 549449728 | bytes 18268160 | tf_op jit(solution)/shard_map/bhd,kd->hbk/dot_general | solution.py:135
  117.7 4.6 %multiply_convert_fusion = (bf16[512,512,8]{1,0,2:T(8,128)(2,1)}, bf16[512,512,8]{1,0,2:T(8,128)(2,1)S(1)}) fusion(f32[512,512,8]{1,0,2:T(8,128)S(1)} %get-tuple-element.55, f32[512,8]{0,1:T(8,128)S(1)} %bitcast.150, f32[512,8]{0,1:T(8,128)S(1)} %bitcast.148, f32[512,8]{0,1:T(8,128)S(1)} %bitcast.147, f32[512,512,8]{1,0,2:T(8,128)S(1)} %get-tuple-element.53, ...), kind=kLoop, calls=%fused_computation.10 | loop fusion | flops 18874368 | bytes 25477120 | tf_op jit(solution)/shard_map/convert_element_type | solution.py:139
  122.3 3.6 %fusion.22 = bf16[4,128,128]{1,2,0:T(8,128)(2,1)S(1)} fusion(bf16[4,128,512,8]{2,1,0,3:T(8,128)(2,1)} %bitcast.143, bf16[512,8,128,1]{0,2,3,1:T(8,128)(2,1)S(1)} %bitcast.137), kind=kOutput, calls=%fused_computation.29 | convolution fusion | flops 536936448 | bytes 5373952 | tf_op jit(solution)/shard_map/hbk,bhd->kd/dot_general | solution.py:146
  125.9 1.5 fusion.23
  128.2 7.7 %all-to-all-start.4 = ((bf16[4,128,256]{1,2,0:T(8,128)(2,1)}), bf16[4,128,256]{1,2,0:T(8,128)(2,1)S(1)}, u32[]{:S(2)}, u32[]{:S(2)}) async-start(bf16[4,128,256]{1,2,0:T(8,128)(2,1)} %pad_maximum_fusion.1), calls=%async_computation.4 | async-start | bytes 524288 | tf_op jit(solution)/shard_map/all_to_all | solution.py:163
  135.8 7.8 %fusion.15 = bf16[512,8,128]{0,2,1:T(8,128)(2,1)S(1)} fusion(f32[512,512,8]{1,0,2:T(8,128)} %copy-done.1, f32[8,512]{1,0:T(8,128)S(1)} %get-tuple-element.54, f32[512,512,8]{1,0,2:T(8,128)} %copy-done, f32[8,512]{1,0:T(8,128)S(1)} %fusion.6, f32[8,512]{1,0:T(8,128)S(1)} %get-tuple-element.52, pred[512,512]{0,1:T(8,128)(4,1)S(1)} %get-tuple-element.51, ...), kind=kOutput, calls=%fused_computation.22 | convolution fusion | flops 554172416 | bytes 18268160 | tf_op jit(solution)/shard_map/hbk,kd->bhd/dot_general | solution.py:141
  145.1 5.1 %all-to-all-start.3 = ((bf16[4,128,1024]{1,2,0:T(8,128)(2,1)}), bf16[4,128,1024]{1,2,0:T(8,128)(2,1)S(1)}, u32[]{:S(2)}, u32[]{:S(2)}) async-start(bf16[4,128,1024]{1,2,0:T(8,128)(2,1)} %copy.70), calls=%async_computation.3 | async-start | bytes 2097152 | tf_op jit(solution)/shard_map/all_to_all | solution.py:159
  151.2 22.2 %all-to-all-done.3 = bf16[4,128,1024]{1,2,0:T(8,128)(2,1)S(1)} async-done(((bf16[4,128,1024]{1,2,0:T(8,128)(2,1)}), bf16[4,128,1024]{1,2,0:T(8,128)(2,1)S(1)}, u32[]{:S(2)}, u32[]{:S(2)}) %all-to-all-start.3) | async-done | bytes 1048608 | tf_op jit(solution)/shard_map/all_to_all | solution.py:159
  (50 shorter events, 12.7 us)
Async XLA Ops:
  0.6 14.8 %copy-start.5 = (s32[16]{0:T(128)S(1)}, s32[16]{0:T(128)}, u32[]{:S(2)}) copy-start(s32[16]{0:T(128)} %param.20) | copy-start | bytes 196
  0.6 14.8 %copy-start.4 = (s32[16]{0:T(128)S(1)}, s32[16]{0:T(128)}, u32[]{:S(2)}) copy-start(s32[16]{0:T(128)} %param.21) | copy-start | bytes 196
  0.7 15.1 %copy-start.3 = (s32[1,128]{1,0:T(1,128)S(1)}, s32[1,128]{1,0:T(1,128)}, u32[]{:S(2)}) copy-start(s32[1,128]{1,0:T(1,128)} %param.18) | copy-start | bytes 1540
  7.5 35.6 %all-to-all-start = ((bf16[4,64,5120]{2,1,0:T(8,128)(2,1)}), bf16[4,64,5120]{2,1,0:T(8,128)(2,1)S(1)}, u32[]{:S(2)}, u32[]{:S(2)}) async-start(bf16[4,64,5120]{2,1,0:T(8,128)(2,1)} %bitcast.131), calls=%async_computation | async-start | bytes 5242880 | tf_op jit(solution)/shard_map/all_to_all | solution.py:65
  43.1 31.2 %all-to-all-start.2 = ((bf16[128,4,1024]{2,0,1:T(8,128)(2,1)}), bf16[128,4,1024]{2,0,1:T(8,128)(2,1)}, u32[]{:S(2)}, u32[]{:S(2)}) async-start(bf16[128,4,1024]{2,0,1:T(8,128)(2,1)} %fusion.11), calls=%async_computation.2 | async-start | bytes 2097152 | tf_op jit(solution)/shard_map/all_to_all | solution.py:101
  74.3 34.4 %all-to-all-start.1 = ((bf16[128,4,1280]{2,0,1:T(8,128)(2,1)}), bf16[128,4,1280]{2,0,1:T(8,128)(2,1)S(1)}, u32[]{:S(2)}, u32[]{:S(2)}) async-start(bf16[128,4,1280]{2,0,1:T(8,128)(2,1)} %pad_maximum_fusion), calls=%async_computation.1 | async-start | bytes 2621440 | tf_op jit(solution)/shard_map/all_to_all | solution.py:82
  111.4 3.3 %copy-start.2 = (bf16[64,8,8,128]{3,2,1,0:T(8,128)(2,1)S(1)}, bf16[64,8,8,128]{3,2,1,0:T(8,128)(2,1)}, u32[]{:S(2)}) copy-start(bf16[64,8,8,128]{3,2,1,0:T(8,128)(2,1)} %copy.83) | copy-start | bytes 3145732
  112.9 4.8 %copy-start = (f32[512,512,8]{1,0,2:T(8,128)}, f32[512,512,8]{1,0,2:T(8,128)S(1)}, u32[]{:S(2)}) copy-start(f32[512,512,8]{1,0,2:T(8,128)S(1)} %get-tuple-element.53) | copy-start | bytes 25165828
  117.7 4.6 %copy-start.1 = (f32[512,512,8]{1,0,2:T(8,128)}, f32[512,512,8]{1,0,2:T(8,128)S(1)}, u32[]{:S(2)}) copy-start(f32[512,512,8]{1,0,2:T(8,128)S(1)} %get-tuple-element.55) | copy-start | bytes 25165828
  128.2 16.9 %all-to-all-start.4 = ((bf16[4,128,256]{1,2,0:T(8,128)(2,1)}), bf16[4,128,256]{1,2,0:T(8,128)(2,1)S(1)}, u32[]{:S(2)}, u32[]{:S(2)}) async-start(bf16[4,128,256]{1,2,0:T(8,128)(2,1)} %pad_maximum_fusion.1), calls=%async_computation.4 | async-start | bytes 524288 | tf_op jit(solution)/shard_map/all_to_all | solution.py:163
  145.1 28.4 %all-to-all-start.3 = ((bf16[4,128,1024]{1,2,0:T(8,128)(2,1)}), bf16[4,128,1024]{1,2,0:T(8,128)(2,1)S(1)}, u32[]{:S(2)}, u32[]{:S(2)}) async-start(bf16[4,128,1024]{1,2,0:T(8,128)(2,1)} %copy.70), calls=%async_computation.3 | async-start | bytes 2097152 | tf_op jit(solution)/shard_map/all_to_all | solution.py:159
where the time goes:
time: 176 us; the launch traced here: 175 us
  waiting for transfers between devices  64.2 us (36%)
  blocking collectives  26.7 us (15%)
  starting transfers between devices  26.2 us (15%)
  local copies, waits for them, and re-layouts  24.3 us (14%)
  matrix products  17.5 us (10%)
  other arithmetic  14.9 us (8%)
    all_gather x1, blocking collectives, body(): full_seg = lax.all_gather(segment_labels, 'sp', axis=1, tiled=True)[0]  26.7 us
    all_to_all x1, waiting for transfers between devices, body(): lax.all_to_all(outgoing.reshape(dp_size, capacity, row_width), 'dp', spli...  23.5 us
    all_to_all x1, waiting for transfers between devices, body(): lax.all_to_all(query_back, 'sp', split_axis=0, concat_axis=2, tiled=True)  22.2 us
    all_to_all x1, waiting for transfers between devices, body(): lax.all_to_all(weighted_result.reshape(token_rows, sequence_split_size, p...  17.1 us
    dot_general x1, matrix products, body(): jnp.einsum('hbk,kd->bhd', score_grads, key_part, preferred_element_type=j...  7.8 us
    all_to_all x1, starting transfers between devices, body(): lax.all_to_all(partial_value.astype(jnp.bfloat16), 'sp', split_axis=0, co...  7.66 us
    all_to_all x1, starting transfers between devices, body(): lax.all_to_all(weighted_result.reshape(token_rows, sequence_split_size, p...  5.68 us
    all_to_all x1, starting transfers between devices, body(): lax.all_to_all(query_back, 'sp', split_axis=0, concat_axis=2, tiled=True)  5.09 us
  transfers between devices with their start and end apart: 5, of which 4 were waited for; matrix products, arithmetic and copies ran while one was open for 17% of the time, Pallas kernels for 0%

commit v1 on v0

v1 whole, which is shorter than its diff:
```python
import math

import jax
import jax.numpy as jnp
from jax import lax
from jax.sharding import PartitionSpec as P

QUERY_HEADS = 32
KEY_VALUE_HEADS = 4
HEAD_SIZE = 128
SEGS = 4
GROUP = 8
TESTS = 10


def group_advantage(passes, group_ids):
    reward = passes.astype(jnp.float32) / TESTS
    labels = jnp.arange(group_ids.shape[0] // GROUP, dtype=jnp.int32)
    member = (group_ids[:, None] == labels[None, :]).astype(jnp.float32)
    group_mean = jnp.sum(member * reward[:, None], axis=0) / jnp.sum(member, axis=0)
    return reward - jnp.sum(member * group_mean[None, :], axis=1)


def exchange_rows(rollout_rows, routing, dp_size, sp_size, dp_index, sp_index):
    token_rows = rollout_rows.shape[0]
    capacity = 2 * token_rows // dp_size
    layout_plan = routing.reshape(dp_size, sp_size, token_rows)
    column_plan = lax.dynamic_index_in_dim(layout_plan, sp_index, axis=1, keepdims=False)
    own_plan = lax.dynamic_index_in_dim(column_plan, dp_index, axis=0, keepdims=False)
    targets = jnp.arange(dp_size, dtype=jnp.int32)
    hit_table = (own_plan[:, None] == targets[None, :]).astype(jnp.int32)
    rank_rows = jnp.sum((jnp.cumsum(hit_table, axis=0) - 1) * hit_table, axis=1)
    slot_ids = own_plan * capacity + rank_rows
    slots = jnp.arange(dp_size * capacity, dtype=jnp.int32)
    send_pick = (slots[:, None] == slot_ids[None, :]).astype(rollout_rows.dtype)
    outgoing = jnp.dot(send_pick, rollout_rows, preferred_element_type=jnp.float32).astype(
        rollout_rows.dtype
    )
    arrived = lax.all_to_all(
        outgoing.reshape(dp_size, capacity, -1), "dp", split_axis=0, concat_axis=0, tiled=True
    ).reshape(dp_size * capacity, -1)
    load_table = jnp.sum((column_plan == dp_index).astype(jnp.int32), axis=1)
    end_marks = jnp.cumsum(load_table)
    start_marks = end_marks - load_table
    positions = jnp.arange(token_rows, dtype=jnp.int32)
    source = jnp.sum((positions[:, None] >= end_marks[None, :]).astype(jnp.int32), axis=1)
    chosen_start = jnp.sum(
        jnp.where(source[:, None] == targets[None, :], start_marks[None, :], 0), axis=1
    )
    pick_ids = source * capacity + positions - chosen_start
    recv_pick = (pick_ids[:, None] == slots[None, :]).astype(arrived.dtype)
    return jnp.dot(recv_pick, arrived, preferred_element_type=jnp.float32).astype(arrived.dtype)


def attend(query, grads, key_mat, value_mat, allowed):
    inv_root = 1.0 / math.sqrt(HEAD_SIZE)
    scores = (
        jnp.einsum("tghd,sgd->tghs", query, key_mat, preferred_element_type=jnp.float32) * inv_root
    )
    scores = jnp.where(allowed[:, None, None, :], scores, -1e30)
    row_top = jnp.max(scores, axis=3, keepdims=True)
    scaled_exp = jnp.exp(scores - row_top)
    weights = scaled_exp / jnp.sum(scaled_exp, axis=3, keepdims=True)
    weight_grads = jnp.einsum(
        "tghd,sgd->tghs", grads, value_mat, preferred_element_type=jnp.float32
    )
    row_dot = jnp.sum(weights * weight_grads, axis=3, keepdims=True)
    score_grads = (weights * (weight_grads - row_dot) * inv_root).astype(jnp.bfloat16)
    query_grad = jnp.einsum(
        "tghs,sgd->tghd", score_grads, key_mat, preferred_element_type=jnp.float32
    ).astype(jnp.bfloat16)
    key_part = jnp.einsum("tghs,tghd->sgd", score_grads, query, preferred_element_type=jnp.float32)
    value_part = jnp.einsum(
        "tghs,tghd->sgd", weights.astype(jnp.bfloat16), grads, preferred_element_type=jnp.float32
    )
    return query_grad, key_part, value_part


def body(rollout_rows, routing, segment_labels, upstream, passes, group_ids):
    dp_size = lax.axis_size("dp")
    sp_size = lax.axis_size("sp")
    dp_index = lax.axis_index("dp")
    sp_index = lax.axis_index("sp")
    token_rows = rollout_rows.shape[0]
    query_group = QUERY_HEADS // KEY_VALUE_HEADS
    kv_width = 2 * KEY_VALUE_HEADS * HEAD_SIZE
    seq_len = sp_size * token_rows

    packed = exchange_rows(rollout_rows, routing, dp_size, sp_size, dp_index, sp_index)
    own_seg = segment_labels[0]
    label_cols = jnp.broadcast_to(own_seg.astype(jnp.bfloat16)[:, None], (token_rows, HEAD_SIZE))
    kv_local = jnp.concatenate([packed[:, QUERY_HEADS * HEAD_SIZE :], label_cols], axis=1)
    kv_all = lax.all_gather(kv_local, "sp", axis=0, tiled=True)
    key_mat = kv_all[:, : KEY_VALUE_HEADS * HEAD_SIZE].reshape(seq_len, KEY_VALUE_HEADS, HEAD_SIZE)
    value_mat = kv_all[:, KEY_VALUE_HEADS * HEAD_SIZE : kv_width].reshape(
        seq_len, KEY_VALUE_HEADS, HEAD_SIZE
    )
    key_seg = kv_all[:, kv_width].astype(jnp.int32)

    advantage = group_advantage(passes, group_ids)
    bin_adv = lax.dynamic_slice_in_dim(advantage, dp_index * SEGS, SEGS)
    tok_adv = jnp.sum(
        jnp.where(
            own_seg[:, None] == jnp.arange(SEGS, dtype=jnp.int32)[None, :], bin_adv[None, :], 0.0
        ),
        axis=1,
    )
    weighted = (upstream[0].astype(jnp.float32) * tok_adv[:, None]).astype(jnp.bfloat16)

    query = packed[:, : QUERY_HEADS * HEAD_SIZE].reshape(
        token_rows, KEY_VALUE_HEADS, query_group, HEAD_SIZE
    )
    grads = weighted.reshape(token_rows, KEY_VALUE_HEADS, query_group, HEAD_SIZE)
    query_pos = sp_index * token_rows + jnp.arange(token_rows, dtype=jnp.int32)
    key_pos = jnp.arange(seq_len, dtype=jnp.int32)
    allowed = (own_seg[:, None] == key_seg[None, :]) & (key_pos[None, :] <= query_pos[:, None])

    chunks = max(1, min(KEY_VALUE_HEADS, seq_len // 512))
    if chunks == 1:
        query_grad, key_part, value_part = attend(query, grads, key_mat, value_mat, allowed)
    else:
        per = KEY_VALUE_HEADS // chunks

        def one_chunk(c):
            start = c * per
            return attend(
                lax.dynamic_slice_in_dim(query, start, per, axis=1),
                lax.dynamic_slice_in_dim(grads, start, per, axis=1),
                lax.dynamic_slice_in_dim(key_mat, start, per, axis=1),
                lax.dynamic_slice_in_dim(value_mat, start, per, axis=1),
                allowed,
            )

        qg, kp, vp = lax.map(one_chunk, jnp.arange(chunks, dtype=jnp.int32))
        query_grad = jnp.moveaxis(qg, 0, 1).reshape(token_rows, KEY_VALUE_HEADS, query_group, HEAD_SIZE)
        key_part = jnp.moveaxis(kp, 0, 1).reshape(seq_len, KEY_VALUE_HEADS, HEAD_SIZE)
        value_part = jnp.moveaxis(vp, 0, 1).reshape(seq_len, KEY_VALUE_HEADS, HEAD_SIZE)

    query_gradient = query_grad.reshape(1, token_rows, QUERY_HEADS * HEAD_SIZE)
    partial = jnp.concatenate(
        [
            key_part.reshape(seq_len, KEY_VALUE_HEADS * HEAD_SIZE),
            value_part.reshape(seq_len, KEY_VALUE_HEADS * HEAD_SIZE),
        ],
        axis=1,
    ).astype(jnp.bfloat16)
    kv_grads = lax.psum_scatter(partial, "sp", scatter_dimension=0, tiled=True)
    return (query_gradient, kv_grads.reshape(1, token_rows, kv_width))


def solution(mesh):
    return jax.shard_map(
        body,
        mesh=mesh,
        in_specs=(
            P(("grp", "dp", "sp"), None),
            P("grp"),
            P(("grp", "dp"), "sp"),
            P(("grp", "dp"), "sp", None),
            P("grp"),
            P("grp"),
        ),
        out_specs=(P(("grp", "dp"), "sp", None), P(("grp", "dp"), "sp", None)),
        check_vma=False,
    )
```

time: 176 us -> 158 us (0.90)
  blocking collectives: 26.7 us -> 0 us
  starting transfers between devices: 26.2 us -> 4.62 us
  waiting for transfers between devices: 64.2 us -> 81.2 us
  between operations: 0.91 us -> 14.2 us
  matrix products: 17.5 us -> 27.4 us
  other arithmetic: 14.9 us -> 9.38 us
  local copies, waits for them, and re-layouts: 24.3 us -> 20 us
    all_to_all x5 -> x1, waiting for transfers between devices: 64.2 us -> 30.6 us  [exchange_rows(): lax.all_to_all(outgoing.reshape(dp_size, capacity, -1), 'dp', split_axis=...]
    all_gather x0 -> x1, waiting for transfers between devices: none -> 28.1 us  [body(): kv_all = lax.all_gather(kv_local, 'sp', axis=0, tiled=True)]
    all_gather x1 -> x0, blocking collectives: 26.7 us -> none  [body(): full_seg = lax.all_gather(segment_labels, 'sp', axis=1, tiled=True)[0]]
    reduce_scatter x0 -> x1, waiting for transfers between devices: none -> 22.4 us  [body(): kv_grads = lax.psum_scatter(partial, 'sp', scatter_dimension=0, tiled=True)]
    all_to_all x5 -> x1, starting transfers between devices: 26.2 us -> 4.54 us  [exchange_rows(): lax.all_to_all(outgoing.reshape(dp_size, capacity, -1), 'dp', split_axis=...]
    sub x0 -> x1, matrix products: none -> 11.9 us  [attend(): weight_grads - row_dot]
    convert_element_type x3, other arithmetic: 8.4 us -> 1.14 us  [the longest x1 1.05 us: body(): key_seg = kv_all[:, kv_width].astype(jnp.int32)]
    convert_element_type x2 -> x1, local copies, waits for them, and re-layouts: 1.06 us -> 8 us  [attend(): (weights * (weight_grads - row_dot) * inv_root).astype(jnp.bfloat16)]
  transfers between devices with their start and end apart: 5 -> 3, of which waited for: 4 -> 3; matrix products, arithmetic and copies ran while one was open for 17% -> 6% of each run, Pallas kernels for 0% -> 0%
where the time goes in v1:
time: 158 us; the launch traced here: 157 us
  waiting for transfers between devices  81.2 us (51%)
  matrix products  27.4 us (17%)
  local copies, waits for them, and re-layouts  20 us (13%)
  between operations  14.2 us (9%)
  other arithmetic  9.38 us (6%)
  starting transfers between devices  4.62 us (3%)
    all_to_all x1, waiting for transfers between devices, exchange_rows(): lax.all_to_all(outgoing.reshape(dp_size, capacity, -1), 'dp', split_axis=...  30.6 us
    all_gather x1, waiting for transfers between devices, body(): kv_all = lax.all_gather(kv_local, 'sp', axis=0, tiled=True)  28.1 us
    reduce_scatter x1, waiting for transfers between devices, body(): kv_grads = lax.psum_scatter(partial, 'sp', scatter_dimension=0, tiled=True)  22.4 us
    sub x1, matrix products, attend(): weight_grads - row_dot  11.9 us
    convert_element_type x1, local copies, waits for them, and re-layouts, attend(): (weights * (weight_grads - row_dot) * inv_root).astype(jnp.bfloat16)  8 us
    all_to_all x1, starting transfers between devices, exchange_rows(): lax.all_to_all(outgoing.reshape(dp_size, capacity, -1), 'dp', split_axis=...  4.54 us
    dot_general x1, matrix products, attend(): jnp.einsum('tghs,tghd->sgd', score_grads, query, preferred_element_type=j...  3.78 us
    sub x1, other arithmetic, attend(): scaled_exp = jnp.exp(scores - row_top)  3.52 us
  transfers between devices with their start and end apart: 3, of which 3 were waited for; matrix products, arithmetic and copies ran while one was open for 6% of the time, Pallas kernels for 0%

profile of v1, /device:TPU:0, one launch (start us, length us, event | category | flops | bytes accessed | tf_op | source)
XLA Modules:
  0.0 156.8 jit_solution(13236080469183093057)
XLA Ops:
  7.2 0.8 dynamic-slice_bitcast_fusion
  9.1 2.4 %convolution_convert_fusion = bf16[256,5120]{1,0:T(8,128)(2,1)} fusion(bf16[128,5120]{1,0:T(8,128)(2,1)S(1)} %copy-done, s32[128]{0:T(128)S(1)} %multiply_add_fusion), kind=kOutput, calls=%fused_computation.9 | convolution fusion | flops 336887808 | bytes 3932672 | tf_op jit(solution)/shard_map/dot_general | solution.py:36
  11.5 4.5 %all-to-all-start = ((bf16[4,64,5120]{2,1,0:T(8,128)(2,1)}), bf16[4,64,5120]{2,1,0:T(8,128)(2,1)}, u32[]{:S(2)}, u32[]{:S(2)}) async-start(bf16[4,64,5120]{2,1,0:T(8,128)(2,1)} %bitcast.71), calls=%async_computation | async-start | bytes 5242880 | tf_op jit(solution)/shard_map/all_to_all | solution.py:39
  16.1 0.9 fusion.34
  17.4 30.6 %all-to-all-done = bf16[4,64,5120]{2,1,0:T(8,128)(2,1)} async-done(((bf16[4,64,5120]{2,1,0:T(8,128)(2,1)}), bf16[4,64,5120]{2,1,0:T(8,128)(2,1)}, u32[]{:S(2)}, u32[]{:S(2)}) %all-to-all-start) | async-done | bytes 2621472 | tf_op jit(solution)/shard_map/all_to_all | solution.py:39
  48.1 2.3 %convolution_convert_fusion.1 = bf16[128,5120]{1,0:T(8,128)(2,1)S(1)} fusion(bf16[256,5120]{1,0:T(8,128)(2,1)} %bitcast.5, s32[128]{0:T(128)S(1)} %add_subtract_fusion), kind=kOutput, calls=%fused_computation.11 | convolution fusion | flops 336232448 | bytes 3932672 | tf_op jit(solution)/shard_map/dot_general | solution.py:52
  50.5 0.7 pad_maximum_fusion.1
  51.3 2.6 %copy.59 = f32[1,128,4096]{1,2,0:T(8,128)} copy(bf16[1,128,4096]{2,1,0:T(8,128)(2,1)} %param.9) | data formatting | bytes 3145728 | tf_op jit(solution)/shard_map/convert_element_type | solution.py:108
  54.7 28.1 %all-gather.2.cloned.1.call-done = bf16[512,1152]{1,0:T(8,128)(2,1)} async-done(((bf16[128,1152]{1,0:T(8,128)(2,1)}), bf16[512,1152]{1,0:T(8,128)(2,1)}) %all-gather.2.cloned.1.call-update) | async-done | bytes 1179664 | tf_op jit(solution)/shard_map/all_gather | solution.py:93
  82.8 2.1 %fusion.38 = (bf16[512,512]{1,0:T(8,128)(2,1)}, bf16[512,512]{1,0:T(8,128)(2,1)S(1)}) fusion(bf16[512,1152]{1,0:T(8,128)(2,1)} %all-gather.2.cloned.1.call-done), kind=kLoop, calls=%fused_computation.66 | loop fusion | bytes 2097152 | tf_op jit(solution)/shard_map/slice | solution.py:95
  85.3 1.2 reshape.175
  86.5 1.3 fusion.19
  87.8 1.1 convert_reduce_fusion
  89.0 3.5 %fusion.39 = (f32[128,4,8]{0,2,1:T(8,128)S(1)}, f32[128,4,8,512]{0,3,2,1:T(8,128)S(1)}) fusion(f32[4,512,128,8]{2,1,3,0:T(8,128)S(1)} %fusion.19, pred[128,512]{0,1:T(8,128)(4,1)S(1)} %fusion.30), kind=kOutput, calls=%fused_computation.67 | output fusion | flops 12583423 | bytes 16859136 | tf_op jit(solution)/shard_map/sub | solution.py:62
  92.5 2.8 %fusion.15 = bf16[4,128,512]{2,1,0:T(8,128)(2,1)} fusion(f32[128,4,8,512]{0,3,2,1:T(8,128)S(1)} %get-tuple-element.13, f32[128,4,8]{0,2,1:T(8,128)S(1)} %get-tuple-element.12, f32[128,4,8,128]{0,3,2,1:T(8,128)S(1)} %bitcast.76, f32[128]{0:T(128)S(1)} %select_reduce_fusion.2), kind=kOutput, calls=%fused_computation.23 | convolution fusion | flops 542375936 | bytes 11026944 | tf_op jit(solution)/shard_map/tghs,tghd->sgd/dot_general | solution.py:73
  95.9 11.9 %fusion.4 = bf16[128,4,8,512]{0,3,2,1:T(8,128)(2,1)} fusion(bf16[512,4,128,1]{2,1,0,3:T(4,128)(2,1)S(1)} %bitcast.79, f32[128,4,8,512]{0,3,2,1:T(8,128)} %copy-done.5, f32[128,4,8]{0,2,1:T(8,128)S(1)} %get-tuple-element.12, f32[128,4,8,128]{0,3,2,1:T(8,128)} %bitcast.75, f32[128]{0:T(128)S(1)} %select_reduce_fusion.2), kind=kOutput, calls=%fused_computation.6 | convolution fusion | flops 1090523648 | bytes 15221248 | tf_op jit(solution)/shard_map/sub | solution.py:68
  107.8 1.3 copy.44
  109.0 8.0 %copy.41 = bf16[128,4,8,512]{3,2,1,0:T(8,128)(2,1)} copy(bf16[128,4,8,512]{0,3,2,1:T(8,128)(2,1)} %fusion.4) | data formatting | bytes 8388608 | tf_op jit(solution)/shard_map/convert_element_type | solution.py:68
  117.0 3.8 %fusion.18 = bf16[4,128,512]{2,1,0:T(8,128)(2,1)} fusion(bf16[128,4,8,128]{3,2,1,0:T(8,128)(2,1)S(1)} %bitcast.73, bf16[128,4,8,512]{3,2,1,0:T(8,128)(2,1)} %copy.41), kind=kOutput, calls=%fused_computation.24 | convolution fusion | flops 537133056 | bytes 5767168 | tf_op jit(solution)/shard_map/tghs,tghd->sgd/dot_general | solution.py:72
  120.8 1.3 copy.43
  122.1 1.1 pad_maximum_fusion
  123.2 2.9 %convolution_convert_fusion.2 = bf16[4,128,128,8]{2,1,3,0:T(8,128)(2,1)S(1)} fusion(bf16[512,4,128,1]{0,2,3,1:T(8,128)(2,1)S(1)} %copy.49, bf16[128,4,8,512]{0,3,2,1:T(8,128)(2,1)} %fusion.4), kind=kOutput, calls=%fused_computation.20 | convolution fusion | flops 537395200 | bytes 5767168 | tf_op jit(solution)/shard_map/tghs,sgd->tghd/dot_general | solution.py:69
  126.2 1.3 copy.45
  127.5 22.4 %reduce-scatter.2.cloned.1.call-done = bf16[128,1024]{1,0:T(8,128)(2,1)} async-done(((bf16[512,1024]{1,0:T(8,128)(2,1)}), bf16[128,1024]{1,0:T(8,128)(2,1)}) %reduce-scatter.2.cloned.1.call-update) | async-done | bytes 262160 | tf_op jit(solution)/shard_map/reduce_scatter | solution.py:147
  (41 shorter events, 3.7 us)
Async XLA Ops:
  7.2 2.0 %copy-start = (bf16[128,5120]{1,0:T(8,128)(2,1)S(1)}, bf16[128,5120]{1,0:T(8,128)(2,1)}, u32[]{:S(2)}) copy-start(bf16[128,5120]{1,0:T(8,128)(2,1)} %param.6) | copy-start | bytes 3932164
  9.1 8.3 %copy-start.2 = (s32[1,128]{1,0:T(1,128)S(1)}, s32[1,128]{1,0:T(1,128)}, u32[]{:S(2)}) copy-start(s32[1,128]{1,0:T(1,128)} %param.8) | copy-start | bytes 1540
  11.5 36.6 %all-to-all-start = ((bf16[4,64,5120]{2,1,0:T(8,128)(2,1)}), bf16[4,64,5120]{2,1,0:T(8,128)(2,1)}, u32[]{:S(2)}, u32[]{:S(2)}) async-start(bf16[4,64,5120]{2,1,0:T(8,128)(2,1)} %bitcast.71), calls=%async_computation | async-start | bytes 5242880 | tf_op jit(solution)/shard_map/all_to_all | solution.py:39
  16.0 66.8 %all-gather.2.cloned.1.call-start = ((), (), s32[]{:S(2)}) async-start(), calls=%async_computation.2 | async-start | bytes 1474560 | tf_op jit(solution)/shard_map/all_gather | solution.py:93
  48.1 5.9 %copy-start.4 = (s32[16]{0:T(128)S(1)}, s32[16]{0:T(128)}, u32[]{:S(2)}) copy-start(s32[16]{0:T(128)} %param.10) | copy-start | bytes 196
  48.1 5.9 %copy-start.3 = (s32[16]{0:T(128)S(1)}, s32[16]{0:T(128)}, u32[]{:S(2)}) copy-start(s32[16]{0:T(128)} %param.11) | copy-start | bytes 196
  51.3 98.7 %reduce-scatter.2.cloned.1.call-start = ((), (), s32[]{:S(2)}) async-start(), calls=%async_computation.3 | async-start | bytes 1310720 | tf_op jit(solution)/shard_map/reduce_scatter | solution.py:147
  89.0 3.5 %copy-start.1 = (f32[1,128,4096]{1,2,0:T(8,128)S(1)}, f32[1,128,4096]{1,2,0:T(8,128)}, u32[]{:S(2)}) copy-start(f32[1,128,4096]{1,2,0:T(8,128)} %copy.59) | copy-start | bytes 6291460
  92.5 3.4 %copy-start.5 = (f32[128,4,8,512]{0,3,2,1:T(8,128)}, f32[128,4,8,512]{0,3,2,1:T(8,128)S(1)}, u32[]{:S(2)}) copy-start(f32[128,4,8,512]{0,3,2,1:T(8,128)S(1)} %get-tuple-element.13) | copy-start | bytes 25165828
Sparse Core Ops, SparseCore 0:
  51.4 31.3 all-gather.1
  123.4 26.5 reduce-scatter.1

commit v2 on v1

--- a/solution.py
+++ b/solution.py
@@ -90,7 +90,11 @@
     own_seg = segment_labels[0]
     label_cols = jnp.broadcast_to(own_seg.astype(jnp.bfloat16)[:, None], (token_rows, HEAD_SIZE))
     kv_local = jnp.concatenate([packed[:, QUERY_HEADS * HEAD_SIZE :], label_cols], axis=1)
-    kv_all = lax.all_gather(kv_local, "sp", axis=0, tiled=True)
+    kv_rel = [kv_local] + [
+        lax.ppermute(kv_local, "sp", [(k, k + shift) for k in range(sp_size - shift)])
+        for shift in range(1, sp_size)
+    ]
+    kv_all = jnp.concatenate(kv_rel, axis=0)
     key_mat = kv_all[:, : KEY_VALUE_HEADS * HEAD_SIZE].reshape(seq_len, KEY_VALUE_HEADS, HEAD_SIZE)
     value_mat = kv_all[:, KEY_VALUE_HEADS * HEAD_SIZE : kv_width].reshape(
         seq_len, KEY_VALUE_HEADS, HEAD_SIZE
@@ -112,8 +116,13 @@
     )
     grads = weighted.reshape(token_rows, KEY_VALUE_HEADS, query_group, HEAD_SIZE)
     query_pos = sp_index * token_rows + jnp.arange(token_rows, dtype=jnp.int32)
-    key_pos = jnp.arange(seq_len, dtype=jnp.int32)
-    allowed = (own_seg[:, None] == key_seg[None, :]) & (key_pos[None, :] <= query_pos[:, None])
+    rel_block = jnp.arange(seq_len, dtype=jnp.int32) // token_rows
+    key_pos = (sp_index - rel_block) * token_rows + jnp.arange(seq_len, dtype=jnp.int32) % token_rows
+    allowed = (
+        (own_seg[:, None] == key_seg[None, :])
+        & (key_pos[None, :] <= query_pos[:, None])
+        & (key_pos[None, :] >= 0)
+    )
 
     chunks = max(1, min(KEY_VALUE_HEADS, seq_len // 512))
     if chunks == 1:
@@ -139,12 +148,19 @@
     query_gradient = query_grad.reshape(1, token_rows, QUERY_HEADS * HEAD_SIZE)
     partial = jnp.concatenate(
         [
-            key_part.reshape(seq_len, KEY_VALUE_HEADS * HEAD_SIZE),
-            value_part.reshape(seq_len, KEY_VALUE_HEADS * HEAD_SIZE),
+            key_part.reshape(sp_size, token_rows, KEY_VALUE_HEADS * HEAD_SIZE),
+            value_part.reshape(sp_size, token_rows, KEY_VALUE_HEADS * HEAD_SIZE),
         ],
-        axis=1,
-    ).astype(jnp.bfloat16)
-    kv_grads = lax.psum_scatter(partial, "sp", scatter_dimension=0, tiled=True)
+        axis=2,
+    )
+    kv_total = partial[0]
+    for shift in range(1, sp_size):
+        kv_total = kv_total + lax.ppermute(
+            partial[shift].astype(jnp.bfloat16),
+            "sp",
+            [(k, k - shift) for k in range(shift, sp_size)],
+        ).astype(jnp.float32)
+    kv_grads = kv_total.astype(jnp.bfloat16)
     return (query_gradient, kv_grads.reshape(1, token_rows, kv_width))
 
 

time: 158 us -> 152 us (0.962)
  the two profiles are of different devices: /device:TPU:0 before, /device:TPU:8 now
where the time goes in v2:
time: 152 us; the launch traced here: 151 us
  waiting for transfers between devices  63.5 us (42%)
  local copies, waits for them, and re-layouts  31.2 us (21%)
  matrix products  24.8 us (16%)
  starting transfers between devices  17.3 us (11%)
  other arithmetic  13.5 us (9%)
    all_to_all x1, waiting for transfers between devices, exchange_rows(): lax.all_to_all(outgoing.reshape(dp_size, capacity, -1), 'dp', split_axis=...  29.4 us
    ppermute x3, waiting for transfers between devices, body(): lax.ppermute(kv_local, 'sp', [(k, k + shift) for k in range(sp_size - shi...  19.5 us
    ppermute x3, waiting for transfers between devices, body(): lax.ppermute(partial[shift].astype(jnp.bfloat16), 'sp', [(k, k - shift) f...  14.6 us
    sub x1, matrix products, attend(): weight_grads - row_dot  11.6 us
    convert_element_type x1, local copies, waits for them, and re-layouts, attend(): (weights * (weight_grads - row_dot) * inv_root).astype(jnp.bfloat16)  8 us
    ppermute x3, starting transfers between devices, body(): lax.ppermute(kv_local, 'sp', [(k, k + shift) for k in range(sp_size - shi...  7.89 us
    unnamed x29, local copies, waits for them, and re-layouts  6.62 us
    ppermute x3, starting transfers between devices, body(): lax.ppermute(partial[shift].astype(jnp.bfloat16), 'sp', [(k, k - shift) f...  4.71 us
  transfers between devices with their start and end apart: 7, of which 5 were waited for; matrix products, arithmetic and copies ran while one was open for 6% of the time, Pallas kernels for 0%

profile of v2, /device:TPU:8, one launch (start us, length us, event | category | flops | bytes accessed | tf_op | source)
XLA Modules:
  0.0 151.1 jit_solution(8230903689094797270)
XLA Ops:
  2.6 2.4 %convolution_convert_fusion = bf16[256,5120]{1,0:T(8,128)(2,1)} fusion(bf16[128,5120]{1,0:T(8,128)(2,1)S(1)} %copy-done, s32[128]{0:T(128)S(1)} %multiply_add_fusion), kind=kOutput, calls=%fused_computation.9 | convolution fusion | flops 336887808 | bytes 3932672 | tf_op jit(solution)/shard_map/dot_general | solution.py:36
  5.0 4.7 %all-to-all-start = ((bf16[4,64,5120]{2,1,0:T(8,128)(2,1)}), bf16[4,64,5120]{2,1,0:T(8,128)(2,1)}, u32[]{:S(2)}, u32[]{:S(2)}) async-start(bf16[4,64,5120]{2,1,0:T(8,128)(2,1)} %bitcast.88), calls=%async_computation | async-start | bytes 5242880 | tf_op jit(solution)/shard_map/all_to_all | solution.py:39
  11.5 29.4 %all-to-all-done = bf16[4,64,5120]{2,1,0:T(8,128)(2,1)} async-done(((bf16[4,64,5120]{2,1,0:T(8,128)(2,1)}), bf16[4,64,5120]{2,1,0:T(8,128)(2,1)}, u32[]{:S(2)}, u32[]{:S(2)}) %all-to-all-start) | async-done | bytes 2621472 | tf_op jit(solution)/shard_map/all_to_all | solution.py:39
  41.0 2.3 %convolution_convert_fusion.1 = bf16[128,5120]{1,0:T(8,128)(2,1)S(1)} fusion(bf16[256,5120]{1,0:T(8,128)(2,1)} %bitcast.5, s32[128]{0:T(128)S(1)} %add_subtract_fusion), kind=kOutput, calls=%fused_computation.11 | convolution fusion | flops 336232448 | bytes 3932672 | tf_op jit(solution)/shard_map/dot_general | solution.py:52
  45.9 5.1 %collective-permute-start.1 = (bf16[128,1152]{1,0:T(8,128)(2,1)}, bf16[128,1152]{1,0:T(8,128)(2,1)S(1)}, u32[]{:S(2)}, u32[]{:S(2)}) collective-permute-start(bf16[128,1152]{1,0:T(8,128)(2,1)} %pad_maximum_fusion.3), channel_id=1, source_target_pairs={{0,2},{1,3},{4,6},{5,7},{8,10},{9,11},{12,14},{13,15},{16,18},{17,... | collective-permute-start | bytes 884744 | tf_op jit(solution)/shard_map/ppermute | solution.py:94
  51.0 2.1 %collective-permute-start = (bf16[128,1152]{1,0:T(8,128)(2,1)}, bf16[128,1152]{1,0:T(8,128)(2,1)}, u32[]{:S(2)}, u32[]{:S(2)}) collective-permute-start(bf16[128,1152]{1,0:T(8,128)(2,1)} %pad_maximum_fusion.3), channel_id=1, source_target_pairs={{0,1},{1,2},{2,3},{4,5},{5,6},{6,7},{8,9},{9,10},{10,11},{12,13},{... | collective-permute-start | bytes 884744 | tf_op jit(solution)/shard_map/ppermute | solution.py:94
  53.1 1.7 %copy.59 = f32[1,128,4096]{1,2,0:T(8,128)} copy(bf16[1,128,4096]{2,1,0:T(8,128)(2,1)S(1)} %copy-done.8) | data formatting | bytes 3145728 | tf_op jit(solution)/shard_map/convert_element_type | solution.py:112
  56.4 13.3 %collective-permute-done.1 = bf16[128,1152]{1,0:T(8,128)(2,1)S(1)} collective-permute-done((bf16[128,1152]{1,0:T(8,128)(2,1)}, bf16[128,1152]{1,0:T(8,128)(2,1)S(1)}, u32[]{:S(2)}, u32[]{:S(2)}) %collective-permute-start.1) | collective-permute-done | bytes 294944 | tf_op jit(solution)/shard_map/ppermute | solution.py:94
  69.6 6.2 %collective-permute-done = bf16[128,1152]{1,0:T(8,128)(2,1)} collective-permute-done((bf16[128,1152]{1,0:T(8,128)(2,1)}, bf16[128,1152]{1,0:T(8,128)(2,1)}, u32[]{:S(2)}, u32[]{:S(2)}) %collective-permute-start) | collective-permute-done | bytes 294944 | tf_op jit(solution)/shard_map/ppermute | solution.py:94
  77.7 2.0 %reshape.223 = bf16[512,4,128]{2,1,0:T(4,128)(2,1)} reshape(bf16[512,512]{1,0:T(8,128)(2,1)} %slice.40) | data formatting | bytes 1048576 | tf_op jit(solution)/shard_map/reshape | solution.py:98
  81.0 2.0 %pad_maximum_fusion.2 = bf16[512,512]{1,0:T(8,128)(2,1)} fusion(bf16[128,1152]{1,0:T(8,128)(2,1)S(1)} %collective-permute-done.2, bf16[128,1152]{1,0:T(8,128)(2,1)} %copy-done.5, bf16[128,1152]{1,0:T(8,128)(2,1)} %collective-permute-done, bf16[128,128]{1,0:T(8,128)(2,1)S(1)} %broadcast_in_dim.32, bf16[128,1024]{1,0:T(8,128)(2,1)S(1)} %slice.39), kind=kLoop, calls=%fused_computation.38 | loop fusion | flops 2621440 | bytes 1703936 | tf_op jit(solution)/shard_map/slice | solution.py:99
  83.0 2.0 %reshape.225 = bf16[512,4,128]{2,1,0:T(4,128)(2,1)} reshape(bf16[512,512]{1,0:T(8,128)(2,1)} %pad_maximum_fusion.2) | data formatting | bytes 1048576 | tf_op jit(solution)/shard_map/reshape | solution.py:99
  87.5 3.5 %fusion.51 = (f32[128,4,8]{0,2,1:T(8,128)S(1)}, f32[128,4,8,512]{0,3,2,1:T(8,128)S(1)}) fusion(f32[4,512,128,8]{2,1,3,0:T(8,128)S(1)} %fusion.16, pred[128,512]{0,1:T(8,128)(4,1)S(1)} %and_and_fusion), kind=kOutput, calls=%fused_computation.93 | output fusion | flops 12583423 | bytes 16859136 | tf_op jit(solution)/shard_map/sub | solution.py:62
  92.5 1.7 %copy-done.12 = f32[128,4,8,512]{0,3,2,1:T(8,128)} copy-done((f32[128,4,8,512]{0,3,2,1:T(8,128)}, f32[128,4,8,512]{0,3,2,1:T(8,128)S(1)}, u32[]{:S(2)}) %copy-start.12) | copy-done | bytes 8388632
  94.3 11.6 %fusion.4 = bf16[128,4,8,512]{0,3,2,1:T(8,128)(2,1)} fusion(bf16[512,4,128,1]{2,1,0,3:T(4,128)(2,1)} %bitcast.95, f32[128,4,8,512]{0,3,2,1:T(8,128)} %copy-done.12, f32[128,4,8]{0,2,1:T(8,128)S(1)} %get-tuple-element.13, f32[128,4,8,128]{0,3,2,1:T(8,128)} %bitcast.92, f32[128]{0:T(128)S(1)} %select_reduce_fusion.2), kind=kOutput, calls=%fused_computation.6 | convolution fusion | flops 1090523648 | bytes 15221248 | tf_op jit(solution)/shard_map/sub | solution.py:68
  108.7 8.0 %copy.41 = bf16[128,4,8,512]{3,2,1,0:T(8,128)(2,1)} copy(bf16[128,4,8,512]{0,3,2,1:T(8,128)(2,1)} %fusion.4) | data formatting | bytes 8388608 | tf_op jit(solution)/shard_map/convert_element_type | solution.py:68
  116.7 4.0 %convolution_bitcast_fusion = f32[512,4,128]{0,2,1:T(8,128)} fusion(bf16[128,4,8,128]{3,2,1,0:T(8,128)(2,1)S(1)} %bitcast.90, bf16[128,4,8,512]{3,2,1,0:T(8,128)(2,1)} %copy.41), kind=kOutput, calls=%fused_computation.26 | convolution fusion | flops 536870912 | bytes 6291456 | tf_op jit(solution)/shard_map/tghs,tghd->sgd/dot_general | solution.py:72
  120.7 2.6 %reshape.227 = f32[4,128,512]{1,0,2:T(4,128)} reshape(f32[512,4,128]{0,2,1:T(8,128)} %convolution_bitcast_fusion) | data formatting | bytes 2097152 | tf_op jit(solution)/shard_map/reshape | solution.py:151
  128.7 1.9 %collective-permute-start.3 = (bf16[128,1024]{1,0:T(8,128)(2,1)}, bf16[128,1024]{1,0:T(8,128)(2,1)}, u32[]{:S(2)}, u32[]{:S(2)}) collective-permute-start(bf16[128,1024]{1,0:T(8,128)(2,1)} %get-tuple-element.10), channel_id=1, source_target_pairs={{1,0},{2,1},{3,2},{5,4},{6,5},{7,6},{9,8},{10,9},{11,10},{13,12},{... | collective-permute-start | bytes 786440 | tf_op jit(solution)/shard_map/ppermute | solution.py:158
  130.6 1.8 %convolution_convert_fusion.2 = bf16[4,128,128,8]{2,1,3,0:T(8,128)(2,1)} fusion(bf16[512,4,128,1]{0,2,3,1:T(8,128)(2,1)S(1)} %copy-done.3, bf16[128,4,8,512]{0,3,2,1:T(8,128)(2,1)S(1)} %copy-done.1), kind=kOutput, calls=%fused_computation.24 | convolution fusion | flops 537395200 | bytes 5767168 | tf_op jit(solution)/shard_map/tghs,sgd->tghd/dot_general | solution.py:69
  132.4 2.3 %copy.45 = bf16[1,128,4096]{2,1,0:T(8,128)(2,1)} copy(bf16[1,128,4096]{1,2,0:T(8,128)(2,1)} %bitcast.91) | data formatting | bytes 2097152
  134.6 5.1 %collective-permute-done.4 = bf16[128,1024]{1,0:T(8,128)(2,1)} collective-permute-done((bf16[128,1024]{1,0:T(8,128)(2,1)}, bf16[128,1024]{1,0:T(8,128)(2,1)}, u32[]{:S(2)}, u32[]{:S(2)}) %collective-permute-start.4) | collective-permute-done | bytes 262176 | tf_op jit(solution)/shard_map/ppermute | solution.py:158
  139.7 9.5 %collective-permute-done.3 = bf16[128,1024]{1,0:T(8,128)(2,1)} collective-permute-done((bf16[128,1024]{1,0:T(8,128)(2,1)}, bf16[128,1024]{1,0:T(8,128)(2,1)}, u32[]{:S(2)}, u32[]{:S(2)}) %collective-permute-start.3) | collective-permute-done | bytes 262176 | tf_op jit(solution)/shard_map/ppermute | solution.py:158
  149.2 2.0 %fusion.33 = bf16[1,128,1024]{2,1,0:T(8,128)(2,1)} fusion(bf16[128,1024]{1,0:T(8,128)(2,1)} %collective-permute-done.5, bf16[128,1024]{1,0:T(8,128)(2,1)} %collective-permute-done.4, bf16[128,1024]{1,0:T(8,128)(2,1)} %collective-permute-done.3, f32[4,128,512]{2,1,0:T(8,128)S(1)} %copy.44, f32[4,128,512]{2,1,0:T(8,128)S(1)} %copy.43), kind=kLoop, calls=%fused_computation.47 | loop fusion | flops 1048576 | bytes 3145728 | tf_op jit(solution)/shard_map/reshape | solution.py:164
  (69 shorter events, 23.3 us)
Async XLA Ops:
  0.6 2.0 %copy-start = (bf16[128,5120]{1,0:T(8,128)(2,1)S(1)}, bf16[128,5120]{1,0:T(8,128)(2,1)}, u32[]{:S(2)}) copy-start(bf16[128,5120]{1,0:T(8,128)(2,1)} %param.6) | copy-start | bytes 3932164
  4.9 5.8 %copy-start.11 = (s32[16]{0:T(128)S(1)}, s32[16]{0:T(128)}, u32[]{:S(2)}) copy-start(s32[16]{0:T(128)} %param.10) | copy-start | bytes 196
  5.0 5.8 %copy-start.10 = (s32[16]{0:T(128)S(1)}, s32[16]{0:T(128)}, u32[]{:S(2)}) copy-start(s32[16]{0:T(128)} %param.11) | copy-start | bytes 196
  5.0 6.3 %copy-start.9 = (s32[1,128]{1,0:T(1,128)S(1)}, s32[1,128]{1,0:T(1,128)}, u32[]{:S(2)}) copy-start(s32[1,128]{1,0:T(1,128)} %param.8) | copy-start | bytes 1540
  5.0 36.0 %all-to-all-start = ((bf16[4,64,5120]{2,1,0:T(8,128)(2,1)}), bf16[4,64,5120]{2,1,0:T(8,128)(2,1)}, u32[]{:S(2)}, u32[]{:S(2)}) async-start(bf16[4,64,5120]{2,1,0:T(8,128)(2,1)} %bitcast.88), calls=%async_computation | async-start | bytes 5242880 | tf_op jit(solution)/shard_map/all_to_all | solution.py:39
  9.6 43.5 %copy-start.8 = (bf16[1,128,4096]{2,1,0:T(8,128)(2,1)S(1)}, bf16[1,128,4096]{2,1,0:T(8,128)(2,1)}, u32[]{:S(2)}) copy-start(bf16[1,128,4096]{2,1,0:T(8,128)(2,1)} %param.9) | copy-start | bytes 3145732
  43.3 1.1 copy-start.4
  45.2 11.2 %collective-permute-start.2 = (bf16[128,1152]{1,0:T(8,128)(2,1)}, bf16[128,1152]{1,0:T(8,128)(2,1)S(1)}, u32[]{:S(2)}, u32[]{:S(2)}) collective-permute-start(bf16[128,1152]{1,0:T(8,128)(2,1)} %pad_maximum_fusion.3), channel_id=1, source_target_pairs={{0,3},{4,7},{8,11},{12,15},{16,19},{20,23},{24,27},{28,31}} | collective-permute-start | bytes 884744 | tf_op jit(solution)/shard_map/ppermute | solution.py:94
  45.9 23.8 %collective-permute-start.1 = (bf16[128,1152]{1,0:T(8,128)(2,1)}, bf16[128,1152]{1,0:T(8,128)(2,1)S(1)}, u32[]{:S(2)}, u32[]{:S(2)}) collective-permute-start(bf16[128,1152]{1,0:T(8,128)(2,1)} %pad_maximum_fusion.3), channel_id=1, source_target_pairs={{0,2},{1,3},{4,6},{5,7},{8,10},{9,11},{12,14},{13,15},{16,18},{17,... | collective-permute-start | bytes 884744 | tf_op jit(solution)/shard_map/ppermute | solution.py:94
  51.0 24.9 %collective-permute-start = (bf16[128,1152]{1,0:T(8,128)(2,1)}, bf16[128,1152]{1,0:T(8,128)(2,1)}, u32[]{:S(2)}, u32[]{:S(2)}) collective-permute-start(bf16[128,1152]{1,0:T(8,128)(2,1)} %pad_maximum_fusion.3), channel_id=1, source_target_pairs={{0,1},{1,2},{2,3},{4,5},{5,6},{6,7},{8,9},{9,10},{10,11},{12,13},{... | collective-permute-start | bytes 884744 | tf_op jit(solution)/shard_map/ppermute | solution.py:94
  69.6 10.1 %copy-start.5 = (bf16[128,1152]{1,0:T(8,128)(2,1)}, bf16[128,1152]{1,0:T(8,128)(2,1)S(1)}, u32[]{:S(2)}) copy-start(bf16[128,1152]{1,0:T(8,128)(2,1)S(1)} %collective-permute-done.1) | copy-start | bytes 884740
  81.0 5.3 %copy-start.2 = (bf16[512,4,128,1]{0,2,3,1:T(8,128)(2,1)}, bf16[512,4,128,1]{0,2,3,1:T(8,128)(2,1)S(1)}, u32[]{:S(2)}) copy-start(bf16[512,4,128,1]{0,2,3,1:T(8,128)(2,1)S(1)} %copy.49) | copy-start | bytes 1572868
  85.0 1.3 copy-start.6
  87.5 3.5 %copy-start.7 = (f32[1,128,4096]{1,2,0:T(8,128)S(1)}, f32[1,128,4096]{1,2,0:T(8,128)}, u32[]{:S(2)}) copy-start(f32[1,128,4096]{1,2,0:T(8,128)} %copy.59) | copy-start | bytes 6291460
  91.0 3.2 %copy-start.12 = (f32[128,4,8,512]{0,3,2,1:T(8,128)}, f32[128,4,8,512]{0,3,2,1:T(8,128)S(1)}, u32[]{:S(2)}) copy-start(f32[128,4,8,512]{0,3,2,1:T(8,128)S(1)} %get-tuple-element.14) | copy-start | bytes 25165828
  124.8 5.8 %copy-start.1 = (bf16[128,4,8,512]{0,3,2,1:T(8,128)(2,1)S(1)}, bf16[128,4,8,512]{0,3,2,1:T(8,128)(2,1)}, u32[]{:S(2)}) copy-start(bf16[128,4,8,512]{0,3,2,1:T(8,128)(2,1)} %fusion.4) | copy-start | bytes 12582916
  124.8 5.8 %copy-start.3 = (bf16[512,4,128,1]{0,2,3,1:T(8,128)(2,1)S(1)}, bf16[512,4,128,1]{0,2,3,1:T(8,128)(2,1)}, u32[]{:S(2)}) copy-start(bf16[512,4,128,1]{0,2,3,1:T(8,128)(2,1)} %copy-done.2) | copy-start | bytes 1572868
  125.9 8.8 %collective-permute-start.5 = (bf16[128,1024]{1,0:T(8,128)(2,1)}, bf16[128,1024]{1,0:T(8,128)(2,1)}, u32[]{:S(2)}, u32[]{:S(2)}) collective-permute-start(bf16[128,1024]{1,0:T(8,128)(2,1)} %get-tuple-element.11), channel_id=1, source_target_pairs={{3,0},{7,4},{11,8},{15,12},{19,16},{23,20},{27,24},{31,28}} | collective-permute-start | bytes 786440 | tf_op jit(solution)/shard_map/ppermute | solution.py:158
  127.4 12.3 %collective-permute-start.4 = (bf16[128,1024]{1,0:T(8,128)(2,1)}, bf16[128,1024]{1,0:T(8,128)(2,1)}, u32[]{:S(2)}, u32[]{:S(2)}) collective-permute-start(bf16[128,1024]{1,0:T(8,128)(2,1)} %get-tuple-element.12), channel_id=1, source_target_pairs={{2,0},{3,1},{6,4},{7,5},{10,8},{11,9},{14,12},{15,13},{18,16},{19,... | collective-permute-start | bytes 786440 | tf_op jit(solution)/shard_map/ppermute | solution.py:158
  128.7 20.5 %collective-permute-start.3 = (bf16[128,1024]{1,0:T(8,128)(2,1)}, bf16[128,1024]{1,0:T(8,128)(2,1)}, u32[]{:S(2)}, u32[]{:S(2)}) collective-permute-start(bf16[128,1024]{1,0:T(8,128)(2,1)} %get-tuple-element.10), channel_id=1, source_target_pairs={{1,0},{2,1},{3,2},{5,4},{6,5},{7,6},{9,8},{10,9},{11,10},{13,12},{... | collective-permute-start | bytes 786440 | tf_op jit(solution)/shard_map/ppermute | solution.py:158

commit v3 on v2

--- a/solution.py
+++ b/solution.py
@@ -84,7 +84,9 @@
     token_rows = rollout_rows.shape[0]
     query_group = QUERY_HEADS // KEY_VALUE_HEADS
     kv_width = 2 * KEY_VALUE_HEADS * HEAD_SIZE
-    seq_len = sp_size * token_rows
+    longest_segment = sp_size * token_rows // 2
+    reach = min(sp_size - 1, (longest_segment + token_rows - 2) // token_rows)
+    seq_len = (reach + 1) * token_rows
 
     packed = exchange_rows(rollout_rows, routing, dp_size, sp_size, dp_index, sp_index)
     own_seg = segment_labels[0]
@@ -92,7 +94,7 @@
     kv_local = jnp.concatenate([packed[:, QUERY_HEADS * HEAD_SIZE :], label_cols], axis=1)
     kv_rel = [kv_local] + [
         lax.ppermute(kv_local, "sp", [(k, k + shift) for k in range(sp_size - shift)])
-        for shift in range(1, sp_size)
+        for shift in range(1, reach + 1)
     ]
     kv_all = jnp.concatenate(kv_rel, axis=0)
     key_mat = kv_all[:, : KEY_VALUE_HEADS * HEAD_SIZE].reshape(seq_len, KEY_VALUE_HEADS, HEAD_SIZE)
@@ -148,13 +150,13 @@
     query_gradient = query_grad.reshape(1, token_rows, QUERY_HEADS * HEAD_SIZE)
     partial = jnp.concatenate(
         [
-            key_part.reshape(sp_size, token_rows, KEY_VALUE_HEADS * HEAD_SIZE),
-            value_part.reshape(sp_size, token_rows, KEY_VALUE_HEADS * HEAD_SIZE),
+            key_part.reshape(reach + 1, token_rows, KEY_VALUE_HEADS * HEAD_SIZE),
+            value_part.reshape(reach + 1, token_rows, KEY_VALUE_HEADS * HEAD_SIZE),
         ],
         axis=2,
     )
     kv_total = partial[0]
-    for shift in range(1, sp_size):
+    for shift in range(1, reach + 1):
         kv_total = kv_total + lax.ppermute(
             partial[shift].astype(jnp.bfloat16),
             "sp",

time: 152 us -> 137 us (0.901)
  the two profiles are of different devices: /device:TPU:8 before, /device:TPU:0 now
where the time goes in v3:
time: 137 us; the launch traced here: 136 us
  waiting for transfers between devices  56.3 us (41%)
  local copies, waits for them, and re-layouts  30.2 us (22%)
  matrix products  23 us (17%)
  starting transfers between devices  16.2 us (12%)
  other arithmetic  9.46 us (7%)
    all_to_all x1, waiting for transfers between devices, exchange_rows(): lax.all_to_all(outgoing.reshape(dp_size, capacity, -1), 'dp', split_axis=...  30.2 us
    ppermute x2, waiting for transfers between devices, body(): lax.ppermute(partial[shift].astype(jnp.bfloat16), 'sp', [(k, k - shift) f...  21 us
    sub x1, matrix products, attend(): weight_grads - row_dot  10 us
    ppermute x2, starting transfers between devices, body(): lax.ppermute(kv_local, 'sp', [(k, k + shift) for k in range(sp_size - shi...  8.96 us
    unnamed x26, local copies, waits for them, and re-layouts  6.62 us
    convert_element_type x1, local copies, waits for them, and re-layouts, attend(): (weights * (weight_grads - row_dot) * inv_root).astype(jnp.bfloat16)  5.06 us
    ppermute x2, waiting for transfers between devices, body(): lax.ppermute(kv_local, 'sp', [(k, k + shift) for k in range(sp_size - shi...  5.02 us
    all_to_all x1, starting transfers between devices, exchange_rows(): lax.all_to_all(outgoing.reshape(dp_size, capacity, -1), 'dp', split_axis=...  4.67 us
  transfers between devices with their start and end apart: 5, of which 5 were waited for; matrix products, arithmetic and copies ran while one was open for 6% of the time, Pallas kernels for 0%

profile of v3, /device:TPU:0, one launch (start us, length us, event | category | flops | bytes accessed | tf_op | source)
XLA Modules:
  0.0 136.0 jit_solution(9975896829985807439)
XLA Ops:
  2.6 2.4 %convolution_convert_fusion = bf16[256,5120]{1,0:T(8,128)(2,1)} fusion(bf16[128,5120]{1,0:T(8,128)(2,1)S(1)} %copy-done, s32[128]{0:T(128)S(1)} %multiply_add_fusion), kind=kOutput, calls=%fused_computation.2 | convolution fusion | flops 336887808 | bytes 3932672 | tf_op jit(solution)/shard_map/dot_general | solution.py:36
  5.0 4.7 %all-to-all-start = ((bf16[4,64,5120]{2,1,0:T(8,128)(2,1)}), bf16[4,64,5120]{2,1,0:T(8,128)(2,1)}, u32[]{:S(2)}, u32[]{:S(2)}) async-start(bf16[4,64,5120]{2,1,0:T(8,128)(2,1)} %bitcast.80), calls=%async_computation | async-start | bytes 5242880 | tf_op jit(solution)/shard_map/all_to_all | solution.py:39
  11.4 30.2 %all-to-all-done = bf16[4,64,5120]{2,1,0:T(8,128)(2,1)} async-done(((bf16[4,64,5120]{2,1,0:T(8,128)(2,1)}), bf16[4,64,5120]{2,1,0:T(8,128)(2,1)}, u32[]{:S(2)}, u32[]{:S(2)}) %all-to-all-start) | async-done | bytes 2621472 | tf_op jit(solution)/shard_map/all_to_all | solution.py:39
  41.7 2.3 %convolution_convert_fusion.1 = bf16[128,5120]{1,0:T(8,128)(2,1)S(1)} fusion(bf16[256,5120]{1,0:T(8,128)(2,1)} %bitcast.5, s32[128]{0:T(128)S(1)} %add_subtract_fusion), kind=kOutput, calls=%fused_computation.10 | convolution fusion | flops 336232448 | bytes 3932672 | tf_op jit(solution)/shard_map/dot_general | solution.py:52
  44.8 4.3 %collective-permute-start = (bf16[128,1152]{1,0:T(8,128)(2,1)}, bf16[128,1152]{1,0:T(8,128)(2,1)S(1)}, u32[]{:S(2)}, u32[]{:S(2)}) collective-permute-start(bf16[128,1152]{1,0:T(8,128)(2,1)} %pad_maximum_fusion.2), channel_id=1, source_target_pairs={{0,1},{1,2},{2,3},{4,5},{5,6},{6,7},{8,9},{9,10},{10,11},{12,13},{... | collective-permute-start | bytes 884744 | tf_op jit(solution)/shard_map/ppermute | solution.py:96
  49.1 4.7 %collective-permute-start.1 = (bf16[128,1152]{1,0:T(8,128)(2,1)}, bf16[128,1152]{1,0:T(8,128)(2,1)S(1)}, u32[]{:S(2)}, u32[]{:S(2)}) collective-permute-start(bf16[128,1152]{1,0:T(8,128)(2,1)} %pad_maximum_fusion.2), channel_id=1, source_target_pairs={{0,2},{1,3},{4,6},{5,7},{8,10},{9,11},{12,14},{13,15},{16,18},{17,... | collective-permute-start | bytes 884744 | tf_op jit(solution)/shard_map/ppermute | solution.py:96
  53.8 2.6 %copy.59 = f32[1,128,4096]{1,2,0:T(8,128)} copy(bf16[1,128,4096]{2,1,0:T(8,128)(2,1)} %param.9) | data formatting | bytes 3145728 | tf_op jit(solution)/shard_map/convert_element_type | solution.py:114
  56.8 4.9 %collective-permute-done.1 = bf16[128,1152]{1,0:T(8,128)(2,1)S(1)} collective-permute-done((bf16[128,1152]{1,0:T(8,128)(2,1)}, bf16[128,1152]{1,0:T(8,128)(2,1)S(1)}, u32[]{:S(2)}, u32[]{:S(2)}) %collective-permute-start.1) | collective-permute-done | bytes 294944 | tf_op jit(solution)/shard_map/ppermute | solution.py:96
  62.6 1.8 %reshape.222 = bf16[384,4,128]{2,1,0:T(4,128)(2,1)} reshape(bf16[384,512]{1,0:T(8,128)(2,1)} %slice.35) | data formatting | bytes 786432 | tf_op jit(solution)/shard_map/reshape | solution.py:100
  67.1 1.9 %fusion.47 = (f32[128,4,8]{0,2,1:T(8,128)S(1)}, f32[128,4,8,384]{0,3,2,1:T(8,128)S(1)}) fusion(f32[4,384,128,8]{2,1,3,0:T(8,128)S(1)} %fusion.15, pred[128,384]{0,1:T(8,128)(4,1)S(1)} %and_and_fusion), kind=kOutput, calls=%fused_computation.88 | output fusion | flops 9437567 | bytes 12648448 | tf_op jit(solution)/shard_map/sub | solution.py:62
  69.0 2.7 %copy-done.10 = f32[128,4,8,384]{0,3,2,1:T(8,128)} copy-done((f32[128,4,8,384]{0,3,2,1:T(8,128)}, f32[128,4,8,384]{0,3,2,1:T(8,128)S(1)}, u32[]{:S(2)}) %copy-start.10) | copy-done | bytes 6291480
  71.7 2.0 %fusion.12 = f32[384,4,128]{0,2,1:T(8,128)} fusion(f32[128,4,8,384]{0,3,2,1:T(8,128)S(1)} %get-tuple-element.13, f32[128,4,8]{0,2,1:T(8,128)S(1)} %get-tuple-element.12, f32[128,4,8,128]{0,3,2,1:T(8,128)S(1)} %bitcast.85, f32[128]{0:T(128)S(1)} %select_reduce_fusion.2), kind=kOutput, calls=%fused_computation.21 | convolution fusion | flops 406847488 | bytes 9191936 | tf_op jit(solution)/shard_map/tghs,tghd->sgd/dot_general | solution.py:73
  73.6 2.3 %copy.44 = f32[384,4,128]{2,1,0:T(4,128)} copy(f32[384,4,128]{0,2,1:T(8,128)} %fusion.12) | data formatting | bytes 1572864 | tf_op jit(solution)/shard_map/tghs,tghd->sgd/transpose | solution.py:73
  75.9 2.3 %reshape.227 = f32[3,128,512]{2,1,0:T(8,128)} reshape(f32[384,4,128]{2,1,0:T(4,128)} %copy.44) | data formatting | bytes 1572864 | tf_op jit(solution)/shard_map/reshape | solution.py:154
  78.2 1.7 %pad_maximum_fusion.1 = bf16[384,512]{1,0:T(8,128)(2,1)} fusion(bf16[128,1152]{1,0:T(8,128)(2,1)} %copy-done.4, bf16[128,1152]{1,0:T(8,128)(2,1)} %copy-done.2, bf16[128,128]{1,0:T(8,128)(2,1)S(1)} %broadcast_in_dim.32, bf16[128,1024]{1,0:T(8,128)(2,1)S(1)} %slice.34), kind=kLoop, calls=%fused_computation.32 | loop fusion | flops 1572864 | bytes 1277952 | tf_op jit(solution)/shard_map/slice | solution.py:101
  80.0 1.8 %reshape.224 = bf16[384,4,128]{2,1,0:T(4,128)(2,1)} reshape(bf16[384,512]{1,0:T(8,128)(2,1)} %pad_maximum_fusion.1) | data formatting | bytes 786432 | tf_op jit(solution)/shard_map/reshape | solution.py:101
  81.8 10.0 %fusion.4 = bf16[128,4,8,384]{0,3,2,1:T(8,128)(2,1)} fusion(bf16[384,4,128,1]{2,1,0,3:T(4,128)(2,1)} %bitcast.87, f32[128,4,8,384]{0,3,2,1:T(8,128)} %copy-done.10, f32[128,4,8]{0,2,1:T(8,128)S(1)} %get-tuple-element.12, f32[128,4,8,128]{0,3,2,1:T(8,128)} %bitcast.84, f32[128]{0:T(128)S(1)} %select_reduce_fusion.2), kind=kOutput, calls=%fused_computation.7 | convolution fusion | flops 818418048 | bytes 11944448 | tf_op jit(solution)/shard_map/sub | solution.py:68
  91.9 5.1 %copy.41 = bf16[128,4,8,384]{3,2,1,0:T(8,128)(2,1)} copy(bf16[128,4,8,384]{0,3,2,1:T(8,128)(2,1)} %fusion.4) | data formatting | bytes 6291456 | tf_op jit(solution)/shard_map/convert_element_type | solution.py:68
  96.9 3.5 %convolution_bitcast_fusion = f32[384,4,128]{0,2,1:T(8,128)} fusion(bf16[128,4,8,128]{3,2,1,0:T(8,128)(2,1)S(1)} %bitcast.82, bf16[128,4,8,384]{3,2,1,0:T(8,128)(2,1)} %copy.41), kind=kOutput, calls=%fused_computation.22 | convolution fusion | flops 402653184 | bytes 4980736 | tf_op jit(solution)/shard_map/tghs,tghd->sgd/dot_general | solution.py:72
  109.2 1.7 %convolution_convert_fusion.2 = bf16[4,128,128,8]{2,1,3,0:T(8,128)(2,1)} fusion(bf16[384,4,128,1]{0,2,3,1:T(8,128)(2,1)S(1)} %copy.49, bf16[128,4,8,384]{0,3,2,1:T(8,128)(2,1)S(1)} %copy-done.1), kind=kOutput, calls=%fused_computation.20 | convolution fusion | flops 403177472 | bytes 4587520 | tf_op jit(solution)/shard_map/tghs,sgd->tghd/dot_general | solution.py:69
  111.0 2.3 %copy.45 = bf16[1,128,4096]{2,1,0:T(8,128)(2,1)} copy(bf16[1,128,4096]{1,2,0:T(8,128)(2,1)} %bitcast.83) | data formatting | bytes 2097152
  113.2 9.3 %collective-permute-done.2 = bf16[128,1024]{1,0:T(8,128)(2,1)S(1)} collective-permute-done((bf16[128,1024]{1,0:T(8,128)(2,1)}, bf16[128,1024]{1,0:T(8,128)(2,1)S(1)}, u32[]{:S(2)}, u32[]{:S(2)}) %collective-permute-start.2) | collective-permute-done | bytes 262176 | tf_op jit(solution)/shard_map/ppermute | solution.py:160
  122.5 11.7 %collective-permute-done.3 = bf16[128,1024]{1,0:T(8,128)(2,1)} collective-permute-done((bf16[128,1024]{1,0:T(8,128)(2,1)}, bf16[128,1024]{1,0:T(8,128)(2,1)}, u32[]{:S(2)}, u32[]{:S(2)}) %collective-permute-start.3) | collective-permute-done | bytes 262176 | tf_op jit(solution)/shard_map/ppermute | solution.py:160
  134.2 1.8 %fusion.29 = bf16[1,128,1024]{2,1,0:T(8,128)(2,1)} fusion(bf16[128,1024]{1,0:T(8,128)(2,1)} %collective-permute-done.3, bf16[128,1024]{1,0:T(8,128)(2,1)S(1)} %collective-permute-done.2, f32[3,128,1024]{2,1,0:T(8,128)S(1)} %constant_dynamic-update-slice_fusion), kind=kLoop, calls=%fused_computation.37 | loop fusion | flops 655360 | bytes 1310720 | tf_op jit(solution)/shard_map/reshape | solution.py:166
  (63 shorter events, 17.2 us)
Async XLA Ops:
  0.6 2.0 %copy-start = (bf16[128,5120]{1,0:T(8,128)(2,1)S(1)}, bf16[128,5120]{1,0:T(8,128)(2,1)}, u32[]{:S(2)}) copy-start(bf16[128,5120]{1,0:T(8,128)(2,1)} %param.6) | copy-start | bytes 3932164
  4.9 5.7 %copy-start.9 = (s32[16]{0:T(128)S(1)}, s32[16]{0:T(128)}, u32[]{:S(2)}) copy-start(s32[16]{0:T(128)} %param.10) | copy-start | bytes 196
  5.0 5.7 %copy-start.8 = (s32[16]{0:T(128)S(1)}, s32[16]{0:T(128)}, u32[]{:S(2)}) copy-start(s32[16]{0:T(128)} %param.11) | copy-start | bytes 196
  5.0 6.2 %copy-start.7 = (s32[1,128]{1,0:T(1,128)S(1)}, s32[1,128]{1,0:T(1,128)}, u32[]{:S(2)}) copy-start(s32[1,128]{1,0:T(1,128)} %param.8) | copy-start | bytes 1540
  5.0 36.7 %all-to-all-start = ((bf16[4,64,5120]{2,1,0:T(8,128)(2,1)}), bf16[4,64,5120]{2,1,0:T(8,128)(2,1)}, u32[]{:S(2)}, u32[]{:S(2)}) async-start(bf16[4,64,5120]{2,1,0:T(8,128)(2,1)} %bitcast.80), calls=%async_computation | async-start | bytes 5242880 | tf_op jit(solution)/shard_map/all_to_all | solution.py:39
  44.8 12.0 %collective-permute-start = (bf16[128,1152]{1,0:T(8,128)(2,1)}, bf16[128,1152]{1,0:T(8,128)(2,1)S(1)}, u32[]{:S(2)}, u32[]{:S(2)}) collective-permute-start(bf16[128,1152]{1,0:T(8,128)(2,1)} %pad_maximum_fusion.2), channel_id=1, source_target_pairs={{0,1},{1,2},{2,3},{4,5},{5,6},{6,7},{8,9},{9,10},{10,11},{12,13},{... | collective-permute-start | bytes 884744 | tf_op jit(solution)/shard_map/ppermute | solution.py:96
  49.1 12.6 %collective-permute-start.1 = (bf16[128,1152]{1,0:T(8,128)(2,1)}, bf16[128,1152]{1,0:T(8,128)(2,1)S(1)}, u32[]{:S(2)}, u32[]{:S(2)}) collective-permute-start(bf16[128,1152]{1,0:T(8,128)(2,1)} %pad_maximum_fusion.2), channel_id=1, source_target_pairs={{0,2},{1,3},{4,6},{5,7},{8,10},{9,11},{12,14},{13,15},{16,18},{17,... | collective-permute-start | bytes 884744 | tf_op jit(solution)/shard_map/ppermute | solution.py:96
  56.8 7.6 %copy-start.2 = (bf16[128,1152]{1,0:T(8,128)(2,1)}, bf16[128,1152]{1,0:T(8,128)(2,1)S(1)}, u32[]{:S(2)}) copy-start(bf16[128,1152]{1,0:T(8,128)(2,1)S(1)} %collective-permute-done) | copy-start | bytes 884740
  61.7 2.7 %copy-start.4 = (bf16[128,1152]{1,0:T(8,128)(2,1)}, bf16[128,1152]{1,0:T(8,128)(2,1)S(1)}, u32[]{:S(2)}) copy-start(bf16[128,1152]{1,0:T(8,128)(2,1)S(1)} %collective-permute-done.1) | copy-start | bytes 884740
  65.6 1.1 copy-start.3
  65.7 1.1 copy-start.5
  67.1 4.5 %copy-start.6 = (f32[1,128,4096]{1,2,0:T(8,128)S(1)}, f32[1,128,4096]{1,2,0:T(8,128)}, u32[]{:S(2)}) copy-start(f32[1,128,4096]{1,2,0:T(8,128)} %copy.59) | copy-start | bytes 6291460
  69.0 2.7 %copy-start.10 = (f32[128,4,8,384]{0,3,2,1:T(8,128)}, f32[128,4,8,384]{0,3,2,1:T(8,128)S(1)}, u32[]{:S(2)}) copy-start(f32[128,4,8,384]{0,3,2,1:T(8,128)S(1)} %get-tuple-element.13) | copy-start | bytes 18874372
  103.1 6.1 %copy-start.1 = (bf16[128,4,8,384]{0,3,2,1:T(8,128)(2,1)S(1)}, bf16[128,4,8,384]{0,3,2,1:T(8,128)(2,1)}, u32[]{:S(2)}) copy-start(bf16[128,4,8,384]{0,3,2,1:T(8,128)(2,1)} %fusion.4) | copy-start | bytes 9437188
  106.6 15.9 %collective-permute-start.2 = (bf16[128,1024]{1,0:T(8,128)(2,1)}, bf16[128,1024]{1,0:T(8,128)(2,1)S(1)}, u32[]{:S(2)}, u32[]{:S(2)}) collective-permute-start(bf16[128,1024]{1,0:T(8,128)(2,1)} %get-tuple-element.10), channel_id=1, source_target_pairs={{1,0},{2,1},{3,2},{5,4},{6,5},{7,6},{9,8},{10,9},{11,10},{13,12},{... | collective-permute-start | bytes 786440 | tf_op jit(solution)/shard_map/ppermute | solution.py:160
  107.9 26.3 %collective-permute-start.3 = (bf16[128,1024]{1,0:T(8,128)(2,1)}, bf16[128,1024]{1,0:T(8,128)(2,1)}, u32[]{:S(2)}, u32[]{:S(2)}) collective-permute-start(bf16[128,1024]{1,0:T(8,128)(2,1)} %get-tuple-element.11), channel_id=1, source_target_pairs={{2,0},{3,1},{6,4},{7,5},{10,8},{11,9},{14,12},{15,13},{18,16},{19,... | collective-permute-start | bytes 786440 | tf_op jit(solution)/shard_map/ppermute | solution.py:160

commit v4 on v3

--- a/solution.py
+++ b/solution.py
@@ -3,6 +3,7 @@
 import jax
 import jax.numpy as jnp
 from jax import lax
+from jax.experimental import pallas as pl
 from jax.sharding import PartitionSpec as P
 
 QUERY_HEADS = 32
@@ -76,6 +77,80 @@
     return query_grad, key_part, value_part
 
 
+def attend_kernel(q_ref, g_ref, k_ref, v_ref, m_ref, dq_ref, kp_ref, vp_ref):
+    inv_root = 1.0 / math.sqrt(HEAD_SIZE)
+    key_mat = k_ref[...]
+    value_mat = v_ref[...]
+    allowed = m_ref[...] > 0.5
+    key_sum = jnp.zeros(kp_ref.shape, jnp.float32)
+    value_sum = jnp.zeros(vp_ref.shape, jnp.float32)
+    for head in range(q_ref.shape[1] // HEAD_SIZE):
+        cols = slice(head * HEAD_SIZE, (head + 1) * HEAD_SIZE)
+        query_head = q_ref[:, cols]
+        grad_head = g_ref[:, cols]
+        scores = (
+            lax.dot_general(
+                query_head, key_mat, (((1,), (1,)), ((), ())), preferred_element_type=jnp.float32
+            )
+            * inv_root
+        )
+        scores = jnp.where(allowed, scores, -1e30)
+        row_top = jnp.max(scores, axis=1, keepdims=True)
+        scaled_exp = jnp.exp(scores - row_top)
+        weights = scaled_exp / jnp.sum(scaled_exp, axis=1, keepdims=True)
+        weight_grads = lax.dot_general(
+            grad_head, value_mat, (((1,), (1,)), ((), ())), preferred_element_type=jnp.float32
+        )
+        row_dot = jnp.sum(weights * weight_grads, axis=1, keepdims=True)
+        score_grads = (weights * (weight_grads - row_dot) * inv_root).astype(jnp.bfloat16)
+        dq_ref[:, cols] = jnp.dot(
+            score_grads, key_mat, preferred_element_type=jnp.float32
+        ).astype(dq_ref.dtype)
+        key_sum = key_sum + lax.dot_general(
+            score_grads, query_head, (((0,), (0,)), ((), ())), preferred_element_type=jnp.float32
+        )
+        value_sum = value_sum + lax.dot_general(
+            weights.astype(jnp.bfloat16),
+            grad_head,
+            (((0,), (0,)), ((), ())),
+            preferred_element_type=jnp.float32,
+        )
+    kp_ref[...] = key_sum
+    vp_ref[...] = value_sum
+
+
+def attend_pallas(packed, weighted, kv_all, mask):
+    token_rows = packed.shape[0]
+    key_rows = kv_all.shape[0]
+    group_width = QUERY_HEADS // KEY_VALUE_HEADS * HEAD_SIZE
+    flops = 10 * token_rows * key_rows * HEAD_SIZE * QUERY_HEADS
+    bytes_accessed = 2 * (3 * token_rows * QUERY_HEADS * HEAD_SIZE) + 2 * key_rows * 1024 * 3 + 4 * token_rows * key_rows
+    return pl.pallas_call(
+        attend_kernel,
+        grid=(KEY_VALUE_HEADS,),
+        in_specs=[
+            pl.BlockSpec((token_rows, group_width), lambda g: (0, g)),
+            pl.BlockSpec((token_rows, group_width), lambda g: (0, g)),
+            pl.BlockSpec((key_rows, HEAD_SIZE), lambda g: (0, g)),
+            pl.BlockSpec((key_rows, HEAD_SIZE), lambda g: (0, KEY_VALUE_HEADS + g)),
+            pl.BlockSpec((token_rows, key_rows), lambda g: (0, 0)),
+        ],
+        out_specs=[
+            pl.BlockSpec((token_rows, group_width), lambda g: (0, g)),
+            pl.BlockSpec((key_rows, HEAD_SIZE), lambda g: (0, g)),
+            pl.BlockSpec((key_rows, HEAD_SIZE), lambda g: (0, g)),
+        ],
+        out_shape=[
+            jax.ShapeDtypeStruct((token_rows, QUERY_HEADS * HEAD_SIZE), jnp.bfloat16),
+            jax.ShapeDtypeStruct((key_rows, KEY_VALUE_HEADS * HEAD_SIZE), jnp.float32),
+            jax.ShapeDtypeStruct((key_rows, KEY_VALUE_HEADS * HEAD_SIZE), jnp.float32),
+        ],
+        cost_estimate=pl.CostEstimate(
+            flops=flops, transcendentals=token_rows * key_rows * QUERY_HEADS, bytes_accessed=bytes_accessed
+        ),
+    )(packed, weighted, kv_all, kv_all, mask)
+
+
 def body(rollout_rows, routing, segment_labels, upstream, passes, group_ids):
     dp_size = lax.axis_size("dp")
     sp_size = lax.axis_size("sp")
@@ -97,10 +172,6 @@
         for shift in range(1, reach + 1)
     ]
     kv_all = jnp.concatenate(kv_rel, axis=0)
-    key_mat = kv_all[:, : KEY_VALUE_HEADS * HEAD_SIZE].reshape(seq_len, KEY_VALUE_HEADS, HEAD_SIZE)
-    value_mat = kv_all[:, KEY_VALUE_HEADS * HEAD_SIZE : kv_width].reshape(
-        seq_len, KEY_VALUE_HEADS, HEAD_SIZE
-    )
     key_seg = kv_all[:, kv_width].astype(jnp.int32)
 
     advantage = group_advantage(passes, group_ids)
@@ -113,10 +184,6 @@
     )
     weighted = (upstream[0].astype(jnp.float32) * tok_adv[:, None]).astype(jnp.bfloat16)
 
-    query = packed[:, : QUERY_HEADS * HEAD_SIZE].reshape(
-        token_rows, KEY_VALUE_HEADS, query_group, HEAD_SIZE
-    )
-    grads = weighted.reshape(token_rows, KEY_VALUE_HEADS, query_group, HEAD_SIZE)
     query_pos = sp_index * token_rows + jnp.arange(token_rows, dtype=jnp.int32)
     rel_block = jnp.arange(seq_len, dtype=jnp.int32) // token_rows
     key_pos = (sp_index - rel_block) * token_rows + jnp.arange(seq_len, dtype=jnp.int32) % token_rows
@@ -125,28 +192,9 @@
         & (key_pos[None, :] <= query_pos[:, None])
         & (key_pos[None, :] >= 0)
     )
-
-    chunks = max(1, min(KEY_VALUE_HEADS, seq_len // 512))
-    if chunks == 1:
-        query_grad, key_part, value_part = attend(query, grads, key_mat, value_mat, allowed)
-    else:
-        per = KEY_VALUE_HEADS // chunks
-
-        def one_chunk(c):
-            start = c * per
-            return attend(
-                lax.dynamic_slice_in_dim(query, start, per, axis=1),
-                lax.dynamic_slice_in_dim(grads, start, per, axis=1),
-                lax.dynamic_slice_in_dim(key_mat, start, per, axis=1),
-                lax.dynamic_slice_in_dim(value_mat, start, per, axis=1),
-                allowed,
-            )
-
-        qg, kp, vp = lax.map(one_chunk, jnp.arange(chunks, dtype=jnp.int32))
-        query_grad = jnp.moveaxis(qg, 0, 1).reshape(token_rows, KEY_VALUE_HEADS, query_group, HEAD_SIZE)
-        key_part = jnp.moveaxis(kp, 0, 1).reshape(seq_len, KEY_VALUE_HEADS, HEAD_SIZE)
-        value_part = jnp.moveaxis(vp, 0, 1).reshape(seq_len, KEY_VALUE_HEADS, HEAD_SIZE)
-
+    query_grad, key_part, value_part = attend_pallas(
+        packed, weighted, kv_all, allowed.astype(jnp.float32)
+    )
     query_gradient = query_grad.reshape(1, token_rows, QUERY_HEADS * HEAD_SIZE)
     partial = jnp.concatenate(
         [

time: 137 us -> 112 us (0.82)
  local copies, waits for them, and re-layouts: 30.2 us -> 1.04 us
  Pallas kernels: 0 us -> 19.5 us
  matrix products: 23 us -> 4.65 us
  waiting for transfers between devices: 56.3 us -> 61.4 us
  other arithmetic: 9.46 us -> 7.54 us
    pallas_call x0 -> x1, Pallas kernels: none -> 19.5 us  [attend_pallas(): pl.pallas_call(attend_kernel, grid=(KEY_VALUE_HEADS,), in_specs=[pl.Block...]
    sub x1 -> x0, matrix products: 10 us -> none  [attend(): weight_grads - row_dot]
    reshape x5 -> x0, local copies, waits for them, and re-layouts: 8.44 us -> none  [the longest x2 3.07 us: body(): kv_all[:, :KEY_VALUE_HEADS * HEAD_SIZE]]
    dot_general x4 -> x0, matrix products: 8.27 us -> none  [the longest x1 3.54 us: attend(): jnp.einsum('tghs,tghd->sgd', score_grads, query, preferred_element_type=j...]
    convert_element_type x2 -> x0, local copies, waits for them, and re-layouts: 7.63 us -> none  [the longest x1 5.06 us: attend(): (weights * (weight_grads - row_dot) * inv_root).astype(jnp.bfloat16)]
    unnamed x26 -> x18, local copies, waits for them, and re-layouts: 6.62 us -> 0.04 us
    transpose x2 -> x0, local copies, waits for them, and re-layouts: 3.73 us -> none  [the longest x1 2.29 us: attend(): jnp.einsum('tghs,tghd->sgd', weights.astype(jnp.bfloat16), grads, preferr...]
    ppermute x2, waiting for transfers between devices: 21 us -> 24.7 us  [body(): lax.ppermute(partial[shift].astype(jnp.bfloat16), 'sp', [(k, k - shift) f...]
  transfers between devices with their start and end apart: 5 -> 5, of which waited for: 5 -> 5; matrix products, arithmetic and copies ran while one was open for 6% -> 3% of each run, Pallas kernels for 0% -> 0%
where the time goes in v4:
time: 112 us; the launch traced here: 111 us
  waiting for transfers between devices  61.4 us (55%)
  Pallas kernels  19.5 us (17%)
  starting transfers between devices  16.1 us (14%)
  other arithmetic  7.54 us (7%)
  matrix products  4.65 us (4%)
    all_to_all x1, waiting for transfers between devices, exchange_rows(): lax.all_to_all(outgoing.reshape(dp_size, capacity, -1), 'dp', split_axis=...  28.9 us
    ppermute x2, waiting for transfers between devices, body(): lax.ppermute(partial[shift].astype(jnp.bfloat16), 'sp', [(k, k - shift) f...  24.7 us
    pallas_call x1, Pallas kernels, attend_pallas(): pl.pallas_call(attend_kernel, grid=(KEY_VALUE_HEADS,), in_specs=[pl.Block...  19.5 us
    ppermute x2, starting transfers between devices, body(): lax.ppermute(kv_local, 'sp', [(k, k + shift) for k in range(sp_size - shi...  8.8 us
    ppermute x2, waiting for transfers between devices, body(): lax.ppermute(kv_local, 'sp', [(k, k + shift) for k in range(sp_size - shi...  7.75 us
    all_to_all x1, starting transfers between devices, exchange_rows(): lax.all_to_all(outgoing.reshape(dp_size, capacity, -1), 'dp', split_axis=...  4.68 us
    ppermute x2, starting transfers between devices, body(): lax.ppermute(partial[shift].astype(jnp.bfloat16), 'sp', [(k, k - shift) f...  2.58 us
    dot_general x1, matrix products, exchange_rows(): jnp.dot(send_pick, rollout_rows, preferred_element_type=jnp.float32)  2.36 us
  transfers between devices with their start and end apart: 5, of which 5 were waited for; matrix products, arithmetic and copies ran while one was open for 3% of the time, Pallas kernels for 0%

profile of v4, /device:TPU:0, one launch (start us, length us, event | category | flops | bytes accessed | tf_op | source)
XLA Modules:
  0.0 111.1 jit_solution(13637450432225030449)
XLA Ops:
  0.7 0.8 dynamic-slice_bitcast_fusion
  1.5 0.2 reduce_window_sum.18
  1.7 0.2 select_reduce_fusion
  1.9 0.7 multiply_add_fusion
  2.6 2.4 %convolution_convert_fusion = bf16[256,5120]{1,0:T(8,128)(2,1)} fusion(bf16[128,5120]{1,0:T(8,128)(2,1)S(1)} %copy-done, s32[128]{0:T(128)S(1)} %multiply_add_fusion), kind=kOutput, calls=%fused_computation | convolution fusion | flops 336887808 | bytes 3932672 | tf_op jit(solution)/shard_map/dot_general | solution.py:37
  5.0 4.7 %all-to-all-start = ((bf16[4,64,5120]{2,1,0:T(8,128)(2,1)}), bf16[4,64,5120]{2,1,0:T(8,128)(2,1)}, u32[]{:S(2)}, u32[]{:S(2)}) async-start(bf16[4,64,5120]{2,1,0:T(8,128)(2,1)} %bitcast.36), calls=%async_computation | async-start | bytes 5242880 | tf_op jit(solution)/shard_map/all_to_all | solution.py:40
  9.9 0.9 fusion.19
  10.8 0.2 reduce-window.7
  11.2 0.2 select_reduce_fusion.1
  11.5 1.3 %fusion.g_ref = bf16[128,4096]{1,0:T(8,128)(2,1)} fusion(bf16[1,128,4096]{2,1,0:T(8,128)(2,1)S(1)} %copy-done.5, f32[128]{0:T(128)S(1)} %select_reduce_fusion.2), kind=kLoop, calls=%fused_computation.3 | loop fusion | flops 1572864 | bytes 2097664 | tf_op jit(solution)/shard_map/convert_element_type | solution.py:185
  12.7 28.9 %all-to-all-done = bf16[4,64,5120]{2,1,0:T(8,128)(2,1)} async-done(((bf16[4,64,5120]{2,1,0:T(8,128)(2,1)}), bf16[4,64,5120]{2,1,0:T(8,128)(2,1)}, u32[]{:S(2)}, u32[]{:S(2)}) %all-to-all-start) | async-done | bytes 2621472 | tf_op jit(solution)/shard_map/all_to_all | solution.py:40
  41.7 2.3 %convolution_convert_fusion.1.q_ref = bf16[128,5120]{1,0:T(8,128)(2,1)S(1)} fusion(bf16[256,5120]{1,0:T(8,128)(2,1)} %bitcast.5, s32[128]{0:T(128)S(1)} %add_subtract_fusion), kind=kOutput, calls=%fused_computation.1 | convolution fusion | flops 336232448 | bytes 3932672 | tf_op jit(solution)/shard_map/dot_general | solution.py:53
  44.1 4.3 %collective-permute-start = (bf16[128,1152]{1,0:T(8,128)(2,1)S(1)}, bf16[128,1152]{1,0:T(8,128)(2,1)S(1)}, u32[]{:S(2)}, u32[]{:S(2)}) collective-permute-start(bf16[128,1152]{1,0:T(8,128)(2,1)S(1)} %pad_maximum_fusion.2), channel_id=1, source_target_pairs={{0,1},{1,2},{2,3},{4,5},{5,6},{6,7},{8,9},{9,10},{10,11},{12,13},{... | collective-permute-start | bytes 884744 | tf_op jit(solution)/shard_map/ppermute | solution.py:171
  48.4 4.5 %collective-permute-start.1 = (bf16[128,1152]{1,0:T(8,128)(2,1)S(1)}, bf16[128,1152]{1,0:T(8,128)(2,1)S(1)}, u32[]{:S(2)}, u32[]{:S(2)}) collective-permute-start(bf16[128,1152]{1,0:T(8,128)(2,1)S(1)} %pad_maximum_fusion.2), channel_id=1, source_target_pairs={{0,2},{1,3},{4,6},{5,7},{8,10},{9,11},{12,14},{13,15},{16,18},{17,... | collective-permute-start | bytes 884744 | tf_op jit(solution)/shard_map/ppermute | solution.py:171
  53.0 2.8 %collective-permute-done = bf16[128,1152]{1,0:T(8,128)(2,1)S(1)} collective-permute-done((bf16[128,1152]{1,0:T(8,128)(2,1)S(1)}, bf16[128,1152]{1,0:T(8,128)(2,1)S(1)}, u32[]{:S(2)}, u32[]{:S(2)}) %collective-permute-start) | collective-permute-done | bytes 294944 | tf_op jit(solution)/shard_map/ppermute | solution.py:171
  55.8 4.9 %collective-permute-done.1 = bf16[128,1152]{1,0:T(8,128)(2,1)S(1)} collective-permute-done((bf16[128,1152]{1,0:T(8,128)(2,1)S(1)}, bf16[128,1152]{1,0:T(8,128)(2,1)S(1)}, u32[]{:S(2)}, u32[]{:S(2)}) %collective-permute-start.1) | collective-permute-done | bytes 294944 | tf_op jit(solution)/shard_map/ppermute | solution.py:171
  61.0 0.8 and_convert_fusion.m_ref
  61.8 19.5 %shard_map.77 = (bf16[128,4096]{1,0:T(8,128)(2,1)}, f32[384,512]{1,0:T(8,128)}, f32[384,512]{1,0:T(8,128)}) custom-call(bf16[128,5120]{1,0:T(8,128)(2,1)} %copy-done.3, bf16[128,4096]{1,0:T(8,128)(2,1)} %fusion.g_ref, bf16[384,1152]{1,0:T(8,128)(2,1)} %copy-done.4, bf16[384,1152]{1,0:T(8,128)(2,1)} %copy-done.4, f32[128,384]{1,0:T(8,128)} %and_convert_fusion.m_ref), custom_call_target="tpu_custom_call" | custom-call | flops 2013265920 | bytes 5701632 | tf_op jit(solution)/shard_map/pallas_call | solution.py:128
  81.3 1.6 %fusion.1 = bf16[3,128,1024]{2,1,0:T(8,128)(2,1)S(1)} fusion(f32[3,128,512]{2,1,0:T(8,128)} %bitcast.39, f32[3,128,512]{2,1,0:T(8,128)} %bitcast.37), kind=kLoop, calls=%fused_computation.7 | loop fusion | flops 1572864 | bytes 2359296 | tf_op jit(solution)/shard_map/convert.3
  83.0 1.3 %collective-permute-start.2 = (bf16[128,1024]{1,0:T(8,128)(2,1)S(1)}, bf16[128,1024]{1,0:T(8,128)(2,1)S(1)}, u32[]{:S(2)}, u32[]{:S(2)}) collective-permute-start(bf16[128,1024]{1,0:T(8,128)(2,1)S(1)} %get-tuple-element.10), channel_id=1, source_target_pairs={{1,0},{2,1},{3,2},{5,4},{6,5},{7,6},{9,8},{10,9},{11,10},{13,12},{... | collective-permute-start | bytes 786440 | tf_op jit(solution)/shard_map/ppermute | solution.py:208
  84.3 1.3 %collective-permute-start.3 = (bf16[128,1024]{1,0:T(8,128)(2,1)S(1)}, bf16[128,1024]{1,0:T(8,128)(2,1)S(1)}, u32[]{:S(2)}, u32[]{:S(2)}) collective-permute-start(bf16[128,1024]{1,0:T(8,128)(2,1)S(1)} %get-tuple-element.11), channel_id=1, source_target_pairs={{2,0},{3,1},{6,4},{7,5},{10,8},{11,9},{14,12},{15,13},{18,16},{19,... | collective-permute-start | bytes 786440 | tf_op jit(solution)/shard_map/ppermute | solution.py:208
  85.6 13.1 %collective-permute-done.2 = bf16[128,1024]{1,0:T(8,128)(2,1)S(1)} collective-permute-done((bf16[128,1024]{1,0:T(8,128)(2,1)S(1)}, bf16[128,1024]{1,0:T(8,128)(2,1)S(1)}, u32[]{:S(2)}, u32[]{:S(2)}) %collective-permute-start.2) | collective-permute-done | bytes 262176 | tf_op jit(solution)/shard_map/ppermute | solution.py:208
  98.7 11.6 %collective-permute-done.3 = bf16[128,1024]{1,0:T(8,128)(2,1)S(1)} collective-permute-done((bf16[128,1024]{1,0:T(8,128)(2,1)S(1)}, bf16[128,1024]{1,0:T(8,128)(2,1)S(1)}, u32[]{:S(2)}, u32[]{:S(2)}) %collective-permute-start.3) | collective-permute-done | bytes 262176 | tf_op jit(solution)/shard_map/ppermute | solution.py:208
  110.3 0.8 fusion.7
  (39 shorter events, 1.0 us)
Async XLA Ops:
  0.6 2.0 %copy-start = (bf16[128,5120]{1,0:T(8,128)(2,1)S(1)}, bf16[128,5120]{1,0:T(8,128)(2,1)}, u32[]{:S(2)}) copy-start(bf16[128,5120]{1,0:T(8,128)(2,1)} %param.6) | copy-start | bytes 3932164
  5.0 4.7 %copy-start.8 = (s32[16]{0:T(128)S(1)}, s32[16]{0:T(128)}, u32[]{:S(2)}) copy-start(s32[16]{0:T(128)} %param.10) | copy-start | bytes 196
  5.0 4.7 %copy-start.7 = (s32[16]{0:T(128)S(1)}, s32[16]{0:T(128)}, u32[]{:S(2)}) copy-start(s32[16]{0:T(128)} %param.11) | copy-start | bytes 196
  5.0 6.2 %copy-start.6 = (s32[1,128]{1,0:T(1,128)S(1)}, s32[1,128]{1,0:T(1,128)}, u32[]{:S(2)}) copy-start(s32[1,128]{1,0:T(1,128)} %param.8) | copy-start | bytes 1540
  5.0 6.5 %copy-start.5 = (bf16[1,128,4096]{2,1,0:T(8,128)(2,1)S(1)}, bf16[1,128,4096]{2,1,0:T(8,128)(2,1)}, u32[]{:S(2)}) copy-start(bf16[1,128,4096]{2,1,0:T(8,128)(2,1)} %param.9) | copy-start | bytes 3145732
  5.0 36.7 %all-to-all-start = ((bf16[4,64,5120]{2,1,0:T(8,128)(2,1)}), bf16[4,64,5120]{2,1,0:T(8,128)(2,1)}, u32[]{:S(2)}, u32[]{:S(2)}) async-start(bf16[4,64,5120]{2,1,0:T(8,128)(2,1)} %bitcast.36), calls=%async_computation | async-start | bytes 5242880 | tf_op jit(solution)/shard_map/all_to_all | solution.py:40
  44.0 17.8 %copy-start.3 = (bf16[128,5120]{1,0:T(8,128)(2,1)}, bf16[128,5120]{1,0:T(8,128)(2,1)S(1)}, u32[]{:S(2)}) copy-start(bf16[128,5120]{1,0:T(8,128)(2,1)S(1)} %convolution_convert_fusion.1.q_ref) | copy-start | bytes 3932164
  44.1 11.7 %collective-permute-start = (bf16[128,1152]{1,0:T(8,128)(2,1)S(1)}, bf16[128,1152]{1,0:T(8,128)(2,1)S(1)}, u32[]{:S(2)}, u32[]{:S(2)}) collective-permute-start(bf16[128,1152]{1,0:T(8,128)(2,1)S(1)} %pad_maximum_fusion.2), channel_id=1, source_target_pairs={{0,1},{1,2},{2,3},{4,5},{5,6},{6,7},{8,9},{9,10},{10,11},{12,13},{... | collective-permute-start | bytes 884744 | tf_op jit(solution)/shard_map/ppermute | solution.py:171
  48.4 12.3 %collective-permute-start.1 = (bf16[128,1152]{1,0:T(8,128)(2,1)S(1)}, bf16[128,1152]{1,0:T(8,128)(2,1)S(1)}, u32[]{:S(2)}, u32[]{:S(2)}) collective-permute-start(bf16[128,1152]{1,0:T(8,128)(2,1)S(1)} %pad_maximum_fusion.2), channel_id=1, source_target_pairs={{0,2},{1,3},{4,6},{5,7},{8,10},{9,11},{12,14},{13,15},{16,18},{17,... | collective-permute-start | bytes 884744 | tf_op jit(solution)/shard_map/ppermute | solution.py:171
  60.8 1.0 copy-start.4
  81.3 29.0 %copy-start.1 = (f32[384,512]{1,0:T(8,128)S(1)}, f32[384,512]{1,0:T(8,128)}, u32[]{:S(2)}) copy-start(f32[384,512]{1,0:T(8,128)} %get-tuple-element.6) | copy-start | bytes 2359300
  81.3 29.0 %copy-start.2 = (f32[384,512]{1,0:T(8,128)S(1)}, f32[384,512]{1,0:T(8,128)}, u32[]{:S(2)}) copy-start(f32[384,512]{1,0:T(8,128)} %get-tuple-element.7) | copy-start | bytes 2359300
  83.0 15.7 %collective-permute-start.2 = (bf16[128,1024]{1,0:T(8,128)(2,1)S(1)}, bf16[128,1024]{1,0:T(8,128)(2,1)S(1)}, u32[]{:S(2)}, u32[]{:S(2)}) collective-permute-start(bf16[128,1024]{1,0:T(8,128)(2,1)S(1)} %get-tuple-element.10), channel_id=1, source_target_pairs={{1,0},{2,1},{3,2},{5,4},{6,5},{7,6},{9,8},{10,9},{11,10},{13,12},{... | collective-permute-start | bytes 786440 | tf_op jit(solution)/shard_map/ppermute | solution.py:208
  84.3 26.0 %collective-permute-start.3 = (bf16[128,1024]{1,0:T(8,128)(2,1)S(1)}, bf16[128,1024]{1,0:T(8,128)(2,1)S(1)}, u32[]{:S(2)}, u32[]{:S(2)}) collective-permute-start(bf16[128,1024]{1,0:T(8,128)(2,1)S(1)} %get-tuple-element.11), channel_id=1, source_target_pairs={{2,0},{3,1},{6,4},{7,5},{10,8},{11,9},{14,12},{15,13},{18,16},{19,... | collective-permute-start | bytes 786440 | tf_op jit(solution)/shard_map/ppermute | solution.py:208

commit v5 on v4

--- a/solution.py
+++ b/solution.py
@@ -34,12 +34,17 @@
     slot_ids = own_plan * capacity + rank_rows
     slots = jnp.arange(dp_size * capacity, dtype=jnp.int32)
     send_pick = (slots[:, None] == slot_ids[None, :]).astype(rollout_rows.dtype)
-    outgoing = jnp.dot(send_pick, rollout_rows, preferred_element_type=jnp.float32).astype(
-        rollout_rows.dtype
-    )
-    arrived = lax.all_to_all(
-        outgoing.reshape(dp_size, capacity, -1), "dp", split_axis=0, concat_axis=0, tiled=True
-    ).reshape(dp_size * capacity, -1)
+
+    def send(columns):
+        outgoing = jnp.dot(send_pick, columns, preferred_element_type=jnp.float32).astype(
+            columns.dtype
+        )
+        return lax.all_to_all(
+            outgoing.reshape(dp_size, capacity, -1), "dp", split_axis=0, concat_axis=0, tiled=True
+        ).reshape(dp_size * capacity, -1)
+
+    arrived_kv = send(rollout_rows[:, QUERY_HEADS * HEAD_SIZE :])
+    arrived_q = send(rollout_rows[:, : QUERY_HEADS * HEAD_SIZE])
     load_table = jnp.sum((column_plan == dp_index).astype(jnp.int32), axis=1)
     end_marks = jnp.cumsum(load_table)
     start_marks = end_marks - load_table
@@ -49,8 +54,12 @@
         jnp.where(source[:, None] == targets[None, :], start_marks[None, :], 0), axis=1
     )
     pick_ids = source * capacity + positions - chosen_start
-    recv_pick = (pick_ids[:, None] == slots[None, :]).astype(arrived.dtype)
-    return jnp.dot(recv_pick, arrived, preferred_element_type=jnp.float32).astype(arrived.dtype)
+    recv_pick = (pick_ids[:, None] == slots[None, :]).astype(arrived_kv.dtype)
+
+    def receive(arrived):
+        return jnp.dot(recv_pick, arrived, preferred_element_type=jnp.float32).astype(arrived.dtype)
+
+    return receive(arrived_q), receive(arrived_kv)
 
 
 def attend(query, grads, key_mat, value_mat, allowed):
@@ -163,10 +172,10 @@
     reach = min(sp_size - 1, (longest_segment + token_rows - 2) // token_rows)
     seq_len = (reach + 1) * token_rows
 
-    packed = exchange_rows(rollout_rows, routing, dp_size, sp_size, dp_index, sp_index)
+    packed_q, packed_kv = exchange_rows(rollout_rows, routing, dp_size, sp_size, dp_index, sp_index)
     own_seg = segment_labels[0]
     label_cols = jnp.broadcast_to(own_seg.astype(jnp.bfloat16)[:, None], (token_rows, HEAD_SIZE))
-    kv_local = jnp.concatenate([packed[:, QUERY_HEADS * HEAD_SIZE :], label_cols], axis=1)
+    kv_local = jnp.concatenate([packed_kv, label_cols], axis=1)
     kv_rel = [kv_local] + [
         lax.ppermute(kv_local, "sp", [(k, k + shift) for k in range(sp_size - shift)])
         for shift in range(1, reach + 1)
@@ -193,7 +202,7 @@
         & (key_pos[None, :] >= 0)
     )
     query_grad, key_part, value_part = attend_pallas(
-        packed, weighted, kv_all, allowed.astype(jnp.float32)
+        packed_q, weighted, kv_all, allowed.astype(jnp.float32)
     )
     query_gradient = query_grad.reshape(1, token_rows, QUERY_HEADS * HEAD_SIZE)
     partial = jnp.concatenate(

time: 112 us -> 93.5 us (0.83)
  waiting for transfers between devices: 61.4 us -> 39.2 us
  starting transfers between devices: 16.1 us -> 19.2 us
    all_to_all x1 -> x2, waiting for transfers between devices: 28.9 us -> 10.6 us  [send(): lax.all_to_all(outgoing.reshape(dp_size, capacity, -1), 'dp', split_axis=...]
    ppermute x2, waiting for transfers between devices: 24.7 us -> 20 us  [body(): lax.ppermute(partial[shift].astype(jnp.bfloat16), 'sp', [(k, k - shift) f...]
    all_to_all x1 -> x2, starting transfers between devices: 4.68 us -> 7.97 us  [send(): lax.all_to_all(outgoing.reshape(dp_size, capacity, -1), 'dp', split_axis=...]
    dot_general x2 -> x4, matrix products: 4.65 us -> 5.75 us  [the longest x2 4.02 us: send(): jnp.dot(send_pick, columns, preferred_element_type=jnp.float32)]
  transfers between devices with their start and end apart: 5 -> 6, of which waited for: 5 -> 6; matrix products, arithmetic and copies ran while one was open for 3% -> 7% of each run, Pallas kernels for 0% -> 0%
where the time goes in v5:
time: 93.5 us; the launch traced here: 93 us
  waiting for transfers between devices  39.2 us (42%)
  Pallas kernels  19.4 us (21%)
  starting transfers between devices  19.2 us (21%)
  other arithmetic  7.51 us (8%)
  matrix products  5.75 us (6%)
  local copies, waits for them, and re-layouts  1.01 us (1%)
    ppermute x2, waiting for transfers between devices, body(): lax.ppermute(partial[shift].astype(jnp.bfloat16), 'sp', [(k, k - shift) f...  20 us
    pallas_call x1, Pallas kernels, attend_pallas(): pl.pallas_call(attend_kernel, grid=(KEY_VALUE_HEADS,), in_specs=[pl.Block...  19.4 us
    all_to_all x2, waiting for transfers between devices, send(): lax.all_to_all(outgoing.reshape(dp_size, capacity, -1), 'dp', split_axis=...  10.6 us
    ppermute x2, starting transfers between devices, body(): lax.ppermute(kv_local, 'sp', [(k, k + shift) for k in range(sp_size - shi...  8.68 us
    ppermute x2, waiting for transfers between devices, body(): lax.ppermute(kv_local, 'sp', [(k, k + shift) for k in range(sp_size - shi...  8.68 us
    all_to_all x2, starting transfers between devices, send(): lax.all_to_all(outgoing.reshape(dp_size, capacity, -1), 'dp', split_axis=...  7.97 us
    dot_general x2, matrix products, send(): jnp.dot(send_pick, columns, preferred_element_type=jnp.float32)  4.02 us
    ppermute x2, starting transfers between devices, body(): lax.ppermute(partial[shift].astype(jnp.bfloat16), 'sp', [(k, k - shift) f...  2.58 us
  transfers between devices with their start and end apart: 6, of which 6 were waited for; matrix products, arithmetic and copies ran while one was open for 7% of the time, Pallas kernels for 0%

profile of v5, /device:TPU:0, one launch (start us, length us, event | category | flops | bytes accessed | tf_op | source)
XLA Modules:
  0.0 93.0 jit_solution(3191718135329211118)
XLA Ops:
  0.7 0.8 dynamic-slice_bitcast_fusion
  1.9 0.7 multiply_add_fusion
  2.6 2.0 %convolution_convert_fusion.2 = bf16[256,1024]{1,0:T(8,128)(2,1)} fusion(bf16[128,5120]{1,0:T(8,128)(2,1)} %param.6, s32[128]{0:T(128)S(1)} %multiply_add_fusion), kind=kOutput, calls=%fused_computation.8 | convolution fusion | flops 67403776 | bytes 786944 | tf_op jit(solution)/shard_map/dot_general | solution.py:39
  4.6 4.4 %all-to-all-start.1 = ((bf16[4,64,1024]{2,1,0:T(8,128)(2,1)}), bf16[4,64,1024]{2,1,0:T(8,128)(2,1)S(1)}, u32[]{:S(2)}, u32[]{:S(2)}) async-start(bf16[4,64,1024]{2,1,0:T(8,128)(2,1)} %bitcast.8), calls=%async_computation.1 | async-start | bytes 1048576 | tf_op jit(solution)/shard_map/all_to_all | solution.py:42
  9.0 0.9 fusion.23
  10.8 1.3 %fusion.g_ref = bf16[128,4096]{1,0:T(8,128)(2,1)} fusion(bf16[1,128,4096]{2,1,0:T(8,128)(2,1)S(1)} %copy-done.4, f32[128]{0:T(128)S(1)} %select_reduce_fusion.2), kind=kLoop, calls=%fused_computation.3 | loop fusion | flops 1572864 | bytes 2097664 | tf_op jit(solution)/shard_map/convert_element_type | solution.py:194
  12.0 2.0 %convolution_convert_fusion = bf16[256,4096]{1,0:T(8,128)(2,1)} fusion(bf16[128,5120]{1,0:T(8,128)(2,1)S(1)} %copy-done.2, s32[128]{0:T(128)S(1)} %multiply_add_fusion), kind=kOutput, calls=%fused_computation | convolution fusion | flops 269516800 | bytes 3146240 | tf_op jit(solution)/shard_map/dot_general | solution.py:39
  14.0 3.8 %all-to-all-done.1 = bf16[4,64,1024]{2,1,0:T(8,128)(2,1)S(1)} async-done(((bf16[4,64,1024]{2,1,0:T(8,128)(2,1)}), bf16[4,64,1024]{2,1,0:T(8,128)(2,1)S(1)}, u32[]{:S(2)}, u32[]{:S(2)}) %all-to-all-start.1) | async-done | bytes 524320 | tf_op jit(solution)/shard_map/all_to_all | solution.py:42
  17.8 3.6 %all-to-all-start = ((bf16[4,64,4096]{2,1,0:T(8,128)(2,1)}), bf16[4,64,4096]{2,1,0:T(8,128)(2,1)S(1)}, u32[]{:S(2)}, u32[]{:S(2)}) async-start(bf16[4,64,4096]{2,1,0:T(8,128)(2,1)} %bitcast.4), calls=%async_computation | async-start | bytes 4194304 | tf_op jit(solution)/shard_map/all_to_all | solution.py:42
  21.4 0.3 convolution_convert_fusion.3
  21.8 4.2 %collective-permute-start = (bf16[128,1152]{1,0:T(8,128)(2,1)S(1)}, bf16[128,1152]{1,0:T(8,128)(2,1)S(1)}, u32[]{:S(2)}, u32[]{:S(2)}) collective-permute-start(bf16[128,1152]{1,0:T(8,128)(2,1)S(1)} %pad_maximum_fusion.2), channel_id=1, source_target_pairs={{0,1},{1,2},{2,3},{4,5},{5,6},{6,7},{8,9},{9,10},{10,11},{12,13},{... | collective-permute-start | bytes 884744 | tf_op jit(solution)/shard_map/ppermute | solution.py:180
  26.0 4.5 %collective-permute-start.1 = (bf16[128,1152]{1,0:T(8,128)(2,1)S(1)}, bf16[128,1152]{1,0:T(8,128)(2,1)S(1)}, u32[]{:S(2)}, u32[]{:S(2)}) collective-permute-start(bf16[128,1152]{1,0:T(8,128)(2,1)S(1)} %pad_maximum_fusion.2), channel_id=1, source_target_pairs={{0,2},{1,3},{4,6},{5,7},{8,10},{9,11},{12,14},{13,15},{16,18},{17,... | collective-permute-start | bytes 884744 | tf_op jit(solution)/shard_map/ppermute | solution.py:180
  30.6 2.8 %collective-permute-done = bf16[128,1152]{1,0:T(8,128)(2,1)S(1)} collective-permute-done((bf16[128,1152]{1,0:T(8,128)(2,1)S(1)}, bf16[128,1152]{1,0:T(8,128)(2,1)S(1)}, u32[]{:S(2)}, u32[]{:S(2)}) %collective-permute-start) | collective-permute-done | bytes 294944 | tf_op jit(solution)/shard_map/ppermute | solution.py:180
  33.4 5.9 %collective-permute-done.1 = bf16[128,1152]{1,0:T(8,128)(2,1)S(1)} collective-permute-done((bf16[128,1152]{1,0:T(8,128)(2,1)S(1)}, bf16[128,1152]{1,0:T(8,128)(2,1)S(1)}, u32[]{:S(2)}, u32[]{:S(2)}) %collective-permute-start.1) | collective-permute-done | bytes 294944 | tf_op jit(solution)/shard_map/ppermute | solution.py:180
  39.5 0.8 and_convert_fusion.m_ref
  40.3 6.8 %all-to-all-done = bf16[4,64,4096]{2,1,0:T(8,128)(2,1)S(1)} async-done(((bf16[4,64,4096]{2,1,0:T(8,128)(2,1)}), bf16[4,64,4096]{2,1,0:T(8,128)(2,1)S(1)}, u32[]{:S(2)}, u32[]{:S(2)}) %all-to-all-start) | async-done | bytes 2097184 | tf_op jit(solution)/shard_map/all_to_all | solution.py:42
  47.1 1.5 %convolution_convert_fusion.1.q_ref = bf16[128,4096]{1,0:T(8,128)(2,1)} fusion(bf16[256,4096]{1,0:T(8,128)(2,1)S(1)} %bitcast.38, s32[128]{0:T(128)S(1)} %add_subtract_fusion), kind=kOutput, calls=%fused_computation.1 | convolution fusion | flops 268992512 | bytes 3146240 | tf_op jit(solution)/shard_map/dot_general | solution.py:60
  48.5 19.4 %shard_map.77 = (bf16[128,4096]{1,0:T(8,128)(2,1)}, f32[384,512]{1,0:T(8,128)}, f32[384,512]{1,0:T(8,128)}) custom-call(bf16[128,4096]{1,0:T(8,128)(2,1)} %convolution_convert_fusion.1.q_ref, bf16[128,4096]{1,0:T(8,128)(2,1)} %fusion.g_ref, bf16[384,1152]{1,0:T(8,128)(2,1)} %copy-done.3, bf16[384,1152]{1,0:T(8,128)(2,1)} %copy-done.3, ...), custom_call_target="tpu_custom_call" | custom-call | flops 2013265920 | bytes 5701632 | tf_op jit(solution)/shard_map/pallas_call | solution.py:137
  68.0 1.6 %fusion.1 = bf16[3,128,1024]{2,1,0:T(8,128)(2,1)S(1)} fusion(f32[3,128,512]{2,1,0:T(8,128)} %bitcast.41, f32[3,128,512]{2,1,0:T(8,128)} %bitcast.39), kind=kLoop, calls=%fused_computation.7 | loop fusion | flops 1572864 | bytes 2359296 | tf_op jit(solution)/shard_map/convert.3
  69.6 1.3 %collective-permute-start.2 = (bf16[128,1024]{1,0:T(8,128)(2,1)S(1)}, bf16[128,1024]{1,0:T(8,128)(2,1)S(1)}, u32[]{:S(2)}, u32[]{:S(2)}) collective-permute-start(bf16[128,1024]{1,0:T(8,128)(2,1)S(1)} %get-tuple-element.10), channel_id=1, source_target_pairs={{1,0},{2,1},{3,2},{5,4},{6,5},{7,6},{9,8},{10,9},{11,10},{13,12},{... | collective-permute-start | bytes 786440 | tf_op jit(solution)/shard_map/ppermute | solution.py:217
  70.9 1.3 %collective-permute-start.3 = (bf16[128,1024]{1,0:T(8,128)(2,1)S(1)}, bf16[128,1024]{1,0:T(8,128)(2,1)S(1)}, u32[]{:S(2)}, u32[]{:S(2)}) collective-permute-start(bf16[128,1024]{1,0:T(8,128)(2,1)S(1)} %get-tuple-element.11), channel_id=1, source_target_pairs={{2,0},{3,1},{6,4},{7,5},{10,8},{11,9},{14,12},{15,13},{18,16},{19,... | collective-permute-start | bytes 786440 | tf_op jit(solution)/shard_map/ppermute | solution.py:217
  72.2 7.8 %collective-permute-done.2 = bf16[128,1024]{1,0:T(8,128)(2,1)S(1)} collective-permute-done((bf16[128,1024]{1,0:T(8,128)(2,1)S(1)}, bf16[128,1024]{1,0:T(8,128)(2,1)S(1)}, u32[]{:S(2)}, u32[]{:S(2)}) %collective-permute-start.2) | collective-permute-done | bytes 262176 | tf_op jit(solution)/shard_map/ppermute | solution.py:217
  80.0 12.2 %collective-permute-done.3 = bf16[128,1024]{1,0:T(8,128)(2,1)S(1)} collective-permute-done((bf16[128,1024]{1,0:T(8,128)(2,1)S(1)}, bf16[128,1024]{1,0:T(8,128)(2,1)S(1)}, u32[]{:S(2)}, u32[]{:S(2)}) %collective-permute-start.3) | collective-permute-done | bytes 262176 | tf_op jit(solution)/shard_map/ppermute | solution.py:217
  92.2 0.8 fusion.9
  (40 shorter events, 1.7 us)
Async XLA Ops:
  0.6 9.5 %copy-start.7 = (s32[16]{0:T(128)S(1)}, s32[16]{0:T(128)}, u32[]{:S(2)}) copy-start(s32[16]{0:T(128)} %param.10) | copy-start | bytes 196
  0.6 9.5 %copy-start.6 = (s32[16]{0:T(128)S(1)}, s32[16]{0:T(128)}, u32[]{:S(2)}) copy-start(s32[16]{0:T(128)} %param.11) | copy-start | bytes 196
  0.7 10.0 %copy-start.5 = (s32[1,128]{1,0:T(1,128)S(1)}, s32[1,128]{1,0:T(1,128)}, u32[]{:S(2)}) copy-start(s32[1,128]{1,0:T(1,128)} %param.8) | copy-start | bytes 1540
  0.7 10.1 %copy-start.4 = (bf16[1,128,4096]{2,1,0:T(8,128)(2,1)S(1)}, bf16[1,128,4096]{2,1,0:T(8,128)(2,1)}, u32[]{:S(2)}) copy-start(bf16[1,128,4096]{2,1,0:T(8,128)(2,1)} %param.9) | copy-start | bytes 3145732
  4.6 7.4 %copy-start.2 = (bf16[128,5120]{1,0:T(8,128)(2,1)S(1)}, bf16[128,5120]{1,0:T(8,128)(2,1)}, u32[]{:S(2)}) copy-start(bf16[128,5120]{1,0:T(8,128)(2,1)} %param.6) | copy-start | bytes 3932164
  4.6 13.2 %all-to-all-start.1 = ((bf16[4,64,1024]{2,1,0:T(8,128)(2,1)}), bf16[4,64,1024]{2,1,0:T(8,128)(2,1)S(1)}, u32[]{:S(2)}, u32[]{:S(2)}) async-start(bf16[4,64,1024]{2,1,0:T(8,128)(2,1)} %bitcast.8), calls=%async_computation.1 | async-start | bytes 1048576 | tf_op jit(solution)/shard_map/all_to_all | solution.py:42
  17.8 29.2 %all-to-all-start = ((bf16[4,64,4096]{2,1,0:T(8,128)(2,1)}), bf16[4,64,4096]{2,1,0:T(8,128)(2,1)S(1)}, u32[]{:S(2)}, u32[]{:S(2)}) async-start(bf16[4,64,4096]{2,1,0:T(8,128)(2,1)} %bitcast.4), calls=%async_computation | async-start | bytes 4194304 | tf_op jit(solution)/shard_map/all_to_all | solution.py:42
  21.8 11.6 %collective-permute-start = (bf16[128,1152]{1,0:T(8,128)(2,1)S(1)}, bf16[128,1152]{1,0:T(8,128)(2,1)S(1)}, u32[]{:S(2)}, u32[]{:S(2)}) collective-permute-start(bf16[128,1152]{1,0:T(8,128)(2,1)S(1)} %pad_maximum_fusion.2), channel_id=1, source_target_pairs={{0,1},{1,2},{2,3},{4,5},{5,6},{6,7},{8,9},{9,10},{10,11},{12,13},{... | collective-permute-start | bytes 884744 | tf_op jit(solution)/shard_map/ppermute | solution.py:180
  26.0 13.2 %collective-permute-start.1 = (bf16[128,1152]{1,0:T(8,128)(2,1)S(1)}, bf16[128,1152]{1,0:T(8,128)(2,1)S(1)}, u32[]{:S(2)}, u32[]{:S(2)}) collective-permute-start(bf16[128,1152]{1,0:T(8,128)(2,1)S(1)} %pad_maximum_fusion.2), channel_id=1, source_target_pairs={{0,2},{1,3},{4,6},{5,7},{8,10},{9,11},{12,14},{13,15},{16,18},{17,... | collective-permute-start | bytes 884744 | tf_op jit(solution)/shard_map/ppermute | solution.py:180
  39.3 9.2 %copy-start.3 = (bf16[384,1152]{1,0:T(8,128)(2,1)}, bf16[384,1152]{1,0:T(8,128)(2,1)S(1)}, u32[]{:S(2)}) copy-start(bf16[384,1152]{1,0:T(8,128)(2,1)S(1)} %pad_maximum_fusion.1.k_ref.v_ref) | copy-start | bytes 2654212
  67.9 24.2 %copy-start = (f32[384,512]{1,0:T(8,128)S(1)}, f32[384,512]{1,0:T(8,128)}, u32[]{:S(2)}) copy-start(f32[384,512]{1,0:T(8,128)} %get-tuple-element.6) | copy-start | bytes 2359300
  67.9 24.2 %copy-start.1 = (f32[384,512]{1,0:T(8,128)S(1)}, f32[384,512]{1,0:T(8,128)}, u32[]{:S(2)}) copy-start(f32[384,512]{1,0:T(8,128)} %get-tuple-element.7) | copy-start | bytes 2359300
  69.6 10.4 %collective-permute-start.2 = (bf16[128,1024]{1,0:T(8,128)(2,1)S(1)}, bf16[128,1024]{1,0:T(8,128)(2,1)S(1)}, u32[]{:S(2)}, u32[]{:S(2)}) collective-permute-start(bf16[128,1024]{1,0:T(8,128)(2,1)S(1)} %get-tuple-element.10), channel_id=1, source_target_pairs={{1,0},{2,1},{3,2},{5,4},{6,5},{7,6},{9,8},{10,9},{11,10},{13,12},{... | collective-permute-start | bytes 786440 | tf_op jit(solution)/shard_map/ppermute | solution.py:217
  70.9 21.3 %collective-permute-start.3 = (bf16[128,1024]{1,0:T(8,128)(2,1)S(1)}, bf16[128,1024]{1,0:T(8,128)(2,1)S(1)}, u32[]{:S(2)}, u32[]{:S(2)}) collective-permute-start(bf16[128,1024]{1,0:T(8,128)(2,1)S(1)} %get-tuple-element.11), channel_id=1, source_target_pairs={{2,0},{3,1},{6,4},{7,5},{10,8},{11,9},{14,12},{15,13},{18,16},{19,... | collective-permute-start | bytes 786440 | tf_op jit(solution)/shard_map/ppermute | solution.py:217

commit v6 on v5

--- a/solution.py
+++ b/solution.py
@@ -44,7 +44,8 @@
         ).reshape(dp_size * capacity, -1)
 
     arrived_kv = send(rollout_rows[:, QUERY_HEADS * HEAD_SIZE :])
-    arrived_q = send(rollout_rows[:, : QUERY_HEADS * HEAD_SIZE])
+    half = QUERY_HEADS * HEAD_SIZE // 2
+    arrived_q = [send(rollout_rows[:, part * half : (part + 1) * half]) for part in range(2)]
     load_table = jnp.sum((column_plan == dp_index).astype(jnp.int32), axis=1)
     end_marks = jnp.cumsum(load_table)
     start_marks = end_marks - load_table
@@ -59,7 +60,7 @@
     def receive(arrived):
         return jnp.dot(recv_pick, arrived, preferred_element_type=jnp.float32).astype(arrived.dtype)
 
-    return receive(arrived_q), receive(arrived_kv)
+    return [receive(part) for part in arrived_q], receive(arrived_kv)
 
 
 def attend(query, grads, key_mat, value_mat, allowed):
@@ -128,20 +129,21 @@
     vp_ref[...] = value_sum
 
 
-def attend_pallas(packed, weighted, kv_all, mask):
+def attend_pallas(packed, weighted, kv_all, mask, first_group, groups):
     token_rows = packed.shape[0]
     key_rows = kv_all.shape[0]
     group_width = QUERY_HEADS // KEY_VALUE_HEADS * HEAD_SIZE
-    flops = 10 * token_rows * key_rows * HEAD_SIZE * QUERY_HEADS
-    bytes_accessed = 2 * (3 * token_rows * QUERY_HEADS * HEAD_SIZE) + 2 * key_rows * 1024 * 3 + 4 * token_rows * key_rows
+    heads = groups * (QUERY_HEADS // KEY_VALUE_HEADS)
+    flops = 10 * token_rows * key_rows * HEAD_SIZE * heads
+    bytes_accessed = 6 * token_rows * heads * HEAD_SIZE + 12 * key_rows * groups * HEAD_SIZE + 4 * token_rows * key_rows
     return pl.pallas_call(
         attend_kernel,
-        grid=(KEY_VALUE_HEADS,),
+        grid=(groups,),
         in_specs=[
             pl.BlockSpec((token_rows, group_width), lambda g: (0, g)),
             pl.BlockSpec((token_rows, group_width), lambda g: (0, g)),
-            pl.BlockSpec((key_rows, HEAD_SIZE), lambda g: (0, g)),
-            pl.BlockSpec((key_rows, HEAD_SIZE), lambda g: (0, KEY_VALUE_HEADS + g)),
+            pl.BlockSpec((key_rows, HEAD_SIZE), lambda g: (0, first_group + g)),
+            pl.BlockSpec((key_rows, HEAD_SIZE), lambda g: (0, KEY_VALUE_HEADS + first_group + g)),
             pl.BlockSpec((token_rows, key_rows), lambda g: (0, 0)),
         ],
         out_specs=[
@@ -150,9 +152,9 @@
             pl.BlockSpec((key_rows, HEAD_SIZE), lambda g: (0, g)),
         ],
         out_shape=[
-            jax.ShapeDtypeStruct((token_rows, QUERY_HEADS * HEAD_SIZE), jnp.bfloat16),
-            jax.ShapeDtypeStruct((key_rows, KEY_VALUE_HEADS * HEAD_SIZE), jnp.float32),
-            jax.ShapeDtypeStruct((key_rows, KEY_VALUE_HEADS * HEAD_SIZE), jnp.float32),
+            jax.ShapeDtypeStruct((token_rows, groups * group_width), jnp.bfloat16),
+            jax.ShapeDtypeStruct((key_rows, groups * HEAD_SIZE), jnp.float32),
+            jax.ShapeDtypeStruct((key_rows, groups * HEAD_SIZE), jnp.float32),
         ],
         cost_estimate=pl.CostEstimate(
             flops=flops, transcendentals=token_rows * key_rows * QUERY_HEADS, bytes_accessed=bytes_accessed
@@ -201,25 +203,36 @@
         & (key_pos[None, :] <= query_pos[:, None])
         & (key_pos[None, :] >= 0)
     )
-    query_grad, key_part, value_part = attend_pallas(
-        packed_q, weighted, kv_all, allowed.astype(jnp.float32)
-    )
-    query_gradient = query_grad.reshape(1, token_rows, QUERY_HEADS * HEAD_SIZE)
-    partial = jnp.concatenate(
-        [
-            key_part.reshape(reach + 1, token_rows, KEY_VALUE_HEADS * HEAD_SIZE),
-            value_part.reshape(reach + 1, token_rows, KEY_VALUE_HEADS * HEAD_SIZE),
-        ],
-        axis=2,
-    )
-    kv_total = partial[0]
-    for shift in range(1, reach + 1):
-        kv_total = kv_total + lax.ppermute(
-            partial[shift].astype(jnp.bfloat16),
-            "sp",
-            [(k, k - shift) for k in range(shift, sp_size)],
-        ).astype(jnp.float32)
-    kv_grads = kv_total.astype(jnp.bfloat16)
+    mask = allowed.astype(jnp.float32)
+    groups = KEY_VALUE_HEADS // 2
+    half = QUERY_HEADS * HEAD_SIZE // 2
+    query_parts, key_parts, value_parts = [], [], []
+    for part in range(2):
+        query_grad, key_part, value_part = attend_pallas(
+            packed_q[part],
+            weighted[:, part * half : (part + 1) * half],
+            kv_all,
+            mask,
+            part * groups,
+            groups,
+        )
+        partial = jnp.concatenate([key_part, value_part], axis=1).reshape(
+            reach + 1, token_rows, 2 * groups * HEAD_SIZE
+        )
+        total = partial[0]
+        for shift in range(1, reach + 1):
+            total = total + lax.ppermute(
+                partial[shift].astype(jnp.bfloat16),
+                "sp",
+                [(k, k - shift) for k in range(shift, sp_size)],
+            ).astype(jnp.float32)
+        query_parts.append(query_grad)
+        key_parts.append(total[:, : groups * HEAD_SIZE])
+        value_parts.append(total[:, groups * HEAD_SIZE :])
+    query_gradient = jnp.concatenate(query_parts, axis=1).reshape(
+        1, token_rows, QUERY_HEADS * HEAD_SIZE
+    )
+    kv_grads = jnp.concatenate(key_parts + value_parts, axis=1).astype(jnp.bfloat16)
     return (query_gradient, kv_grads.reshape(1, token_rows, kv_width))
 
 

time: 93.5 us -> 99 us (1.059)
  waiting for transfers between devices: 39.2 us -> 30.7 us
  starting transfers between devices: 19.2 us -> 25.1 us
  local copies, waits for them, and re-layouts: 1.01 us -> 6.37 us
  Pallas kernels: 19.4 us -> 21.5 us
  matrix products: 5.75 us -> 7.4 us
  other arithmetic: 7.51 us -> 6.11 us
    all_to_all x2 -> x3, waiting for transfers between devices: 10.6 us -> 2.8 us  [send(): lax.all_to_all(outgoing.reshape(dp_size, capacity, -1), 'dp', split_axis=...]
    all_to_all x2 -> x3, starting transfers between devices: 7.97 us -> 11.3 us  [send(): lax.all_to_all(outgoing.reshape(dp_size, capacity, -1), 'dp', split_axis=...]
    ppermute x2 -> x4, starting transfers between devices: 2.58 us -> 5.17 us  [body(): lax.ppermute(partial[shift].astype(jnp.bfloat16), 'sp', [(k, k - shift) f...]
    concatenate x0 -> x4, local copies, waits for them, and re-layouts: none -> 2.19 us  [the longest x2 2.16 us: body(): jnp.concatenate([key_part, value_part], axis=1)]
    pallas_call x1 -> x2, Pallas kernels: 19.4 us -> 21.5 us  [attend_pallas(): pl.pallas_call(attend_kernel, grid=(groups,), in_specs=[pl.BlockSpec((tok...]
    unnamed x16 -> x18, local copies, waits for them, and re-layouts: 0.03 us -> 2.11 us
    ppermute x2 -> x4, waiting for transfers between devices: 20 us -> 18.2 us  [body(): lax.ppermute(partial[shift].astype(jnp.bfloat16), 'sp', [(k, k - shift) f...]
    another operation x2 -> x5, other arithmetic: 1.78 us -> 0.37 us
  transfers between devices with their start and end apart: 6 -> 9, of which waited for: 6 -> 6; matrix products, arithmetic and copies ran while one was open for 7% -> 15% of each run, Pallas kernels for 0% -> 22%
where the time goes in v6:
time: 99 us; the launch traced here: 98.3 us
  waiting for transfers between devices  30.7 us (31%)
  starting transfers between devices  25.1 us (25%)
  Pallas kernels  21.5 us (22%)
  matrix products  7.4 us (7%)
  local copies, waits for them, and re-layouts  6.37 us (6%)
  other arithmetic  6.11 us (6%)
  between operations  1.02 us (1%)
    pallas_call x2, Pallas kernels, attend_pallas(): pl.pallas_call(attend_kernel, grid=(groups,), in_specs=[pl.BlockSpec((tok...  21.5 us
    ppermute x4, waiting for transfers between devices, body(): lax.ppermute(partial[shift].astype(jnp.bfloat16), 'sp', [(k, k - shift) f...  18.2 us
    all_to_all x3, starting transfers between devices, send(): lax.all_to_all(outgoing.reshape(dp_size, capacity, -1), 'dp', split_axis=...  11.3 us
    ppermute x2, waiting for transfers between devices, body(): lax.ppermute(kv_local, 'sp', [(k, k + shift) for k in range(sp_size - shi...  9.68 us
    ppermute x2, starting transfers between devices, body(): lax.ppermute(kv_local, 'sp', [(k, k + shift) for k in range(sp_size - shi...  8.69 us
    ppermute x4, starting transfers between devices, body(): lax.ppermute(partial[shift].astype(jnp.bfloat16), 'sp', [(k, k - shift) f...  5.17 us
    dot_general x3, matrix products, send(): jnp.dot(send_pick, columns, preferred_element_type=jnp.float32)  4.84 us
    all_to_all x3, waiting for transfers between devices, send(): lax.all_to_all(outgoing.reshape(dp_size, capacity, -1), 'dp', split_axis=...  2.8 us
  transfers between devices with their start and end apart: 9, of which 6 were waited for; matrix products, arithmetic and copies ran while one was open for 15% of the time, Pallas kernels for 22%

profile of v6, /device:TPU:0, one launch (start us, length us, event | category | flops | bytes accessed | tf_op | source)
XLA Modules:
  0.0 98.3 jit_solution(15846283205800727249)
XLA Ops:
  2.6 2.0 %convolution_convert_fusion.4 = bf16[256,1024]{1,0:T(8,128)(2,1)} fusion(bf16[128,5120]{1,0:T(8,128)(2,1)} %param.6, s32[128]{0:T(128)S(1)} %multiply_add_fusion), kind=kOutput, calls=%fused_computation.6 | convolution fusion | flops 67403776 | bytes 786944 | tf_op jit(solution)/shard_map/dot_general | solution.py:39
  4.6 4.2 %all-to-all-start.1 = ((bf16[4,64,1024]{2,1,0:T(8,128)(2,1)}), bf16[4,64,1024]{2,1,0:T(8,128)(2,1)S(1)}, u32[]{:S(2)}, u32[]{:S(2)}) async-start(bf16[4,64,1024]{2,1,0:T(8,128)(2,1)} %bitcast.8), calls=%async_computation.1 | async-start | bytes 1048576 | tf_op jit(solution)/shard_map/all_to_all | solution.py:42
  9.8 1.4 %convolution_convert_fusion = bf16[256,2048]{1,0:T(8,128)(2,1)} fusion(bf16[128,5120]{1,0:T(8,128)(2,1)S(1)} %copy-done, s32[128]{0:T(128)S(1)} %multiply_add_fusion), kind=kOutput, calls=%fused_computation | convolution fusion | flops 134774784 | bytes 1573376 | tf_op jit(solution)/shard_map/dot_general | solution.py:39
  11.2 1.4 %convolution_convert_fusion.1 = bf16[256,2048]{1,0:T(8,128)(2,1)} fusion(bf16[128,5120]{1,0:T(8,128)(2,1)S(1)} %copy-done, s32[128]{0:T(128)S(1)} %multiply_add_fusion), kind=kOutput, calls=%fused_computation.1 | convolution fusion | flops 134774784 | bytes 1573376 | tf_op jit(solution)/shard_map/dot_general | solution.py:39
  13.8 1.1 %fusion.27 = (bf16[128,2048]{1,0:T(8,128)(2,1)}, bf16[128,2048]{1,0:T(8,128)(2,1)}) fusion(bf16[128,4096]{1,0:T(8,128)(2,1)S(1)} %fusion), kind=kLoop, calls=%fused_computation.77 | loop fusion | bytes 2097152 | tf_op jit(solution)/shard_map/slice | solution.py:213
  14.9 2.8 %all-to-all-done.1 = bf16[4,64,1024]{2,1,0:T(8,128)(2,1)S(1)} async-done(((bf16[4,64,1024]{2,1,0:T(8,128)(2,1)}), bf16[4,64,1024]{2,1,0:T(8,128)(2,1)S(1)}, u32[]{:S(2)}, u32[]{:S(2)}) %all-to-all-start.1) | async-done | bytes 524320 | tf_op jit(solution)/shard_map/all_to_all | solution.py:42
  17.7 3.5 %all-to-all-start.2 = ((bf16[4,64,2048]{2,1,0:T(8,128)(2,1)}), bf16[4,64,2048]{2,1,0:T(8,128)(2,1)S(1)}, u32[]{:S(2)}, u32[]{:S(2)}) async-start(bf16[4,64,2048]{2,1,0:T(8,128)(2,1)} %bitcast.10), calls=%async_computation.2 | async-start | bytes 2097152 | tf_op jit(solution)/shard_map/all_to_all | solution.py:42
  21.6 5.2 %collective-permute-start.1 = (bf16[128,1152]{1,0:T(8,128)(2,1)S(1)}, bf16[128,1152]{1,0:T(8,128)(2,1)S(1)}, u32[]{:S(2)}, u32[]{:S(2)}) collective-permute-start(bf16[128,1152]{1,0:T(8,128)(2,1)S(1)} %pad_maximum_fusion.1), channel_id=1, source_target_pairs={{0,2},{1,3},{4,6},{5,7},{8,10},{9,11},{12,14},{13,15},{16,18},{17,... | collective-permute-start | bytes 884744 | tf_op jit(solution)/shard_map/ppermute | solution.py:182
  26.8 3.5 %collective-permute-start = (bf16[128,1152]{1,0:T(8,128)(2,1)S(1)}, bf16[128,1152]{1,0:T(8,128)(2,1)S(1)}, u32[]{:S(2)}, u32[]{:S(2)}) collective-permute-start(bf16[128,1152]{1,0:T(8,128)(2,1)S(1)} %pad_maximum_fusion.1), channel_id=1, source_target_pairs={{0,1},{1,2},{2,3},{4,5},{5,6},{6,7},{8,9},{9,10},{10,11},{12,13},{... | collective-permute-start | bytes 884744 | tf_op jit(solution)/shard_map/ppermute | solution.py:182
  30.3 3.9 %collective-permute-done.1 = bf16[128,1152]{1,0:T(8,128)(2,1)S(1)} collective-permute-done((bf16[128,1152]{1,0:T(8,128)(2,1)S(1)}, bf16[128,1152]{1,0:T(8,128)(2,1)S(1)}, u32[]{:S(2)}, u32[]{:S(2)}) %collective-permute-start.1) | collective-permute-done | bytes 294944 | tf_op jit(solution)/shard_map/ppermute | solution.py:182
  34.2 5.8 %collective-permute-done = bf16[128,1152]{1,0:T(8,128)(2,1)S(1)} collective-permute-done((bf16[128,1152]{1,0:T(8,128)(2,1)S(1)}, bf16[128,1152]{1,0:T(8,128)(2,1)S(1)}, u32[]{:S(2)}, u32[]{:S(2)}) %collective-permute-start) | collective-permute-done | bytes 294944 | tf_op jit(solution)/shard_map/ppermute | solution.py:182
  41.1 3.5 %all-to-all-start = ((bf16[4,64,2048]{2,1,0:T(8,128)(2,1)}), bf16[4,64,2048]{2,1,0:T(8,128)(2,1)S(1)}, u32[]{:S(2)}, u32[]{:S(2)}) async-start(bf16[4,64,2048]{2,1,0:T(8,128)(2,1)} %bitcast.4), calls=%async_computation | async-start | bytes 2097152 | tf_op jit(solution)/shard_map/all_to_all | solution.py:42
  44.6 1.1 %convolution_convert_fusion.2.q_ref = bf16[128,2048]{1,0:T(8,128)(2,1)} fusion(bf16[256,2048]{1,0:T(8,128)(2,1)S(1)} %bitcast.32, s32[128]{0:T(128)S(1)} %add_subtract_fusion), kind=kOutput, calls=%fused_computation.2 | convolution fusion | flops 134512640 | bytes 1573376 | tf_op jit(solution)/shard_map/dot_general | solution.py:61
  45.7 10.7 %shard_map.78 = (bf16[128,2048]{1,0:T(8,128)(2,1)}, f32[384,256]{1,0:T(8,128)}, f32[384,256]{1,0:T(8,128)}) custom-call(bf16[128,2048]{1,0:T(8,128)(2,1)} %convolution_convert_fusion.2.q_ref, bf16[128,2048]{1,0:T(8,128)(2,1)} %get-tuple-element.17.g_ref, bf16[384,1152]{1,0:T(8,128)(2,1)} %copy-done.1, bf16[384,1152]{1,0:T(8,128)(2,1)} %copy-done.1, ...), custom_call_target="tpu_custom_call" | custom-call | flops 1006632960 | bytes 2949120 | tf_op jit(solution)/shard_map/pallas_call | solution.py:139
  58.7 1.3 %collective-permute-start.4 = (bf16[128,512]{1,0:T(8,128)(2,1)S(1)}, bf16[128,512]{1,0:T(8,128)(2,1)S(1)}, u32[]{:S(2)}, u32[]{:S(2)}) collective-permute-start(bf16[128,512]{1,0:T(8,128)(2,1)S(1)} %get-tuple-element.20), channel_id=1, source_target_pairs={{1,0},{2,1},{3,2},{5,4},{6,5},{7,6},{9,8},{10,9},{11,10},{13,12},{... | collective-permute-start | bytes 393224 | tf_op jit(solution)/shard_map/ppermute | solution.py:224
  60.0 1.3 %collective-permute-start.5 = (bf16[128,512]{1,0:T(8,128)(2,1)S(1)}, bf16[128,512]{1,0:T(8,128)(2,1)S(1)}, u32[]{:S(2)}, u32[]{:S(2)}) collective-permute-start(bf16[128,512]{1,0:T(8,128)(2,1)S(1)} %get-tuple-element.21), channel_id=1, source_target_pairs={{2,0},{3,1},{6,4},{7,5},{10,8},{11,9},{14,12},{15,13},{18,16},{19,... | collective-permute-start | bytes 393224 | tf_op jit(solution)/shard_map/ppermute | solution.py:224
  61.3 1.1 %convolution_convert_fusion.3.q_ref = bf16[128,2048]{1,0:T(8,128)(2,1)} fusion(bf16[256,2048]{1,0:T(8,128)(2,1)S(1)} %bitcast.33, s32[128]{0:T(128)S(1)} %add_subtract_fusion), kind=kOutput, calls=%fused_computation.3 | convolution fusion | flops 134512640 | bytes 1573376 | tf_op jit(solution)/shard_map/dot_general | solution.py:61
  62.4 10.8 %shard_map.77 = (bf16[128,2048]{1,0:T(8,128)(2,1)}, f32[384,256]{1,0:T(8,128)}, f32[384,256]{1,0:T(8,128)}) custom-call(bf16[128,2048]{1,0:T(8,128)(2,1)} %convolution_convert_fusion.3.q_ref, bf16[128,2048]{1,0:T(8,128)(2,1)} %get-tuple-element.16.g_ref, bf16[384,1152]{1,0:T(8,128)(2,1)} %copy-done.1, bf16[384,1152]{1,0:T(8,128)(2,1)} %copy-done.1, ...), custom_call_target="tpu_custom_call" | custom-call | flops 1006632960 | bytes 2949120 | tf_op jit(solution)/shard_map/pallas_call | solution.py:139
  74.3 1.1 %constant_dynamic-update-slice_fusion = f32[384,512]{1,0:T(8,128)S(1)} fusion(f32[384,512]{1,0:T(8,128)S(1)} %constant_dynamic-update-slice_fusion.1, f32[384,256]{1,0:T(8,128)} %get-tuple-element.11), kind=kLoop, calls=%fused_computation.40 | loop fusion | bytes 786432 | tf_op jit(solution)/shard_map/concatenate | solution.py:219
  75.5 1.3 %collective-permute-start.2 = (bf16[128,512]{1,0:T(8,128)(2,1)S(1)}, bf16[128,512]{1,0:T(8,128)(2,1)S(1)}, u32[]{:S(2)}, u32[]{:S(2)}) collective-permute-start(bf16[128,512]{1,0:T(8,128)(2,1)S(1)} %get-tuple-element.18), channel_id=1, source_target_pairs={{1,0},{2,1},{3,2},{5,4},{6,5},{7,6},{9,8},{10,9},{11,10},{13,12},{... | collective-permute-start | bytes 393224 | tf_op jit(solution)/shard_map/ppermute | solution.py:224
  76.8 1.3 %collective-permute-start.3 = (bf16[128,512]{1,0:T(8,128)(2,1)S(1)}, bf16[128,512]{1,0:T(8,128)(2,1)S(1)}, u32[]{:S(2)}, u32[]{:S(2)}) collective-permute-start(bf16[128,512]{1,0:T(8,128)(2,1)S(1)} %get-tuple-element.19), channel_id=1, source_target_pairs={{2,0},{3,1},{6,4},{7,5},{10,8},{11,9},{14,12},{15,13},{18,16},{19,... | collective-permute-start | bytes 393224 | tf_op jit(solution)/shard_map/ppermute | solution.py:224
  78.1 1.1 %maximum_bitcast_fusion = bf16[1,128,4096]{2,1,0:T(8,128)(2,1)} fusion(bf16[128,2048]{1,0:T(8,128)(2,1)S(1)} %copy-done.3, bf16[128,2048]{1,0:T(8,128)(2,1)S(1)} %copy-done.4), kind=kLoop, calls=%fused_computation.8 | loop fusion | flops 2097152 | bytes 2097152 | tf_op jit(solution)/shard_map/reshape | solution.py:232
  80.1 9.9 %collective-permute-done.2 = bf16[128,512]{1,0:T(8,128)(2,1)S(1)} collective-permute-done((bf16[128,512]{1,0:T(8,128)(2,1)S(1)}, bf16[128,512]{1,0:T(8,128)(2,1)S(1)}, u32[]{:S(2)}, u32[]{:S(2)}) %collective-permute-start.2) | collective-permute-done | bytes 131104 | tf_op jit(solution)/shard_map/ppermute | solution.py:224
  90.0 7.5 %collective-permute-done.3 = bf16[128,512]{1,0:T(8,128)(2,1)S(1)} collective-permute-done((bf16[128,512]{1,0:T(8,128)(2,1)S(1)}, bf16[128,512]{1,0:T(8,128)(2,1)S(1)}, u32[]{:S(2)}, u32[]{:S(2)}) %collective-permute-start.3) | collective-permute-done | bytes 131104 | tf_op jit(solution)/shard_map/ppermute | solution.py:224
  (61 shorter events, 10.3 us)
Async XLA Ops:
  0.6 9.1 %copy-start = (bf16[128,5120]{1,0:T(8,128)(2,1)S(1)}, bf16[128,5120]{1,0:T(8,128)(2,1)}, u32[]{:S(2)}) copy-start(bf16[128,5120]{1,0:T(8,128)(2,1)} %param.6) | copy-start | bytes 3932164
  4.6 13.0 %all-to-all-start.1 = ((bf16[4,64,1024]{2,1,0:T(8,128)(2,1)}), bf16[4,64,1024]{2,1,0:T(8,128)(2,1)S(1)}, u32[]{:S(2)}, u32[]{:S(2)}) async-start(bf16[4,64,1024]{2,1,0:T(8,128)(2,1)} %bitcast.8), calls=%async_computation.1 | async-start | bytes 1048576 | tf_op jit(solution)/shard_map/all_to_all | solution.py:42
  9.7 3.3 %copy-start.5 = (s32[1,128]{1,0:T(1,128)S(1)}, s32[1,128]{1,0:T(1,128)}, u32[]{:S(2)}) copy-start(s32[1,128]{1,0:T(1,128)} %param.8) | copy-start | bytes 1540
  9.7 3.3 %copy-start.7 = (s32[16]{0:T(128)S(1)}, s32[16]{0:T(128)}, u32[]{:S(2)}) copy-start(s32[16]{0:T(128)} %param.10) | copy-start | bytes 196
  9.7 3.3 %copy-start.6 = (s32[16]{0:T(128)S(1)}, s32[16]{0:T(128)}, u32[]{:S(2)}) copy-start(s32[16]{0:T(128)} %param.11) | copy-start | bytes 196
  9.7 3.8 %copy-start.2 = (bf16[1,128,4096]{2,1,0:T(8,128)(2,1)S(1)}, bf16[1,128,4096]{2,1,0:T(8,128)(2,1)}, u32[]{:S(2)}) copy-start(bf16[1,128,4096]{2,1,0:T(8,128)(2,1)} %param.9) | copy-start | bytes 3145732
  17.7 23.4 %all-to-all-start.2 = ((bf16[4,64,2048]{2,1,0:T(8,128)(2,1)}), bf16[4,64,2048]{2,1,0:T(8,128)(2,1)S(1)}, u32[]{:S(2)}, u32[]{:S(2)}) async-start(bf16[4,64,2048]{2,1,0:T(8,128)(2,1)} %bitcast.10), calls=%async_computation.2 | async-start | bytes 2097152 | tf_op jit(solution)/shard_map/all_to_all | solution.py:42
  21.6 12.6 %collective-permute-start.1 = (bf16[128,1152]{1,0:T(8,128)(2,1)S(1)}, bf16[128,1152]{1,0:T(8,128)(2,1)S(1)}, u32[]{:S(2)}, u32[]{:S(2)}) collective-permute-start(bf16[128,1152]{1,0:T(8,128)(2,1)S(1)} %pad_maximum_fusion.1), channel_id=1, source_target_pairs={{0,2},{1,3},{4,6},{5,7},{8,10},{9,11},{12,14},{13,15},{16,18},{17,... | collective-permute-start | bytes 884744 | tf_op jit(solution)/shard_map/ppermute | solution.py:182
  26.8 13.2 %collective-permute-start = (bf16[128,1152]{1,0:T(8,128)(2,1)S(1)}, bf16[128,1152]{1,0:T(8,128)(2,1)S(1)}, u32[]{:S(2)}, u32[]{:S(2)}) collective-permute-start(bf16[128,1152]{1,0:T(8,128)(2,1)S(1)} %pad_maximum_fusion.1), channel_id=1, source_target_pairs={{0,1},{1,2},{2,3},{4,5},{5,6},{6,7},{8,9},{9,10},{10,11},{12,13},{... | collective-permute-start | bytes 884744 | tf_op jit(solution)/shard_map/ppermute | solution.py:182
  40.1 5.6 %copy-start.1 = (bf16[384,1152]{1,0:T(8,128)(2,1)}, bf16[384,1152]{1,0:T(8,128)(2,1)S(1)}, u32[]{:S(2)}) copy-start(bf16[384,1152]{1,0:T(8,128)(2,1)S(1)} %pad_maximum_fusion.k_ref.v_ref) | copy-start | bytes 2654212
  41.1 20.2 %all-to-all-start = ((bf16[4,64,2048]{2,1,0:T(8,128)(2,1)}), bf16[4,64,2048]{2,1,0:T(8,128)(2,1)S(1)}, u32[]{:S(2)}, u32[]{:S(2)}) async-start(bf16[4,64,2048]{2,1,0:T(8,128)(2,1)} %bitcast.4), calls=%async_computation | async-start | bytes 2097152 | tf_op jit(solution)/shard_map/all_to_all | solution.py:42
  58.7 20.5 %collective-permute-start.4 = (bf16[128,512]{1,0:T(8,128)(2,1)S(1)}, bf16[128,512]{1,0:T(8,128)(2,1)S(1)}, u32[]{:S(2)}, u32[]{:S(2)}) collective-permute-start(bf16[128,512]{1,0:T(8,128)(2,1)S(1)} %get-tuple-element.20), channel_id=1, source_target_pairs={{1,0},{2,1},{3,2},{5,4},{6,5},{7,6},{9,8},{10,9},{11,10},{13,12},{... | collective-permute-start | bytes 393224 | tf_op jit(solution)/shard_map/ppermute | solution.py:224
  60.0 20.1 %collective-permute-start.5 = (bf16[128,512]{1,0:T(8,128)(2,1)S(1)}, bf16[128,512]{1,0:T(8,128)(2,1)S(1)}, u32[]{:S(2)}, u32[]{:S(2)}) collective-permute-start(bf16[128,512]{1,0:T(8,128)(2,1)S(1)} %get-tuple-element.21), channel_id=1, source_target_pairs={{2,0},{3,1},{6,4},{7,5},{10,8},{11,9},{14,12},{15,13},{18,16},{19,... | collective-permute-start | bytes 393224 | tf_op jit(solution)/shard_map/ppermute | solution.py:224
  74.3 3.8 %copy-start.3 = (bf16[128,2048]{1,0:T(8,128)(2,1)S(1)}, bf16[128,2048]{1,0:T(8,128)(2,1)}, u32[]{:S(2)}) copy-start(bf16[128,2048]{1,0:T(8,128)(2,1)} %get-tuple-element.9) | copy-start | bytes 1572868
  74.3 3.8 %copy-start.4 = (bf16[128,2048]{1,0:T(8,128)(2,1)S(1)}, bf16[128,2048]{1,0:T(8,128)(2,1)}, u32[]{:S(2)}) copy-start(bf16[128,2048]{1,0:T(8,128)(2,1)} %get-tuple-element.8) | copy-start | bytes 1572868
  75.5 14.5 %collective-permute-start.2 = (bf16[128,512]{1,0:T(8,128)(2,1)S(1)}, bf16[128,512]{1,0:T(8,128)(2,1)S(1)}, u32[]{:S(2)}, u32[]{:S(2)}) collective-permute-start(bf16[128,512]{1,0:T(8,128)(2,1)S(1)} %get-tuple-element.18), channel_id=1, source_target_pairs={{1,0},{2,1},{3,2},{5,4},{6,5},{7,6},{9,8},{10,9},{11,10},{13,12},{... | collective-permute-start | bytes 393224 | tf_op jit(solution)/shard_map/ppermute | solution.py:224
  76.8 20.7 %collective-permute-start.3 = (bf16[128,512]{1,0:T(8,128)(2,1)S(1)}, bf16[128,512]{1,0:T(8,128)(2,1)S(1)}, u32[]{:S(2)}, u32[]{:S(2)}) collective-permute-start(bf16[128,512]{1,0:T(8,128)(2,1)S(1)} %get-tuple-element.19), channel_id=1, source_target_pairs={{2,0},{3,1},{6,4},{7,5},{10,8},{11,9},{14,12},{15,13},{18,16},{19,... | collective-permute-start | bytes 393224 | tf_op jit(solution)/shard_map/ppermute | solution.py:224

commit v7 on v6

--- a/solution.py
+++ b/solution.py
@@ -44,8 +44,7 @@
         ).reshape(dp_size * capacity, -1)
 
     arrived_kv = send(rollout_rows[:, QUERY_HEADS * HEAD_SIZE :])
-    half = QUERY_HEADS * HEAD_SIZE // 2
-    arrived_q = [send(rollout_rows[:, part * half : (part + 1) * half]) for part in range(2)]
+    arrived_q = send(rollout_rows[:, : QUERY_HEADS * HEAD_SIZE])
     load_table = jnp.sum((column_plan == dp_index).astype(jnp.int32), axis=1)
     end_marks = jnp.cumsum(load_table)
     start_marks = end_marks - load_table
@@ -60,7 +59,7 @@
     def receive(arrived):
         return jnp.dot(recv_pick, arrived, preferred_element_type=jnp.float32).astype(arrived.dtype)
 
-    return [receive(part) for part in arrived_q], receive(arrived_kv)
+    return receive(arrived_q), receive(arrived_kv)
 
 
 def attend(query, grads, key_mat, value_mat, allowed):
@@ -100,30 +99,25 @@
         grad_head = g_ref[:, cols]
         scores = (
             lax.dot_general(
-                query_head, key_mat, (((1,), (1,)), ((), ())), preferred_element_type=jnp.float32
+                key_mat, query_head, (((1,), (1,)), ((), ())), preferred_element_type=jnp.float32
             )
             * inv_root
         )
         scores = jnp.where(allowed, scores, -1e30)
-        row_top = jnp.max(scores, axis=1, keepdims=True)
+        row_top = jnp.max(scores, axis=0, keepdims=True)
         scaled_exp = jnp.exp(scores - row_top)
-        weights = scaled_exp / jnp.sum(scaled_exp, axis=1, keepdims=True)
+        weights = scaled_exp / jnp.sum(scaled_exp, axis=0, keepdims=True)
         weight_grads = lax.dot_general(
-            grad_head, value_mat, (((1,), (1,)), ((), ())), preferred_element_type=jnp.float32
-        )
-        row_dot = jnp.sum(weights * weight_grads, axis=1, keepdims=True)
+            value_mat, grad_head, (((1,), (1,)), ((), ())), preferred_element_type=jnp.float32
+        )
+        row_dot = jnp.sum(weights * weight_grads, axis=0, keepdims=True)
         score_grads = (weights * (weight_grads - row_dot) * inv_root).astype(jnp.bfloat16)
-        dq_ref[:, cols] = jnp.dot(
-            score_grads, key_mat, preferred_element_type=jnp.float32
+        dq_ref[:, cols] = lax.dot_general(
+            score_grads, key_mat, (((0,), (0,)), ((), ())), preferred_element_type=jnp.float32
         ).astype(dq_ref.dtype)
-        key_sum = key_sum + lax.dot_general(
-            score_grads, query_head, (((0,), (0,)), ((), ())), preferred_element_type=jnp.float32
-        )
-        value_sum = value_sum + lax.dot_general(
-            weights.astype(jnp.bfloat16),
-            grad_head,
-            (((0,), (0,)), ((), ())),
-            preferred_element_type=jnp.float32,
+        key_sum = key_sum + jnp.dot(score_grads, query_head, preferred_element_type=jnp.float32)
+        value_sum = value_sum + jnp.dot(
+            weights.astype(jnp.bfloat16), grad_head, preferred_element_type=jnp.float32
         )
     kp_ref[...] = key_sum
     vp_ref[...] = value_sum
@@ -140,11 +134,11 @@
         attend_kernel,
         grid=(groups,),
         in_specs=[
-            pl.BlockSpec((token_rows, group_width), lambda g: (0, g)),
-            pl.BlockSpec((token_rows, group_width), lambda g: (0, g)),
+            pl.BlockSpec((token_rows, group_width), lambda g: (0, first_group + g)),
+            pl.BlockSpec((token_rows, group_width), lambda g: (0, first_group + g)),
             pl.BlockSpec((key_rows, HEAD_SIZE), lambda g: (0, first_group + g)),
             pl.BlockSpec((key_rows, HEAD_SIZE), lambda g: (0, KEY_VALUE_HEADS + first_group + g)),
-            pl.BlockSpec((token_rows, key_rows), lambda g: (0, 0)),
+            pl.BlockSpec((key_rows, token_rows), lambda g: (0, 0)),
         ],
         out_specs=[
             pl.BlockSpec((token_rows, group_width), lambda g: (0, g)),
@@ -203,14 +197,13 @@
         & (key_pos[None, :] <= query_pos[:, None])
         & (key_pos[None, :] >= 0)
     )
-    mask = allowed.astype(jnp.float32)
+    mask = allowed.T.astype(jnp.float32)
     groups = KEY_VALUE_HEADS // 2
-    half = QUERY_HEADS * HEAD_SIZE // 2
     query_parts, key_parts, value_parts = [], [], []
     for part in range(2):
         query_grad, key_part, value_part = attend_pallas(
-            packed_q[part],
-            weighted[:, part * half : (part + 1) * half],
+            packed_q,
+            weighted,
             kv_all,
             mask,
             part * groups,

time: 99 us -> 92.3 us (0.932)
  local copies, waits for them, and re-layouts: 6.37 us -> 1.21 us
  waiting for transfers between devices: 30.7 us -> 35.1 us
  starting transfers between devices: 25.1 us -> 21.8 us
  Pallas kernels: 21.5 us -> 19.6 us
  matrix products: 7.4 us -> 5.76 us
  other arithmetic: 6.11 us -> 7.22 us
    all_to_all x3 -> x2, waiting for transfers between devices: 2.8 us -> 10.5 us  [send(): lax.all_to_all(outgoing.reshape(dp_size, capacity, -1), 'dp', split_axis=...]
    all_to_all x3 -> x2, starting transfers between devices: 11.3 us -> 7.84 us  [send(): lax.all_to_all(outgoing.reshape(dp_size, capacity, -1), 'dp', split_axis=...]
    ppermute x4, waiting for transfers between devices: 18.2 us -> 16 us  [body(): lax.ppermute(partial[shift].astype(jnp.bfloat16), 'sp', [(k, k - shift) f...]
    concatenate x2, local copies, waits for them, and re-layouts: 2.16 us -> 0.08 us  [body(): jnp.concatenate([key_part, value_part], axis=1)]
    unnamed x18 -> x26, local copies, waits for them, and re-layouts: 2.11 us -> 0.13 us
    pallas_call x2, Pallas kernels: 21.5 us -> 19.6 us  [attend_pallas(): pl.pallas_call(attend_kernel, grid=(groups,), in_specs=[pl.BlockSpec((tok...]
    slice x1 -> x0, local copies, waits for them, and re-layouts: 1.09 us -> none  [body(): weighted[:, part * half:(part + 1) * half]]
    ppermute x2, waiting for transfers between devices: 9.68 us -> 8.68 us  [body(): lax.ppermute(kv_local, 'sp', [(k, k + shift) for k in range(sp_size - shi...]
  transfers between devices with their start and end apart: 9 -> 8, of which waited for: 6 -> 7; matrix products, arithmetic and copies ran while one was open for 15% -> 8% of each run, Pallas kernels for 22% -> 0%
where the time goes in v7:
time: 92.3 us; the launch traced here: 91.8 us
  waiting for transfers between devices  35.1 us (38%)
  starting transfers between devices  21.8 us (24%)
  Pallas kernels  19.6 us (21%)
  other arithmetic  7.22 us (8%)
  matrix products  5.76 us (6%)
  local copies, waits for them, and re-layouts  1.21 us (1%)
  between operations  1.02 us (1%)
    pallas_call x2, Pallas kernels, attend_pallas(): pl.pallas_call(attend_kernel, grid=(groups,), in_specs=[pl.BlockSpec((tok...  19.6 us
    ppermute x4, waiting for transfers between devices, body(): lax.ppermute(partial[shift].astype(jnp.bfloat16), 'sp', [(k, k - shift) f...  16 us
    all_to_all x2, waiting for transfers between devices, send(): lax.all_to_all(outgoing.reshape(dp_size, capacity, -1), 'dp', split_axis=...  10.5 us
    ppermute x2, starting transfers between devices, body(): lax.ppermute(kv_local, 'sp', [(k, k + shift) for k in range(sp_size - shi...  8.68 us
    ppermute x2, waiting for transfers between devices, body(): lax.ppermute(kv_local, 'sp', [(k, k + shift) for k in range(sp_size - shi...  8.68 us
    all_to_all x2, starting transfers between devices, send(): lax.all_to_all(outgoing.reshape(dp_size, capacity, -1), 'dp', split_axis=...  7.84 us
    ppermute x4, starting transfers between devices, body(): lax.ppermute(partial[shift].astype(jnp.bfloat16), 'sp', [(k, k - shift) f...  5.3 us
    dot_general x2, matrix products, send(): jnp.dot(send_pick, columns, preferred_element_type=jnp.float32)  4.03 us
  transfers between devices with their start and end apart: 8, of which 7 were waited for; matrix products, arithmetic and copies ran while one was open for 8% of the time, Pallas kernels for 0%

profile of v7, /device:TPU:0, one launch (start us, length us, event | category | flops | bytes accessed | tf_op | source)
XLA Modules:
  0.0 91.8 jit_solution(11449424610103885032)
XLA Ops:
  2.6 2.0 %convolution_convert_fusion.2 = bf16[256,1024]{1,0:T(8,128)(2,1)} fusion(bf16[128,5120]{1,0:T(8,128)(2,1)} %param.6, s32[128]{0:T(128)S(1)} %multiply_add_fusion), kind=kOutput, calls=%fused_computation.4 | convolution fusion | flops 67403776 | bytes 786944 | tf_op jit(solution)/shard_map/dot_general | solution.py:39
  4.7 4.2 %all-to-all-start.1 = ((bf16[4,64,1024]{2,1,0:T(8,128)(2,1)}), bf16[4,64,1024]{2,1,0:T(8,128)(2,1)S(1)}, u32[]{:S(2)}, u32[]{:S(2)}) async-start(bf16[4,64,1024]{2,1,0:T(8,128)(2,1)} %bitcast.8), calls=%async_computation.1 | async-start | bytes 1048576 | tf_op jit(solution)/shard_map/all_to_all | solution.py:42
  8.9 0.9 fusion.20
  10.7 1.3 %fusion.g_ref = bf16[128,4096]{1,0:T(8,128)(2,1)} fusion(bf16[1,128,4096]{2,1,0:T(8,128)(2,1)S(1)} %copy-done.2, f32[128]{0:T(128)S(1)} %select_reduce_fusion.2), kind=kLoop, calls=%fused_computation.3 | loop fusion | flops 1572864 | bytes 2097664 | tf_op jit(solution)/shard_map/convert_element_type | solution.py:190
  11.9 2.0 %convolution_convert_fusion = bf16[256,4096]{1,0:T(8,128)(2,1)} fusion(bf16[128,5120]{1,0:T(8,128)(2,1)S(1)} %copy-done.1, s32[128]{0:T(128)S(1)} %multiply_add_fusion), kind=kOutput, calls=%fused_computation | convolution fusion | flops 269516800 | bytes 3146240 | tf_op jit(solution)/shard_map/dot_general | solution.py:39
  13.9 3.8 %all-to-all-done.1 = bf16[4,64,1024]{2,1,0:T(8,128)(2,1)S(1)} async-done(((bf16[4,64,1024]{2,1,0:T(8,128)(2,1)}), bf16[4,64,1024]{2,1,0:T(8,128)(2,1)S(1)}, u32[]{:S(2)}, u32[]{:S(2)}) %all-to-all-start.1) | async-done | bytes 524320 | tf_op jit(solution)/shard_map/all_to_all | solution.py:42
  17.7 3.6 %all-to-all-start = ((bf16[4,64,4096]{2,1,0:T(8,128)(2,1)}), bf16[4,64,4096]{2,1,0:T(8,128)(2,1)S(1)}, u32[]{:S(2)}, u32[]{:S(2)}) async-start(bf16[4,64,4096]{2,1,0:T(8,128)(2,1)} %bitcast.4), calls=%async_computation | async-start | bytes 4194304 | tf_op jit(solution)/shard_map/all_to_all | solution.py:42
  21.7 4.2 %collective-permute-start = (bf16[128,1152]{1,0:T(8,128)(2,1)S(1)}, bf16[128,1152]{1,0:T(8,128)(2,1)S(1)}, u32[]{:S(2)}, u32[]{:S(2)}) collective-permute-start(bf16[128,1152]{1,0:T(8,128)(2,1)S(1)} %pad_maximum_fusion.1), channel_id=1, source_target_pairs={{0,1},{1,2},{2,3},{4,5},{5,6},{6,7},{8,9},{9,10},{10,11},{12,13},{... | collective-permute-start | bytes 884744 | tf_op jit(solution)/shard_map/ppermute | solution.py:176
  25.9 4.5 %collective-permute-start.1 = (bf16[128,1152]{1,0:T(8,128)(2,1)S(1)}, bf16[128,1152]{1,0:T(8,128)(2,1)S(1)}, u32[]{:S(2)}, u32[]{:S(2)}) collective-permute-start(bf16[128,1152]{1,0:T(8,128)(2,1)S(1)} %pad_maximum_fusion.1), channel_id=1, source_target_pairs={{0,2},{1,3},{4,6},{5,7},{8,10},{9,11},{12,14},{13,15},{16,18},{17,... | collective-permute-start | bytes 884744 | tf_op jit(solution)/shard_map/ppermute | solution.py:176
  30.5 2.8 %collective-permute-done = bf16[128,1152]{1,0:T(8,128)(2,1)S(1)} collective-permute-done((bf16[128,1152]{1,0:T(8,128)(2,1)S(1)}, bf16[128,1152]{1,0:T(8,128)(2,1)S(1)}, u32[]{:S(2)}, u32[]{:S(2)}) %collective-permute-start) | collective-permute-done | bytes 294944 | tf_op jit(solution)/shard_map/ppermute | solution.py:176
  33.3 5.9 %collective-permute-done.1 = bf16[128,1152]{1,0:T(8,128)(2,1)S(1)} collective-permute-done((bf16[128,1152]{1,0:T(8,128)(2,1)S(1)}, bf16[128,1152]{1,0:T(8,128)(2,1)S(1)}, u32[]{:S(2)}, u32[]{:S(2)}) %collective-permute-start.1) | collective-permute-done | bytes 294944 | tf_op jit(solution)/shard_map/ppermute | solution.py:176
  39.4 0.9 and_convert_fusion.m_ref
  40.3 6.7 %all-to-all-done = bf16[4,64,4096]{2,1,0:T(8,128)(2,1)S(1)} async-done(((bf16[4,64,4096]{2,1,0:T(8,128)(2,1)}), bf16[4,64,4096]{2,1,0:T(8,128)(2,1)S(1)}, u32[]{:S(2)}, u32[]{:S(2)}) %all-to-all-start) | async-done | bytes 2097184 | tf_op jit(solution)/shard_map/all_to_all | solution.py:42
  47.0 1.5 %convolution_convert_fusion.1.q_ref = bf16[128,4096]{1,0:T(8,128)(2,1)} fusion(bf16[256,4096]{1,0:T(8,128)(2,1)S(1)} %bitcast.29, s32[128]{0:T(128)S(1)} %add_subtract_fusion), kind=kOutput, calls=%fused_computation.1 | convolution fusion | flops 268992512 | bytes 3146240 | tf_op jit(solution)/shard_map/dot_general | solution.py:60
  48.4 9.8 %shard_map.77 = (bf16[128,2048]{1,0:T(8,128)(2,1)}, f32[384,256]{1,0:T(8,128)}, f32[384,256]{1,0:T(8,128)}) custom-call(bf16[128,4096]{1,0:T(8,128)(2,1)} %convolution_convert_fusion.1.q_ref, bf16[128,4096]{1,0:T(8,128)(2,1)} %fusion.g_ref, bf16[384,1152]{1,0:T(8,128)(2,1)} %copy-done, bf16[384,1152]{1,0:T(8,128)(2,1)} %copy-done, ...), custom_call_target="tpu_custom_call" | custom-call | flops 1006632960 | bytes 2949120 | tf_op jit(solution)/shard_map/pallas_call | solution.py:133
  58.2 9.9 %shard_map.78 = (bf16[128,2048]{1,0:T(8,128)(2,1)}, f32[384,256]{1,0:T(8,128)}, f32[384,256]{1,0:T(8,128)}) custom-call(bf16[128,4096]{1,0:T(8,128)(2,1)} %convolution_convert_fusion.1.q_ref, bf16[128,4096]{1,0:T(8,128)(2,1)} %fusion.g_ref, bf16[384,1152]{1,0:T(8,128)(2,1)} %copy-done, bf16[384,1152]{1,0:T(8,128)(2,1)} %copy-done, ...), custom_call_target="tpu_custom_call" | custom-call | flops 1006632960 | bytes 2949120 | tf_op jit(solution)/shard_map/pallas_call | solution.py:133
  68.3 1.4 %collective-permute-start.2 = (bf16[128,512]{1,0:T(8,128)(2,1)S(1)}, bf16[128,512]{1,0:T(8,128)(2,1)S(1)}, u32[]{:S(2)}, u32[]{:S(2)}) collective-permute-start(bf16[128,512]{1,0:T(8,128)(2,1)S(1)} %get-tuple-element.16), channel_id=1, source_target_pairs={{1,0},{2,1},{3,2},{5,4},{6,5},{7,6},{9,8},{10,9},{11,10},{13,12},{... | collective-permute-start | bytes 393224 | tf_op jit(solution)/shard_map/ppermute | solution.py:217
  69.7 1.3 %collective-permute-start.3 = (bf16[128,512]{1,0:T(8,128)(2,1)S(1)}, bf16[128,512]{1,0:T(8,128)(2,1)S(1)}, u32[]{:S(2)}, u32[]{:S(2)}) collective-permute-start(bf16[128,512]{1,0:T(8,128)(2,1)S(1)} %get-tuple-element.17), channel_id=1, source_target_pairs={{2,0},{3,1},{6,4},{7,5},{10,8},{11,9},{14,12},{15,13},{18,16},{19,... | collective-permute-start | bytes 393224 | tf_op jit(solution)/shard_map/ppermute | solution.py:217
  71.2 1.3 %collective-permute-start.4 = (bf16[128,512]{1,0:T(8,128)(2,1)S(1)}, bf16[128,512]{1,0:T(8,128)(2,1)S(1)}, u32[]{:S(2)}, u32[]{:S(2)}) collective-permute-start(bf16[128,512]{1,0:T(8,128)(2,1)S(1)} %get-tuple-element.18), channel_id=1, source_target_pairs={{1,0},{2,1},{3,2},{5,4},{6,5},{7,6},{9,8},{10,9},{11,10},{13,12},{... | collective-permute-start | bytes 393224 | tf_op jit(solution)/shard_map/ppermute | solution.py:217
  72.5 1.3 %collective-permute-start.5 = (bf16[128,512]{1,0:T(8,128)(2,1)S(1)}, bf16[128,512]{1,0:T(8,128)(2,1)S(1)}, u32[]{:S(2)}, u32[]{:S(2)}) collective-permute-start(bf16[128,512]{1,0:T(8,128)(2,1)S(1)} %get-tuple-element.19), channel_id=1, source_target_pairs={{2,0},{3,1},{6,4},{7,5},{10,8},{11,9},{14,12},{15,13},{18,16},{19,... | collective-permute-start | bytes 393224 | tf_op jit(solution)/shard_map/ppermute | solution.py:217
  73.9 1.1 %maximum_bitcast_fusion = bf16[1,128,4096]{2,1,0:T(8,128)(2,1)} fusion(bf16[128,2048]{1,0:T(8,128)(2,1)S(1)} %copy-done.4, bf16[128,2048]{1,0:T(8,128)(2,1)S(1)} %copy-done.3), kind=kLoop, calls=%fused_computation.6 | loop fusion | flops 2097152 | bytes 2097152 | tf_op jit(solution)/shard_map/reshape | solution.py:225
  74.9 1.1 %collective-permute-done.2 = bf16[128,512]{1,0:T(8,128)(2,1)S(1)} collective-permute-done((bf16[128,512]{1,0:T(8,128)(2,1)S(1)}, bf16[128,512]{1,0:T(8,128)(2,1)S(1)}, u32[]{:S(2)}, u32[]{:S(2)}) %collective-permute-start.2) | collective-permute-done | bytes 131104 | tf_op jit(solution)/shard_map/ppermute | solution.py:217
  76.0 10.8 %collective-permute-done.3 = bf16[128,512]{1,0:T(8,128)(2,1)S(1)} collective-permute-done((bf16[128,512]{1,0:T(8,128)(2,1)S(1)}, bf16[128,512]{1,0:T(8,128)(2,1)S(1)}, u32[]{:S(2)}, u32[]{:S(2)}) %collective-permute-start.3) | collective-permute-done | bytes 131104 | tf_op jit(solution)/shard_map/ppermute | solution.py:217
  86.9 4.1 %collective-permute-done.5 = bf16[128,512]{1,0:T(8,128)(2,1)S(1)} collective-permute-done((bf16[128,512]{1,0:T(8,128)(2,1)S(1)}, bf16[128,512]{1,0:T(8,128)(2,1)S(1)}, u32[]{:S(2)}, u32[]{:S(2)}) %collective-permute-start.5) | collective-permute-done | bytes 131104 | tf_op jit(solution)/shard_map/ppermute | solution.py:217
  (64 shorter events, 4.6 us)
Async XLA Ops:
  0.6 9.4 %copy-start.11 = (s32[16]{0:T(128)S(1)}, s32[16]{0:T(128)}, u32[]{:S(2)}) copy-start(s32[16]{0:T(128)} %param.10) | copy-start | bytes 196
  0.6 9.4 %copy-start.10 = (s32[16]{0:T(128)S(1)}, s32[16]{0:T(128)}, u32[]{:S(2)}) copy-start(s32[16]{0:T(128)} %param.11) | copy-start | bytes 196
  0.7 9.9 %copy-start.9 = (s32[1,128]{1,0:T(1,128)S(1)}, s32[1,128]{1,0:T(1,128)}, u32[]{:S(2)}) copy-start(s32[1,128]{1,0:T(1,128)} %param.8) | copy-start | bytes 1540
  0.7 10.0 %copy-start.2 = (bf16[1,128,4096]{2,1,0:T(8,128)(2,1)S(1)}, bf16[1,128,4096]{2,1,0:T(8,128)(2,1)}, u32[]{:S(2)}) copy-start(bf16[1,128,4096]{2,1,0:T(8,128)(2,1)} %param.9) | copy-start | bytes 3145732
  1.6 10.4 %copy-start.1 = (bf16[128,5120]{1,0:T(8,128)(2,1)S(1)}, bf16[128,5120]{1,0:T(8,128)(2,1)}, u32[]{:S(2)}) copy-start(bf16[128,5120]{1,0:T(8,128)(2,1)} %param.6) | copy-start | bytes 3932164
  4.7 13.1 %all-to-all-start.1 = ((bf16[4,64,1024]{2,1,0:T(8,128)(2,1)}), bf16[4,64,1024]{2,1,0:T(8,128)(2,1)S(1)}, u32[]{:S(2)}, u32[]{:S(2)}) async-start(bf16[4,64,1024]{2,1,0:T(8,128)(2,1)} %bitcast.8), calls=%async_computation.1 | async-start | bytes 1048576 | tf_op jit(solution)/shard_map/all_to_all | solution.py:42
  17.7 29.2 %all-to-all-start = ((bf16[4,64,4096]{2,1,0:T(8,128)(2,1)}), bf16[4,64,4096]{2,1,0:T(8,128)(2,1)S(1)}, u32[]{:S(2)}, u32[]{:S(2)}) async-start(bf16[4,64,4096]{2,1,0:T(8,128)(2,1)} %bitcast.4), calls=%async_computation | async-start | bytes 4194304 | tf_op jit(solution)/shard_map/all_to_all | solution.py:42
  21.7 11.6 %collective-permute-start = (bf16[128,1152]{1,0:T(8,128)(2,1)S(1)}, bf16[128,1152]{1,0:T(8,128)(2,1)S(1)}, u32[]{:S(2)}, u32[]{:S(2)}) collective-permute-start(bf16[128,1152]{1,0:T(8,128)(2,1)S(1)} %pad_maximum_fusion.1), channel_id=1, source_target_pairs={{0,1},{1,2},{2,3},{4,5},{5,6},{6,7},{8,9},{9,10},{10,11},{12,13},{... | collective-permute-start | bytes 884744 | tf_op jit(solution)/shard_map/ppermute | solution.py:176
  25.9 13.2 %collective-permute-start.1 = (bf16[128,1152]{1,0:T(8,128)(2,1)S(1)}, bf16[128,1152]{1,0:T(8,128)(2,1)S(1)}, u32[]{:S(2)}, u32[]{:S(2)}) collective-permute-start(bf16[128,1152]{1,0:T(8,128)(2,1)S(1)} %pad_maximum_fusion.1), channel_id=1, source_target_pairs={{0,2},{1,3},{4,6},{5,7},{8,10},{9,11},{12,14},{13,15},{16,18},{17,... | collective-permute-start | bytes 884744 | tf_op jit(solution)/shard_map/ppermute | solution.py:176
  39.2 9.2 %copy-start = (bf16[384,1152]{1,0:T(8,128)(2,1)}, bf16[384,1152]{1,0:T(8,128)(2,1)S(1)}, u32[]{:S(2)}) copy-start(bf16[384,1152]{1,0:T(8,128)(2,1)S(1)} %pad_maximum_fusion.k_ref.v_ref) | copy-start | bytes 2654212
  58.2 9.9 %copy-start.8 = (f32[384,256]{1,0:T(8,128)S(1)}, f32[384,256]{1,0:T(8,128)}, u32[]{:S(2)}) copy-start(f32[384,256]{1,0:T(8,128)} %get-tuple-element.10) | copy-start | bytes 1179652
  58.2 9.9 %copy-start.7 = (f32[384,256]{1,0:T(8,128)S(1)}, f32[384,256]{1,0:T(8,128)}, u32[]{:S(2)}) copy-start(f32[384,256]{1,0:T(8,128)} %get-tuple-element.11) | copy-start | bytes 1179652
  68.1 3.0 %copy-start.6 = (f32[384,256]{1,0:T(8,128)S(1)}, f32[384,256]{1,0:T(8,128)}, u32[]{:S(2)}) copy-start(f32[384,256]{1,0:T(8,128)} %get-tuple-element.12) | copy-start | bytes 1179652
  68.1 3.0 %copy-start.5 = (f32[384,256]{1,0:T(8,128)S(1)}, f32[384,256]{1,0:T(8,128)}, u32[]{:S(2)}) copy-start(f32[384,256]{1,0:T(8,128)} %get-tuple-element.13) | copy-start | bytes 1179652
  68.3 5.6 %copy-start.3 = (bf16[128,2048]{1,0:T(8,128)(2,1)S(1)}, bf16[128,2048]{1,0:T(8,128)(2,1)}, u32[]{:S(2)}) copy-start(bf16[128,2048]{1,0:T(8,128)(2,1)} %get-tuple-element.8) | copy-start | bytes 1572868
  68.3 5.6 %copy-start.4 = (bf16[128,2048]{1,0:T(8,128)(2,1)S(1)}, bf16[128,2048]{1,0:T(8,128)(2,1)}, u32[]{:S(2)}) copy-start(bf16[128,2048]{1,0:T(8,128)(2,1)} %get-tuple-element.9) | copy-start | bytes 1572868
  68.3 7.7 %collective-permute-start.2 = (bf16[128,512]{1,0:T(8,128)(2,1)S(1)}, bf16[128,512]{1,0:T(8,128)(2,1)S(1)}, u32[]{:S(2)}, u32[]{:S(2)}) collective-permute-start(bf16[128,512]{1,0:T(8,128)(2,1)S(1)} %get-tuple-element.16), channel_id=1, source_target_pairs={{1,0},{2,1},{3,2},{5,4},{6,5},{7,6},{9,8},{10,9},{11,10},{13,12},{... | collective-permute-start | bytes 393224 | tf_op jit(solution)/shard_map/ppermute | solution.py:217
  69.7 17.1 %collective-permute-start.3 = (bf16[128,512]{1,0:T(8,128)(2,1)S(1)}, bf16[128,512]{1,0:T(8,128)(2,1)S(1)}, u32[]{:S(2)}, u32[]{:S(2)}) collective-permute-start(bf16[128,512]{1,0:T(8,128)(2,1)S(1)} %get-tuple-element.17), channel_id=1, source_target_pairs={{2,0},{3,1},{6,4},{7,5},{10,8},{11,9},{14,12},{15,13},{18,16},{19,... | collective-permute-start | bytes 393224 | tf_op jit(solution)/shard_map/ppermute | solution.py:217
  71.2 15.6 %collective-permute-start.4 = (bf16[128,512]{1,0:T(8,128)(2,1)S(1)}, bf16[128,512]{1,0:T(8,128)(2,1)S(1)}, u32[]{:S(2)}, u32[]{:S(2)}) collective-permute-start(bf16[128,512]{1,0:T(8,128)(2,1)S(1)} %get-tuple-element.18), channel_id=1, source_target_pairs={{1,0},{2,1},{3,2},{5,4},{6,5},{7,6},{9,8},{10,9},{11,10},{13,12},{... | collective-permute-start | bytes 393224 | tf_op jit(solution)/shard_map/ppermute | solution.py:217
  72.5 18.5 %collective-permute-start.5 = (bf16[128,512]{1,0:T(8,128)(2,1)S(1)}, bf16[128,512]{1,0:T(8,128)(2,1)S(1)}, u32[]{:S(2)}, u32[]{:S(2)}) collective-permute-start(bf16[128,512]{1,0:T(8,128)(2,1)S(1)} %get-tuple-element.19), channel_id=1, source_target_pairs={{2,0},{3,1},{6,4},{7,5},{10,8},{11,9},{14,12},{15,13},{18,16},{19,... | collective-permute-start | bytes 393224 | tf_op jit(solution)/shard_map/ppermute | solution.py:217

commit v8 on v7

--- a/solution.py
+++ b/solution.py
@@ -5,6 +5,7 @@
 from jax import lax
 from jax.experimental import pallas as pl
 from jax.sharding import PartitionSpec as P
+
 
 QUERY_HEADS = 32
 KEY_VALUE_HEADS = 4
@@ -60,30 +61,6 @@
         return jnp.dot(recv_pick, arrived, preferred_element_type=jnp.float32).astype(arrived.dtype)
 
     return receive(arrived_q), receive(arrived_kv)
-
-
-def attend(query, grads, key_mat, value_mat, allowed):
-    inv_root = 1.0 / math.sqrt(HEAD_SIZE)
-    scores = (
-        jnp.einsum("tghd,sgd->tghs", query, key_mat, preferred_element_type=jnp.float32) * inv_root
-    )
-    scores = jnp.where(allowed[:, None, None, :], scores, -1e30)
-    row_top = jnp.max(scores, axis=3, keepdims=True)
-    scaled_exp = jnp.exp(scores - row_top)
-    weights = scaled_exp / jnp.sum(scaled_exp, axis=3, keepdims=True)
-    weight_grads = jnp.einsum(
-        "tghd,sgd->tghs", grads, value_mat, preferred_element_type=jnp.float32
-    )
-    row_dot = jnp.sum(weights * weight_grads, axis=3, keepdims=True)
-    score_grads = (weights * (weight_grads - row_dot) * inv_root).astype(jnp.bfloat16)
-    query_grad = jnp.einsum(
-        "tghs,sgd->tghd", score_grads, key_mat, preferred_element_type=jnp.float32
-    ).astype(jnp.bfloat16)
-    key_part = jnp.einsum("tghs,tghd->sgd", score_grads, query, preferred_element_type=jnp.float32)
-    value_part = jnp.einsum(
-        "tghs,tghd->sgd", weights.astype(jnp.bfloat16), grads, preferred_element_type=jnp.float32
-    )
-    return query_grad, key_part, value_part
 
 
 def attend_kernel(q_ref, g_ref, k_ref, v_ref, m_ref, dq_ref, kp_ref, vp_ref):
@@ -156,13 +133,12 @@
     )(packed, weighted, kv_all, kv_all, mask)
 
 
-def body(rollout_rows, routing, segment_labels, upstream, passes, group_ids):
+def step(rollout_rows, routing, segment_labels, upstream, passes, group_ids):
     dp_size = lax.axis_size("dp")
     sp_size = lax.axis_size("sp")
     dp_index = lax.axis_index("dp")
     sp_index = lax.axis_index("sp")
     token_rows = rollout_rows.shape[0]
-    query_group = QUERY_HEADS // KEY_VALUE_HEADS
     kv_width = 2 * KEY_VALUE_HEADS * HEAD_SIZE
     longest_segment = sp_size * token_rows // 2
     reach = min(sp_size - 1, (longest_segment + token_rows - 2) // token_rows)
@@ -202,23 +178,19 @@
     query_parts, key_parts, value_parts = [], [], []
     for part in range(2):
         query_grad, key_part, value_part = attend_pallas(
-            packed_q,
-            weighted,
-            kv_all,
-            mask,
-            part * groups,
-            groups,
+            packed_q, weighted, kv_all, mask, part * groups, groups
         )
         partial = jnp.concatenate([key_part, value_part], axis=1).reshape(
             reach + 1, token_rows, 2 * groups * HEAD_SIZE
         )
         total = partial[0]
         for shift in range(1, reach + 1):
-            total = total + lax.ppermute(
+            arrived = lax.ppermute(
                 partial[shift].astype(jnp.bfloat16),
                 "sp",
                 [(k, k - shift) for k in range(shift, sp_size)],
-            ).astype(jnp.float32)
+            )
+            total = total + arrived.astype(jnp.float32)
         query_parts.append(query_grad)
         key_parts.append(total[:, : groups * HEAD_SIZE])
         value_parts.append(total[:, groups * HEAD_SIZE :])
@@ -231,7 +203,7 @@
 
 def solution(mesh):
     return jax.shard_map(
-        body,
+        step,
         mesh=mesh,
         in_specs=(
             P(("grp", "dp", "sp"), None),

time: 92.3 us -> 92.3 us (level)
  no operation moved by 1% of the time
where the time goes in v8:
time: 92.3 us; the launch traced here: 91.8 us
  waiting for transfers between devices  35.2 us (38%)
  starting transfers between devices  21.8 us (24%)
  Pallas kernels  19.6 us (21%)
  other arithmetic  7.22 us (8%)
  matrix products  5.76 us (6%)
  local copies, waits for them, and re-layouts  1.21 us (1%)
  between operations  1.02 us (1%)
    pallas_call x2, Pallas kernels, attend_pallas(): pl.pallas_call(attend_kernel, grid=(groups,), in_specs=[pl.BlockSpec((tok...  19.6 us
    ppermute x4, waiting for transfers between devices, step(): lax.ppermute(partial[shift].astype(jnp.bfloat16), 'sp', [(k, k - shift) f...  16 us
    all_to_all x2, waiting for transfers between devices, send(): lax.all_to_all(outgoing.reshape(dp_size, capacity, -1), 'dp', split_axis=...  10.5 us
    ppermute x2, starting transfers between devices, step(): lax.ppermute(kv_local, 'sp', [(k, k + shift) for k in range(sp_size - shi...  8.68 us
    ppermute x2, waiting for transfers between devices, step(): lax.ppermute(kv_local, 'sp', [(k, k + shift) for k in range(sp_size - shi...  8.68 us
    all_to_all x2, starting transfers between devices, send(): lax.all_to_all(outgoing.reshape(dp_size, capacity, -1), 'dp', split_axis=...  7.84 us
    ppermute x4, starting transfers between devices, step(): lax.ppermute(partial[shift].astype(jnp.bfloat16), 'sp', [(k, k - shift) f...  5.3 us
    dot_general x2, matrix products, send(): jnp.dot(send_pick, columns, preferred_element_type=jnp.float32)  4.03 us
  transfers between devices with their start and end apart: 8, of which 7 were waited for; matrix products, arithmetic and copies ran while one was open for 8% of the time, Pallas kernels for 0%

profile of v8, /device:TPU:0, one launch (start us, length us, event | category | flops | bytes accessed | tf_op | source)
XLA Modules:
  0.0 91.8 jit_solution(11449424610103885032)
XLA Ops:
  2.6 2.0 %convolution_convert_fusion.2 = bf16[256,1024]{1,0:T(8,128)(2,1)} fusion(bf16[128,5120]{1,0:T(8,128)(2,1)} %param.6, s32[128]{0:T(128)S(1)} %multiply_add_fusion), kind=kOutput, calls=%fused_computation.4 | convolution fusion | flops 67403776 | bytes 786944 | tf_op jit(solution)/shard_map/dot_general | solution.py:40
  4.7 4.2 %all-to-all-start.1 = ((bf16[4,64,1024]{2,1,0:T(8,128)(2,1)}), bf16[4,64,1024]{2,1,0:T(8,128)(2,1)S(1)}, u32[]{:S(2)}, u32[]{:S(2)}) async-start(bf16[4,64,1024]{2,1,0:T(8,128)(2,1)} %bitcast.8), calls=%async_computation.1 | async-start | bytes 1048576 | tf_op jit(solution)/shard_map/all_to_all | solution.py:43
  8.9 0.9 fusion.20
  10.7 1.3 %fusion.g_ref = bf16[128,4096]{1,0:T(8,128)(2,1)} fusion(bf16[1,128,4096]{2,1,0:T(8,128)(2,1)S(1)} %copy-done.2, f32[128]{0:T(128)S(1)} %select_reduce_fusion.2), kind=kLoop, calls=%fused_computation.3 | loop fusion | flops 1572864 | bytes 2097664 | tf_op jit(solution)/shard_map/convert_element_type | solution.py:166
  11.9 2.0 %convolution_convert_fusion = bf16[256,4096]{1,0:T(8,128)(2,1)} fusion(bf16[128,5120]{1,0:T(8,128)(2,1)S(1)} %copy-done.1, s32[128]{0:T(128)S(1)} %multiply_add_fusion), kind=kOutput, calls=%fused_computation | convolution fusion | flops 269516800 | bytes 3146240 | tf_op jit(solution)/shard_map/dot_general | solution.py:40
  13.9 3.8 %all-to-all-done.1 = bf16[4,64,1024]{2,1,0:T(8,128)(2,1)S(1)} async-done(((bf16[4,64,1024]{2,1,0:T(8,128)(2,1)}), bf16[4,64,1024]{2,1,0:T(8,128)(2,1)S(1)}, u32[]{:S(2)}, u32[]{:S(2)}) %all-to-all-start.1) | async-done | bytes 524320 | tf_op jit(solution)/shard_map/all_to_all | solution.py:43
  17.7 3.6 %all-to-all-start = ((bf16[4,64,4096]{2,1,0:T(8,128)(2,1)}), bf16[4,64,4096]{2,1,0:T(8,128)(2,1)S(1)}, u32[]{:S(2)}, u32[]{:S(2)}) async-start(bf16[4,64,4096]{2,1,0:T(8,128)(2,1)} %bitcast.4), calls=%async_computation | async-start | bytes 4194304 | tf_op jit(solution)/shard_map/all_to_all | solution.py:43
  21.7 4.2 %collective-permute-start = (bf16[128,1152]{1,0:T(8,128)(2,1)S(1)}, bf16[128,1152]{1,0:T(8,128)(2,1)S(1)}, u32[]{:S(2)}, u32[]{:S(2)}) collective-permute-start(bf16[128,1152]{1,0:T(8,128)(2,1)S(1)} %pad_maximum_fusion.1), channel_id=1, source_target_pairs={{0,1},{1,2},{2,3},{4,5},{5,6},{6,7},{8,9},{9,10},{10,11},{12,13},{... | collective-permute-start | bytes 884744 | tf_op jit(solution)/shard_map/ppermute | solution.py:152
  25.9 4.5 %collective-permute-start.1 = (bf16[128,1152]{1,0:T(8,128)(2,1)S(1)}, bf16[128,1152]{1,0:T(8,128)(2,1)S(1)}, u32[]{:S(2)}, u32[]{:S(2)}) collective-permute-start(bf16[128,1152]{1,0:T(8,128)(2,1)S(1)} %pad_maximum_fusion.1), channel_id=1, source_target_pairs={{0,2},{1,3},{4,6},{5,7},{8,10},{9,11},{12,14},{13,15},{16,18},{17,... | collective-permute-start | bytes 884744 | tf_op jit(solution)/shard_map/ppermute | solution.py:152
  30.5 2.8 %collective-permute-done = bf16[128,1152]{1,0:T(8,128)(2,1)S(1)} collective-permute-done((bf16[128,1152]{1,0:T(8,128)(2,1)S(1)}, bf16[128,1152]{1,0:T(8,128)(2,1)S(1)}, u32[]{:S(2)}, u32[]{:S(2)}) %collective-permute-start) | collective-permute-done | bytes 294944 | tf_op jit(solution)/shard_map/ppermute | solution.py:152
  33.3 5.9 %collective-permute-done.1 = bf16[128,1152]{1,0:T(8,128)(2,1)S(1)} collective-permute-done((bf16[128,1152]{1,0:T(8,128)(2,1)S(1)}, bf16[128,1152]{1,0:T(8,128)(2,1)S(1)}, u32[]{:S(2)}, u32[]{:S(2)}) %collective-permute-start.1) | collective-permute-done | bytes 294944 | tf_op jit(solution)/shard_map/ppermute | solution.py:152
  39.4 0.9 and_convert_fusion.m_ref
  40.3 6.7 %all-to-all-done = bf16[4,64,4096]{2,1,0:T(8,128)(2,1)S(1)} async-done(((bf16[4,64,4096]{2,1,0:T(8,128)(2,1)}), bf16[4,64,4096]{2,1,0:T(8,128)(2,1)S(1)}, u32[]{:S(2)}, u32[]{:S(2)}) %all-to-all-start) | async-done | bytes 2097184 | tf_op jit(solution)/shard_map/all_to_all | solution.py:43
  47.0 1.5 %convolution_convert_fusion.1.q_ref = bf16[128,4096]{1,0:T(8,128)(2,1)} fusion(bf16[256,4096]{1,0:T(8,128)(2,1)S(1)} %bitcast.29, s32[128]{0:T(128)S(1)} %add_subtract_fusion), kind=kOutput, calls=%fused_computation.1 | convolution fusion | flops 268992512 | bytes 3146240 | tf_op jit(solution)/shard_map/dot_general | solution.py:61
  48.4 9.8 %shard_map.77 = (bf16[128,2048]{1,0:T(8,128)(2,1)}, f32[384,256]{1,0:T(8,128)}, f32[384,256]{1,0:T(8,128)}) custom-call(bf16[128,4096]{1,0:T(8,128)(2,1)} %convolution_convert_fusion.1.q_ref, bf16[128,4096]{1,0:T(8,128)(2,1)} %fusion.g_ref, bf16[384,1152]{1,0:T(8,128)(2,1)} %copy-done, bf16[384,1152]{1,0:T(8,128)(2,1)} %copy-done, ...), custom_call_target="tpu_custom_call" | custom-call | flops 1006632960 | bytes 2949120 | tf_op jit(solution)/shard_map/pallas_call | solution.py:110
  58.2 9.9 %shard_map.78 = (bf16[128,2048]{1,0:T(8,128)(2,1)}, f32[384,256]{1,0:T(8,128)}, f32[384,256]{1,0:T(8,128)}) custom-call(bf16[128,4096]{1,0:T(8,128)(2,1)} %convolution_convert_fusion.1.q_ref, bf16[128,4096]{1,0:T(8,128)(2,1)} %fusion.g_ref, bf16[384,1152]{1,0:T(8,128)(2,1)} %copy-done, bf16[384,1152]{1,0:T(8,128)(2,1)} %copy-done, ...), custom_call_target="tpu_custom_call" | custom-call | flops 1006632960 | bytes 2949120 | tf_op jit(solution)/shard_map/pallas_call | solution.py:110
  68.3 1.4 %collective-permute-start.2 = (bf16[128,512]{1,0:T(8,128)(2,1)S(1)}, bf16[128,512]{1,0:T(8,128)(2,1)S(1)}, u32[]{:S(2)}, u32[]{:S(2)}) collective-permute-start(bf16[128,512]{1,0:T(8,128)(2,1)S(1)} %get-tuple-element.16), channel_id=1, source_target_pairs={{1,0},{2,1},{3,2},{5,4},{6,5},{7,6},{9,8},{10,9},{11,10},{13,12},{... | collective-permute-start | bytes 393224 | tf_op jit(solution)/shard_map/ppermute | solution.py:188
  69.7 1.3 %collective-permute-start.3 = (bf16[128,512]{1,0:T(8,128)(2,1)S(1)}, bf16[128,512]{1,0:T(8,128)(2,1)S(1)}, u32[]{:S(2)}, u32[]{:S(2)}) collective-permute-start(bf16[128,512]{1,0:T(8,128)(2,1)S(1)} %get-tuple-element.17), channel_id=1, source_target_pairs={{2,0},{3,1},{6,4},{7,5},{10,8},{11,9},{14,12},{15,13},{18,16},{19,... | collective-permute-start | bytes 393224 | tf_op jit(solution)/shard_map/ppermute | solution.py:188
  71.2 1.3 %collective-permute-start.4 = (bf16[128,512]{1,0:T(8,128)(2,1)S(1)}, bf16[128,512]{1,0:T(8,128)(2,1)S(1)}, u32[]{:S(2)}, u32[]{:S(2)}) collective-permute-start(bf16[128,512]{1,0:T(8,128)(2,1)S(1)} %get-tuple-element.18), channel_id=1, source_target_pairs={{1,0},{2,1},{3,2},{5,4},{6,5},{7,6},{9,8},{10,9},{11,10},{13,12},{... | collective-permute-start | bytes 393224 | tf_op jit(solution)/shard_map/ppermute | solution.py:188
  72.5 1.3 %collective-permute-start.5 = (bf16[128,512]{1,0:T(8,128)(2,1)S(1)}, bf16[128,512]{1,0:T(8,128)(2,1)S(1)}, u32[]{:S(2)}, u32[]{:S(2)}) collective-permute-start(bf16[128,512]{1,0:T(8,128)(2,1)S(1)} %get-tuple-element.19), channel_id=1, source_target_pairs={{2,0},{3,1},{6,4},{7,5},{10,8},{11,9},{14,12},{15,13},{18,16},{19,... | collective-permute-start | bytes 393224 | tf_op jit(solution)/shard_map/ppermute | solution.py:188
  73.9 1.1 %maximum_bitcast_fusion = bf16[1,128,4096]{2,1,0:T(8,128)(2,1)} fusion(bf16[128,2048]{1,0:T(8,128)(2,1)S(1)} %copy-done.4, bf16[128,2048]{1,0:T(8,128)(2,1)S(1)} %copy-done.3), kind=kLoop, calls=%fused_computation.6 | loop fusion | flops 2097152 | bytes 2097152 | tf_op jit(solution)/shard_map/reshape | solution.py:197
  74.9 1.1 %collective-permute-done.2 = bf16[128,512]{1,0:T(8,128)(2,1)S(1)} collective-permute-done((bf16[128,512]{1,0:T(8,128)(2,1)S(1)}, bf16[128,512]{1,0:T(8,128)(2,1)S(1)}, u32[]{:S(2)}, u32[]{:S(2)}) %collective-permute-start.2) | collective-permute-done | bytes 131104 | tf_op jit(solution)/shard_map/ppermute | solution.py:188
  76.0 10.8 %collective-permute-done.3 = bf16[128,512]{1,0:T(8,128)(2,1)S(1)} collective-permute-done((bf16[128,512]{1,0:T(8,128)(2,1)S(1)}, bf16[128,512]{1,0:T(8,128)(2,1)S(1)}, u32[]{:S(2)}, u32[]{:S(2)}) %collective-permute-start.3) | collective-permute-done | bytes 131104 | tf_op jit(solution)/shard_map/ppermute | solution.py:188
  86.9 4.1 %collective-permute-done.5 = bf16[128,512]{1,0:T(8,128)(2,1)S(1)} collective-permute-done((bf16[128,512]{1,0:T(8,128)(2,1)S(1)}, bf16[128,512]{1,0:T(8,128)(2,1)S(1)}, u32[]{:S(2)}, u32[]{:S(2)}) %collective-permute-start.5) | collective-permute-done | bytes 131104 | tf_op jit(solution)/shard_map/ppermute | solution.py:188
  (64 shorter events, 4.6 us)
Async XLA Ops:
  0.6 9.4 %copy-start.11 = (s32[16]{0:T(128)S(1)}, s32[16]{0:T(128)}, u32[]{:S(2)}) copy-start(s32[16]{0:T(128)} %param.10) | copy-start | bytes 196
  0.6 9.4 %copy-start.10 = (s32[16]{0:T(128)S(1)}, s32[16]{0:T(128)}, u32[]{:S(2)}) copy-start(s32[16]{0:T(128)} %param.11) | copy-start | bytes 196
  0.7 9.9 %copy-start.9 = (s32[1,128]{1,0:T(1,128)S(1)}, s32[1,128]{1,0:T(1,128)}, u32[]{:S(2)}) copy-start(s32[1,128]{1,0:T(1,128)} %param.8) | copy-start | bytes 1540
  0.7 10.0 %copy-start.2 = (bf16[1,128,4096]{2,1,0:T(8,128)(2,1)S(1)}, bf16[1,128,4096]{2,1,0:T(8,128)(2,1)}, u32[]{:S(2)}) copy-start(bf16[1,128,4096]{2,1,0:T(8,128)(2,1)} %param.9) | copy-start | bytes 3145732
  1.6 10.4 %copy-start.1 = (bf16[128,5120]{1,0:T(8,128)(2,1)S(1)}, bf16[128,5120]{1,0:T(8,128)(2,1)}, u32[]{:S(2)}) copy-start(bf16[128,5120]{1,0:T(8,128)(2,1)} %param.6) | copy-start | bytes 3932164
  4.7 13.1 %all-to-all-start.1 = ((bf16[4,64,1024]{2,1,0:T(8,128)(2,1)}), bf16[4,64,1024]{2,1,0:T(8,128)(2,1)S(1)}, u32[]{:S(2)}, u32[]{:S(2)}) async-start(bf16[4,64,1024]{2,1,0:T(8,128)(2,1)} %bitcast.8), calls=%async_computation.1 | async-start | bytes 1048576 | tf_op jit(solution)/shard_map/all_to_all | solution.py:43
  17.7 29.2 %all-to-all-start = ((bf16[4,64,4096]{2,1,0:T(8,128)(2,1)}), bf16[4,64,4096]{2,1,0:T(8,128)(2,1)S(1)}, u32[]{:S(2)}, u32[]{:S(2)}) async-start(bf16[4,64,4096]{2,1,0:T(8,128)(2,1)} %bitcast.4), calls=%async_computation | async-start | bytes 4194304 | tf_op jit(solution)/shard_map/all_to_all | solution.py:43
  21.7 11.6 %collective-permute-start = (bf16[128,1152]{1,0:T(8,128)(2,1)S(1)}, bf16[128,1152]{1,0:T(8,128)(2,1)S(1)}, u32[]{:S(2)}, u32[]{:S(2)}) collective-permute-start(bf16[128,1152]{1,0:T(8,128)(2,1)S(1)} %pad_maximum_fusion.1), channel_id=1, source_target_pairs={{0,1},{1,2},{2,3},{4,5},{5,6},{6,7},{8,9},{9,10},{10,11},{12,13},{... | collective-permute-start | bytes 884744 | tf_op jit(solution)/shard_map/ppermute | solution.py:152
  25.9 13.2 %collective-permute-start.1 = (bf16[128,1152]{1,0:T(8,128)(2,1)S(1)}, bf16[128,1152]{1,0:T(8,128)(2,1)S(1)}, u32[]{:S(2)}, u32[]{:S(2)}) collective-permute-start(bf16[128,1152]{1,0:T(8,128)(2,1)S(1)} %pad_maximum_fusion.1), channel_id=1, source_target_pairs={{0,2},{1,3},{4,6},{5,7},{8,10},{9,11},{12,14},{13,15},{16,18},{17,... | collective-permute-start | bytes 884744 | tf_op jit(solution)/shard_map/ppermute | solution.py:152
  39.2 9.2 %copy-start = (bf16[384,1152]{1,0:T(8,128)(2,1)}, bf16[384,1152]{1,0:T(8,128)(2,1)S(1)}, u32[]{:S(2)}) copy-start(bf16[384,1152]{1,0:T(8,128)(2,1)S(1)} %pad_maximum_fusion.k_ref.v_ref) | copy-start | bytes 2654212
  58.2 9.9 %copy-start.8 = (f32[384,256]{1,0:T(8,128)S(1)}, f32[384,256]{1,0:T(8,128)}, u32[]{:S(2)}) copy-start(f32[384,256]{1,0:T(8,128)} %get-tuple-element.10) | copy-start | bytes 1179652
  58.2 9.9 %copy-start.7 = (f32[384,256]{1,0:T(8,128)S(1)}, f32[384,256]{1,0:T(8,128)}, u32[]{:S(2)}) copy-start(f32[384,256]{1,0:T(8,128)} %get-tuple-element.11) | copy-start | bytes 1179652
  68.1 3.0 %copy-start.6 = (f32[384,256]{1,0:T(8,128)S(1)}, f32[384,256]{1,0:T(8,128)}, u32[]{:S(2)}) copy-start(f32[384,256]{1,0:T(8,128)} %get-tuple-element.12) | copy-start | bytes 1179652
  68.1 3.0 %copy-start.5 = (f32[384,256]{1,0:T(8,128)S(1)}, f32[384,256]{1,0:T(8,128)}, u32[]{:S(2)}) copy-start(f32[384,256]{1,0:T(8,128)} %get-tuple-element.13) | copy-start | bytes 1179652
  68.3 5.6 %copy-start.3 = (bf16[128,2048]{1,0:T(8,128)(2,1)S(1)}, bf16[128,2048]{1,0:T(8,128)(2,1)}, u32[]{:S(2)}) copy-start(bf16[128,2048]{1,0:T(8,128)(2,1)} %get-tuple-element.8) | copy-start | bytes 1572868
  68.3 5.6 %copy-start.4 = (bf16[128,2048]{1,0:T(8,128)(2,1)S(1)}, bf16[128,2048]{1,0:T(8,128)(2,1)}, u32[]{:S(2)}) copy-start(bf16[128,2048]{1,0:T(8,128)(2,1)} %get-tuple-element.9) | copy-start | bytes 1572868
  68.3 7.7 %collective-permute-start.2 = (bf16[128,512]{1,0:T(8,128)(2,1)S(1)}, bf16[128,512]{1,0:T(8,128)(2,1)S(1)}, u32[]{:S(2)}, u32[]{:S(2)}) collective-permute-start(bf16[128,512]{1,0:T(8,128)(2,1)S(1)} %get-tuple-element.16), channel_id=1, source_target_pairs={{1,0},{2,1},{3,2},{5,4},{6,5},{7,6},{9,8},{10,9},{11,10},{13,12},{... | collective-permute-start | bytes 393224 | tf_op jit(solution)/shard_map/ppermute | solution.py:188
  69.7 17.1 %collective-permute-start.3 = (bf16[128,512]{1,0:T(8,128)(2,1)S(1)}, bf16[128,512]{1,0:T(8,128)(2,1)S(1)}, u32[]{:S(2)}, u32[]{:S(2)}) collective-permute-start(bf16[128,512]{1,0:T(8,128)(2,1)S(1)} %get-tuple-element.17), channel_id=1, source_target_pairs={{2,0},{3,1},{6,4},{7,5},{10,8},{11,9},{14,12},{15,13},{18,16},{19,... | collective-permute-start | bytes 393224 | tf_op jit(solution)/shard_map/ppermute | solution.py:188
  71.2 15.6 %collective-permute-start.4 = (bf16[128,512]{1,0:T(8,128)(2,1)S(1)}, bf16[128,512]{1,0:T(8,128)(2,1)S(1)}, u32[]{:S(2)}, u32[]{:S(2)}) collective-permute-start(bf16[128,512]{1,0:T(8,128)(2,1)S(1)} %get-tuple-element.18), channel_id=1, source_target_pairs={{1,0},{2,1},{3,2},{5,4},{6,5},{7,6},{9,8},{10,9},{11,10},{13,12},{... | collective-permute-start | bytes 393224 | tf_op jit(solution)/shard_map/ppermute | solution.py:188
  72.5 18.5 %collective-permute-start.5 = (bf16[128,512]{1,0:T(8,128)(2,1)S(1)}, bf16[128,512]{1,0:T(8,128)(2,1)S(1)}, u32[]{:S(2)}, u32[]{:S(2)}) collective-permute-start(bf16[128,512]{1,0:T(8,128)(2,1)S(1)} %get-tuple-element.19), channel_id=1, source_target_pairs={{2,0},{3,1},{6,4},{7,5},{10,8},{11,9},{14,12},{15,13},{18,16},{19,... | collective-permute-start | bytes 393224 | tf_op jit(solution)/shard_map/ppermute | solution.py:188

commit v9 on v8

--- a/solution.py
+++ b/solution.py
@@ -32,20 +32,7 @@
     targets = jnp.arange(dp_size, dtype=jnp.int32)
     hit_table = (own_plan[:, None] == targets[None, :]).astype(jnp.int32)
     rank_rows = jnp.sum((jnp.cumsum(hit_table, axis=0) - 1) * hit_table, axis=1)
-    slot_ids = own_plan * capacity + rank_rows
     slots = jnp.arange(dp_size * capacity, dtype=jnp.int32)
-    send_pick = (slots[:, None] == slot_ids[None, :]).astype(rollout_rows.dtype)
-
-    def send(columns):
-        outgoing = jnp.dot(send_pick, columns, preferred_element_type=jnp.float32).astype(
-            columns.dtype
-        )
-        return lax.all_to_all(
-            outgoing.reshape(dp_size, capacity, -1), "dp", split_axis=0, concat_axis=0, tiled=True
-        ).reshape(dp_size * capacity, -1)
-
-    arrived_kv = send(rollout_rows[:, QUERY_HEADS * HEAD_SIZE :])
-    arrived_q = send(rollout_rows[:, : QUERY_HEADS * HEAD_SIZE])
     load_table = jnp.sum((column_plan == dp_index).astype(jnp.int32), axis=1)
     end_marks = jnp.cumsum(load_table)
     start_marks = end_marks - load_table
@@ -54,13 +41,38 @@
     chosen_start = jnp.sum(
         jnp.where(source[:, None] == targets[None, :], start_marks[None, :], 0), axis=1
     )
-    pick_ids = source * capacity + positions - chosen_start
-    recv_pick = (pick_ids[:, None] == slots[None, :]).astype(arrived_kv.dtype)
-
-    def receive(arrived):
-        return jnp.dot(recv_pick, arrived, preferred_element_type=jnp.float32).astype(arrived.dtype)
-
-    return receive(arrived_q), receive(arrived_kv)
+
+    def send(columns, by_permute):
+        target_slot = (own_plan - dp_index) % dp_size if by_permute else own_plan
+        send_pick = (slots[:, None] == (target_slot * capacity + rank_rows)[None, :]).astype(
+            columns.dtype
+        )
+        outgoing = jnp.dot(send_pick, columns, preferred_element_type=jnp.float32).astype(
+            columns.dtype
+        ).reshape(dp_size, capacity, -1)
+        if by_permute:
+            arrived = jnp.stack(
+                [outgoing[0]]
+                + [
+                    lax.ppermute(
+                        outgoing[shift], "dp", [(k, (k + shift) % dp_size) for k in range(dp_size)]
+                    )
+                    for shift in range(1, dp_size)
+                ]
+            )
+            source_slot = (dp_index - source) % dp_size
+        else:
+            arrived = lax.all_to_all(outgoing, "dp", split_axis=0, concat_axis=0, tiled=True)
+            source_slot = source
+        pick_ids = source_slot * capacity + positions - chosen_start
+        recv_pick = (pick_ids[:, None] == slots[None, :]).astype(columns.dtype)
+        return jnp.dot(
+            recv_pick, arrived.reshape(dp_size * capacity, -1), preferred_element_type=jnp.float32
+        ).astype(columns.dtype)
+
+    packed_kv = send(rollout_rows[:, QUERY_HEADS * HEAD_SIZE :], True)
+    packed_q = send(rollout_rows[:, : QUERY_HEADS * HEAD_SIZE], False)
+    return packed_q, packed_kv
 
 
 def attend_kernel(q_ref, g_ref, k_ref, v_ref, m_ref, dq_ref, kp_ref, vp_ref):

time: 92.3 us -> 91.1 us (0.987)
  other arithmetic: 7.22 us -> 11.5 us
  waiting for transfers between devices: 35.2 us -> 31 us
  starting transfers between devices: 21.8 us -> 20.5 us
    all_to_all x2 -> x1, waiting for transfers between devices: 10.5 us -> 0.01 us  [send(): lax.all_to_all(outgoing, 'dp', split_axis=0, concat_axis=0, tiled=True)]
    ppermute x4, waiting for transfers between devices: 16 us -> 22 us  [step(): lax.ppermute(partial[shift].astype(jnp.bfloat16), 'sp', [(k, k - shift) f...]
    all_to_all x2 -> x1, starting transfers between devices: 7.84 us -> 3.74 us  [send(): lax.all_to_all(outgoing, 'dp', split_axis=0, concat_axis=0, tiled=True)]
    ppermute x0 -> x3, starting transfers between devices: none -> 3.48 us  [send(): lax.ppermute(outgoing[shift], 'dp', [(k, (k + shift) % dp_size) for k in...]
    another operation x5 -> x6, other arithmetic: 0.38 us -> 2.01 us  [the longest x1 1.04 us: send(): jnp.stack([outgoing[0]] + [lax.ppermute(outgoing[shift], 'dp', [(k, (k +...]
  transfers between devices with their start and end apart: 8 -> 10, of which waited for: 7 -> 5; matrix products, arithmetic and copies ran while one was open for 8% -> 13% of each run, Pallas kernels for 0% -> 0%
where the time goes in v9:
time: 91.1 us; the launch traced here: 90.6 us
  waiting for transfers between devices  31 us (34%)
  starting transfers between devices  20.5 us (23%)
  Pallas kernels  19.6 us (22%)
  other arithmetic  11.5 us (13%)
  matrix products  4.96 us (5%)
  local copies, waits for them, and re-layouts  1.94 us (2%)
  between operations  0.99 us (1%)
    ppermute x4, waiting for transfers between devices, step(): lax.ppermute(partial[shift].astype(jnp.bfloat16), 'sp', [(k, k - shift) f...  22 us
    pallas_call x2, Pallas kernels, attend_pallas(): pl.pallas_call(attend_kernel, grid=(groups,), in_specs=[pl.BlockSpec((tok...  19.6 us
    ppermute x2, waiting for transfers between devices, step(): lax.ppermute(kv_local, 'sp', [(k, k + shift) for k in range(sp_size - shi...  9 us
    ppermute x2, starting transfers between devices, step(): lax.ppermute(kv_local, 'sp', [(k, k + shift) for k in range(sp_size - shi...  8 us
    ppermute x4, starting transfers between devices, step(): lax.ppermute(partial[shift].astype(jnp.bfloat16), 'sp', [(k, k - shift) f...  5.3 us
    all_to_all x1, starting transfers between devices, send(): lax.all_to_all(outgoing, 'dp', split_axis=0, concat_axis=0, tiled=True)  3.74 us
    ppermute x3, starting transfers between devices, send(): lax.ppermute(outgoing[shift], 'dp', [(k, (k + shift) % dp_size) for k in...  3.48 us
    dot_general x2, matrix products, send(): jnp.dot(send_pick, columns, preferred_element_type=jnp.float32)  3.24 us
  transfers between devices with their start and end apart: 10, of which 5 were waited for; matrix products, arithmetic and copies ran while one was open for 13% of the time, Pallas kernels for 0%

profile of v9, /device:TPU:0, one launch (start us, length us, event | category | flops | bytes accessed | tf_op | source)
XLA Modules:
  0.0 90.6 jit_solution(7006300320668982123)
XLA Ops:
  0.7 0.8 dynamic-slice_bitcast_fusion
  2.6 1.2 %convolution_convert_fusion.2 = bf16[256,1024]{1,0:T(8,128)(2,1)S(1)} fusion(bf16[128,5120]{1,0:T(8,128)(2,1)} %param.6, s32[128]{0:T(128)S(1)} %get-tuple-element.30), kind=kOutput, calls=%fused_computation.4 | convolution fusion | flops 67403776 | bytes 786944 | tf_op jit(solution)/shard_map/dot_general | solution.py:50
  4.6 3.0 %collective-permute-start.1 = (bf16[64,1024]{1,0:T(8,128)(2,1)}, bf16[64,1024]{1,0:T(8,128)(2,1)S(1)}, u32[]{:S(2)}, u32[]{:S(2)}) collective-permute-start(bf16[64,1024]{1,0:T(8,128)(2,1)} %get-tuple-element.18), channel_id=1, source_target_pairs={{0,8},{4,12},{8,0},{12,4},{1,9},{5,13},{9,1},{13,5},{2,10},{6,14},... | collective-permute-start | bytes 393224 | tf_op jit(solution)/shard_map/ppermute | solution.py:57
  8.0 2.0 %convolution_convert_fusion = bf16[256,4096]{1,0:T(8,128)(2,1)} fusion(bf16[128,5120]{1,0:T(8,128)(2,1)S(1)} %copy-done.1, s32[128]{0:T(128)S(1)} %get-tuple-element.31), kind=kOutput, calls=%fused_computation | convolution fusion | flops 269516800 | bytes 3146240 | tf_op jit(solution)/shard_map/dot_general | solution.py:50
  10.1 3.7 %all-to-all-start = ((bf16[4,64,4096]{2,1,0:T(8,128)(2,1)}), bf16[4,64,4096]{2,1,0:T(8,128)(2,1)S(1)}, u32[]{:S(2)}, u32[]{:S(2)}) async-start(bf16[4,64,4096]{2,1,0:T(8,128)(2,1)} %bitcast.34), calls=%async_computation | async-start | bytes 4194304 | tf_op jit(solution)/shard_map/all_to_all | solution.py:65
  13.8 0.9 fusion.20
  18.8 1.3 %fusion.g_ref = bf16[128,4096]{1,0:T(8,128)(2,1)} fusion(bf16[1,128,4096]{2,1,0:T(8,128)(2,1)S(1)} %copy-done.2, f32[128]{0:T(128)S(1)} %select_reduce_fusion.2), kind=kLoop, calls=%fused_computation.3 | loop fusion | flops 1572864 | bytes 2097664 | tf_op jit(solution)/shard_map/convert_element_type | solution.py:178
  20.1 1.0 %pad_maximum_fusion.1 = bf16[4,64,1024]{2,1,0:T(8,128)(2,1)S(1)} fusion(bf16[1,64,1024]{2,1,0:T(8,128)(2,1)} %bitcast.11, bf16[1,64,1024]{2,1,0:T(8,128)(2,1)S(1)} %bitcast.36, bf16[1,64,1024]{2,1,0:T(8,128)(2,1)} %bitcast.9, bf16[1,64,1024]{2,1,0:T(8,128)(2,1)S(1)} %get-tuple-element.16), kind=kLoop, calls=%fused_computation.9 | loop fusion | flops 786432 | bytes 1048576 | tf_op jit(solution)/shard_map/stack | solution.py:54
  21.5 3.5 %collective-permute-start.3 = (bf16[128,1152]{1,0:T(8,128)(2,1)S(1)}, bf16[128,1152]{1,0:T(8,128)(2,1)S(1)}, u32[]{:S(2)}, u32[]{:S(2)}) collective-permute-start(bf16[128,1152]{1,0:T(8,128)(2,1)S(1)} %pad_maximum_fusion.2), channel_id=1, source_target_pairs={{0,1},{1,2},{2,3},{4,5},{5,6},{6,7},{8,9},{9,10},{10,11},{12,13},{... | collective-permute-start | bytes 884744 | tf_op jit(solution)/shard_map/ppermute | solution.py:164
  25.1 4.5 %collective-permute-start.4 = (bf16[128,1152]{1,0:T(8,128)(2,1)S(1)}, bf16[128,1152]{1,0:T(8,128)(2,1)S(1)}, u32[]{:S(2)}, u32[]{:S(2)}) collective-permute-start(bf16[128,1152]{1,0:T(8,128)(2,1)S(1)} %pad_maximum_fusion.2), channel_id=1, source_target_pairs={{0,2},{1,3},{4,6},{5,7},{8,10},{9,11},{12,14},{13,15},{16,18},{17,... | collective-permute-start | bytes 884744 | tf_op jit(solution)/shard_map/ppermute | solution.py:164
  29.6 2.8 %collective-permute-done.3 = bf16[128,1152]{1,0:T(8,128)(2,1)S(1)} collective-permute-done((bf16[128,1152]{1,0:T(8,128)(2,1)S(1)}, bf16[128,1152]{1,0:T(8,128)(2,1)S(1)}, u32[]{:S(2)}, u32[]{:S(2)}) %collective-permute-start.3) | collective-permute-done | bytes 294944 | tf_op jit(solution)/shard_map/ppermute | solution.py:164
  32.4 6.2 %collective-permute-done.4 = bf16[128,1152]{1,0:T(8,128)(2,1)S(1)} collective-permute-done((bf16[128,1152]{1,0:T(8,128)(2,1)S(1)}, bf16[128,1152]{1,0:T(8,128)(2,1)S(1)}, u32[]{:S(2)}, u32[]{:S(2)}) %collective-permute-start.4) | collective-permute-done | bytes 294944 | tf_op jit(solution)/shard_map/ppermute | solution.py:164
  38.9 0.9 %and_convert_fusion.m_ref = f32[384,128]{1,0:T(8,128)} fusion(s32[128]{0:T(128)S(1)} %iota_add_fusion, s32[128]{0:T(128)S(1)} %bitcast.41, s32[384]{0:T(512)S(1)} %fusion.18, s32[384]{0:T(512)S(1)} %convert_reduce_fusion, pred[384]{0:T(512)(128)(4,1)S(1)} %broadcast_compare_fusion), kind=kLoop, calls=%fused_computation.20 | loop fusion | flops 245760 | bytes 201088 | tf_op jit(solution)/shard_map/convert_element_type | solution.py:188
  39.8 1.5 %convolution_convert_fusion.1.q_ref = bf16[128,4096]{1,0:T(8,128)(2,1)} fusion(bf16[256,4096]{1,0:T(8,128)(2,1)S(1)} %bitcast.33, s32[128]{0:T(128)S(1)} %get-tuple-element.29), kind=kOutput, calls=%fused_computation.1 | convolution fusion | flops 268992512 | bytes 3146240 | tf_op jit(solution)/shard_map/dot_general | solution.py:69
  41.2 9.8 %shard_map.77 = (bf16[128,2048]{1,0:T(8,128)(2,1)}, f32[384,256]{1,0:T(8,128)}, f32[384,256]{1,0:T(8,128)}) custom-call(bf16[128,4096]{1,0:T(8,128)(2,1)} %convolution_convert_fusion.1.q_ref, bf16[128,4096]{1,0:T(8,128)(2,1)} %fusion.g_ref, bf16[384,1152]{1,0:T(8,128)(2,1)} %copy-done, bf16[384,1152]{1,0:T(8,128)(2,1)} %copy-done, ...), custom_call_target="tpu_custom_call" | custom-call | flops 1006632960 | bytes 2949120 | tf_op jit(solution)/shard_map/pallas_call | solution.py:122
  51.0 9.9 %shard_map.78 = (bf16[128,2048]{1,0:T(8,128)(2,1)}, f32[384,256]{1,0:T(8,128)}, f32[384,256]{1,0:T(8,128)}) custom-call(bf16[128,4096]{1,0:T(8,128)(2,1)} %convolution_convert_fusion.1.q_ref, bf16[128,4096]{1,0:T(8,128)(2,1)} %fusion.g_ref, bf16[384,1152]{1,0:T(8,128)(2,1)} %copy-done, bf16[384,1152]{1,0:T(8,128)(2,1)} %copy-done, ...), custom_call_target="tpu_custom_call" | custom-call | flops 1006632960 | bytes 2949120 | tf_op jit(solution)/shard_map/pallas_call | solution.py:122
  61.1 1.4 %collective-permute-start.5 = (bf16[128,512]{1,0:T(8,128)(2,1)S(1)}, bf16[128,512]{1,0:T(8,128)(2,1)S(1)}, u32[]{:S(2)}, u32[]{:S(2)}) collective-permute-start(bf16[128,512]{1,0:T(8,128)(2,1)S(1)} %get-tuple-element.20), channel_id=1, source_target_pairs={{1,0},{2,1},{3,2},{5,4},{6,5},{7,6},{9,8},{10,9},{11,10},{13,12},{... | collective-permute-start | bytes 393224 | tf_op jit(solution)/shard_map/ppermute | solution.py:200
  62.5 1.3 %collective-permute-start.6 = (bf16[128,512]{1,0:T(8,128)(2,1)S(1)}, bf16[128,512]{1,0:T(8,128)(2,1)S(1)}, u32[]{:S(2)}, u32[]{:S(2)}) collective-permute-start(bf16[128,512]{1,0:T(8,128)(2,1)S(1)} %get-tuple-element.21), channel_id=1, source_target_pairs={{2,0},{3,1},{6,4},{7,5},{10,8},{11,9},{14,12},{15,13},{18,16},{19,... | collective-permute-start | bytes 393224 | tf_op jit(solution)/shard_map/ppermute | solution.py:200
  64.0 1.3 %collective-permute-start.7 = (bf16[128,512]{1,0:T(8,128)(2,1)S(1)}, bf16[128,512]{1,0:T(8,128)(2,1)S(1)}, u32[]{:S(2)}, u32[]{:S(2)}) collective-permute-start(bf16[128,512]{1,0:T(8,128)(2,1)S(1)} %get-tuple-element.22), channel_id=1, source_target_pairs={{1,0},{2,1},{3,2},{5,4},{6,5},{7,6},{9,8},{10,9},{11,10},{13,12},{... | collective-permute-start | bytes 393224 | tf_op jit(solution)/shard_map/ppermute | solution.py:200
  65.3 1.3 %collective-permute-start.8 = (bf16[128,512]{1,0:T(8,128)(2,1)S(1)}, bf16[128,512]{1,0:T(8,128)(2,1)S(1)}, u32[]{:S(2)}, u32[]{:S(2)}) collective-permute-start(bf16[128,512]{1,0:T(8,128)(2,1)S(1)} %get-tuple-element.23), channel_id=1, source_target_pairs={{2,0},{3,1},{6,4},{7,5},{10,8},{11,9},{14,12},{15,13},{18,16},{19,... | collective-permute-start | bytes 393224 | tf_op jit(solution)/shard_map/ppermute | solution.py:200
  66.6 1.1 %maximum_bitcast_fusion = bf16[1,128,4096]{2,1,0:T(8,128)(2,1)} fusion(bf16[128,2048]{1,0:T(8,128)(2,1)S(1)} %copy-done.4, bf16[128,2048]{1,0:T(8,128)(2,1)S(1)} %copy-done.3), kind=kLoop, calls=%fused_computation.6 | loop fusion | flops 2097152 | bytes 2097152 | tf_op jit(solution)/shard_map/reshape | solution.py:209
  67.7 6.8 %collective-permute-done.5 = bf16[128,512]{1,0:T(8,128)(2,1)S(1)} collective-permute-done((bf16[128,512]{1,0:T(8,128)(2,1)S(1)}, bf16[128,512]{1,0:T(8,128)(2,1)S(1)}, u32[]{:S(2)}, u32[]{:S(2)}) %collective-permute-start.5) | collective-permute-done | bytes 131104 | tf_op jit(solution)/shard_map/ppermute | solution.py:200
  74.6 8.6 %collective-permute-done.6 = bf16[128,512]{1,0:T(8,128)(2,1)S(1)} collective-permute-done((bf16[128,512]{1,0:T(8,128)(2,1)S(1)}, bf16[128,512]{1,0:T(8,128)(2,1)S(1)}, u32[]{:S(2)}, u32[]{:S(2)}) %collective-permute-start.6) | collective-permute-done | bytes 131104 | tf_op jit(solution)/shard_map/ppermute | solution.py:200
  83.2 6.6 %collective-permute-done.8 = bf16[128,512]{1,0:T(8,128)(2,1)S(1)} collective-permute-done((bf16[128,512]{1,0:T(8,128)(2,1)S(1)}, bf16[128,512]{1,0:T(8,128)(2,1)S(1)}, u32[]{:S(2)}, u32[]{:S(2)}) %collective-permute-start.8) | collective-permute-done | bytes 131104 | tf_op jit(solution)/shard_map/ppermute | solution.py:200
  (68 shorter events, 8.3 us)
Async XLA Ops:
  0.6 7.4 %copy-start.1 = (bf16[128,5120]{1,0:T(8,128)(2,1)S(1)}, bf16[128,5120]{1,0:T(8,128)(2,1)}, u32[]{:S(2)}) copy-start(bf16[128,5120]{1,0:T(8,128)(2,1)} %param.6) | copy-start | bytes 3932164
  4.6 15.5 %collective-permute-start.1 = (bf16[64,1024]{1,0:T(8,128)(2,1)}, bf16[64,1024]{1,0:T(8,128)(2,1)S(1)}, u32[]{:S(2)}, u32[]{:S(2)}) collective-permute-start(bf16[64,1024]{1,0:T(8,128)(2,1)} %get-tuple-element.18), channel_id=1, source_target_pairs={{0,8},{4,12},{8,0},{12,4},{1,9},{5,13},{9,1},{13,5},{2,10},{6,14},... | collective-permute-start | bytes 393224 | tf_op jit(solution)/shard_map/ppermute | solution.py:57
  7.5 12.6 %collective-permute-start.2 = (bf16[64,1024]{1,0:T(8,128)(2,1)}, bf16[64,1024]{1,0:T(8,128)(2,1)}, u32[]{:S(2)}, u32[]{:S(2)}) collective-permute-start(bf16[64,1024]{1,0:T(8,128)(2,1)} %get-tuple-element.17), channel_id=1, source_target_pairs={{0,12},{4,0},{8,4},{12,8},{1,13},{5,1},{9,5},{13,9},{2,14},{6,2},{... | collective-permute-start | bytes 393224 | tf_op jit(solution)/shard_map/ppermute | solution.py:57
  7.5 12.6 %collective-permute-start = (bf16[64,1024]{1,0:T(8,128)(2,1)S(1)}, bf16[64,1024]{1,0:T(8,128)(2,1)}, u32[]{:S(2)}, u32[]{:S(2)}) collective-permute-start(bf16[64,1024]{1,0:T(8,128)(2,1)S(1)} %get-tuple-element.19), channel_id=1, source_target_pairs={{0,4},{4,8},{8,12},{12,0},{1,5},{5,9},{9,13},{13,1},{2,6},{6,10},{... | collective-permute-start | bytes 393224 | tf_op jit(solution)/shard_map/ppermute | solution.py:57
  10.0 7.7 %copy-start.10 = (s32[16]{0:T(128)S(1)}, s32[16]{0:T(128)}, u32[]{:S(2)}) copy-start(s32[16]{0:T(128)} %param.11) | copy-start | bytes 196
  10.1 8.7 %copy-start.9 = (s32[1,128]{1,0:T(1,128)S(1)}, s32[1,128]{1,0:T(1,128)}, u32[]{:S(2)}) copy-start(s32[1,128]{1,0:T(1,128)} %param.8) | copy-start | bytes 1540
  10.1 8.8 %copy-start.2 = (bf16[1,128,4096]{2,1,0:T(8,128)(2,1)S(1)}, bf16[1,128,4096]{2,1,0:T(8,128)(2,1)}, u32[]{:S(2)}) copy-start(bf16[1,128,4096]{2,1,0:T(8,128)(2,1)} %param.9) | copy-start | bytes 3145732
  10.1 29.7 %all-to-all-start = ((bf16[4,64,4096]{2,1,0:T(8,128)(2,1)}), bf16[4,64,4096]{2,1,0:T(8,128)(2,1)S(1)}, u32[]{:S(2)}, u32[]{:S(2)}) async-start(bf16[4,64,4096]{2,1,0:T(8,128)(2,1)} %bitcast.34), calls=%async_computation | async-start | bytes 4194304 | tf_op jit(solution)/shard_map/all_to_all | solution.py:65
  21.5 10.9 %collective-permute-start.3 = (bf16[128,1152]{1,0:T(8,128)(2,1)S(1)}, bf16[128,1152]{1,0:T(8,128)(2,1)S(1)}, u32[]{:S(2)}, u32[]{:S(2)}) collective-permute-start(bf16[128,1152]{1,0:T(8,128)(2,1)S(1)} %pad_maximum_fusion.2), channel_id=1, source_target_pairs={{0,1},{1,2},{2,3},{4,5},{5,6},{6,7},{8,9},{9,10},{10,11},{12,13},{... | collective-permute-start | bytes 884744 | tf_op jit(solution)/shard_map/ppermute | solution.py:164
  25.1 13.5 %collective-permute-start.4 = (bf16[128,1152]{1,0:T(8,128)(2,1)S(1)}, bf16[128,1152]{1,0:T(8,128)(2,1)S(1)}, u32[]{:S(2)}, u32[]{:S(2)}) collective-permute-start(bf16[128,1152]{1,0:T(8,128)(2,1)S(1)} %pad_maximum_fusion.2), channel_id=1, source_target_pairs={{0,2},{1,3},{4,6},{5,7},{8,10},{9,11},{12,14},{13,15},{16,18},{17,... | collective-permute-start | bytes 884744 | tf_op jit(solution)/shard_map/ppermute | solution.py:164
  38.7 2.5 %copy-start = (bf16[384,1152]{1,0:T(8,128)(2,1)}, bf16[384,1152]{1,0:T(8,128)(2,1)S(1)}, u32[]{:S(2)}) copy-start(bf16[384,1152]{1,0:T(8,128)(2,1)S(1)} %pad_maximum_fusion.k_ref.v_ref) | copy-start | bytes 2654212
  51.0 9.9 %copy-start.8 = (f32[384,256]{1,0:T(8,128)S(1)}, f32[384,256]{1,0:T(8,128)}, u32[]{:S(2)}) copy-start(f32[384,256]{1,0:T(8,128)} %get-tuple-element.10) | copy-start | bytes 1179652
  51.0 9.9 %copy-start.7 = (f32[384,256]{1,0:T(8,128)S(1)}, f32[384,256]{1,0:T(8,128)}, u32[]{:S(2)}) copy-start(f32[384,256]{1,0:T(8,128)} %get-tuple-element.11) | copy-start | bytes 1179652
  60.9 3.0 %copy-start.6 = (f32[384,256]{1,0:T(8,128)S(1)}, f32[384,256]{1,0:T(8,128)}, u32[]{:S(2)}) copy-start(f32[384,256]{1,0:T(8,128)} %get-tuple-element.12) | copy-start | bytes 1179652
  60.9 3.0 %copy-start.5 = (f32[384,256]{1,0:T(8,128)S(1)}, f32[384,256]{1,0:T(8,128)}, u32[]{:S(2)}) copy-start(f32[384,256]{1,0:T(8,128)} %get-tuple-element.13) | copy-start | bytes 1179652
  61.0 5.6 %copy-start.3 = (bf16[128,2048]{1,0:T(8,128)(2,1)S(1)}, bf16[128,2048]{1,0:T(8,128)(2,1)}, u32[]{:S(2)}) copy-start(bf16[128,2048]{1,0:T(8,128)(2,1)} %get-tuple-element.8) | copy-start | bytes 1572868
  61.0 5.6 %copy-start.4 = (bf16[128,2048]{1,0:T(8,128)(2,1)S(1)}, bf16[128,2048]{1,0:T(8,128)(2,1)}, u32[]{:S(2)}) copy-start(bf16[128,2048]{1,0:T(8,128)(2,1)} %get-tuple-element.9) | copy-start | bytes 1572868
  61.1 13.5 %collective-permute-start.5 = (bf16[128,512]{1,0:T(8,128)(2,1)S(1)}, bf16[128,512]{1,0:T(8,128)(2,1)S(1)}, u32[]{:S(2)}, u32[]{:S(2)}) collective-permute-start(bf16[128,512]{1,0:T(8,128)(2,1)S(1)} %get-tuple-element.20), channel_id=1, source_target_pairs={{1,0},{2,1},{3,2},{5,4},{6,5},{7,6},{9,8},{10,9},{11,10},{13,12},{... | collective-permute-start | bytes 393224 | tf_op jit(solution)/shard_map/ppermute | solution.py:200
  62.5 20.6 %collective-permute-start.6 = (bf16[128,512]{1,0:T(8,128)(2,1)S(1)}, bf16[128,512]{1,0:T(8,128)(2,1)S(1)}, u32[]{:S(2)}, u32[]{:S(2)}) collective-permute-start(bf16[128,512]{1,0:T(8,128)(2,1)S(1)} %get-tuple-element.21), channel_id=1, source_target_pairs={{2,0},{3,1},{6,4},{7,5},{10,8},{11,9},{14,12},{15,13},{18,16},{19,... | collective-permute-start | bytes 393224 | tf_op jit(solution)/shard_map/ppermute | solution.py:200
  64.0 19.2 %collective-permute-start.7 = (bf16[128,512]{1,0:T(8,128)(2,1)S(1)}, bf16[128,512]{1,0:T(8,128)(2,1)S(1)}, u32[]{:S(2)}, u32[]{:S(2)}) collective-permute-start(bf16[128,512]{1,0:T(8,128)(2,1)S(1)} %get-tuple-element.22), channel_id=1, source_target_pairs={{1,0},{2,1},{3,2},{5,4},{6,5},{7,6},{9,8},{10,9},{11,10},{13,12},{... | collective-permute-start | bytes 393224 | tf_op jit(solution)/shard_map/ppermute | solution.py:200
  65.3 24.4 %collective-permute-start.8 = (bf16[128,512]{1,0:T(8,128)(2,1)S(1)}, bf16[128,512]{1,0:T(8,128)(2,1)S(1)}, u32[]{:S(2)}, u32[]{:S(2)}) collective-permute-start(bf16[128,512]{1,0:T(8,128)(2,1)S(1)} %get-tuple-element.23), channel_id=1, source_target_pairs={{2,0},{3,1},{6,4},{7,5},{10,8},{11,9},{14,12},{15,13},{18,16},{19,... | collective-permute-start | bytes 393224 | tf_op jit(solution)/shard_map/ppermute | solution.py:200

commit v10 on v9

--- a/solution.py
+++ b/solution.py
@@ -1,3 +1,4 @@
+import functools
 import math
 
 import jax
@@ -75,74 +76,92 @@
     return packed_q, packed_kv
 
 
-def attend_kernel(q_ref, g_ref, k_ref, v_ref, m_ref, dq_ref, kp_ref, vp_ref):
+def attend_kernel(q_ref, g_ref, kv_ref, m_ref, dq_ref, local_ref, send_ref, *, first_group):
     inv_root = 1.0 / math.sqrt(HEAD_SIZE)
-    key_mat = k_ref[...]
-    value_mat = v_ref[...]
-    allowed = m_ref[...] > 0.5
-    key_sum = jnp.zeros(kp_ref.shape, jnp.float32)
-    value_sum = jnp.zeros(vp_ref.shape, jnp.float32)
-    for head in range(q_ref.shape[1] // HEAD_SIZE):
-        cols = slice(head * HEAD_SIZE, (head + 1) * HEAD_SIZE)
-        query_head = q_ref[:, cols]
-        grad_head = g_ref[:, cols]
-        scores = (
-            lax.dot_general(
-                key_mat, query_head, (((1,), (1,)), ((), ())), preferred_element_type=jnp.float32
-            )
-            * inv_root
-        )
-        scores = jnp.where(allowed, scores, -1e30)
-        row_top = jnp.max(scores, axis=0, keepdims=True)
-        scaled_exp = jnp.exp(scores - row_top)
-        weights = scaled_exp / jnp.sum(scaled_exp, axis=0, keepdims=True)
-        weight_grads = lax.dot_general(
-            value_mat, grad_head, (((1,), (1,)), ((), ())), preferred_element_type=jnp.float32
-        )
-        row_dot = jnp.sum(weights * weight_grads, axis=0, keepdims=True)
-        score_grads = (weights * (weight_grads - row_dot) * inv_root).astype(jnp.bfloat16)
-        dq_ref[:, cols] = lax.dot_general(
-            score_grads, key_mat, (((0,), (0,)), ((), ())), preferred_element_type=jnp.float32
-        ).astype(dq_ref.dtype)
-        key_sum = key_sum + jnp.dot(score_grads, query_head, preferred_element_type=jnp.float32)
-        value_sum = value_sum + jnp.dot(
-            weights.astype(jnp.bfloat16), grad_head, preferred_element_type=jnp.float32
-        )
-    kp_ref[...] = key_sum
-    vp_ref[...] = value_sum
-
-
-def attend_pallas(packed, weighted, kv_all, mask, first_group, groups):
+    token_rows = q_ref.shape[0]
+    groups = local_ref.shape[1] // (2 * HEAD_SIZE)
+    query_group = QUERY_HEADS // KEY_VALUE_HEADS
+    bias = m_ref[...]
+    for local_group in range(groups):
+        group = first_group + local_group
+        key_mat = kv_ref[:, group * HEAD_SIZE : (group + 1) * HEAD_SIZE]
+        value_mat = kv_ref[
+            :, (KEY_VALUE_HEADS + group) * HEAD_SIZE : (KEY_VALUE_HEADS + group + 1) * HEAD_SIZE
+        ]
+        key_sum = jnp.zeros(key_mat.shape, jnp.float32)
+        value_sum = jnp.zeros(value_mat.shape, jnp.float32)
+        for head in range(query_group):
+            cols = slice(
+                (local_group * query_group + head) * HEAD_SIZE,
+                (local_group * query_group + head + 1) * HEAD_SIZE,
+            )
+            query_head = q_ref[:, cols]
+            grad_head = g_ref[:, cols]
+            scores = (
+                lax.dot_general(
+                    key_mat, query_head, (((1,), (1,)), ((), ())), preferred_element_type=jnp.float32
+                )
+                * inv_root
+                + bias
+            )
+            row_top = jnp.max(scores, axis=0, keepdims=True)
+            scaled_exp = jnp.exp(scores - row_top)
+            weights = scaled_exp * (1.0 / jnp.sum(scaled_exp, axis=0, keepdims=True))
+            weight_grads = lax.dot_general(
+                value_mat, grad_head, (((1,), (1,)), ((), ())), preferred_element_type=jnp.float32
+            )
+            row_dot = jnp.sum(weights * weight_grads, axis=0, keepdims=True)
+            score_grads = (weights * (weight_grads - row_dot) * inv_root).astype(jnp.bfloat16)
+            dq_ref[:, cols] = lax.dot_general(
+                score_grads, key_mat, (((0,), (0,)), ((), ())), preferred_element_type=jnp.float32
+            ).astype(dq_ref.dtype)
+            key_sum = key_sum + jnp.dot(score_grads, query_head, preferred_element_type=jnp.float32)
+            value_sum = value_sum + jnp.dot(
+                weights.astype(jnp.bfloat16), grad_head, preferred_element_type=jnp.float32
+            )
+        key_cols = slice(local_group * HEAD_SIZE, (local_group + 1) * HEAD_SIZE)
+        value_cols = slice((groups + local_group) * HEAD_SIZE, (groups + local_group + 1) * HEAD_SIZE)
+        local_ref[:, key_cols] = key_sum[:token_rows]
+        local_ref[:, value_cols] = value_sum[:token_rows]
+        for back in range(send_ref.shape[0]):
+            rows = slice((back + 1) * token_rows, (back + 2) * token_rows)
+            send_ref[back, :, key_cols] = key_sum[rows].astype(send_ref.dtype)
+            send_ref[back, :, value_cols] = value_sum[rows].astype(send_ref.dtype)
+
+
+def attend_pallas(packed, weighted, kv_all, bias, part, groups):
     token_rows = packed.shape[0]
     key_rows = kv_all.shape[0]
-    group_width = QUERY_HEADS // KEY_VALUE_HEADS * HEAD_SIZE
+    reach = key_rows // token_rows - 1
+    part_width = groups * (QUERY_HEADS // KEY_VALUE_HEADS) * HEAD_SIZE
+    kv_width = 2 * groups * HEAD_SIZE
     heads = groups * (QUERY_HEADS // KEY_VALUE_HEADS)
     flops = 10 * token_rows * key_rows * HEAD_SIZE * heads
-    bytes_accessed = 6 * token_rows * heads * HEAD_SIZE + 12 * key_rows * groups * HEAD_SIZE + 4 * token_rows * key_rows
+    bytes_accessed = 6 * token_rows * part_width + 2 * key_rows * kv_all.shape[1] + 4 * token_rows * key_rows
+    whole = lambda i: (0, 0)
     return pl.pallas_call(
-        attend_kernel,
-        grid=(groups,),
+        functools.partial(attend_kernel, first_group=part * groups),
+        grid=(1,),
         in_specs=[
-            pl.BlockSpec((token_rows, group_width), lambda g: (0, first_group + g)),
-            pl.BlockSpec((token_rows, group_width), lambda g: (0, first_group + g)),
-            pl.BlockSpec((key_rows, HEAD_SIZE), lambda g: (0, first_group + g)),
-            pl.BlockSpec((key_rows, HEAD_SIZE), lambda g: (0, KEY_VALUE_HEADS + first_group + g)),
-            pl.BlockSpec((key_rows, token_rows), lambda g: (0, 0)),
+            pl.BlockSpec((token_rows, part_width), lambda i: (0, part)),
+            pl.BlockSpec((token_rows, part_width), lambda i: (0, part)),
+            pl.BlockSpec(kv_all.shape, whole),
+            pl.BlockSpec(bias.shape, whole),
         ],
         out_specs=[
-            pl.BlockSpec((token_rows, group_width), lambda g: (0, g)),
-            pl.BlockSpec((key_rows, HEAD_SIZE), lambda g: (0, g)),
-            pl.BlockSpec((key_rows, HEAD_SIZE), lambda g: (0, g)),
+            pl.BlockSpec((token_rows, part_width), whole),
+            pl.BlockSpec((token_rows, kv_width), whole),
+            pl.BlockSpec((reach, token_rows, kv_width), lambda i: (0, 0, 0)),
         ],
         out_shape=[
-            jax.ShapeDtypeStruct((token_rows, groups * group_width), jnp.bfloat16),
-            jax.ShapeDtypeStruct((key_rows, groups * HEAD_SIZE), jnp.float32),
-            jax.ShapeDtypeStruct((key_rows, groups * HEAD_SIZE), jnp.float32),
+            jax.ShapeDtypeStruct((token_rows, part_width), jnp.bfloat16),
+            jax.ShapeDtypeStruct((token_rows, kv_width), jnp.float32),
+            jax.ShapeDtypeStruct((reach, token_rows, kv_width), jnp.bfloat16),
         ],
         cost_estimate=pl.CostEstimate(
-            flops=flops, transcendentals=token_rows * key_rows * QUERY_HEADS, bytes_accessed=bytes_accessed
+            flops=flops, transcendentals=token_rows * key_rows * heads, bytes_accessed=bytes_accessed
         ),
-    )(packed, weighted, kv_all, kv_all, mask)
+    )(packed, weighted, kv_all, bias)
 
 
 def step(rollout_rows, routing, segment_labels, upstream, passes, group_ids):
@@ -185,22 +204,16 @@
         & (key_pos[None, :] <= query_pos[:, None])
         & (key_pos[None, :] >= 0)
     )
-    mask = allowed.T.astype(jnp.float32)
+    bias = jnp.where(allowed.T, 0.0, -1e30).astype(jnp.float32)
     groups = KEY_VALUE_HEADS // 2
     query_parts, key_parts, value_parts = [], [], []
     for part in range(2):
-        query_grad, key_part, value_part = attend_pallas(
-            packed_q, weighted, kv_all, mask, part * groups, groups
+        query_grad, total, outgoing = attend_pallas(
+            packed_q, weighted, kv_all, bias, part, groups
         )
-        partial = jnp.concatenate([key_part, value_part], axis=1).reshape(
-            reach + 1, token_rows, 2 * groups * HEAD_SIZE
-        )
-        total = partial[0]
         for shift in range(1, reach + 1):
             arrived = lax.ppermute(
-                partial[shift].astype(jnp.bfloat16),
-                "sp",
-                [(k, k - shift) for k in range(shift, sp_size)],
+                outgoing[shift - 1], "sp", [(k, k - shift) for k in range(shift, sp_size)]
             )
             total = total + arrived.astype(jnp.float32)
         query_parts.append(query_grad)

time: 91.1 us -> 110 us (1.21)
  waiting for transfers between devices: 31 us -> 45.9 us
  matrix products: 4.96 us -> 6.23 us
    ppermute x3, waiting for transfers between devices: 0.01 us -> 20.8 us  [send(): lax.ppermute(outgoing[shift], 'dp', [(k, (k + shift) % dp_size) for k in...]
    ppermute x4, waiting for transfers between devices: 22 us -> 18.2 us  [step(): lax.ppermute(outgoing[shift - 1], 'sp', [(k, k - shift) for k in range(sh...]
    ppermute x2, waiting for transfers between devices: 9 us -> 6.91 us  [step(): lax.ppermute(kv_local, 'sp', [(k, k + shift) for k in range(sp_size - shi...]
    dot_general x2, matrix products: 3.24 us -> 4.51 us  [send(): jnp.dot(send_pick, columns, preferred_element_type=jnp.float32)]
  transfers between devices with their start and end apart: 10 -> 10, of which waited for: 5 -> 6; matrix products, arithmetic and copies ran while one was open for 13% -> 13% of each run, Pallas kernels for 0% -> 0%
where the time goes in v10:
time: 110 us; the launch traced here: 109 us
  waiting for transfers between devices  45.9 us (42%)
  starting transfers between devices  21.2 us (19%)
  Pallas kernels  19.7 us (18%)
  other arithmetic  12.2 us (11%)
  matrix products  6.23 us (6%)
  local copies, waits for them, and re-layouts  2.64 us (2%)
    ppermute x3, waiting for transfers between devices, send(): lax.ppermute(outgoing[shift], 'dp', [(k, (k + shift) % dp_size) for k in...  20.8 us
    pallas_call x2, Pallas kernels, attend_pallas(): pl.pallas_call(functools.partial(attend_kernel, first_group=part * groups...  19.7 us
    ppermute x4, waiting for transfers between devices, step(): lax.ppermute(outgoing[shift - 1], 'sp', [(k, k - shift) for k in range(sh...  18.2 us
    ppermute x2, starting transfers between devices, step(): lax.ppermute(kv_local, 'sp', [(k, k + shift) for k in range(sp_size - shi...  9 us
    ppermute x2, waiting for transfers between devices, step(): lax.ppermute(kv_local, 'sp', [(k, k + shift) for k in range(sp_size - shi...  6.91 us
    ppermute x4, starting transfers between devices, step(): lax.ppermute(outgoing[shift - 1], 'sp', [(k, k - shift) for k in range(sh...  5.3 us
    dot_general x2, matrix products, send(): jnp.dot(send_pick, columns, preferred_element_type=jnp.float32)  4.51 us
    all_to_all x1, starting transfers between devices, send(): lax.all_to_all(outgoing, 'dp', split_axis=0, concat_axis=0, tiled=True)  4.37 us
  transfers between devices with their start and end apart: 10, of which 6 were waited for; matrix products, arithmetic and copies ran while one was open for 13% of the time, Pallas kernels for 0%

profile of v10, /device:TPU:0, one launch (start us, length us, event | category | flops | bytes accessed | tf_op | source)
XLA Modules:
  0.0 108.9 jit_solution(14350533926852959910)
XLA Ops:
  2.5 3.3 %convolution_convert_fusion = bf16[256,4096]{1,0:T(8,128)(2,1)} fusion(bf16[128,5120]{1,0:T(8,128)(2,1)} %param.6, s32[128]{0:T(128)S(1)} %get-tuple-element.31), kind=kOutput, calls=%fused_computation | convolution fusion | flops 269516800 | bytes 3146240 | tf_op jit(solution)/shard_map/dot_general | solution.py:51
  5.8 4.4 %all-to-all-start = ((bf16[4,64,4096]{2,1,0:T(8,128)(2,1)}), bf16[4,64,4096]{2,1,0:T(8,128)(2,1)S(1)}, u32[]{:S(2)}, u32[]{:S(2)}) async-start(bf16[4,64,4096]{2,1,0:T(8,128)(2,1)} %bitcast.42), calls=%async_computation | async-start | bytes 4194304 | tf_op jit(solution)/shard_map/all_to_all | solution.py:66
  10.1 1.2 %convolution_convert_fusion.2 = bf16[256,1024]{1,0:T(8,128)(2,1)S(1)} fusion(bf16[128,5120]{1,0:T(8,128)(2,1)} %param.6, s32[128]{0:T(128)S(1)} %get-tuple-element.30), kind=kOutput, calls=%fused_computation.4 | convolution fusion | flops 67403776 | bytes 786944 | tf_op jit(solution)/shard_map/dot_general | solution.py:51
  12.1 1.8 %collective-permute-start.2 = (bf16[64,1024]{1,0:T(8,128)(2,1)}, bf16[64,1024]{1,0:T(8,128)(2,1)S(1)}, u32[]{:S(2)}, u32[]{:S(2)}) collective-permute-start(bf16[64,1024]{1,0:T(8,128)(2,1)} %get-tuple-element.17), channel_id=1, source_target_pairs={{0,12},{4,0},{8,4},{12,8},{1,13},{5,1},{9,5},{13,9},{2,14},{6,2},{... | collective-permute-start | bytes 393224 | tf_op jit(solution)/shard_map/ppermute | solution.py:58
  19.5 1.2 %fusion.g_ref = bf16[128,4096]{1,0:T(8,128)(2,1)} fusion(bf16[1,128,4096]{2,1,0:T(8,128)(2,1)S(1)} %copy-done.1, f32[128]{0:T(128)S(1)} %select_reduce_fusion.2), kind=kLoop, calls=%fused_computation.3 | loop fusion | flops 1572864 | bytes 2097664 | tf_op jit(solution)/shard_map/convert_element_type | solution.py:197
  20.7 16.1 %collective-permute-done.2 = bf16[64,1024]{1,0:T(8,128)(2,1)S(1)} collective-permute-done((bf16[64,1024]{1,0:T(8,128)(2,1)}, bf16[64,1024]{1,0:T(8,128)(2,1)S(1)}, u32[]{:S(2)}, u32[]{:S(2)}) %collective-permute-start.2) | collective-permute-done | bytes 131104 | tf_op jit(solution)/shard_map/ppermute | solution.py:58
  36.8 4.7 %collective-permute-done.1 = bf16[64,1024]{1,0:T(8,128)(2,1)} collective-permute-done((bf16[64,1024]{1,0:T(8,128)(2,1)}, bf16[64,1024]{1,0:T(8,128)(2,1)}, u32[]{:S(2)}, u32[]{:S(2)}) %collective-permute-start.1) | collective-permute-done | bytes 131104 | tf_op jit(solution)/shard_map/ppermute | solution.py:58
  41.5 1.0 pad_maximum_fusion.1
  43.0 5.3 %collective-permute-start.4 = (bf16[128,1152]{1,0:T(8,128)(2,1)S(1)}, bf16[128,1152]{1,0:T(8,128)(2,1)S(1)}, u32[]{:S(2)}, u32[]{:S(2)}) collective-permute-start(bf16[128,1152]{1,0:T(8,128)(2,1)S(1)} %pad_maximum_fusion.2), channel_id=1, source_target_pairs={{0,2},{1,3},{4,6},{5,7},{8,10},{9,11},{12,14},{13,15},{16,18},{17,... | collective-permute-start | bytes 884744 | tf_op jit(solution)/shard_map/ppermute | solution.py:183
  48.3 3.7 %collective-permute-start.3 = (bf16[128,1152]{1,0:T(8,128)(2,1)S(1)}, bf16[128,1152]{1,0:T(8,128)(2,1)S(1)}, u32[]{:S(2)}, u32[]{:S(2)}) collective-permute-start(bf16[128,1152]{1,0:T(8,128)(2,1)S(1)} %pad_maximum_fusion.2), channel_id=1, source_target_pairs={{0,1},{1,2},{2,3},{4,5},{5,6},{6,7},{8,9},{9,10},{10,11},{12,13},{... | collective-permute-start | bytes 884744 | tf_op jit(solution)/shard_map/ppermute | solution.py:183
  52.0 3.6 %collective-permute-done.4 = bf16[128,1152]{1,0:T(8,128)(2,1)S(1)} collective-permute-done((bf16[128,1152]{1,0:T(8,128)(2,1)S(1)}, bf16[128,1152]{1,0:T(8,128)(2,1)S(1)}, u32[]{:S(2)}, u32[]{:S(2)}) %collective-permute-start.4) | collective-permute-done | bytes 294944 | tf_op jit(solution)/shard_map/ppermute | solution.py:183
  55.7 3.3 %collective-permute-done.3 = bf16[128,1152]{1,0:T(8,128)(2,1)S(1)} collective-permute-done((bf16[128,1152]{1,0:T(8,128)(2,1)S(1)}, bf16[128,1152]{1,0:T(8,128)(2,1)S(1)}, u32[]{:S(2)}, u32[]{:S(2)}) %collective-permute-start.3) | collective-permute-done | bytes 294944 | tf_op jit(solution)/shard_map/ppermute | solution.py:183
  59.2 0.9 and_select_fusion.m_ref
  60.1 1.5 %convolution_convert_fusion.1.q_ref = bf16[128,4096]{1,0:T(8,128)(2,1)} fusion(bf16[256,4096]{1,0:T(8,128)(2,1)S(1)} %bitcast.41, s32[128]{0:T(128)S(1)} %get-tuple-element.29), kind=kOutput, calls=%fused_computation.1 | convolution fusion | flops 268992512 | bytes 3146240 | tf_op jit(solution)/shard_map/dot_general | solution.py:70
  61.6 9.8 %shard_map.78 = (bf16[128,2048]{1,0:T(8,128)(2,1)}, f32[128,512]{1,0:T(8,128)}, bf16[2,128,512]{2,1,0:T(8,128)(2,1)}) custom-call(bf16[128,4096]{1,0:T(8,128)(2,1)} %convolution_convert_fusion.1.q_ref, bf16[128,4096]{1,0:T(8,128)(2,1)} %fusion.g_ref, bf16[384,1152]{1,0:T(8,128)(2,1)} %copy-done, f32[384,128]{1,0:T(8,128)} %and_select_fusion.m_ref), custom_call_target="tpu_custom_call" | custom-call | flops 1006632960 | bytes 2654208 | tf_op jit(solution)/shard_map/pallas_call | solution.py:142
  71.4 9.9 %shard_map.77 = (bf16[128,2048]{1,0:T(8,128)(2,1)}, f32[128,512]{1,0:T(8,128)}, bf16[2,128,512]{2,1,0:T(8,128)(2,1)}) custom-call(bf16[128,4096]{1,0:T(8,128)(2,1)} %convolution_convert_fusion.1.q_ref, bf16[128,4096]{1,0:T(8,128)(2,1)} %fusion.g_ref, bf16[384,1152]{1,0:T(8,128)(2,1)} %copy-done, f32[384,128]{1,0:T(8,128)} %and_select_fusion.m_ref), custom_call_target="tpu_custom_call" | custom-call | flops 1006632960 | bytes 2654208 | tf_op jit(solution)/shard_map/pallas_call | solution.py:142
  81.3 1.4 %collective-permute-start.8 = (bf16[128,512]{1,0:T(8,128)(2,1)S(1)}, bf16[128,512]{1,0:T(8,128)(2,1)S(1)}, u32[]{:S(2)}, u32[]{:S(2)}) collective-permute-start(bf16[128,512]{1,0:T(8,128)(2,1)S(1)} %get-tuple-element.23), channel_id=1, source_target_pairs={{2,0},{3,1},{6,4},{7,5},{10,8},{11,9},{14,12},{15,13},{18,16},{19,... | collective-permute-start | bytes 393224 | tf_op jit(solution)/shard_map/ppermute | solution.py:215
  82.8 1.3 %collective-permute-start.7 = (bf16[128,512]{1,0:T(8,128)(2,1)S(1)}, bf16[128,512]{1,0:T(8,128)(2,1)S(1)}, u32[]{:S(2)}, u32[]{:S(2)}) collective-permute-start(bf16[128,512]{1,0:T(8,128)(2,1)S(1)} %get-tuple-element.22), channel_id=1, source_target_pairs={{1,0},{2,1},{3,2},{5,4},{6,5},{7,6},{9,8},{10,9},{11,10},{13,12},{... | collective-permute-start | bytes 393224 | tf_op jit(solution)/shard_map/ppermute | solution.py:215
  84.1 1.0 slice_bitcast_fusion.4
  85.1 1.3 %collective-permute-start.6 = (bf16[128,512]{1,0:T(8,128)(2,1)S(1)}, bf16[128,512]{1,0:T(8,128)(2,1)S(1)}, u32[]{:S(2)}, u32[]{:S(2)}) collective-permute-start(bf16[128,512]{1,0:T(8,128)(2,1)S(1)} %get-tuple-element.21), channel_id=1, source_target_pairs={{2,0},{3,1},{6,4},{7,5},{10,8},{11,9},{14,12},{15,13},{18,16},{19,... | collective-permute-start | bytes 393224 | tf_op jit(solution)/shard_map/ppermute | solution.py:215
  86.4 1.3 %collective-permute-start.5 = (bf16[128,512]{1,0:T(8,128)(2,1)S(1)}, bf16[128,512]{1,0:T(8,128)(2,1)S(1)}, u32[]{:S(2)}, u32[]{:S(2)}) collective-permute-start(bf16[128,512]{1,0:T(8,128)(2,1)S(1)} %get-tuple-element.20), channel_id=1, source_target_pairs={{1,0},{2,1},{3,2},{5,4},{6,5},{7,6},{9,8},{10,9},{11,10},{13,12},{... | collective-permute-start | bytes 393224 | tf_op jit(solution)/shard_map/ppermute | solution.py:215
  87.7 2.1 %maximum_bitcast_fusion = bf16[1,128,4096]{2,1,0:T(8,128)(2,1)} fusion(bf16[128,2048]{1,0:T(8,128)(2,1)S(1)} %copy-done.2, bf16[128,2048]{1,0:T(8,128)(2,1)} %get-tuple-element.8), kind=kLoop, calls=%fused_computation.6 | loop fusion | flops 2097152 | bytes 2097152 | tf_op jit(solution)/shard_map/reshape | solution.py:222
  89.8 10.2 %collective-permute-done.8 = bf16[128,512]{1,0:T(8,128)(2,1)S(1)} collective-permute-done((bf16[128,512]{1,0:T(8,128)(2,1)S(1)}, bf16[128,512]{1,0:T(8,128)(2,1)S(1)}, u32[]{:S(2)}, u32[]{:S(2)}) %collective-permute-start.8) | collective-permute-done | bytes 131104 | tf_op jit(solution)/shard_map/ppermute | solution.py:215
  100.1 8.0 %collective-permute-done.6 = bf16[128,512]{1,0:T(8,128)(2,1)S(1)} collective-permute-done((bf16[128,512]{1,0:T(8,128)(2,1)S(1)}, bf16[128,512]{1,0:T(8,128)(2,1)S(1)}, u32[]{:S(2)}, u32[]{:S(2)}) %collective-permute-start.6) | collective-permute-done | bytes 131104 | tf_op jit(solution)/shard_map/ppermute | solution.py:215
  (56 shorter events, 9.7 us)
Async XLA Ops:
  5.8 12.6 %copy-start.7 = (s32[16]{0:T(128)S(1)}, s32[16]{0:T(128)}, u32[]{:S(2)}) copy-start(s32[16]{0:T(128)} %param.11) | copy-start | bytes 196
  5.8 13.6 %copy-start.6 = (s32[1,128]{1,0:T(1,128)S(1)}, s32[1,128]{1,0:T(1,128)}, u32[]{:S(2)}) copy-start(s32[1,128]{1,0:T(1,128)} %param.8) | copy-start | bytes 1540
  5.8 13.7 %copy-start.1 = (bf16[1,128,4096]{2,1,0:T(8,128)(2,1)S(1)}, bf16[1,128,4096]{2,1,0:T(8,128)(2,1)}, u32[]{:S(2)}) copy-start(bf16[1,128,4096]{2,1,0:T(8,128)(2,1)} %param.9) | copy-start | bytes 3145732
  5.8 54.3 %all-to-all-start = ((bf16[4,64,4096]{2,1,0:T(8,128)(2,1)}), bf16[4,64,4096]{2,1,0:T(8,128)(2,1)S(1)}, u32[]{:S(2)}, u32[]{:S(2)}) async-start(bf16[4,64,4096]{2,1,0:T(8,128)(2,1)} %bitcast.42), calls=%async_computation | async-start | bytes 4194304 | tf_op jit(solution)/shard_map/all_to_all | solution.py:66
  12.1 24.7 %collective-permute-start.2 = (bf16[64,1024]{1,0:T(8,128)(2,1)}, bf16[64,1024]{1,0:T(8,128)(2,1)S(1)}, u32[]{:S(2)}, u32[]{:S(2)}) collective-permute-start(bf16[64,1024]{1,0:T(8,128)(2,1)} %get-tuple-element.17), channel_id=1, source_target_pairs={{0,12},{4,0},{8,4},{12,8},{1,13},{5,1},{9,5},{13,9},{2,14},{6,2},{... | collective-permute-start | bytes 393224 | tf_op jit(solution)/shard_map/ppermute | solution.py:58
  13.9 27.6 %collective-permute-start.1 = (bf16[64,1024]{1,0:T(8,128)(2,1)}, bf16[64,1024]{1,0:T(8,128)(2,1)}, u32[]{:S(2)}, u32[]{:S(2)}) collective-permute-start(bf16[64,1024]{1,0:T(8,128)(2,1)} %get-tuple-element.18), channel_id=1, source_target_pairs={{0,8},{4,12},{8,0},{12,4},{1,9},{5,13},{9,1},{13,5},{2,10},{6,14},... | collective-permute-start | bytes 393224 | tf_op jit(solution)/shard_map/ppermute | solution.py:58
  14.4 27.1 %collective-permute-start = (bf16[64,1024]{1,0:T(8,128)(2,1)S(1)}, bf16[64,1024]{1,0:T(8,128)(2,1)}, u32[]{:S(2)}, u32[]{:S(2)}) collective-permute-start(bf16[64,1024]{1,0:T(8,128)(2,1)S(1)} %get-tuple-element.19), channel_id=1, source_target_pairs={{0,4},{4,8},{8,12},{12,0},{1,5},{5,9},{9,13},{13,1},{2,6},{6,10},{... | collective-permute-start | bytes 393224 | tf_op jit(solution)/shard_map/ppermute | solution.py:58
  43.0 12.7 %collective-permute-start.4 = (bf16[128,1152]{1,0:T(8,128)(2,1)S(1)}, bf16[128,1152]{1,0:T(8,128)(2,1)S(1)}, u32[]{:S(2)}, u32[]{:S(2)}) collective-permute-start(bf16[128,1152]{1,0:T(8,128)(2,1)S(1)} %pad_maximum_fusion.2), channel_id=1, source_target_pairs={{0,2},{1,3},{4,6},{5,7},{8,10},{9,11},{12,14},{13,15},{16,18},{17,... | collective-permute-start | bytes 884744 | tf_op jit(solution)/shard_map/ppermute | solution.py:183
  48.3 10.6 %collective-permute-start.3 = (bf16[128,1152]{1,0:T(8,128)(2,1)S(1)}, bf16[128,1152]{1,0:T(8,128)(2,1)S(1)}, u32[]{:S(2)}, u32[]{:S(2)}) collective-permute-start(bf16[128,1152]{1,0:T(8,128)(2,1)S(1)} %pad_maximum_fusion.2), channel_id=1, source_target_pairs={{0,1},{1,2},{2,3},{4,5},{5,6},{6,7},{8,9},{9,10},{10,11},{12,13},{... | collective-permute-start | bytes 884744 | tf_op jit(solution)/shard_map/ppermute | solution.py:183
  59.0 2.5 %copy-start = (bf16[384,1152]{1,0:T(8,128)(2,1)}, bf16[384,1152]{1,0:T(8,128)(2,1)S(1)}, u32[]{:S(2)}) copy-start(bf16[384,1152]{1,0:T(8,128)(2,1)S(1)} %pad_maximum_fusion.kv_ref) | copy-start | bytes 2654212
  71.4 9.9 %copy-start.5 = (bf16[2,128,512]{2,1,0:T(8,128)(2,1)S(1)}, bf16[2,128,512]{2,1,0:T(8,128)(2,1)}, u32[]{:S(2)}) copy-start(bf16[2,128,512]{2,1,0:T(8,128)(2,1)} %get-tuple-element.13) | copy-start | bytes 786436
  71.4 16.3 %copy-start.2 = (bf16[128,2048]{1,0:T(8,128)(2,1)S(1)}, bf16[128,2048]{1,0:T(8,128)(2,1)}, u32[]{:S(2)}) copy-start(bf16[128,2048]{1,0:T(8,128)(2,1)} %get-tuple-element.9) | copy-start | bytes 1572868
  81.3 18.7 %copy-start.4 = (f32[128,512]{1,0:T(8,128)S(1)}, f32[128,512]{1,0:T(8,128)}, u32[]{:S(2)}) copy-start(f32[128,512]{1,0:T(8,128)} %get-tuple-element.12) | copy-start | bytes 786436
  81.3 26.7 %copy-start.3 = (f32[128,512]{1,0:T(8,128)S(1)}, f32[128,512]{1,0:T(8,128)}, u32[]{:S(2)}) copy-start(f32[128,512]{1,0:T(8,128)} %get-tuple-element.10) | copy-start | bytes 786436
  81.3 18.6 %collective-permute-start.8 = (bf16[128,512]{1,0:T(8,128)(2,1)S(1)}, bf16[128,512]{1,0:T(8,128)(2,1)S(1)}, u32[]{:S(2)}, u32[]{:S(2)}) collective-permute-start(bf16[128,512]{1,0:T(8,128)(2,1)S(1)} %get-tuple-element.23), channel_id=1, source_target_pairs={{2,0},{3,1},{6,4},{7,5},{10,8},{11,9},{14,12},{15,13},{18,16},{19,... | collective-permute-start | bytes 393224 | tf_op jit(solution)/shard_map/ppermute | solution.py:215
  82.8 17.2 %collective-permute-start.7 = (bf16[128,512]{1,0:T(8,128)(2,1)S(1)}, bf16[128,512]{1,0:T(8,128)(2,1)S(1)}, u32[]{:S(2)}, u32[]{:S(2)}) collective-permute-start(bf16[128,512]{1,0:T(8,128)(2,1)S(1)} %get-tuple-element.22), channel_id=1, source_target_pairs={{1,0},{2,1},{3,2},{5,4},{6,5},{7,6},{9,8},{10,9},{11,10},{13,12},{... | collective-permute-start | bytes 393224 | tf_op jit(solution)/shard_map/ppermute | solution.py:215
  85.1 23.0 %collective-permute-start.6 = (bf16[128,512]{1,0:T(8,128)(2,1)S(1)}, bf16[128,512]{1,0:T(8,128)(2,1)S(1)}, u32[]{:S(2)}, u32[]{:S(2)}) collective-permute-start(bf16[128,512]{1,0:T(8,128)(2,1)S(1)} %get-tuple-element.21), channel_id=1, source_target_pairs={{2,0},{3,1},{6,4},{7,5},{10,8},{11,9},{14,12},{15,13},{18,16},{19,... | collective-permute-start | bytes 393224 | tf_op jit(solution)/shard_map/ppermute | solution.py:215
  86.4 21.7 %collective-permute-start.5 = (bf16[128,512]{1,0:T(8,128)(2,1)S(1)}, bf16[128,512]{1,0:T(8,128)(2,1)S(1)}, u32[]{:S(2)}, u32[]{:S(2)}) collective-permute-start(bf16[128,512]{1,0:T(8,128)(2,1)S(1)} %get-tuple-element.20), channel_id=1, source_target_pairs={{1,0},{2,1},{3,2},{5,4},{6,5},{7,6},{9,8},{10,9},{11,10},{13,12},{... | collective-permute-start | bytes 393224 | tf_op jit(solution)/shard_map/ppermute | solution.py:215

commit v11 on v10

--- a/solution.py
+++ b/solution.py
@@ -72,11 +72,11 @@
         ).astype(columns.dtype)
 
     packed_kv = send(rollout_rows[:, QUERY_HEADS * HEAD_SIZE :], True)
-    packed_q = send(rollout_rows[:, : QUERY_HEADS * HEAD_SIZE], False)
+    packed_q = send(rollout_rows[:, : QUERY_HEADS * HEAD_SIZE], True)
     return packed_q, packed_kv
 
 
-def attend_kernel(q_ref, g_ref, kv_ref, m_ref, dq_ref, local_ref, send_ref, *, first_group):
+def attend_kernel(q_ref, g_ref, kv_ref, m_ref, dq_ref, local_ref, *send_refs, first_group):
     inv_root = 1.0 / math.sqrt(HEAD_SIZE)
     token_rows = q_ref.shape[0]
     groups = local_ref.shape[1] // (2 * HEAD_SIZE)
@@ -123,10 +123,10 @@
         value_cols = slice((groups + local_group) * HEAD_SIZE, (groups + local_group + 1) * HEAD_SIZE)
         local_ref[:, key_cols] = key_sum[:token_rows]
         local_ref[:, value_cols] = value_sum[:token_rows]
-        for back in range(send_ref.shape[0]):
+        for back, send_ref in enumerate(send_refs):
             rows = slice((back + 1) * token_rows, (back + 2) * token_rows)
-            send_ref[back, :, key_cols] = key_sum[rows].astype(send_ref.dtype)
-            send_ref[back, :, value_cols] = value_sum[rows].astype(send_ref.dtype)
+            send_ref[:, key_cols] = key_sum[rows].astype(send_ref.dtype)
+            send_ref[:, value_cols] = value_sum[rows].astype(send_ref.dtype)
 
 
 def attend_pallas(packed, weighted, kv_all, bias, part, groups):
@@ -149,15 +149,14 @@
             pl.BlockSpec(bias.shape, whole),
         ],
         out_specs=[
-            pl.BlockSpec((token_rows, part_width), whole),
-            pl.BlockSpec((token_rows, kv_width), whole),
-            pl.BlockSpec((reach, token_rows, kv_width), lambda i: (0, 0, 0)),
-        ],
+            pl.BlockSpec((token_rows, part_width), whole)
+        ]
+        + [pl.BlockSpec((token_rows, kv_width), whole) for _ in range(reach + 1)],
         out_shape=[
             jax.ShapeDtypeStruct((token_rows, part_width), jnp.bfloat16),
             jax.ShapeDtypeStruct((token_rows, kv_width), jnp.float32),
-            jax.ShapeDtypeStruct((reach, token_rows, kv_width), jnp.bfloat16),
-        ],
+        ]
+        + [jax.ShapeDtypeStruct((token_rows, kv_width), jnp.bfloat16) for _ in range(reach)],
         cost_estimate=pl.CostEstimate(
             flops=flops, transcendentals=token_rows * key_rows * heads, bytes_accessed=bytes_accessed
         ),
@@ -208,7 +207,7 @@
     groups = KEY_VALUE_HEADS // 2
     query_parts, key_parts, value_parts = [], [], []
     for part in range(2):
-        query_grad, total, outgoing = attend_pallas(
+        query_grad, total, *outgoing = attend_pallas(
             packed_q, weighted, kv_all, bias, part, groups
         )
         for shift in range(1, reach + 1):

time: 110 us -> 103 us (0.936)
  starting transfers between devices: 21.2 us -> 19 us
  other arithmetic: 12.2 us -> 10.5 us
  waiting for transfers between devices: 45.9 us -> 44.5 us
  matrix products: 6.23 us -> 4.88 us
    all_to_all x1 -> x0, starting transfers between devices: 4.37 us -> none  [send(): lax.all_to_all(outgoing, 'dp', split_axis=0, concat_axis=0, tiled=True)]
    ppermute x3 -> x6, waiting for transfers between devices: 20.8 us -> 17.9 us  [send(): lax.ppermute(outgoing[shift], 'dp', [(k, (k + shift) % dp_size) for k in...]
    ppermute x3 -> x6, starting transfers between devices: 2.57 us -> 5.28 us  [send(): lax.ppermute(outgoing[shift], 'dp', [(k, (k + shift) % dp_size) for k in...]
    dot_general x2, matrix products: 4.51 us -> 3.15 us  [send(): jnp.dot(send_pick, columns, preferred_element_type=jnp.float32)]
    another operation x1 -> x2, other arithmetic: 1.04 us -> 2.34 us  [send(): jnp.stack([outgoing[0]] + [lax.ppermute(outgoing[shift], 'dp', [(k, (k +...]
  transfers between devices with their start and end apart: 10 -> 12, of which waited for: 6 -> 6; matrix products, arithmetic and copies ran while one was open for 13% -> 8% of each run, Pallas kernels for 0% -> 0%
where the time goes in v11:
time: 103 us; the launch traced here: 102 us
  waiting for transfers between devices  44.5 us (43%)
  Pallas kernels  19.7 us (19%)
  starting transfers between devices  19 us (18%)
  other arithmetic  10.5 us (10%)
  matrix products  4.88 us (5%)
  local copies, waits for them, and re-layouts  2.66 us (3%)
    pallas_call x2, Pallas kernels, attend_pallas(): pl.pallas_call(functools.partial(attend_kernel, first_group=part * groups...  19.7 us
    ppermute x4, waiting for transfers between devices, step(): lax.ppermute(outgoing[shift - 1], 'sp', [(k, k - shift) for k in range(sh...  19.2 us
    ppermute x6, waiting for transfers between devices, send(): lax.ppermute(outgoing[shift], 'dp', [(k, (k + shift) % dp_size) for k in...  17.9 us
    ppermute x2, starting transfers between devices, step(): lax.ppermute(kv_local, 'sp', [(k, k + shift) for k in range(sp_size - shi...  8.44 us
    ppermute x2, waiting for transfers between devices, step(): lax.ppermute(kv_local, 'sp', [(k, k + shift) for k in range(sp_size - shi...  7.35 us
    ppermute x4, starting transfers between devices, step(): lax.ppermute(outgoing[shift - 1], 'sp', [(k, k - shift) for k in range(sh...  5.29 us
    ppermute x6, starting transfers between devices, send(): lax.ppermute(outgoing[shift], 'dp', [(k, (k + shift) % dp_size) for k in...  5.28 us
    dot_general x2, matrix products, send(): jnp.dot(send_pick, columns, preferred_element_type=jnp.float32)  3.15 us
  transfers between devices with their start and end apart: 12, of which 6 were waited for; matrix products, arithmetic and copies ran while one was open for 8% of the time, Pallas kernels for 0%

profile of v11, /device:TPU:0, one launch (start us, length us, event | category | flops | bytes accessed | tf_op | source)
XLA Modules:
  0.0 102.1 jit_solution(15889453543700209174)
XLA Ops:
  3.8 1.9 %convolution_convert_fusion = bf16[256,4096]{1,0:T(8,128)(2,1)S(1)} fusion(bf16[128,5120]{1,0:T(8,128)(2,1)} %param.6, s32[128]{0:T(128)S(1)} %get-tuple-element.33), kind=kOutput, calls=%fused_computation | convolution fusion | flops 269516800 | bytes 3146240 | tf_op jit(solution)/shard_map/dot_general | solution.py:51
  5.8 1.0 slice_bitcast_fusion
  6.8 2.4 %collective-permute-start.2 = (bf16[64,4096]{1,0:T(8,128)(2,1)}, bf16[64,4096]{1,0:T(8,128)(2,1)S(1)}, u32[]{:S(2)}, u32[]{:S(2)}) collective-permute-start(bf16[64,4096]{1,0:T(8,128)(2,1)} %get-tuple-element.21), channel_id=1, source_target_pairs={{0,12},{4,0},{8,4},{12,8},{1,13},{5,1},{9,5},{13,9},{2,14},{6,2},{... | collective-permute-start | bytes 1572872 | tf_op jit(solution)/shard_map/ppermute | solution.py:58
  9.7 1.2 %convolution_convert_fusion.2 = bf16[256,1024]{1,0:T(8,128)(2,1)S(1)} fusion(bf16[128,5120]{1,0:T(8,128)(2,1)} %param.6, s32[128]{0:T(128)S(1)} %get-tuple-element.33), kind=kOutput, calls=%fused_computation.5 | convolution fusion | flops 67403776 | bytes 786944 | tf_op jit(solution)/shard_map/dot_general | solution.py:51
  11.8 1.7 %collective-permute-start.4 = (bf16[64,1024]{1,0:T(8,128)(2,1)}, bf16[64,1024]{1,0:T(8,128)(2,1)}, u32[]{:S(2)}, u32[]{:S(2)}) collective-permute-start(bf16[64,1024]{1,0:T(8,128)(2,1)} %get-tuple-element.26), channel_id=1, source_target_pairs={{0,8},{4,12},{8,0},{12,4},{1,9},{5,13},{9,1},{13,5},{2,10},{6,14},... | collective-permute-start | bytes 393224 | tf_op jit(solution)/shard_map/ppermute | solution.py:58
  14.0 1.3 %fusion.g_ref = bf16[128,4096]{1,0:T(8,128)(2,1)} fusion(bf16[1,128,4096]{2,1,0:T(8,128)(2,1)S(1)} %copy-done.1, f32[128]{0:T(128)S(1)} %select_reduce_fusion.2), kind=kLoop, calls=%fused_computation.4 | loop fusion | flops 1572864 | bytes 2097664 | tf_op jit(solution)/shard_map/convert_element_type | solution.py:196
  15.3 16.2 %collective-permute-done.5 = bf16[64,1024]{1,0:T(8,128)(2,1)S(1)} collective-permute-done((bf16[64,1024]{1,0:T(8,128)(2,1)}, bf16[64,1024]{1,0:T(8,128)(2,1)S(1)}, u32[]{:S(2)}, u32[]{:S(2)}) %collective-permute-start.5) | collective-permute-done | bytes 131104 | tf_op jit(solution)/shard_map/ppermute | solution.py:58
  32.0 1.7 %collective-permute-done.4 = bf16[64,1024]{1,0:T(8,128)(2,1)} collective-permute-done((bf16[64,1024]{1,0:T(8,128)(2,1)}, bf16[64,1024]{1,0:T(8,128)(2,1)}, u32[]{:S(2)}, u32[]{:S(2)}) %collective-permute-start.4) | collective-permute-done | bytes 131104 | tf_op jit(solution)/shard_map/ppermute | solution.py:58
  33.7 1.0 %pad_maximum_fusion.2 = bf16[4,64,1024]{2,1,0:T(8,128)(2,1)S(1)} fusion(bf16[1,64,1024]{2,1,0:T(8,128)(2,1)S(1)} %bitcast.41, bf16[1,64,1024]{2,1,0:T(8,128)(2,1)} %bitcast.13, bf16[1,64,1024]{2,1,0:T(8,128)(2,1)} %bitcast.12, bf16[1,64,1024]{2,1,0:T(8,128)(2,1)S(1)} %get-tuple-element.24), kind=kLoop, calls=%fused_computation.11 | loop fusion | flops 786432 | bytes 1048576 | tf_op jit(solution)/shard_map/stack | solution.py:55
  35.1 4.8 %collective-permute-start.7 = (bf16[128,1152]{1,0:T(8,128)(2,1)S(1)}, bf16[128,1152]{1,0:T(8,128)(2,1)S(1)}, u32[]{:S(2)}, u32[]{:S(2)}) collective-permute-start(bf16[128,1152]{1,0:T(8,128)(2,1)S(1)} %pad_maximum_fusion.3), channel_id=1, source_target_pairs={{0,2},{1,3},{4,6},{5,7},{8,10},{9,11},{12,14},{13,15},{16,18},{17,... | collective-permute-start | bytes 884744 | tf_op jit(solution)/shard_map/ppermute | solution.py:182
  39.9 3.7 %collective-permute-start.6 = (bf16[128,1152]{1,0:T(8,128)(2,1)S(1)}, bf16[128,1152]{1,0:T(8,128)(2,1)S(1)}, u32[]{:S(2)}, u32[]{:S(2)}) collective-permute-start(bf16[128,1152]{1,0:T(8,128)(2,1)S(1)} %pad_maximum_fusion.3), channel_id=1, source_target_pairs={{0,1},{1,2},{2,3},{4,5},{5,6},{6,7},{8,9},{9,10},{10,11},{12,13},{... | collective-permute-start | bytes 884744 | tf_op jit(solution)/shard_map/ppermute | solution.py:182
  43.6 3.6 %collective-permute-done.7 = bf16[128,1152]{1,0:T(8,128)(2,1)S(1)} collective-permute-done((bf16[128,1152]{1,0:T(8,128)(2,1)S(1)}, bf16[128,1152]{1,0:T(8,128)(2,1)S(1)}, u32[]{:S(2)}, u32[]{:S(2)}) %collective-permute-start.7) | collective-permute-done | bytes 294944 | tf_op jit(solution)/shard_map/ppermute | solution.py:182
  47.2 3.7 %collective-permute-done.6 = bf16[128,1152]{1,0:T(8,128)(2,1)S(1)} collective-permute-done((bf16[128,1152]{1,0:T(8,128)(2,1)S(1)}, bf16[128,1152]{1,0:T(8,128)(2,1)S(1)}, u32[]{:S(2)}, u32[]{:S(2)}) %collective-permute-start.6) | collective-permute-done | bytes 294944 | tf_op jit(solution)/shard_map/ppermute | solution.py:182
  52.1 1.3 %pad_maximum_fusion = bf16[4,64,4096]{2,1,0:T(8,128)(2,1)S(1)} fusion(bf16[1,64,4096]{2,1,0:T(8,128)(2,1)S(1)} %bitcast.39, bf16[1,64,4096]{2,1,0:T(8,128)(2,1)} %bitcast.6, bf16[1,64,4096]{2,1,0:T(8,128)(2,1)S(1)} %bitcast.40, bf16[1,64,4096]{2,1,0:T(8,128)(2,1)S(1)} %get-tuple-element.20), kind=kLoop, calls=%fused_computation.2 | loop fusion | flops 3145728 | bytes 4194304 | tf_op jit(solution)/shard_map/stack | solution.py:55
  53.4 1.5 %convolution_convert_fusion.1.q_ref = bf16[128,4096]{1,0:T(8,128)(2,1)} fusion(bf16[256,4096]{1,0:T(8,128)(2,1)S(1)} %bitcast.37, s32[128]{0:T(128)S(1)} %get-tuple-element.32), kind=kOutput, calls=%fused_computation.1 | convolution fusion | flops 268992512 | bytes 3146240 | tf_op jit(solution)/shard_map/dot_general | solution.py:70
  54.9 9.8 %shard_map.78 = (bf16[128,2048]{1,0:T(8,128)(2,1)}, f32[128,512]{1,0:T(8,128)}, bf16[128,512]{1,0:T(8,128)(2,1)}, bf16[128,512]{1,0:T(8,128)(2,1)}) custom-call(bf16[128,4096]{1,0:T(8,128)(2,1)} %convolution_convert_fusion.1.q_ref, bf16[128,4096]{1,0:T(8,128)(2,1)} %fusion.g_ref, bf16[384,1152]{1,0:T(8,128)(2,1)} %copy-done, f32[384,128]{1,0:T(8,128)} %and_select_fusion.m_ref), custom_call_target="tpu_custom_call" | custom-call | flops 1006632960 | bytes 2654208 | tf_op jit(solution)/shard_map/pallas_call | solution.py:142
  64.7 9.9 %shard_map.77 = (bf16[128,2048]{1,0:T(8,128)(2,1)}, f32[128,512]{1,0:T(8,128)}, bf16[128,512]{1,0:T(8,128)(2,1)}, bf16[128,512]{1,0:T(8,128)(2,1)}) custom-call(bf16[128,4096]{1,0:T(8,128)(2,1)} %convolution_convert_fusion.1.q_ref, bf16[128,4096]{1,0:T(8,128)(2,1)} %fusion.g_ref, bf16[384,1152]{1,0:T(8,128)(2,1)} %copy-done, f32[384,128]{1,0:T(8,128)} %and_select_fusion.m_ref), custom_call_target="tpu_custom_call" | custom-call | flops 1006632960 | bytes 2654208 | tf_op jit(solution)/shard_map/pallas_call | solution.py:142
  74.6 1.4 %collective-permute-start.11 = (bf16[128,512]{1,0:T(8,128)(2,1)S(1)}, bf16[128,512]{1,0:T(8,128)(2,1)S(1)}, u32[]{:S(2)}, u32[]{:S(2)}) collective-permute-start(bf16[128,512]{1,0:T(8,128)(2,1)S(1)} %copy-done.8), channel_id=1, source_target_pairs={{2,0},{3,1},{6,4},{7,5},{10,8},{11,9},{14,12},{15,13},{18,16},{19,... | collective-permute-start | bytes 393224 | tf_op jit(solution)/shard_map/ppermute | solution.py:214
  76.0 1.3 %collective-permute-start.10 = (bf16[128,512]{1,0:T(8,128)(2,1)S(1)}, bf16[128,512]{1,0:T(8,128)(2,1)S(1)}, u32[]{:S(2)}, u32[]{:S(2)}) collective-permute-start(bf16[128,512]{1,0:T(8,128)(2,1)S(1)} %copy-done.7), channel_id=1, source_target_pairs={{1,0},{2,1},{3,2},{5,4},{6,5},{7,6},{9,8},{10,9},{11,10},{13,12},{... | collective-permute-start | bytes 393224 | tf_op jit(solution)/shard_map/ppermute | solution.py:214
  77.3 1.3 %collective-permute-start.9 = (bf16[128,512]{1,0:T(8,128)(2,1)}, bf16[128,512]{1,0:T(8,128)(2,1)S(1)}, u32[]{:S(2)}, u32[]{:S(2)}) collective-permute-start(bf16[128,512]{1,0:T(8,128)(2,1)} %get-tuple-element.14), channel_id=1, source_target_pairs={{2,0},{3,1},{6,4},{7,5},{10,8},{11,9},{14,12},{15,13},{18,16},{19,... | collective-permute-start | bytes 393224 | tf_op jit(solution)/shard_map/ppermute | solution.py:214
  78.6 1.3 %collective-permute-start.8 = (bf16[128,512]{1,0:T(8,128)(2,1)}, bf16[128,512]{1,0:T(8,128)(2,1)S(1)}, u32[]{:S(2)}, u32[]{:S(2)}) collective-permute-start(bf16[128,512]{1,0:T(8,128)(2,1)} %get-tuple-element.13), channel_id=1, source_target_pairs={{1,0},{2,1},{3,2},{5,4},{6,5},{7,6},{9,8},{10,9},{11,10},{13,12},{... | collective-permute-start | bytes 393224 | tf_op jit(solution)/shard_map/ppermute | solution.py:214
  79.9 2.1 %maximum_bitcast_fusion = bf16[1,128,4096]{2,1,0:T(8,128)(2,1)} fusion(bf16[128,2048]{1,0:T(8,128)(2,1)S(1)} %copy-done.2, bf16[128,2048]{1,0:T(8,128)(2,1)} %get-tuple-element.10), kind=kLoop, calls=%fused_computation.7 | loop fusion | flops 2097152 | bytes 2097152 | tf_op jit(solution)/shard_map/reshape | solution.py:221
  82.0 11.2 %collective-permute-done.11 = bf16[128,512]{1,0:T(8,128)(2,1)S(1)} collective-permute-done((bf16[128,512]{1,0:T(8,128)(2,1)S(1)}, bf16[128,512]{1,0:T(8,128)(2,1)S(1)}, u32[]{:S(2)}, u32[]{:S(2)}) %collective-permute-start.11) | collective-permute-done | bytes 131104 | tf_op jit(solution)/shard_map/ppermute | solution.py:214
  93.3 8.0 %collective-permute-done.9 = bf16[128,512]{1,0:T(8,128)(2,1)S(1)} collective-permute-done((bf16[128,512]{1,0:T(8,128)(2,1)}, bf16[128,512]{1,0:T(8,128)(2,1)S(1)}, u32[]{:S(2)}, u32[]{:S(2)}) %collective-permute-start.9) | collective-permute-done | bytes 131104 | tf_op jit(solution)/shard_map/ppermute | solution.py:214
  (63 shorter events, 7.9 us)
Async XLA Ops:
  5.7 7.9 %copy-start.9 = (s32[16]{0:T(128)S(1)}, s32[16]{0:T(128)}, u32[]{:S(2)}) copy-start(s32[16]{0:T(128)} %param.10) | copy-start | bytes 196
  5.7 7.9 %copy-start.6 = (s32[16]{0:T(128)S(1)}, s32[16]{0:T(128)}, u32[]{:S(2)}) copy-start(s32[16]{0:T(128)} %param.11) | copy-start | bytes 196
  5.7 8.2 %copy-start.5 = (s32[1,128]{1,0:T(1,128)S(1)}, s32[1,128]{1,0:T(1,128)}, u32[]{:S(2)}) copy-start(s32[1,128]{1,0:T(1,128)} %param.8) | copy-start | bytes 1540
  5.8 8.3 %copy-start.1 = (bf16[1,128,4096]{2,1,0:T(8,128)(2,1)S(1)}, bf16[1,128,4096]{2,1,0:T(8,128)(2,1)}, u32[]{:S(2)}) copy-start(bf16[1,128,4096]{2,1,0:T(8,128)(2,1)} %param.9) | copy-start | bytes 3145732
  6.8 45.3 %collective-permute-start.2 = (bf16[64,4096]{1,0:T(8,128)(2,1)}, bf16[64,4096]{1,0:T(8,128)(2,1)S(1)}, u32[]{:S(2)}, u32[]{:S(2)}) collective-permute-start(bf16[64,4096]{1,0:T(8,128)(2,1)} %get-tuple-element.21), channel_id=1, source_target_pairs={{0,12},{4,0},{8,4},{12,8},{1,13},{5,1},{9,5},{13,9},{2,14},{6,2},{... | collective-permute-start | bytes 1572872 | tf_op jit(solution)/shard_map/ppermute | solution.py:58
  9.2 42.9 %collective-permute-start.1 = (bf16[64,4096]{1,0:T(8,128)(2,1)S(1)}, bf16[64,4096]{1,0:T(8,128)(2,1)}, u32[]{:S(2)}, u32[]{:S(2)}) collective-permute-start(bf16[64,4096]{1,0:T(8,128)(2,1)S(1)} %get-tuple-element.22), channel_id=1, source_target_pairs={{0,8},{4,12},{8,0},{12,4},{1,9},{5,13},{9,1},{13,5},{2,10},{6,14},... | collective-permute-start | bytes 1572872 | tf_op jit(solution)/shard_map/ppermute | solution.py:58
  11.7 19.8 %collective-permute-start.5 = (bf16[64,1024]{1,0:T(8,128)(2,1)}, bf16[64,1024]{1,0:T(8,128)(2,1)S(1)}, u32[]{:S(2)}, u32[]{:S(2)}) collective-permute-start(bf16[64,1024]{1,0:T(8,128)(2,1)} %get-tuple-element.25), channel_id=1, source_target_pairs={{0,12},{4,0},{8,4},{12,8},{1,13},{5,1},{9,5},{13,9},{2,14},{6,2},{... | collective-permute-start | bytes 393224 | tf_op jit(solution)/shard_map/ppermute | solution.py:58
  11.8 21.8 %collective-permute-start.4 = (bf16[64,1024]{1,0:T(8,128)(2,1)}, bf16[64,1024]{1,0:T(8,128)(2,1)}, u32[]{:S(2)}, u32[]{:S(2)}) collective-permute-start(bf16[64,1024]{1,0:T(8,128)(2,1)} %get-tuple-element.26), channel_id=1, source_target_pairs={{0,8},{4,12},{8,0},{12,4},{1,9},{5,13},{9,1},{13,5},{2,10},{6,14},... | collective-permute-start | bytes 393224 | tf_op jit(solution)/shard_map/ppermute | solution.py:58
  13.6 20.1 %collective-permute-start.3 = (bf16[64,1024]{1,0:T(8,128)(2,1)S(1)}, bf16[64,1024]{1,0:T(8,128)(2,1)}, u32[]{:S(2)}, u32[]{:S(2)}) collective-permute-start(bf16[64,1024]{1,0:T(8,128)(2,1)S(1)} %get-tuple-element.27), channel_id=1, source_target_pairs={{0,4},{4,8},{8,12},{12,0},{1,5},{5,9},{9,13},{13,1},{2,6},{6,10},{... | collective-permute-start | bytes 393224 | tf_op jit(solution)/shard_map/ppermute | solution.py:58
  31.5 20.6 %collective-permute-start = (bf16[64,4096]{1,0:T(8,128)(2,1)S(1)}, bf16[64,4096]{1,0:T(8,128)(2,1)S(1)}, u32[]{:S(2)}, u32[]{:S(2)}) collective-permute-start(bf16[64,4096]{1,0:T(8,128)(2,1)S(1)} %get-tuple-element.23), channel_id=1, source_target_pairs={{0,4},{4,8},{8,12},{12,0},{1,5},{5,9},{9,13},{13,1},{2,6},{6,10},{... | collective-permute-start | bytes 1572872 | tf_op jit(solution)/shard_map/ppermute | solution.py:58
  35.1 12.1 %collective-permute-start.7 = (bf16[128,1152]{1,0:T(8,128)(2,1)S(1)}, bf16[128,1152]{1,0:T(8,128)(2,1)S(1)}, u32[]{:S(2)}, u32[]{:S(2)}) collective-permute-start(bf16[128,1152]{1,0:T(8,128)(2,1)S(1)} %pad_maximum_fusion.3), channel_id=1, source_target_pairs={{0,2},{1,3},{4,6},{5,7},{8,10},{9,11},{12,14},{13,15},{16,18},{17,... | collective-permute-start | bytes 884744 | tf_op jit(solution)/shard_map/ppermute | solution.py:182
  39.9 11.1 %collective-permute-start.6 = (bf16[128,1152]{1,0:T(8,128)(2,1)S(1)}, bf16[128,1152]{1,0:T(8,128)(2,1)S(1)}, u32[]{:S(2)}, u32[]{:S(2)}) collective-permute-start(bf16[128,1152]{1,0:T(8,128)(2,1)S(1)} %pad_maximum_fusion.3), channel_id=1, source_target_pairs={{0,1},{1,2},{2,3},{4,5},{5,6},{6,7},{8,9},{9,10},{10,11},{12,13},{... | collective-permute-start | bytes 884744 | tf_op jit(solution)/shard_map/ppermute | solution.py:182
  51.0 2.4 %copy-start = (bf16[384,1152]{1,0:T(8,128)(2,1)}, bf16[384,1152]{1,0:T(8,128)(2,1)S(1)}, u32[]{:S(2)}) copy-start(bf16[384,1152]{1,0:T(8,128)(2,1)S(1)} %pad_maximum_fusion.1.kv_ref) | copy-start | bytes 2654212
  64.7 9.9 %copy-start.8 = (bf16[128,512]{1,0:T(8,128)(2,1)S(1)}, bf16[128,512]{1,0:T(8,128)(2,1)}, u32[]{:S(2)}) copy-start(bf16[128,512]{1,0:T(8,128)(2,1)} %get-tuple-element.17) | copy-start | bytes 393220
  64.7 11.4 %copy-start.7 = (bf16[128,512]{1,0:T(8,128)(2,1)S(1)}, bf16[128,512]{1,0:T(8,128)(2,1)}, u32[]{:S(2)}) copy-start(bf16[128,512]{1,0:T(8,128)(2,1)} %get-tuple-element.16) | copy-start | bytes 393220
  64.7 15.3 %copy-start.2 = (bf16[128,2048]{1,0:T(8,128)(2,1)S(1)}, bf16[128,2048]{1,0:T(8,128)(2,1)}, u32[]{:S(2)}) copy-start(bf16[128,2048]{1,0:T(8,128)(2,1)} %get-tuple-element.11) | copy-start | bytes 1572868
  64.7 28.6 %copy-start.4 = (f32[128,512]{1,0:T(8,128)S(1)}, f32[128,512]{1,0:T(8,128)}, u32[]{:S(2)}) copy-start(f32[128,512]{1,0:T(8,128)} %get-tuple-element.15) | copy-start | bytes 786436
  74.6 26.7 %copy-start.3 = (f32[128,512]{1,0:T(8,128)S(1)}, f32[128,512]{1,0:T(8,128)}, u32[]{:S(2)}) copy-start(f32[128,512]{1,0:T(8,128)} %get-tuple-element.12) | copy-start | bytes 786436
  74.6 18.6 %collective-permute-start.11 = (bf16[128,512]{1,0:T(8,128)(2,1)S(1)}, bf16[128,512]{1,0:T(8,128)(2,1)S(1)}, u32[]{:S(2)}, u32[]{:S(2)}) collective-permute-start(bf16[128,512]{1,0:T(8,128)(2,1)S(1)} %copy-done.8), channel_id=1, source_target_pairs={{2,0},{3,1},{6,4},{7,5},{10,8},{11,9},{14,12},{15,13},{18,16},{19,... | collective-permute-start | bytes 393224 | tf_op jit(solution)/shard_map/ppermute | solution.py:214
  76.0 17.2 %collective-permute-start.10 = (bf16[128,512]{1,0:T(8,128)(2,1)S(1)}, bf16[128,512]{1,0:T(8,128)(2,1)S(1)}, u32[]{:S(2)}, u32[]{:S(2)}) collective-permute-start(bf16[128,512]{1,0:T(8,128)(2,1)S(1)} %copy-done.7), channel_id=1, source_target_pairs={{1,0},{2,1},{3,2},{5,4},{6,5},{7,6},{9,8},{10,9},{11,10},{13,12},{... | collective-permute-start | bytes 393224 | tf_op jit(solution)/shard_map/ppermute | solution.py:214
  77.3 24.0 %collective-permute-start.9 = (bf16[128,512]{1,0:T(8,128)(2,1)}, bf16[128,512]{1,0:T(8,128)(2,1)S(1)}, u32[]{:S(2)}, u32[]{:S(2)}) collective-permute-start(bf16[128,512]{1,0:T(8,128)(2,1)} %get-tuple-element.14), channel_id=1, source_target_pairs={{2,0},{3,1},{6,4},{7,5},{10,8},{11,9},{14,12},{15,13},{18,16},{19,... | collective-permute-start | bytes 393224 | tf_op jit(solution)/shard_map/ppermute | solution.py:214
  78.6 22.7 %collective-permute-start.8 = (bf16[128,512]{1,0:T(8,128)(2,1)}, bf16[128,512]{1,0:T(8,128)(2,1)S(1)}, u32[]{:S(2)}, u32[]{:S(2)}) collective-permute-start(bf16[128,512]{1,0:T(8,128)(2,1)} %get-tuple-element.13), channel_id=1, source_target_pairs={{1,0},{2,1},{3,2},{5,4},{6,5},{7,6},{9,8},{10,9},{11,10},{13,12},{... | collective-permute-start | bytes 393224 | tf_op jit(solution)/shard_map/ppermute | solution.py:214

commit v12 on v11

--- a/solution.py
+++ b/solution.py
@@ -52,24 +52,28 @@
             columns.dtype
         ).reshape(dp_size, capacity, -1)
         if by_permute:
-            arrived = jnp.stack(
-                [outgoing[0]]
-                + [
-                    lax.ppermute(
-                        outgoing[shift], "dp", [(k, (k + shift) % dp_size) for k in range(dp_size)]
-                    )
-                    for shift in range(1, dp_size)
-                ]
-            )
+            chunks = [outgoing[0]] + [
+                lax.ppermute(
+                    outgoing[shift], "dp", [(k, (k + shift) % dp_size) for k in range(dp_size)]
+                )
+                for shift in range(1, dp_size)
+            ]
             source_slot = (dp_index - source) % dp_size
         else:
             arrived = lax.all_to_all(outgoing, "dp", split_axis=0, concat_axis=0, tiled=True)
+            chunks = [arrived[k] for k in range(dp_size)]
             source_slot = source
         pick_ids = source_slot * capacity + positions - chosen_start
         recv_pick = (pick_ids[:, None] == slots[None, :]).astype(columns.dtype)
-        return jnp.dot(
-            recv_pick, arrived.reshape(dp_size * capacity, -1), preferred_element_type=jnp.float32
-        ).astype(columns.dtype)
+        packed = sum(
+            jnp.dot(
+                recv_pick[:, k * capacity : (k + 1) * capacity],
+                chunk,
+                preferred_element_type=jnp.float32,
+            )
+            for k, chunk in enumerate(chunks)
+        )
+        return packed.astype(columns.dtype)
 
     packed_kv = send(rollout_rows[:, QUERY_HEADS * HEAD_SIZE :], True)
     packed_q = send(rollout_rows[:, : QUERY_HEADS * HEAD_SIZE], True)

time: 103 us -> 90.1 us (0.87)
  waiting for transfers between devices: 44.5 us -> 27.2 us
  matrix products: 4.88 us -> 8.68 us
  starting transfers between devices: 19 us -> 20.5 us
    ppermute x6, waiting for transfers between devices: 17.9 us -> 0.02 us  [send(): lax.ppermute(outgoing[shift], 'dp', [(k, (k + shift) % dp_size) for k in...]
    dot_general x2 -> x8, matrix products: 1.73 us -> 6.74 us  [send(): jnp.dot(recv_pick[:, k * capacity:(k + 1) * capacity], chunk, preferred_e...]
    another operation x5 -> x3, other arithmetic: 2.62 us -> 0.28 us  [the longest x2 2.34 us: send(): jnp.stack([outgoing[0]] + [lax.ppermute(outgoing[shift], 'dp', [(k, (k +...]
    ppermute x6, starting transfers between devices: 5.28 us -> 6.53 us  [send(): lax.ppermute(outgoing[shift], 'dp', [(k, (k + shift) % dp_size) for k in...]
    convert_element_type x1, other arithmetic: 1.26 us -> 2.48 us  [step(): (upstream[0].astype(jnp.float32) * tok_adv[:, None]).astype(jnp.bfloat16)]
    dot_general x2, matrix products: 3.15 us -> 1.93 us  [send(): jnp.dot(send_pick, columns, preferred_element_type=jnp.float32)]
  transfers between devices with their start and end apart: 12 -> 12, of which waited for: 6 -> 5; matrix products, arithmetic and copies ran while one was open for 8% -> 17% of each run, Pallas kernels for 0% -> 0%
where the time goes in v12:
time: 90.1 us; the launch traced here: 89.6 us
  waiting for transfers between devices  27.2 us (30%)
  starting transfers between devices  20.5 us (23%)
  Pallas kernels  19.7 us (22%)
  other arithmetic  9.57 us (11%)
  matrix products  8.68 us (10%)
  local copies, waits for them, and re-layouts  2.87 us (3%)
  between operations  1.02 us (1%)
    ppermute x4, waiting for transfers between devices, step(): lax.ppermute(outgoing[shift - 1], 'sp', [(k, k - shift) for k in range(sh...  20 us
    pallas_call x2, Pallas kernels, attend_pallas(): pl.pallas_call(functools.partial(attend_kernel, first_group=part * groups...  19.7 us
    ppermute x2, starting transfers between devices, step(): lax.ppermute(kv_local, 'sp', [(k, k + shift) for k in range(sp_size - shi...  8.7 us
    ppermute x2, waiting for transfers between devices, step(): lax.ppermute(kv_local, 'sp', [(k, k + shift) for k in range(sp_size - shi...  7.21 us
    dot_general x8, matrix products, send(): jnp.dot(recv_pick[:, k * capacity:(k + 1) * capacity], chunk, preferred_e...  6.74 us
    ppermute x6, starting transfers between devices, send(): lax.ppermute(outgoing[shift], 'dp', [(k, (k + shift) % dp_size) for k in...  6.53 us
    ppermute x4, starting transfers between devices, step(): lax.ppermute(outgoing[shift - 1], 'sp', [(k, k - shift) for k in range(sh...  5.29 us
    convert_element_type x1, other arithmetic, step(): (upstream[0].astype(jnp.float32) * tok_adv[:, None]).astype(jnp.bfloat16)  2.48 us
  transfers between devices with their start and end apart: 12, of which 5 were waited for; matrix products, arithmetic and copies ran while one was open for 17% of the time, Pallas kernels for 0%

profile of v12, /device:TPU:0, one launch (start us, length us, event | category | flops | bytes accessed | tf_op | source)
XLA Modules:
  0.0 89.6 jit_solution(13994601831275378922)
XLA Ops:
  2.6 1.2 %convolution_convert_fusion.1 = bf16[256,1024]{1,0:T(8,128)(2,1)S(1)} fusion(bf16[128,5120]{1,0:T(8,128)(2,1)} %param.6, s32[128]{0:T(128)S(1)} %fusion.39), kind=kOutput, calls=%fused_computation.7 | convolution fusion | flops 67403776 | bytes 786944 | tf_op jit(solution)/shard_map/dot_general | solution.py:51
  5.1 1.9 %collective-permute-start.5 = (bf16[64,1024]{1,0:T(8,128)(2,1)}, bf16[64,1024]{1,0:T(8,128)(2,1)}, u32[]{:S(2)}, u32[]{:S(2)}) collective-permute-start(bf16[64,1024]{1,0:T(8,128)(2,1)} %get-tuple-element.24), channel_id=1, source_target_pairs={{0,12},{4,0},{8,4},{12,8},{1,13},{5,1},{9,5},{13,9},{2,14},{6,2},{... | collective-permute-start | bytes 393224 | tf_op jit(solution)/shard_map/ppermute | solution.py:56
  7.0 2.3 %collective-permute-start.4 = (bf16[64,1024]{1,0:T(8,128)(2,1)}, bf16[64,1024]{1,0:T(8,128)(2,1)S(1)}, u32[]{:S(2)}, u32[]{:S(2)}) collective-permute-start(bf16[64,1024]{1,0:T(8,128)(2,1)} %get-tuple-element.23), channel_id=1, source_target_pairs={{0,8},{4,12},{8,0},{12,4},{1,9},{5,13},{9,1},{13,5},{2,10},{6,14},... | collective-permute-start | bytes 393224 | tf_op jit(solution)/shard_map/ppermute | solution.py:56
  10.0 1.2 %fusion.43 = (bf16[64,4096]{1,0:T(8,128)(2,1)}, bf16[64,4096]{1,0:T(8,128)(2,1)}, bf16[64,4096]{1,0:T(8,128)(2,1)}) fusion(bf16[256,4096]{1,0:T(8,128)(2,1)S(1)} %convolution_convert_fusion), kind=kLoop, calls=%fused_computation.93 | loop fusion | bytes 3145728 | tf_op jit(solution)/shard_map/slice | solution.py:57
  11.2 1.7 %collective-permute-start.2 = (bf16[64,4096]{1,0:T(8,128)(2,1)}, bf16[64,4096]{1,0:T(8,128)(2,1)}, u32[]{:S(2)}, u32[]{:S(2)}) collective-permute-start(bf16[64,4096]{1,0:T(8,128)(2,1)} %get-tuple-element.21), channel_id=1, source_target_pairs={{0,12},{4,0},{8,4},{12,8},{1,13},{5,1},{9,5},{13,9},{2,14},{6,2},{... | collective-permute-start | bytes 1572872 | tf_op jit(solution)/shard_map/ppermute | solution.py:56
  15.1 2.5 %fusion.2.g_ref = bf16[128,4096]{1,0:T(8,128)(2,1)} fusion(bf16[1,128,4096]{2,1,0:T(8,128)(2,1)} %param.9, f32[128]{0:T(128)S(1)} %select_reduce_fusion.2), kind=kLoop, calls=%fused_computation.6 | loop fusion | flops 1572864 | bytes 2097664 | tf_op jit(solution)/shard_map/convert_element_type | solution.py:200
  18.0 1.2 %fusion.14 = f32[128,1024]{1,0:T(8,128)S(1)} fusion(bf16[64,1024]{1,0:T(8,128)(2,1)} %collective-permute-done.5, pred[128,256]{1,0:T(32,128)(4,1)S(1)} %iota_compare_fusion.3), kind=kOutput, calls=%fused_computation.39 | convolution fusion | flops 16777216 | bytes 671744 | tf_op jit(solution)/shard_map/dot_general | solution.py:69
  19.5 4.0 %collective-permute-start.6 = (bf16[128,1152]{1,0:T(8,128)(2,1)S(1)}, bf16[128,1152]{1,0:T(8,128)(2,1)S(1)}, u32[]{:S(2)}, u32[]{:S(2)}) collective-permute-start(bf16[128,1152]{1,0:T(8,128)(2,1)S(1)} %pad_maximum_fusion.1), channel_id=1, source_target_pairs={{0,1},{1,2},{2,3},{4,5},{5,6},{6,7},{8,9},{9,10},{10,11},{12,13},{... | collective-permute-start | bytes 884744 | tf_op jit(solution)/shard_map/ppermute | solution.py:186
  23.5 4.7 %collective-permute-start.7 = (bf16[128,1152]{1,0:T(8,128)(2,1)S(1)}, bf16[128,1152]{1,0:T(8,128)(2,1)S(1)}, u32[]{:S(2)}, u32[]{:S(2)}) collective-permute-start(bf16[128,1152]{1,0:T(8,128)(2,1)S(1)} %pad_maximum_fusion.1), channel_id=1, source_target_pairs={{0,2},{1,3},{4,6},{5,7},{8,10},{9,11},{12,14},{13,15},{16,18},{17,... | collective-permute-start | bytes 884744 | tf_op jit(solution)/shard_map/ppermute | solution.py:186
  28.7 2.2 %collective-permute-done.6 = bf16[128,1152]{1,0:T(8,128)(2,1)S(1)} collective-permute-done((bf16[128,1152]{1,0:T(8,128)(2,1)S(1)}, bf16[128,1152]{1,0:T(8,128)(2,1)S(1)}, u32[]{:S(2)}, u32[]{:S(2)}) %collective-permute-start.6) | collective-permute-done | bytes 294944 | tf_op jit(solution)/shard_map/ppermute | solution.py:186
  30.9 5.0 %collective-permute-done.7 = bf16[128,1152]{1,0:T(8,128)(2,1)S(1)} collective-permute-done((bf16[128,1152]{1,0:T(8,128)(2,1)S(1)}, bf16[128,1152]{1,0:T(8,128)(2,1)S(1)}, u32[]{:S(2)}, u32[]{:S(2)}) %collective-permute-start.7) | collective-permute-done | bytes 294944 | tf_op jit(solution)/shard_map/ppermute | solution.py:186
  37.0 1.5 %fusion.16 = f32[128,4096]{1,0:T(8,128)S(1)} fusion(bf16[64,4096]{1,0:T(8,128)(2,1)} %collective-permute-done.2, pred[128,256]{1,0:T(32,128)(4,1)S(1)} %iota_compare_fusion.3), kind=kOutput, calls=%fused_computation.41 | convolution fusion | flops 67108864 | bytes 2637824 | tf_op jit(solution)/shard_map/dot_general | solution.py:69
  38.6 1.5 %convolution_add_fusion.1 = f32[128,4096]{1,0:T(8,128)S(1)} fusion(f32[128,4096]{1,0:T(8,128)S(1)} %fusion.6, bf16[64,4096]{1,0:T(8,128)(2,1)} %collective-permute-done, pred[128,256]{1,0:T(32,128)(4,1)S(1)} %iota_compare_fusion.3), kind=kOutput, calls=%fused_computation.3 | convolution fusion | flops 67633152 | bytes 4734976 | tf_op jit(solution)/shard_map/dot_general | solution.py:69
  40.1 1.4 %fusion.1.q_ref = bf16[128,4096]{1,0:T(8,128)(2,1)} fusion(f32[128,4096]{1,0:T(8,128)S(1)} %fusion.16, f32[128,4096]{1,0:T(8,128)S(1)} %convolution_add_fusion.1, bf16[64,4096]{1,0:T(8,128)(2,1)S(1)} %collective-permute-done.1, pred[128,256]{1,0:T(32,128)(4,1)S(1)} %iota_compare_fusion.3), kind=kOutput, calls=%fused_computation.4 | convolution fusion | flops 68681728 | bytes 5783552 | tf_op jit(solution)/shard_map/dot_general | solution.py:69
  41.5 9.8 %shard_map.77 = (bf16[128,2048]{1,0:T(8,128)(2,1)}, f32[128,512]{1,0:T(8,128)}, bf16[128,512]{1,0:T(8,128)(2,1)}, bf16[128,512]{1,0:T(8,128)(2,1)}) custom-call(bf16[128,4096]{1,0:T(8,128)(2,1)} %fusion.1.q_ref, bf16[128,4096]{1,0:T(8,128)(2,1)} %fusion.2.g_ref, bf16[384,1152]{1,0:T(8,128)(2,1)} %copy-done.1, f32[384,128]{1,0:T(8,128)} %and_select_fusion.m_ref), custom_call_target="tpu_custom_call" | custom-call | flops 1006632960 | bytes 2654208 | tf_op jit(solution)/shard_map/pallas_call | solution.py:146
  51.4 9.9 %shard_map.78 = (bf16[128,2048]{1,0:T(8,128)(2,1)}, f32[128,512]{1,0:T(8,128)}, bf16[128,512]{1,0:T(8,128)(2,1)}, bf16[128,512]{1,0:T(8,128)(2,1)}) custom-call(bf16[128,4096]{1,0:T(8,128)(2,1)} %fusion.1.q_ref, bf16[128,4096]{1,0:T(8,128)(2,1)} %fusion.2.g_ref, bf16[384,1152]{1,0:T(8,128)(2,1)} %copy-done.1, f32[384,128]{1,0:T(8,128)} %and_select_fusion.m_ref), custom_call_target="tpu_custom_call" | custom-call | flops 1006632960 | bytes 2654208 | tf_op jit(solution)/shard_map/pallas_call | solution.py:146
  61.3 1.4 %collective-permute-start.8 = (bf16[128,512]{1,0:T(8,128)(2,1)S(1)}, bf16[128,512]{1,0:T(8,128)(2,1)S(1)}, u32[]{:S(2)}, u32[]{:S(2)}) collective-permute-start(bf16[128,512]{1,0:T(8,128)(2,1)S(1)} %copy-done.8), channel_id=1, source_target_pairs={{1,0},{2,1},{3,2},{5,4},{6,5},{7,6},{9,8},{10,9},{11,10},{13,12},{... | collective-permute-start | bytes 393224 | tf_op jit(solution)/shard_map/ppermute | solution.py:218
  62.7 1.3 %collective-permute-start.9 = (bf16[128,512]{1,0:T(8,128)(2,1)S(1)}, bf16[128,512]{1,0:T(8,128)(2,1)S(1)}, u32[]{:S(2)}, u32[]{:S(2)}) collective-permute-start(bf16[128,512]{1,0:T(8,128)(2,1)S(1)} %copy-done.7), channel_id=1, source_target_pairs={{2,0},{3,1},{6,4},{7,5},{10,8},{11,9},{14,12},{15,13},{18,16},{19,... | collective-permute-start | bytes 393224 | tf_op jit(solution)/shard_map/ppermute | solution.py:218
  64.0 1.3 %collective-permute-start.10 = (bf16[128,512]{1,0:T(8,128)(2,1)}, bf16[128,512]{1,0:T(8,128)(2,1)S(1)}, u32[]{:S(2)}, u32[]{:S(2)}) collective-permute-start(bf16[128,512]{1,0:T(8,128)(2,1)} %get-tuple-element.16), channel_id=1, source_target_pairs={{1,0},{2,1},{3,2},{5,4},{6,5},{7,6},{9,8},{10,9},{11,10},{13,12},{... | collective-permute-start | bytes 393224 | tf_op jit(solution)/shard_map/ppermute | solution.py:218
  65.3 1.3 %collective-permute-start.11 = (bf16[128,512]{1,0:T(8,128)(2,1)}, bf16[128,512]{1,0:T(8,128)(2,1)S(1)}, u32[]{:S(2)}, u32[]{:S(2)}) collective-permute-start(bf16[128,512]{1,0:T(8,128)(2,1)} %get-tuple-element.17), channel_id=1, source_target_pairs={{2,0},{3,1},{6,4},{7,5},{10,8},{11,9},{14,12},{15,13},{18,16},{19,... | collective-permute-start | bytes 393224 | tf_op jit(solution)/shard_map/ppermute | solution.py:218
  66.6 2.1 %maximum_bitcast_fusion = bf16[1,128,4096]{2,1,0:T(8,128)(2,1)} fusion(bf16[128,2048]{1,0:T(8,128)(2,1)} %get-tuple-element.11, bf16[128,2048]{1,0:T(8,128)(2,1)S(1)} %copy-done.2), kind=kLoop, calls=%fused_computation.12 | loop fusion | flops 2097152 | bytes 2097152 | tf_op jit(solution)/shard_map/reshape | solution.py:225
  68.7 7.5 %collective-permute-done.8 = bf16[128,512]{1,0:T(8,128)(2,1)S(1)} collective-permute-done((bf16[128,512]{1,0:T(8,128)(2,1)S(1)}, bf16[128,512]{1,0:T(8,128)(2,1)S(1)}, u32[]{:S(2)}, u32[]{:S(2)}) %collective-permute-start.8) | collective-permute-done | bytes 131104 | tf_op jit(solution)/shard_map/ppermute | solution.py:218
  76.2 9.2 %collective-permute-done.9 = bf16[128,512]{1,0:T(8,128)(2,1)S(1)} collective-permute-done((bf16[128,512]{1,0:T(8,128)(2,1)S(1)}, bf16[128,512]{1,0:T(8,128)(2,1)S(1)}, u32[]{:S(2)}, u32[]{:S(2)}) %collective-permute-start.9) | collective-permute-done | bytes 131104 | tf_op jit(solution)/shard_map/ppermute | solution.py:218
  85.5 3.3 %collective-permute-done.11 = bf16[128,512]{1,0:T(8,128)(2,1)S(1)} collective-permute-done((bf16[128,512]{1,0:T(8,128)(2,1)}, bf16[128,512]{1,0:T(8,128)(2,1)S(1)}, u32[]{:S(2)}, u32[]{:S(2)}) %collective-permute-start.11) | collective-permute-done | bytes 131104 | tf_op jit(solution)/shard_map/ppermute | solution.py:218
  (69 shorter events, 9.1 us)
Async XLA Ops:
  1.6 7.7 %copy-start = (bf16[128,5120]{1,0:T(8,128)(2,1)S(1)}, bf16[128,5120]{1,0:T(8,128)(2,1)}, u32[]{:S(2)}) copy-start(bf16[128,5120]{1,0:T(8,128)(2,1)} %param.6) | copy-start | bytes 3932164
  4.6 13.0 %collective-permute-start.3 = (bf16[64,1024]{1,0:T(8,128)(2,1)}, bf16[64,1024]{1,0:T(8,128)(2,1)S(1)}, u32[]{:S(2)}, u32[]{:S(2)}) collective-permute-start(bf16[64,1024]{1,0:T(8,128)(2,1)} %get-tuple-element.25), channel_id=1, source_target_pairs={{0,4},{4,8},{8,12},{12,0},{1,5},{5,9},{9,13},{13,1},{2,6},{6,10},{... | collective-permute-start | bytes 393224 | tf_op jit(solution)/shard_map/ppermute | solution.py:56
  5.1 12.9 %collective-permute-start.5 = (bf16[64,1024]{1,0:T(8,128)(2,1)}, bf16[64,1024]{1,0:T(8,128)(2,1)}, u32[]{:S(2)}, u32[]{:S(2)}) collective-permute-start(bf16[64,1024]{1,0:T(8,128)(2,1)} %get-tuple-element.24), channel_id=1, source_target_pairs={{0,12},{4,0},{8,4},{12,8},{1,13},{5,1},{9,5},{13,9},{2,14},{6,2},{... | collective-permute-start | bytes 393224 | tf_op jit(solution)/shard_map/ppermute | solution.py:56
  7.0 12.2 %collective-permute-start.4 = (bf16[64,1024]{1,0:T(8,128)(2,1)}, bf16[64,1024]{1,0:T(8,128)(2,1)S(1)}, u32[]{:S(2)}, u32[]{:S(2)}) collective-permute-start(bf16[64,1024]{1,0:T(8,128)(2,1)} %get-tuple-element.23), channel_id=1, source_target_pairs={{0,8},{4,12},{8,0},{12,4},{1,9},{5,13},{9,1},{13,5},{2,10},{6,14},... | collective-permute-start | bytes 393224 | tf_op jit(solution)/shard_map/ppermute | solution.py:56
  10.0 4.6 %copy-start.5 = (s32[1,128]{1,0:T(1,128)S(1)}, s32[1,128]{1,0:T(1,128)}, u32[]{:S(2)}) copy-start(s32[1,128]{1,0:T(1,128)} %param.8) | copy-start | bytes 1540
  10.0 4.6 %copy-start.9 = (s32[16]{0:T(128)S(1)}, s32[16]{0:T(128)}, u32[]{:S(2)}) copy-start(s32[16]{0:T(128)} %param.10) | copy-start | bytes 196
  10.0 4.7 %copy-start.6 = (s32[16]{0:T(128)S(1)}, s32[16]{0:T(128)}, u32[]{:S(2)}) copy-start(s32[16]{0:T(128)} %param.11) | copy-start | bytes 196
  11.2 27.3 %collective-permute-start = (bf16[64,4096]{1,0:T(8,128)(2,1)}, bf16[64,4096]{1,0:T(8,128)(2,1)}, u32[]{:S(2)}, u32[]{:S(2)}) collective-permute-start(bf16[64,4096]{1,0:T(8,128)(2,1)} %get-tuple-element.22), channel_id=1, source_target_pairs={{0,4},{4,8},{8,12},{12,0},{1,5},{5,9},{9,13},{13,1},{2,6},{6,10},{... | collective-permute-start | bytes 1572872 | tf_op jit(solution)/shard_map/ppermute | solution.py:56
  11.2 25.8 %collective-permute-start.2 = (bf16[64,4096]{1,0:T(8,128)(2,1)}, bf16[64,4096]{1,0:T(8,128)(2,1)}, u32[]{:S(2)}, u32[]{:S(2)}) collective-permute-start(bf16[64,4096]{1,0:T(8,128)(2,1)} %get-tuple-element.21), channel_id=1, source_target_pairs={{0,12},{4,0},{8,4},{12,8},{1,13},{5,1},{9,5},{13,9},{2,14},{6,2},{... | collective-permute-start | bytes 1572872 | tf_op jit(solution)/shard_map/ppermute | solution.py:56
  17.6 22.5 %collective-permute-start.1 = (bf16[64,4096]{1,0:T(8,128)(2,1)}, bf16[64,4096]{1,0:T(8,128)(2,1)S(1)}, u32[]{:S(2)}, u32[]{:S(2)}) collective-permute-start(bf16[64,4096]{1,0:T(8,128)(2,1)} %get-tuple-element.20), channel_id=1, source_target_pairs={{0,8},{4,12},{8,0},{12,4},{1,9},{5,13},{9,1},{13,5},{2,10},{6,14},... | collective-permute-start | bytes 1572872 | tf_op jit(solution)/shard_map/ppermute | solution.py:56
  19.5 11.4 %collective-permute-start.6 = (bf16[128,1152]{1,0:T(8,128)(2,1)S(1)}, bf16[128,1152]{1,0:T(8,128)(2,1)S(1)}, u32[]{:S(2)}, u32[]{:S(2)}) collective-permute-start(bf16[128,1152]{1,0:T(8,128)(2,1)S(1)} %pad_maximum_fusion.1), channel_id=1, source_target_pairs={{0,1},{1,2},{2,3},{4,5},{5,6},{6,7},{8,9},{9,10},{10,11},{12,13},{... | collective-permute-start | bytes 884744 | tf_op jit(solution)/shard_map/ppermute | solution.py:186
  23.5 12.3 %collective-permute-start.7 = (bf16[128,1152]{1,0:T(8,128)(2,1)S(1)}, bf16[128,1152]{1,0:T(8,128)(2,1)S(1)}, u32[]{:S(2)}, u32[]{:S(2)}) collective-permute-start(bf16[128,1152]{1,0:T(8,128)(2,1)S(1)} %pad_maximum_fusion.1), channel_id=1, source_target_pairs={{0,2},{1,3},{4,6},{5,7},{8,10},{9,11},{12,14},{13,15},{16,18},{17,... | collective-permute-start | bytes 884744 | tf_op jit(solution)/shard_map/ppermute | solution.py:186
  36.0 4.1 %copy-start.1 = (bf16[384,1152]{1,0:T(8,128)(2,1)}, bf16[384,1152]{1,0:T(8,128)(2,1)S(1)}, u32[]{:S(2)}) copy-start(bf16[384,1152]{1,0:T(8,128)(2,1)S(1)} %pad_maximum_fusion.kv_ref) | copy-start | bytes 2654212
  51.4 9.9 %copy-start.8 = (bf16[128,512]{1,0:T(8,128)(2,1)S(1)}, bf16[128,512]{1,0:T(8,128)(2,1)}, u32[]{:S(2)}) copy-start(bf16[128,512]{1,0:T(8,128)(2,1)} %get-tuple-element.13) | copy-start | bytes 393220
  51.4 11.3 %copy-start.7 = (bf16[128,512]{1,0:T(8,128)(2,1)S(1)}, bf16[128,512]{1,0:T(8,128)(2,1)}, u32[]{:S(2)}) copy-start(bf16[128,512]{1,0:T(8,128)(2,1)} %get-tuple-element.14) | copy-start | bytes 393220
  51.4 15.2 %copy-start.2 = (bf16[128,2048]{1,0:T(8,128)(2,1)S(1)}, bf16[128,2048]{1,0:T(8,128)(2,1)}, u32[]{:S(2)}) copy-start(bf16[128,2048]{1,0:T(8,128)(2,1)} %get-tuple-element.10) | copy-start | bytes 1572868
  51.4 34.0 %copy-start.4 = (f32[128,512]{1,0:T(8,128)S(1)}, f32[128,512]{1,0:T(8,128)}, u32[]{:S(2)}) copy-start(f32[128,512]{1,0:T(8,128)} %get-tuple-element.12) | copy-start | bytes 786436
  61.3 27.5 %copy-start.3 = (f32[128,512]{1,0:T(8,128)S(1)}, f32[128,512]{1,0:T(8,128)}, u32[]{:S(2)}) copy-start(f32[128,512]{1,0:T(8,128)} %get-tuple-element.15) | copy-start | bytes 786436
  61.3 14.9 %collective-permute-start.8 = (bf16[128,512]{1,0:T(8,128)(2,1)S(1)}, bf16[128,512]{1,0:T(8,128)(2,1)S(1)}, u32[]{:S(2)}, u32[]{:S(2)}) collective-permute-start(bf16[128,512]{1,0:T(8,128)(2,1)S(1)} %copy-done.8), channel_id=1, source_target_pairs={{1,0},{2,1},{3,2},{5,4},{6,5},{7,6},{9,8},{10,9},{11,10},{13,12},{... | collective-permute-start | bytes 393224 | tf_op jit(solution)/shard_map/ppermute | solution.py:218
  62.7 22.7 %collective-permute-start.9 = (bf16[128,512]{1,0:T(8,128)(2,1)S(1)}, bf16[128,512]{1,0:T(8,128)(2,1)S(1)}, u32[]{:S(2)}, u32[]{:S(2)}) collective-permute-start(bf16[128,512]{1,0:T(8,128)(2,1)S(1)} %copy-done.7), channel_id=1, source_target_pairs={{2,0},{3,1},{6,4},{7,5},{10,8},{11,9},{14,12},{15,13},{18,16},{19,... | collective-permute-start | bytes 393224 | tf_op jit(solution)/shard_map/ppermute | solution.py:218
  64.0 21.4 %collective-permute-start.10 = (bf16[128,512]{1,0:T(8,128)(2,1)}, bf16[128,512]{1,0:T(8,128)(2,1)S(1)}, u32[]{:S(2)}, u32[]{:S(2)}) collective-permute-start(bf16[128,512]{1,0:T(8,128)(2,1)} %get-tuple-element.16), channel_id=1, source_target_pairs={{1,0},{2,1},{3,2},{5,4},{6,5},{7,6},{9,8},{10,9},{11,10},{13,12},{... | collective-permute-start | bytes 393224 | tf_op jit(solution)/shard_map/ppermute | solution.py:218
  65.3 23.4 %collective-permute-start.11 = (bf16[128,512]{1,0:T(8,128)(2,1)}, bf16[128,512]{1,0:T(8,128)(2,1)S(1)}, u32[]{:S(2)}, u32[]{:S(2)}) collective-permute-start(bf16[128,512]{1,0:T(8,128)(2,1)} %get-tuple-element.17), channel_id=1, source_target_pairs={{2,0},{3,1},{6,4},{7,5},{10,8},{11,9},{14,12},{15,13},{18,16},{19,... | collective-permute-start | bytes 393224 | tf_op jit(solution)/shard_map/ppermute | solution.py:218

commit v13 on v11

--- a/solution.py
+++ b/solution.py
@@ -129,7 +129,7 @@
             send_ref[:, value_cols] = value_sum[rows].astype(send_ref.dtype)
 
 
-def attend_pallas(packed, weighted, kv_all, bias, part, groups):
+def attend_pallas(packed, weighted, kv_all, bias, first_group, groups):
     token_rows = packed.shape[0]
     key_rows = kv_all.shape[0]
     reach = key_rows // token_rows - 1
@@ -140,11 +140,11 @@
     bytes_accessed = 6 * token_rows * part_width + 2 * key_rows * kv_all.shape[1] + 4 * token_rows * key_rows
     whole = lambda i: (0, 0)
     return pl.pallas_call(
-        functools.partial(attend_kernel, first_group=part * groups),
+        functools.partial(attend_kernel, first_group=first_group),
         grid=(1,),
         in_specs=[
-            pl.BlockSpec((token_rows, part_width), lambda i: (0, part)),
-            pl.BlockSpec((token_rows, part_width), lambda i: (0, part)),
+            pl.BlockSpec((token_rows, part_width), lambda i: (0, first_group // groups)),
+            pl.BlockSpec((token_rows, part_width), lambda i: (0, first_group // groups)),
             pl.BlockSpec(kv_all.shape, whole),
             pl.BlockSpec(bias.shape, whole),
         ],
@@ -204,12 +204,10 @@
         & (key_pos[None, :] >= 0)
     )
     bias = jnp.where(allowed.T, 0.0, -1e30).astype(jnp.float32)
-    groups = KEY_VALUE_HEADS // 2
+    part_groups = (KEY_VALUE_HEADS - KEY_VALUE_HEADS // 4, KEY_VALUE_HEADS // 4)
     query_parts, key_parts, value_parts = [], [], []
-    for part in range(2):
-        query_grad, total, *outgoing = attend_pallas(
-            packed_q, weighted, kv_all, bias, part, groups
-        )
+    for part, groups in enumerate(part_groups):
+        query_grad, total, *outgoing = attend_pallas(packed_q, weighted, kv_all, bias, sum(part_groups[:part]), groups)
         for shift in range(1, reach + 1):
             arrived = lax.ppermute(
                 outgoing[shift - 1], "sp", [(k, k - shift) for k in range(shift, sp_size)]

time: 103 us -> 102 us (level); the launches traced: 102 us -> 99.8 us
  waiting for transfers between devices: 44.5 us -> 42.9 us
    ppermute x4, waiting for transfers between devices: 19.2 us -> 17.4 us  [step(): lax.ppermute(outgoing[shift - 1], 'sp', [(k, k - shift) for k in range(sh...]
  transfers between devices with their start and end apart: 12 -> 12, of which waited for: 6 -> 6; matrix products, arithmetic and copies ran while one was open for 8% -> 7% of each run, Pallas kernels for 0% -> 0%
where the time goes in v13:
time: 102 us; the launch traced here: 99.8 us
  waiting for transfers between devices  42.9 us (42%)
  Pallas kernels  19.7 us (19%)
  starting transfers between devices  19.1 us (19%)
  other arithmetic  9.58 us (9%)
  matrix products  4.88 us (5%)
  local copies, waits for them, and re-layouts  2.81 us (3%)
    pallas_call x2, Pallas kernels, attend_pallas(): pl.pallas_call(functools.partial(attend_kernel, first_group=first_group),...  19.7 us
    ppermute x6, waiting for transfers between devices, send(): lax.ppermute(outgoing[shift], 'dp', [(k, (k + shift) % dp_size) for k in...  18 us
    ppermute x4, waiting for transfers between devices, step(): lax.ppermute(outgoing[shift - 1], 'sp', [(k, k - shift) for k in range(sh...  17.4 us
    ppermute x2, starting transfers between devices, step(): lax.ppermute(kv_local, 'sp', [(k, k + shift) for k in range(sp_size - shi...  8.37 us
    ppermute x2, waiting for transfers between devices, step(): lax.ppermute(kv_local, 'sp', [(k, k + shift) for k in range(sp_size - shi...  7.46 us
    ppermute x6, starting transfers between devices, send(): lax.ppermute(outgoing[shift], 'dp', [(k, (k + shift) % dp_size) for k in...  5.39 us
    ppermute x4, starting transfers between devices, step(): lax.ppermute(outgoing[shift - 1], 'sp', [(k, k - shift) for k in range(sh...  5.3 us
    dot_general x2, matrix products, send(): jnp.dot(send_pick, columns, preferred_element_type=jnp.float32)  3.15 us
  transfers between devices with their start and end apart: 12, of which 6 were waited for; matrix products, arithmetic and copies ran while one was open for 7% of the time, Pallas kernels for 0%

profile of v13, /device:TPU:0, one launch (start us, length us, event | category | flops | bytes accessed | tf_op | source)
XLA Modules:
  0.0 99.8 jit_solution(14563821375322339047)
XLA Ops:
  3.8 1.9 %convolution_convert_fusion = bf16[256,4096]{1,0:T(8,128)(2,1)S(1)} fusion(bf16[128,5120]{1,0:T(8,128)(2,1)} %param.6, s32[128]{0:T(128)S(1)} %get-tuple-element.33), kind=kOutput, calls=%fused_computation | convolution fusion | flops 269516800 | bytes 3146240 | tf_op jit(solution)/shard_map/dot_general | solution.py:51
  5.8 1.2 %slice_bitcast_fusion = (bf16[1,64,4096]{2,1,0:T(8,128)(2,1)S(1)}, bf16[64,4096]{1,0:T(8,128)(2,1)}, bf16[64,4096]{1,0:T(8,128)(2,1)}, bf16[64,4096]{1,0:T(8,128)(2,1)S(1)}) fusion(bf16[256,4096]{1,0:T(8,128)(2,1)S(1)} %convolution_convert_fusion), kind=kLoop, calls=%fused_computation.10 | loop fusion | bytes 4194304 | tf_op jit(solution)/shard_map/slice | solution.py:56
  6.9 2.4 %collective-permute-start.2 = (bf16[64,4096]{1,0:T(8,128)(2,1)}, bf16[64,4096]{1,0:T(8,128)(2,1)S(1)}, u32[]{:S(2)}, u32[]{:S(2)}) collective-permute-start(bf16[64,4096]{1,0:T(8,128)(2,1)} %get-tuple-element.21), channel_id=1, source_target_pairs={{0,12},{4,0},{8,4},{12,8},{1,13},{5,1},{9,5},{13,9},{2,14},{6,2},{... | collective-permute-start | bytes 1572872 | tf_op jit(solution)/shard_map/ppermute | solution.py:58
  9.9 1.2 %convolution_convert_fusion.2 = bf16[256,1024]{1,0:T(8,128)(2,1)S(1)} fusion(bf16[128,5120]{1,0:T(8,128)(2,1)} %param.6, s32[128]{0:T(128)S(1)} %get-tuple-element.33), kind=kOutput, calls=%fused_computation.5 | convolution fusion | flops 67403776 | bytes 786944 | tf_op jit(solution)/shard_map/dot_general | solution.py:51
  12.0 1.7 %collective-permute-start.4 = (bf16[64,1024]{1,0:T(8,128)(2,1)S(1)}, bf16[64,1024]{1,0:T(8,128)(2,1)S(1)}, u32[]{:S(2)}, u32[]{:S(2)}) collective-permute-start(bf16[64,1024]{1,0:T(8,128)(2,1)S(1)} %get-tuple-element.26), channel_id=1, source_target_pairs={{0,8},{4,12},{8,0},{12,4},{1,9},{5,13},{9,1},{13,5},{2,10},{6,14},... | collective-permute-start | bytes 393224 | tf_op jit(solution)/shard_map/ppermute | solution.py:58
  14.2 1.3 %fusion.g_ref = bf16[128,4096]{1,0:T(8,128)(2,1)} fusion(bf16[1,128,4096]{2,1,0:T(8,128)(2,1)S(1)} %copy-done.1, f32[128]{0:T(128)S(1)} %select_reduce_fusion.2), kind=kLoop, calls=%fused_computation.4 | loop fusion | flops 1572864 | bytes 2097664 | tf_op jit(solution)/shard_map/convert_element_type | solution.py:196
  15.4 16.4 %collective-permute-done.5 = bf16[64,1024]{1,0:T(8,128)(2,1)S(1)} collective-permute-done((bf16[64,1024]{1,0:T(8,128)(2,1)}, bf16[64,1024]{1,0:T(8,128)(2,1)S(1)}, u32[]{:S(2)}, u32[]{:S(2)}) %collective-permute-start.5) | collective-permute-done | bytes 131104 | tf_op jit(solution)/shard_map/ppermute | solution.py:58
  32.4 1.6 %collective-permute-done.4 = bf16[64,1024]{1,0:T(8,128)(2,1)S(1)} collective-permute-done((bf16[64,1024]{1,0:T(8,128)(2,1)S(1)}, bf16[64,1024]{1,0:T(8,128)(2,1)S(1)}, u32[]{:S(2)}, u32[]{:S(2)}) %collective-permute-start.4) | collective-permute-done | bytes 131104 | tf_op jit(solution)/shard_map/ppermute | solution.py:58
  34.4 4.7 %collective-permute-start.7 = (bf16[128,1152]{1,0:T(8,128)(2,1)S(1)}, bf16[128,1152]{1,0:T(8,128)(2,1)S(1)}, u32[]{:S(2)}, u32[]{:S(2)}) collective-permute-start(bf16[128,1152]{1,0:T(8,128)(2,1)S(1)} %pad_maximum_fusion.3), channel_id=1, source_target_pairs={{0,2},{1,3},{4,6},{5,7},{8,10},{9,11},{12,14},{13,15},{16,18},{17,... | collective-permute-start | bytes 884744 | tf_op jit(solution)/shard_map/ppermute | solution.py:182
  39.1 3.7 %collective-permute-start.6 = (bf16[128,1152]{1,0:T(8,128)(2,1)S(1)}, bf16[128,1152]{1,0:T(8,128)(2,1)S(1)}, u32[]{:S(2)}, u32[]{:S(2)}) collective-permute-start(bf16[128,1152]{1,0:T(8,128)(2,1)S(1)} %pad_maximum_fusion.3), channel_id=1, source_target_pairs={{0,1},{1,2},{2,3},{4,5},{5,6},{6,7},{8,9},{9,10},{10,11},{12,13},{... | collective-permute-start | bytes 884744 | tf_op jit(solution)/shard_map/ppermute | solution.py:182
  42.9 3.6 %collective-permute-done.7 = bf16[128,1152]{1,0:T(8,128)(2,1)S(1)} collective-permute-done((bf16[128,1152]{1,0:T(8,128)(2,1)S(1)}, bf16[128,1152]{1,0:T(8,128)(2,1)S(1)}, u32[]{:S(2)}, u32[]{:S(2)}) %collective-permute-start.7) | collective-permute-done | bytes 294944 | tf_op jit(solution)/shard_map/ppermute | solution.py:182
  46.5 3.8 %collective-permute-done.6 = bf16[128,1152]{1,0:T(8,128)(2,1)S(1)} collective-permute-done((bf16[128,1152]{1,0:T(8,128)(2,1)S(1)}, bf16[128,1152]{1,0:T(8,128)(2,1)S(1)}, u32[]{:S(2)}, u32[]{:S(2)}) %collective-permute-start.6) | collective-permute-done | bytes 294944 | tf_op jit(solution)/shard_map/ppermute | solution.py:182
  50.6 0.9 and_select_fusion.m_ref
  51.5 1.3 %pad_maximum_fusion = bf16[4,64,4096]{2,1,0:T(8,128)(2,1)S(1)} fusion(bf16[1,64,4096]{2,1,0:T(8,128)(2,1)S(1)} %bitcast.39, bf16[1,64,4096]{2,1,0:T(8,128)(2,1)} %bitcast.6, bf16[1,64,4096]{2,1,0:T(8,128)(2,1)S(1)} %bitcast.40, bf16[1,64,4096]{2,1,0:T(8,128)(2,1)S(1)} %get-tuple-element.20), kind=kLoop, calls=%fused_computation.2 | loop fusion | flops 3145728 | bytes 4194304 | tf_op jit(solution)/shard_map/stack | solution.py:55
  52.8 1.5 %convolution_convert_fusion.1.q_ref = bf16[128,4096]{1,0:T(8,128)(2,1)} fusion(bf16[256,4096]{1,0:T(8,128)(2,1)S(1)} %bitcast.37, s32[128]{0:T(128)S(1)} %get-tuple-element.32), kind=kOutput, calls=%fused_computation.1 | convolution fusion | flops 268992512 | bytes 3146240 | tf_op jit(solution)/shard_map/dot_general | solution.py:70
  54.3 5.9 %shard_map.78 = (bf16[128,1024]{1,0:T(8,128)(2,1)}, f32[128,256]{1,0:T(8,128)}, bf16[128,256]{1,0:T(8,128)(2,1)}, bf16[128,256]{1,0:T(8,128)(2,1)}) custom-call(bf16[128,4096]{1,0:T(8,128)(2,1)} %convolution_convert_fusion.1.q_ref, bf16[128,4096]{1,0:T(8,128)(2,1)} %fusion.g_ref, bf16[384,1152]{1,0:T(8,128)(2,1)} %copy-done, f32[384,128]{1,0:T(8,128)} %and_select_fusion.m_ref), custom_call_target="tpu_custom_call" | custom-call | flops 503316480 | bytes 1867776 | tf_op jit(solution)/shard_map/pallas_call | solution.py:142
  60.2 13.8 %shard_map.77 = (bf16[128,3072]{1,0:T(8,128)(2,1)}, f32[128,768]{1,0:T(8,128)}, bf16[128,768]{1,0:T(8,128)(2,1)}, bf16[128,768]{1,0:T(8,128)(2,1)}) custom-call(bf16[128,4096]{1,0:T(8,128)(2,1)} %convolution_convert_fusion.1.q_ref, bf16[128,4096]{1,0:T(8,128)(2,1)} %fusion.g_ref, bf16[384,1152]{1,0:T(8,128)(2,1)} %copy-done, f32[384,128]{1,0:T(8,128)} %and_select_fusion.m_ref), custom_call_target="tpu_custom_call" | custom-call | flops 1509949440 | bytes 3440640 | tf_op jit(solution)/shard_map/pallas_call | solution.py:142
  74.0 1.4 %collective-permute-start.11 = (bf16[128,256]{1,0:T(8,128)(2,1)S(1)}, bf16[128,256]{1,0:T(8,128)(2,1)S(1)}, u32[]{:S(2)}, u32[]{:S(2)}) collective-permute-start(bf16[128,256]{1,0:T(8,128)(2,1)S(1)} %copy-done.8), channel_id=1, source_target_pairs={{2,0},{3,1},{6,4},{7,5},{10,8},{11,9},{14,12},{15,13},{18,16},{19,... | collective-permute-start | bytes 196616 | tf_op jit(solution)/shard_map/ppermute | solution.py:212
  75.4 1.3 %collective-permute-start.10 = (bf16[128,256]{1,0:T(8,128)(2,1)S(1)}, bf16[128,256]{1,0:T(8,128)(2,1)S(1)}, u32[]{:S(2)}, u32[]{:S(2)}) collective-permute-start(bf16[128,256]{1,0:T(8,128)(2,1)S(1)} %copy-done.7), channel_id=1, source_target_pairs={{1,0},{2,1},{3,2},{5,4},{6,5},{7,6},{9,8},{10,9},{11,10},{13,12},{... | collective-permute-start | bytes 196616 | tf_op jit(solution)/shard_map/ppermute | solution.py:212
  76.7 1.3 %collective-permute-start.9 = (bf16[128,768]{1,0:T(8,128)(2,1)}, bf16[128,768]{1,0:T(8,128)(2,1)S(1)}, u32[]{:S(2)}, u32[]{:S(2)}) collective-permute-start(bf16[128,768]{1,0:T(8,128)(2,1)} %get-tuple-element.14), channel_id=1, source_target_pairs={{2,0},{3,1},{6,4},{7,5},{10,8},{11,9},{14,12},{15,13},{18,16},{19,... | collective-permute-start | bytes 589832 | tf_op jit(solution)/shard_map/ppermute | solution.py:212
  78.0 1.3 %collective-permute-start.8 = (bf16[128,768]{1,0:T(8,128)(2,1)}, bf16[128,768]{1,0:T(8,128)(2,1)S(1)}, u32[]{:S(2)}, u32[]{:S(2)}) collective-permute-start(bf16[128,768]{1,0:T(8,128)(2,1)} %get-tuple-element.13), channel_id=1, source_target_pairs={{1,0},{2,1},{3,2},{5,4},{6,5},{7,6},{9,8},{10,9},{11,10},{13,12},{... | collective-permute-start | bytes 589832 | tf_op jit(solution)/shard_map/ppermute | solution.py:212
  79.3 2.2 %maximum_bitcast_fusion = bf16[1,128,4096]{2,1,0:T(8,128)(2,1)} fusion(bf16[128,1024]{1,0:T(8,128)(2,1)S(1)} %copy-done.3, bf16[128,3072]{1,0:T(8,128)(2,1)} %get-tuple-element.10), kind=kLoop, calls=%fused_computation.7 | loop fusion | flops 2097152 | bytes 2097152 | tf_op jit(solution)/shard_map/reshape | solution.py:219
  81.5 7.6 %collective-permute-done.11 = bf16[128,256]{1,0:T(8,128)(2,1)S(1)} collective-permute-done((bf16[128,256]{1,0:T(8,128)(2,1)S(1)}, bf16[128,256]{1,0:T(8,128)(2,1)S(1)}, u32[]{:S(2)}, u32[]{:S(2)}) %collective-permute-start.11) | collective-permute-done | bytes 65568 | tf_op jit(solution)/shard_map/ppermute | solution.py:212
  89.2 9.8 %collective-permute-done.9 = bf16[128,768]{1,0:T(8,128)(2,1)S(1)} collective-permute-done((bf16[128,768]{1,0:T(8,128)(2,1)}, bf16[128,768]{1,0:T(8,128)(2,1)S(1)}, u32[]{:S(2)}, u32[]{:S(2)}) %collective-permute-start.9) | collective-permute-done | bytes 196640 | tf_op jit(solution)/shard_map/ppermute | solution.py:212
  (63 shorter events, 7.1 us)
Async XLA Ops:
  5.7 8.0 %copy-start.9 = (s32[16]{0:T(128)S(1)}, s32[16]{0:T(128)}, u32[]{:S(2)}) copy-start(s32[16]{0:T(128)} %param.10) | copy-start | bytes 196
  5.7 8.0 %copy-start.6 = (s32[16]{0:T(128)S(1)}, s32[16]{0:T(128)}, u32[]{:S(2)}) copy-start(s32[16]{0:T(128)} %param.11) | copy-start | bytes 196
  5.7 8.3 %copy-start.5 = (s32[1,128]{1,0:T(1,128)S(1)}, s32[1,128]{1,0:T(1,128)}, u32[]{:S(2)}) copy-start(s32[1,128]{1,0:T(1,128)} %param.8) | copy-start | bytes 1540
  5.8 8.4 %copy-start.1 = (bf16[1,128,4096]{2,1,0:T(8,128)(2,1)S(1)}, bf16[1,128,4096]{2,1,0:T(8,128)(2,1)}, u32[]{:S(2)}) copy-start(bf16[1,128,4096]{2,1,0:T(8,128)(2,1)} %param.9) | copy-start | bytes 3145732
  6.9 44.5 %collective-permute-start.2 = (bf16[64,4096]{1,0:T(8,128)(2,1)}, bf16[64,4096]{1,0:T(8,128)(2,1)S(1)}, u32[]{:S(2)}, u32[]{:S(2)}) collective-permute-start(bf16[64,4096]{1,0:T(8,128)(2,1)} %get-tuple-element.21), channel_id=1, source_target_pairs={{0,12},{4,0},{8,4},{12,8},{1,13},{5,1},{9,5},{13,9},{2,14},{6,2},{... | collective-permute-start | bytes 1572872 | tf_op jit(solution)/shard_map/ppermute | solution.py:58
  9.4 42.1 %collective-permute-start.1 = (bf16[64,4096]{1,0:T(8,128)(2,1)}, bf16[64,4096]{1,0:T(8,128)(2,1)}, u32[]{:S(2)}, u32[]{:S(2)}) collective-permute-start(bf16[64,4096]{1,0:T(8,128)(2,1)} %get-tuple-element.22), channel_id=1, source_target_pairs={{0,8},{4,12},{8,0},{12,4},{1,9},{5,13},{9,1},{13,5},{2,10},{6,14},... | collective-permute-start | bytes 1572872 | tf_op jit(solution)/shard_map/ppermute | solution.py:58
  11.9 20.0 %collective-permute-start.5 = (bf16[64,1024]{1,0:T(8,128)(2,1)}, bf16[64,1024]{1,0:T(8,128)(2,1)S(1)}, u32[]{:S(2)}, u32[]{:S(2)}) collective-permute-start(bf16[64,1024]{1,0:T(8,128)(2,1)} %get-tuple-element.25), channel_id=1, source_target_pairs={{0,12},{4,0},{8,4},{12,8},{1,13},{5,1},{9,5},{13,9},{2,14},{6,2},{... | collective-permute-start | bytes 393224 | tf_op jit(solution)/shard_map/ppermute | solution.py:58
  12.0 22.0 %collective-permute-start.4 = (bf16[64,1024]{1,0:T(8,128)(2,1)S(1)}, bf16[64,1024]{1,0:T(8,128)(2,1)S(1)}, u32[]{:S(2)}, u32[]{:S(2)}) collective-permute-start(bf16[64,1024]{1,0:T(8,128)(2,1)S(1)} %get-tuple-element.26), channel_id=1, source_target_pairs={{0,8},{4,12},{8,0},{12,4},{1,9},{5,13},{9,1},{13,5},{2,10},{6,14},... | collective-permute-start | bytes 393224 | tf_op jit(solution)/shard_map/ppermute | solution.py:58
  13.7 20.2 %collective-permute-start.3 = (bf16[64,1024]{1,0:T(8,128)(2,1)S(1)}, bf16[64,1024]{1,0:T(8,128)(2,1)S(1)}, u32[]{:S(2)}, u32[]{:S(2)}) collective-permute-start(bf16[64,1024]{1,0:T(8,128)(2,1)S(1)} %get-tuple-element.27), channel_id=1, source_target_pairs={{0,4},{4,8},{8,12},{12,0},{1,5},{5,9},{9,13},{13,1},{2,6},{6,10},{... | collective-permute-start | bytes 393224 | tf_op jit(solution)/shard_map/ppermute | solution.py:58
  31.8 19.7 %collective-permute-start = (bf16[64,4096]{1,0:T(8,128)(2,1)S(1)}, bf16[64,4096]{1,0:T(8,128)(2,1)S(1)}, u32[]{:S(2)}, u32[]{:S(2)}) collective-permute-start(bf16[64,4096]{1,0:T(8,128)(2,1)S(1)} %get-tuple-element.23), channel_id=1, source_target_pairs={{0,4},{4,8},{8,12},{12,0},{1,5},{5,9},{9,13},{13,1},{2,6},{6,10},{... | collective-permute-start | bytes 1572872 | tf_op jit(solution)/shard_map/ppermute | solution.py:58
  34.4 12.1 %collective-permute-start.7 = (bf16[128,1152]{1,0:T(8,128)(2,1)S(1)}, bf16[128,1152]{1,0:T(8,128)(2,1)S(1)}, u32[]{:S(2)}, u32[]{:S(2)}) collective-permute-start(bf16[128,1152]{1,0:T(8,128)(2,1)S(1)} %pad_maximum_fusion.3), channel_id=1, source_target_pairs={{0,2},{1,3},{4,6},{5,7},{8,10},{9,11},{12,14},{13,15},{16,18},{17,... | collective-permute-start | bytes 884744 | tf_op jit(solution)/shard_map/ppermute | solution.py:182
  39.1 11.2 %collective-permute-start.6 = (bf16[128,1152]{1,0:T(8,128)(2,1)S(1)}, bf16[128,1152]{1,0:T(8,128)(2,1)S(1)}, u32[]{:S(2)}, u32[]{:S(2)}) collective-permute-start(bf16[128,1152]{1,0:T(8,128)(2,1)S(1)} %pad_maximum_fusion.3), channel_id=1, source_target_pairs={{0,1},{1,2},{2,3},{4,5},{5,6},{6,7},{8,9},{9,10},{10,11},{12,13},{... | collective-permute-start | bytes 884744 | tf_op jit(solution)/shard_map/ppermute | solution.py:182
  50.4 2.4 %copy-start = (bf16[384,1152]{1,0:T(8,128)(2,1)}, bf16[384,1152]{1,0:T(8,128)(2,1)S(1)}, u32[]{:S(2)}) copy-start(bf16[384,1152]{1,0:T(8,128)(2,1)S(1)} %pad_maximum_fusion.1.kv_ref) | copy-start | bytes 2654212
  60.2 13.8 %copy-start.8 = (bf16[128,256]{1,0:T(8,128)(2,1)S(1)}, bf16[128,256]{1,0:T(8,128)(2,1)}, u32[]{:S(2)}) copy-start(bf16[128,256]{1,0:T(8,128)(2,1)} %get-tuple-element.17) | copy-start | bytes 196612
  60.2 15.3 %copy-start.7 = (bf16[128,256]{1,0:T(8,128)(2,1)S(1)}, bf16[128,256]{1,0:T(8,128)(2,1)}, u32[]{:S(2)}) copy-start(bf16[128,256]{1,0:T(8,128)(2,1)} %get-tuple-element.16) | copy-start | bytes 196612
  60.2 19.2 %copy-start.3 = (bf16[128,1024]{1,0:T(8,128)(2,1)S(1)}, bf16[128,1024]{1,0:T(8,128)(2,1)}, u32[]{:S(2)}) copy-start(bf16[128,1024]{1,0:T(8,128)(2,1)} %get-tuple-element.11) | copy-start | bytes 786436
  74.0 15.2 %copy-start.4 = (f32[128,256]{1,0:T(8,128)S(1)}, f32[128,256]{1,0:T(8,128)}, u32[]{:S(2)}) copy-start(f32[128,256]{1,0:T(8,128)} %get-tuple-element.15) | copy-start | bytes 393220
  74.0 25.0 %copy-start.2 = (f32[128,768]{1,0:T(8,128)S(1)}, f32[128,768]{1,0:T(8,128)}, u32[]{:S(2)}) copy-start(f32[128,768]{1,0:T(8,128)} %get-tuple-element.12) | copy-start | bytes 1179652
  74.0 15.2 %collective-permute-start.11 = (bf16[128,256]{1,0:T(8,128)(2,1)S(1)}, bf16[128,256]{1,0:T(8,128)(2,1)S(1)}, u32[]{:S(2)}, u32[]{:S(2)}) collective-permute-start(bf16[128,256]{1,0:T(8,128)(2,1)S(1)} %copy-done.8), channel_id=1, source_target_pairs={{2,0},{3,1},{6,4},{7,5},{10,8},{11,9},{14,12},{15,13},{18,16},{19,... | collective-permute-start | bytes 196616 | tf_op jit(solution)/shard_map/ppermute | solution.py:212
  75.4 13.7 %collective-permute-start.10 = (bf16[128,256]{1,0:T(8,128)(2,1)S(1)}, bf16[128,256]{1,0:T(8,128)(2,1)S(1)}, u32[]{:S(2)}, u32[]{:S(2)}) collective-permute-start(bf16[128,256]{1,0:T(8,128)(2,1)S(1)} %copy-done.7), channel_id=1, source_target_pairs={{1,0},{2,1},{3,2},{5,4},{6,5},{7,6},{9,8},{10,9},{11,10},{13,12},{... | collective-permute-start | bytes 196616 | tf_op jit(solution)/shard_map/ppermute | solution.py:212
  76.7 22.2 %collective-permute-start.9 = (bf16[128,768]{1,0:T(8,128)(2,1)}, bf16[128,768]{1,0:T(8,128)(2,1)S(1)}, u32[]{:S(2)}, u32[]{:S(2)}) collective-permute-start(bf16[128,768]{1,0:T(8,128)(2,1)} %get-tuple-element.14), channel_id=1, source_target_pairs={{2,0},{3,1},{6,4},{7,5},{10,8},{11,9},{14,12},{15,13},{18,16},{19,... | collective-permute-start | bytes 589832 | tf_op jit(solution)/shard_map/ppermute | solution.py:212
  78.0 21.0 %collective-permute-start.8 = (bf16[128,768]{1,0:T(8,128)(2,1)}, bf16[128,768]{1,0:T(8,128)(2,1)S(1)}, u32[]{:S(2)}, u32[]{:S(2)}) collective-permute-start(bf16[128,768]{1,0:T(8,128)(2,1)} %get-tuple-element.13), channel_id=1, source_target_pairs={{1,0},{2,1},{3,2},{5,4},{6,5},{7,6},{9,8},{10,9},{11,10},{13,12},{... | collective-permute-start | bytes 589832 | tf_op jit(solution)/shard_map/ppermute | solution.py:212

commit v14 on v13

--- a/solution.py
+++ b/solution.py
@@ -204,18 +204,21 @@
         & (key_pos[None, :] >= 0)
     )
     bias = jnp.where(allowed.T, 0.0, -1e30).astype(jnp.float32)
-    part_groups = (KEY_VALUE_HEADS - KEY_VALUE_HEADS // 4, KEY_VALUE_HEADS // 4)
-    query_parts, key_parts, value_parts = [], [], []
-    for part, groups in enumerate(part_groups):
-        query_grad, total, *outgoing = attend_pallas(packed_q, weighted, kv_all, bias, sum(part_groups[:part]), groups)
-        for shift in range(1, reach + 1):
-            arrived = lax.ppermute(
-                outgoing[shift - 1], "sp", [(k, k - shift) for k in range(shift, sp_size)]
-            )
-            total = total + arrived.astype(jnp.float32)
-        query_parts.append(query_grad)
-        key_parts.append(total[:, : groups * HEAD_SIZE])
-        value_parts.append(total[:, groups * HEAD_SIZE :])
+    query_grad, own_part, *behind = attend_pallas(
+        packed_q, weighted, kv_all, bias, 0, KEY_VALUE_HEADS
+    )
+    carry = behind[reach - 1].astype(jnp.float32) if reach > 0 else None
+    for back in range(reach, 0, -1):
+        arrived = lax.ppermute(
+            carry.astype(jnp.bfloat16), "sp", [(k, k - 1) for k in range(1, sp_size)]
+        )
+        own = behind[back - 2].astype(jnp.float32) if back > 1 else own_part
+        carry = own + arrived.astype(jnp.float32)
+    total = carry if reach > 0 else own_part
+    groups = KEY_VALUE_HEADS
+    query_parts = [query_grad]
+    key_parts = [total[:, : groups * HEAD_SIZE]]
+    value_parts = [total[:, groups * HEAD_SIZE :]]
     query_gradient = jnp.concatenate(query_parts, axis=1).reshape(
         1, token_rows, QUERY_HEADS * HEAD_SIZE
     )

time: 102 us -> 103 us (level); the launches traced: 99.8 us -> 102 us
  waiting for transfers between devices: 42.9 us -> 49.4 us
  starting transfers between devices: 19.1 us -> 16.3 us
  Pallas kernels: 19.7 us -> 17.6 us
    ppermute x4 -> x2, waiting for transfers between devices: 17.4 us -> 24.1 us  [step(): lax.ppermute(carry.astype(jnp.bfloat16), 'sp', [(k, k - 1) for k in range...]
    ppermute x4 -> x2, starting transfers between devices: 5.3 us -> 2.57 us  [step(): lax.ppermute(carry.astype(jnp.bfloat16), 'sp', [(k, k - 1) for k in range...]
    pallas_call x2 -> x1, Pallas kernels: 19.7 us -> 17.6 us  [attend_pallas(): pl.pallas_call(functools.partial(attend_kernel, first_group=first_group),...]
  transfers between devices with their start and end apart: 12 -> 10, of which waited for: 6 -> 6; matrix products, arithmetic and copies ran while one was open for 7% -> 6% of each run, Pallas kernels for 0% -> 0%
where the time goes in v14:
time: 103 us; the launch traced here: 102 us
  waiting for transfers between devices  49.4 us (48%)
  Pallas kernels  17.6 us (17%)
  starting transfers between devices  16.3 us (16%)
  other arithmetic  10.4 us (10%)
  matrix products  4.95 us (5%)
  local copies, waits for them, and re-layouts  2.62 us (3%)
    ppermute x2, waiting for transfers between devices, step(): lax.ppermute(carry.astype(jnp.bfloat16), 'sp', [(k, k - 1) for k in range...  24.1 us
    ppermute x6, waiting for transfers between devices, send(): lax.ppermute(outgoing[shift], 'dp', [(k, (k + shift) % dp_size) for k in...  17.9 us
    pallas_call x1, Pallas kernels, attend_pallas(): pl.pallas_call(functools.partial(attend_kernel, first_group=first_group),...  17.6 us
    ppermute x2, starting transfers between devices, step(): lax.ppermute(kv_local, 'sp', [(k, k + shift) for k in range(sp_size - shi...  8.44 us
    ppermute x2, waiting for transfers between devices, step(): lax.ppermute(kv_local, 'sp', [(k, k + shift) for k in range(sp_size - shi...  7.35 us
    ppermute x6, starting transfers between devices, send(): lax.ppermute(outgoing[shift], 'dp', [(k, (k + shift) % dp_size) for k in...  5.28 us
    dot_general x2, matrix products, send(): jnp.dot(send_pick, columns, preferred_element_type=jnp.float32)  3.15 us
    ppermute x2, starting transfers between devices, step(): lax.ppermute(carry.astype(jnp.bfloat16), 'sp', [(k, k - 1) for k in range...  2.57 us
  transfers between devices with their start and end apart: 10, of which 6 were waited for; matrix products, arithmetic and copies ran while one was open for 6% of the time, Pallas kernels for 0%

profile of v14, /device:TPU:0, one launch (start us, length us, event | category | flops | bytes accessed | tf_op | source)
XLA Modules:
  0.0 102.1 jit_solution(585184181161419470)
XLA Ops:
  0.6 0.9 fusion.17
  3.8 1.9 %convolution_convert_fusion = bf16[256,4096]{1,0:T(8,128)(2,1)S(1)} fusion(bf16[128,5120]{1,0:T(8,128)(2,1)} %param.6, s32[128]{0:T(128)S(1)} %get-tuple-element.21), kind=kOutput, calls=%fused_computation | convolution fusion | flops 269516800 | bytes 3146240 | tf_op jit(solution)/shard_map/dot_general | solution.py:51
  5.8 1.0 slice_bitcast_fusion
  6.8 2.4 %collective-permute-start.2 = (bf16[64,4096]{1,0:T(8,128)(2,1)}, bf16[64,4096]{1,0:T(8,128)(2,1)S(1)}, u32[]{:S(2)}, u32[]{:S(2)}) collective-permute-start(bf16[64,4096]{1,0:T(8,128)(2,1)} %get-tuple-element.13), channel_id=1, source_target_pairs={{0,12},{4,0},{8,4},{12,8},{1,13},{5,1},{9,5},{13,9},{2,14},{6,2},{... | collective-permute-start | bytes 1572872 | tf_op jit(solution)/shard_map/ppermute | solution.py:58
  9.7 1.2 %convolution_convert_fusion.2 = bf16[256,1024]{1,0:T(8,128)(2,1)S(1)} fusion(bf16[128,5120]{1,0:T(8,128)(2,1)} %param.6, s32[128]{0:T(128)S(1)} %get-tuple-element.21), kind=kOutput, calls=%fused_computation.5 | convolution fusion | flops 67403776 | bytes 786944 | tf_op jit(solution)/shard_map/dot_general | solution.py:51
  11.8 1.7 %collective-permute-start.4 = (bf16[64,1024]{1,0:T(8,128)(2,1)}, bf16[64,1024]{1,0:T(8,128)(2,1)}, u32[]{:S(2)}, u32[]{:S(2)}) collective-permute-start(bf16[64,1024]{1,0:T(8,128)(2,1)} %get-tuple-element.18), channel_id=1, source_target_pairs={{0,8},{4,12},{8,0},{12,4},{1,9},{5,13},{9,1},{13,5},{2,10},{6,14},... | collective-permute-start | bytes 393224 | tf_op jit(solution)/shard_map/ppermute | solution.py:58
  14.0 1.3 %fusion.g_ref = bf16[128,4096]{1,0:T(8,128)(2,1)} fusion(bf16[1,128,4096]{2,1,0:T(8,128)(2,1)S(1)} %copy-done.1, f32[128]{0:T(128)S(1)} %select_reduce_fusion.2), kind=kLoop, calls=%fused_computation.4 | loop fusion | flops 1572864 | bytes 2097664 | tf_op jit(solution)/shard_map/convert_element_type | solution.py:196
  15.3 16.2 %collective-permute-done.5 = bf16[64,1024]{1,0:T(8,128)(2,1)S(1)} collective-permute-done((bf16[64,1024]{1,0:T(8,128)(2,1)}, bf16[64,1024]{1,0:T(8,128)(2,1)S(1)}, u32[]{:S(2)}, u32[]{:S(2)}) %collective-permute-start.5) | collective-permute-done | bytes 131104 | tf_op jit(solution)/shard_map/ppermute | solution.py:58
  32.0 1.7 %collective-permute-done.4 = bf16[64,1024]{1,0:T(8,128)(2,1)} collective-permute-done((bf16[64,1024]{1,0:T(8,128)(2,1)}, bf16[64,1024]{1,0:T(8,128)(2,1)}, u32[]{:S(2)}, u32[]{:S(2)}) %collective-permute-start.4) | collective-permute-done | bytes 131104 | tf_op jit(solution)/shard_map/ppermute | solution.py:58
  33.7 1.0 %pad_maximum_fusion.2 = bf16[4,64,1024]{2,1,0:T(8,128)(2,1)S(1)} fusion(bf16[1,64,1024]{2,1,0:T(8,128)(2,1)S(1)} %bitcast.34, bf16[1,64,1024]{2,1,0:T(8,128)(2,1)} %bitcast.13, bf16[1,64,1024]{2,1,0:T(8,128)(2,1)} %bitcast.12, bf16[1,64,1024]{2,1,0:T(8,128)(2,1)S(1)} %get-tuple-element.16), kind=kLoop, calls=%fused_computation.10 | loop fusion | flops 786432 | bytes 1048576 | tf_op jit(solution)/shard_map/stack | solution.py:55
  35.1 4.8 %collective-permute-start.7 = (bf16[128,1152]{1,0:T(8,128)(2,1)S(1)}, bf16[128,1152]{1,0:T(8,128)(2,1)S(1)}, u32[]{:S(2)}, u32[]{:S(2)}) collective-permute-start(bf16[128,1152]{1,0:T(8,128)(2,1)S(1)} %pad_maximum_fusion.3), channel_id=1, source_target_pairs={{0,2},{1,3},{4,6},{5,7},{8,10},{9,11},{12,14},{13,15},{16,18},{17,... | collective-permute-start | bytes 884744 | tf_op jit(solution)/shard_map/ppermute | solution.py:182
  39.9 3.7 %collective-permute-start.6 = (bf16[128,1152]{1,0:T(8,128)(2,1)S(1)}, bf16[128,1152]{1,0:T(8,128)(2,1)S(1)}, u32[]{:S(2)}, u32[]{:S(2)}) collective-permute-start(bf16[128,1152]{1,0:T(8,128)(2,1)S(1)} %pad_maximum_fusion.3), channel_id=1, source_target_pairs={{0,1},{1,2},{2,3},{4,5},{5,6},{6,7},{8,9},{9,10},{10,11},{12,13},{... | collective-permute-start | bytes 884744 | tf_op jit(solution)/shard_map/ppermute | solution.py:182
  43.6 3.6 %collective-permute-done.7 = bf16[128,1152]{1,0:T(8,128)(2,1)S(1)} collective-permute-done((bf16[128,1152]{1,0:T(8,128)(2,1)S(1)}, bf16[128,1152]{1,0:T(8,128)(2,1)S(1)}, u32[]{:S(2)}, u32[]{:S(2)}) %collective-permute-start.7) | collective-permute-done | bytes 294944 | tf_op jit(solution)/shard_map/ppermute | solution.py:182
  47.2 3.7 %collective-permute-done.6 = bf16[128,1152]{1,0:T(8,128)(2,1)S(1)} collective-permute-done((bf16[128,1152]{1,0:T(8,128)(2,1)S(1)}, bf16[128,1152]{1,0:T(8,128)(2,1)S(1)}, u32[]{:S(2)}, u32[]{:S(2)}) %collective-permute-start.6) | collective-permute-done | bytes 294944 | tf_op jit(solution)/shard_map/ppermute | solution.py:182
  51.2 0.9 and_select_fusion.m_ref
  52.1 1.3 %pad_maximum_fusion = bf16[4,64,4096]{2,1,0:T(8,128)(2,1)S(1)} fusion(bf16[1,64,4096]{2,1,0:T(8,128)(2,1)S(1)} %bitcast.32, bf16[1,64,4096]{2,1,0:T(8,128)(2,1)} %bitcast.6, bf16[1,64,4096]{2,1,0:T(8,128)(2,1)S(1)} %bitcast.33, bf16[1,64,4096]{2,1,0:T(8,128)(2,1)S(1)} %get-tuple-element.12), kind=kLoop, calls=%fused_computation.2 | loop fusion | flops 3145728 | bytes 4194304 | tf_op jit(solution)/shard_map/stack | solution.py:55
  53.4 1.5 %convolution_convert_fusion.1.q_ref = bf16[128,4096]{1,0:T(8,128)(2,1)} fusion(bf16[256,4096]{1,0:T(8,128)(2,1)S(1)} %bitcast.30, s32[128]{0:T(128)S(1)} %get-tuple-element.20), kind=kOutput, calls=%fused_computation.1 | convolution fusion | flops 268992512 | bytes 3146240 | tf_op jit(solution)/shard_map/dot_general | solution.py:70
  54.9 17.6 %shard_map.77 = (bf16[128,4096]{1,0:T(8,128)(2,1)}, f32[128,1024]{1,0:T(8,128)}, bf16[128,1024]{1,0:T(8,128)(2,1)}, bf16[128,1024]{1,0:T(8,128)(2,1)}) custom-call(bf16[128,4096]{1,0:T(8,128)(2,1)} %convolution_convert_fusion.1.q_ref, bf16[128,4096]{1,0:T(8,128)(2,1)} %fusion.g_ref, bf16[384,1152]{1,0:T(8,128)(2,1)} %copy-done, f32[384,128]{1,0:T(8,128)} %and_select_fusion.m_ref), custom_call_target="tpu_custom_call" | custom-call | flops 2013265920 | bytes 4227072 | tf_op jit(solution)/shard_map/pallas_call | solution.py:142
  72.6 1.3 %collective-permute-start.8 = (bf16[128,1024]{1,0:T(8,128)(2,1)}, bf16[128,1024]{1,0:T(8,128)(2,1)S(1)}, u32[]{:S(2)}, u32[]{:S(2)}) collective-permute-start(bf16[128,1024]{1,0:T(8,128)(2,1)} %get-tuple-element.9), channel_id=1, source_target_pairs={{1,0},{2,1},{3,2},{5,4},{6,5},{7,6},{9,8},{10,9},{11,10},{13,12},{... | collective-permute-start | bytes 786440 | tf_op jit(solution)/shard_map/ppermute | solution.py:212
  73.9 15.1 %collective-permute-done.8 = bf16[128,1024]{1,0:T(8,128)(2,1)S(1)} collective-permute-done((bf16[128,1024]{1,0:T(8,128)(2,1)}, bf16[128,1024]{1,0:T(8,128)(2,1)S(1)}, u32[]{:S(2)}, u32[]{:S(2)}) %collective-permute-start.8) | collective-permute-done | bytes 262176 | tf_op jit(solution)/shard_map/ppermute | solution.py:212
  89.0 1.0 add_convert_fusion.1
  90.0 1.3 %collective-permute-start.9 = (bf16[128,1024]{1,0:T(8,128)(2,1)S(1)}, bf16[128,1024]{1,0:T(8,128)(2,1)S(1)}, u32[]{:S(2)}, u32[]{:S(2)}) collective-permute-start(bf16[128,1024]{1,0:T(8,128)(2,1)S(1)} %add_convert_fusion.1), channel_id=1, source_target_pairs={{1,0},{2,1},{3,2},{5,4},{6,5},{7,6},{9,8},{10,9},{11,10},{13,12},{... | collective-permute-start | bytes 786440 | tf_op jit(solution)/shard_map/ppermute | solution.py:212
  91.3 9.0 %collective-permute-done.9 = bf16[128,1024]{1,0:T(8,128)(2,1)S(1)} collective-permute-done((bf16[128,1024]{1,0:T(8,128)(2,1)S(1)}, bf16[128,1024]{1,0:T(8,128)(2,1)S(1)}, u32[]{:S(2)}, u32[]{:S(2)}) %collective-permute-start.9) | collective-permute-done | bytes 262176 | tf_op jit(solution)/shard_map/ppermute | solution.py:212
  100.3 1.8 %fusion.2 = bf16[1,128,1024]{2,1,0:T(8,128)(2,1)} fusion(f32[128,1024]{1,0:T(8,128)} %get-tuple-element.7, bf16[128,1024]{1,0:T(8,128)(2,1)S(1)} %collective-permute-done.9), kind=kLoop, calls=%fused_computation.14 | loop fusion | flops 393216 | bytes 1048576 | tf_op jit(solution)/shard_map/reshape | solution.py:226
  (44 shorter events, 5.2 us)
Async XLA Ops:
  5.7 7.9 %copy-start.4 = (s32[16]{0:T(128)S(1)}, s32[16]{0:T(128)}, u32[]{:S(2)}) copy-start(s32[16]{0:T(128)} %param.10) | copy-start | bytes 196
  5.7 7.9 %copy-start.3 = (s32[16]{0:T(128)S(1)}, s32[16]{0:T(128)}, u32[]{:S(2)}) copy-start(s32[16]{0:T(128)} %param.11) | copy-start | bytes 196
  5.7 8.2 %copy-start.2 = (s32[1,128]{1,0:T(1,128)S(1)}, s32[1,128]{1,0:T(1,128)}, u32[]{:S(2)}) copy-start(s32[1,128]{1,0:T(1,128)} %param.8) | copy-start | bytes 1540
  5.8 8.3 %copy-start.1 = (bf16[1,128,4096]{2,1,0:T(8,128)(2,1)S(1)}, bf16[1,128,4096]{2,1,0:T(8,128)(2,1)}, u32[]{:S(2)}) copy-start(bf16[1,128,4096]{2,1,0:T(8,128)(2,1)} %param.9) | copy-start | bytes 3145732
  6.8 45.3 %collective-permute-start.2 = (bf16[64,4096]{1,0:T(8,128)(2,1)}, bf16[64,4096]{1,0:T(8,128)(2,1)S(1)}, u32[]{:S(2)}, u32[]{:S(2)}) collective-permute-start(bf16[64,4096]{1,0:T(8,128)(2,1)} %get-tuple-element.13), channel_id=1, source_target_pairs={{0,12},{4,0},{8,4},{12,8},{1,13},{5,1},{9,5},{13,9},{2,14},{6,2},{... | collective-permute-start | bytes 1572872 | tf_op jit(solution)/shard_map/ppermute | solution.py:58
  9.2 42.9 %collective-permute-start.1 = (bf16[64,4096]{1,0:T(8,128)(2,1)S(1)}, bf16[64,4096]{1,0:T(8,128)(2,1)}, u32[]{:S(2)}, u32[]{:S(2)}) collective-permute-start(bf16[64,4096]{1,0:T(8,128)(2,1)S(1)} %get-tuple-element.14), channel_id=1, source_target_pairs={{0,8},{4,12},{8,0},{12,4},{1,9},{5,13},{9,1},{13,5},{2,10},{6,14},... | collective-permute-start | bytes 1572872 | tf_op jit(solution)/shard_map/ppermute | solution.py:58
  11.7 19.8 %collective-permute-start.5 = (bf16[64,1024]{1,0:T(8,128)(2,1)}, bf16[64,1024]{1,0:T(8,128)(2,1)S(1)}, u32[]{:S(2)}, u32[]{:S(2)}) collective-permute-start(bf16[64,1024]{1,0:T(8,128)(2,1)} %get-tuple-element.17), channel_id=1, source_target_pairs={{0,12},{4,0},{8,4},{12,8},{1,13},{5,1},{9,5},{13,9},{2,14},{6,2},{... | collective-permute-start | bytes 393224 | tf_op jit(solution)/shard_map/ppermute | solution.py:58
  11.8 21.8 %collective-permute-start.4 = (bf16[64,1024]{1,0:T(8,128)(2,1)}, bf16[64,1024]{1,0:T(8,128)(2,1)}, u32[]{:S(2)}, u32[]{:S(2)}) collective-permute-start(bf16[64,1024]{1,0:T(8,128)(2,1)} %get-tuple-element.18), channel_id=1, source_target_pairs={{0,8},{4,12},{8,0},{12,4},{1,9},{5,13},{9,1},{13,5},{2,10},{6,14},... | collective-permute-start | bytes 393224 | tf_op jit(solution)/shard_map/ppermute | solution.py:58
  13.6 20.1 %collective-permute-start.3 = (bf16[64,1024]{1,0:T(8,128)(2,1)S(1)}, bf16[64,1024]{1,0:T(8,128)(2,1)}, u32[]{:S(2)}, u32[]{:S(2)}) collective-permute-start(bf16[64,1024]{1,0:T(8,128)(2,1)S(1)} %get-tuple-element.19), channel_id=1, source_target_pairs={{0,4},{4,8},{8,12},{12,0},{1,5},{5,9},{9,13},{13,1},{2,6},{6,10},{... | collective-permute-start | bytes 393224 | tf_op jit(solution)/shard_map/ppermute | solution.py:58
  31.5 20.6 %collective-permute-start = (bf16[64,4096]{1,0:T(8,128)(2,1)S(1)}, bf16[64,4096]{1,0:T(8,128)(2,1)S(1)}, u32[]{:S(2)}, u32[]{:S(2)}) collective-permute-start(bf16[64,4096]{1,0:T(8,128)(2,1)S(1)} %get-tuple-element.15), channel_id=1, source_target_pairs={{0,4},{4,8},{8,12},{12,0},{1,5},{5,9},{9,13},{13,1},{2,6},{6,10},{... | collective-permute-start | bytes 1572872 | tf_op jit(solution)/shard_map/ppermute | solution.py:58
  35.1 12.1 %collective-permute-start.7 = (bf16[128,1152]{1,0:T(8,128)(2,1)S(1)}, bf16[128,1152]{1,0:T(8,128)(2,1)S(1)}, u32[]{:S(2)}, u32[]{:S(2)}) collective-permute-start(bf16[128,1152]{1,0:T(8,128)(2,1)S(1)} %pad_maximum_fusion.3), channel_id=1, source_target_pairs={{0,2},{1,3},{4,6},{5,7},{8,10},{9,11},{12,14},{13,15},{16,18},{17,... | collective-permute-start | bytes 884744 | tf_op jit(solution)/shard_map/ppermute | solution.py:182
  39.9 11.1 %collective-permute-start.6 = (bf16[128,1152]{1,0:T(8,128)(2,1)S(1)}, bf16[128,1152]{1,0:T(8,128)(2,1)S(1)}, u32[]{:S(2)}, u32[]{:S(2)}) collective-permute-start(bf16[128,1152]{1,0:T(8,128)(2,1)S(1)} %pad_maximum_fusion.3), channel_id=1, source_target_pairs={{0,1},{1,2},{2,3},{4,5},{5,6},{6,7},{8,9},{9,10},{10,11},{12,13},{... | collective-permute-start | bytes 884744 | tf_op jit(solution)/shard_map/ppermute | solution.py:182
  51.0 2.4 %copy-start = (bf16[384,1152]{1,0:T(8,128)(2,1)}, bf16[384,1152]{1,0:T(8,128)(2,1)S(1)}, u32[]{:S(2)}) copy-start(bf16[384,1152]{1,0:T(8,128)(2,1)S(1)} %pad_maximum_fusion.1.kv_ref) | copy-start | bytes 2654212
  72.6 16.4 %collective-permute-start.8 = (bf16[128,1024]{1,0:T(8,128)(2,1)}, bf16[128,1024]{1,0:T(8,128)(2,1)S(1)}, u32[]{:S(2)}, u32[]{:S(2)}) collective-permute-start(bf16[128,1024]{1,0:T(8,128)(2,1)} %get-tuple-element.9), channel_id=1, source_target_pairs={{1,0},{2,1},{3,2},{5,4},{6,5},{7,6},{9,8},{10,9},{11,10},{13,12},{... | collective-permute-start | bytes 786440 | tf_op jit(solution)/shard_map/ppermute | solution.py:212
  90.0 10.3 %collective-permute-start.9 = (bf16[128,1024]{1,0:T(8,128)(2,1)S(1)}, bf16[128,1024]{1,0:T(8,128)(2,1)S(1)}, u32[]{:S(2)}, u32[]{:S(2)}) collective-permute-start(bf16[128,1024]{1,0:T(8,128)(2,1)S(1)} %add_convert_fusion.1), channel_id=1, source_target_pairs={{1,0},{2,1},{3,2},{5,4},{6,5},{7,6},{9,8},{10,9},{11,10},{13,12},{... | collective-permute-start | bytes 786440 | tf_op jit(solution)/shard_map/ppermute | solution.py:212

commit v15 on v12

--- a/solution.py
+++ b/solution.py
@@ -5,6 +5,7 @@
 import jax.numpy as jnp
 from jax import lax
 from jax.experimental import pallas as pl
+from jax.experimental.pallas import tpu as pltpu
 from jax.sharding import PartitionSpec as P
 
 
@@ -43,7 +44,7 @@
         jnp.where(source[:, None] == targets[None, :], start_marks[None, :], 0), axis=1
     )
 
-    def send(columns, by_permute):
+    def send(columns, by_permute, select=True):
         target_slot = (own_plan - dp_index) % dp_size if by_permute else own_plan
         send_pick = (slots[:, None] == (target_slot * capacity + rank_rows)[None, :]).astype(
             columns.dtype
@@ -52,7 +53,7 @@
             columns.dtype
         ).reshape(dp_size, capacity, -1)
         if by_permute:
-            chunks = [outgoing[0]] + [
+            arrived = [outgoing[0]] + [
                 lax.ppermute(
                     outgoing[shift], "dp", [(k, (k + shift) % dp_size) for k in range(dp_size)]
                 )
@@ -61,26 +62,36 @@
             source_slot = (dp_index - source) % dp_size
         else:
             arrived = lax.all_to_all(outgoing, "dp", split_axis=0, concat_axis=0, tiled=True)
-            chunks = [arrived[k] for k in range(dp_size)]
             source_slot = source
         pick_ids = source_slot * capacity + positions - chosen_start
         recv_pick = (pick_ids[:, None] == slots[None, :]).astype(columns.dtype)
-        packed = sum(
-            jnp.dot(
-                recv_pick[:, k * capacity : (k + 1) * capacity],
-                chunk,
-                preferred_element_type=jnp.float32,
-            )
-            for k, chunk in enumerate(chunks)
+        if not select:
+            return list(arrived), recv_pick
+        return jnp.dot(
+            recv_pick, jnp.concatenate(list(arrived), axis=0), preferred_element_type=jnp.float32
+        ).astype(columns.dtype)
+
+    packed_kv = send(rollout_rows[:, QUERY_HEADS * HEAD_SIZE :], True)
+    packed_q = send(rollout_rows[:, : QUERY_HEADS * HEAD_SIZE], True, select=False)
+    return packed_q, packed_kv
+
+
+def attend_kernel(*refs, first_group, chunks, reach):
+    chunk_refs = refs[:chunks]
+    pick_ref, g_ref, kv_ref, m_ref, dq_ref, local_ref = refs[chunks : chunks + 6]
+    send_refs = refs[chunks + 6 : chunks + 6 + reach]
+    q_ref = refs[chunks + 6 + reach]
+    capacity = chunk_refs[0].shape[0]
+    picked = jnp.dot(
+        pick_ref[:, :capacity], chunk_refs[0][...], preferred_element_type=jnp.float32
+    )
+    for k in range(1, chunks):
+        picked = picked + jnp.dot(
+            pick_ref[:, k * capacity : (k + 1) * capacity],
+            chunk_refs[k][...],
+            preferred_element_type=jnp.float32,
         )
-        return packed.astype(columns.dtype)
-
-    packed_kv = send(rollout_rows[:, QUERY_HEADS * HEAD_SIZE :], True)
-    packed_q = send(rollout_rows[:, : QUERY_HEADS * HEAD_SIZE], True)
-    return packed_q, packed_kv
-
-
-def attend_kernel(q_ref, g_ref, kv_ref, m_ref, dq_ref, local_ref, *send_refs, first_group):
+    q_ref[...] = picked.astype(q_ref.dtype)
     inv_root = 1.0 / math.sqrt(HEAD_SIZE)
     token_rows = q_ref.shape[0]
     groups = local_ref.shape[1] // (2 * HEAD_SIZE)
@@ -133,8 +144,9 @@
             send_ref[:, value_cols] = value_sum[rows].astype(send_ref.dtype)
 
 
-def attend_pallas(packed, weighted, kv_all, bias, part, groups):
-    token_rows = packed.shape[0]
+def attend_pallas(q_chunks, q_pick, weighted, kv_all, bias, part, groups):
+    token_rows = weighted.shape[0]
+    capacity = q_chunks[0].shape[0]
     key_rows = kv_all.shape[0]
     reach = key_rows // token_rows - 1
     part_width = groups * (QUERY_HEADS // KEY_VALUE_HEADS) * HEAD_SIZE
@@ -144,10 +156,11 @@
     bytes_accessed = 6 * token_rows * part_width + 2 * key_rows * kv_all.shape[1] + 4 * token_rows * key_rows
     whole = lambda i: (0, 0)
     return pl.pallas_call(
-        functools.partial(attend_kernel, first_group=part * groups),
+        functools.partial(attend_kernel, first_group=part * groups, chunks=len(q_chunks), reach=reach),
         grid=(1,),
-        in_specs=[
-            pl.BlockSpec((token_rows, part_width), lambda i: (0, part)),
+        in_specs=[pl.BlockSpec((capacity, part_width), lambda i: (0, part)) for _ in q_chunks]
+        + [
+            pl.BlockSpec(q_pick.shape, whole),
             pl.BlockSpec((token_rows, part_width), lambda i: (0, part)),
             pl.BlockSpec(kv_all.shape, whole),
             pl.BlockSpec(bias.shape, whole),
@@ -164,7 +177,8 @@
         cost_estimate=pl.CostEstimate(
             flops=flops, transcendentals=token_rows * key_rows * heads, bytes_accessed=bytes_accessed
         ),
-    )(packed, weighted, kv_all, bias)
+        scratch_shapes=[pltpu.VMEM((token_rows, part_width), jnp.bfloat16)],
+    )(*q_chunks, q_pick, weighted, kv_all, bias)
 
 
 def step(rollout_rows, routing, segment_labels, upstream, passes, group_ids):
@@ -212,7 +226,7 @@
     query_parts, key_parts, value_parts = [], [], []
     for part in range(2):
         query_grad, total, *outgoing = attend_pallas(
-            packed_q, weighted, kv_all, bias, part, groups
+            *packed_q, weighted, kv_all, bias, part, groups
         )
         for shift in range(1, reach + 1):
             arrived = lax.ppermute(

time: 90.1 us -> 81.6 us (0.906)
  matrix products: 8.68 us -> 3.23 us
  waiting for transfers between devices: 27.2 us -> 23.1 us
  Pallas kernels: 19.7 us -> 21.2 us
  local copies, waits for them, and re-layouts: 2.87 us -> 3.79 us
    ppermute x4, waiting for transfers between devices: 20 us -> 14.1 us  [step(): lax.ppermute(outgoing[shift - 1], 'sp', [(k, k - shift) for k in range(sh...]
    dot_general x8 -> x1, matrix products: 6.74 us -> 1.3 us  [send(): jnp.dot(recv_pick, jnp.concatenate(list(arrived), axis=0), preferred_elem...]
    pallas_call x2, Pallas kernels: 19.7 us -> 21.2 us  [attend_pallas(): pl.pallas_call(functools.partial(attend_kernel, first_group=part * groups...]
    ppermute x6, waiting for transfers between devices: 0.02 us -> 1.53 us  [send(): lax.ppermute(outgoing[shift], 'dp', [(k, (k + shift) % dp_size) for k in...]
    convert_element_type x1, other arithmetic: 2.48 us -> 1.24 us  [step(): (upstream[0].astype(jnp.float32) * tok_adv[:, None]).astype(jnp.bfloat16)]
    slice x2 -> x1, local copies, waits for them, and re-layouts: 1.95 us -> 1.18 us  [send(): outgoing[shift]]
  transfers between devices with their start and end apart: 12 -> 12, of which waited for: 5 -> 5; matrix products, arithmetic and copies ran while one was open for 17% -> 13% of each run, Pallas kernels for 0% -> 13%
where the time goes in v15:
time: 81.6 us; the launch traced here: 81.2 us
  waiting for transfers between devices  23.1 us (28%)
  Pallas kernels  21.2 us (26%)
  starting transfers between devices  20.1 us (25%)
  other arithmetic  8.84 us (11%)
  local copies, waits for them, and re-layouts  3.79 us (5%)
  matrix products  3.23 us (4%)
  between operations  0.94 us (1%)
    pallas_call x2, Pallas kernels, attend_pallas(): pl.pallas_call(functools.partial(attend_kernel, first_group=part * groups...  21.2 us
    ppermute x4, waiting for transfers between devices, step(): lax.ppermute(outgoing[shift - 1], 'sp', [(k, k - shift) for k in range(sh...  14.1 us
    ppermute x2, starting transfers between devices, step(): lax.ppermute(kv_local, 'sp', [(k, k + shift) for k in range(sp_size - shi...  8.25 us
    ppermute x2, waiting for transfers between devices, step(): lax.ppermute(kv_local, 'sp', [(k, k + shift) for k in range(sp_size - shi...  7.43 us
    ppermute x6, starting transfers between devices, send(): lax.ppermute(outgoing[shift], 'dp', [(k, (k + shift) % dp_size) for k in...  6.24 us
    ppermute x4, starting transfers between devices, step(): lax.ppermute(outgoing[shift - 1], 'sp', [(k, k - shift) for k in range(sh...  5.6 us
    reshape x1, other arithmetic, step(): jnp.concatenate(query_parts, axis=1)  2.09 us
    dot_general x2, matrix products, send(): jnp.dot(send_pick, columns, preferred_element_type=jnp.float32)  1.93 us
  transfers between devices with their start and end apart: 12, of which 5 were waited for; matrix products, arithmetic and copies ran while one was open for 13% of the time, Pallas kernels for 13%

profile of v15, /device:TPU:0, one launch (start us, length us, event | category | flops | bytes accessed | tf_op | source)
XLA Modules:
  0.0 81.2 jit_solution(16043765316762904112)
XLA Ops:
  2.6 1.2 %convolution_convert_fusion.1 = bf16[256,1024]{1,0:T(8,128)(2,1)S(1)} fusion(bf16[128,5120]{1,0:T(8,128)(2,1)} %param.6, s32[128]{0:T(128)S(1)} %fusion.27), kind=kOutput, calls=%fused_computation.3 | convolution fusion | flops 67403776 | bytes 786944 | tf_op jit(solution)/shard_map/dot_general | solution.py:52
  3.8 0.8 fusion.36
  5.1 2.5 %collective-permute-start.4 = (bf16[64,1024]{1,0:T(8,128)(2,1)}, bf16[64,1024]{1,0:T(8,128)(2,1)}, u32[]{:S(2)}, u32[]{:S(2)}) collective-permute-start(bf16[64,1024]{1,0:T(8,128)(2,1)} %get-tuple-element.26), channel_id=1, source_target_pairs={{0,8},{4,12},{8,0},{12,4},{1,9},{5,13},{9,1},{13,5},{2,10},{6,14},... | collective-permute-start | bytes 393224 | tf_op jit(solution)/shard_map/ppermute | solution.py:57
  7.6 1.5 %collective-permute-start.5 = (bf16[64,1024]{1,0:T(8,128)(2,1)}, bf16[64,1024]{1,0:T(8,128)(2,1)}, u32[]{:S(2)}, u32[]{:S(2)}) collective-permute-start(bf16[64,1024]{1,0:T(8,128)(2,1)} %get-tuple-element.25), channel_id=1, source_target_pairs={{0,12},{4,0},{8,4},{12,8},{1,13},{5,1},{9,5},{13,9},{2,14},{6,2},{... | collective-permute-start | bytes 393224 | tf_op jit(solution)/shard_map/ppermute | solution.py:57
  9.8 1.2 %fusion.35 = (bf16[64,4096]{1,0:T(8,128)(2,1)S(1)}, bf16[64,4096]{1,0:T(8,128)(2,1)}, bf16[64,4096]{1,0:T(8,128)(2,1)}, bf16[64,4096]{1,0:T(8,128)(2,1)}) fusion(bf16[256,4096]{1,0:T(8,128)(2,1)S(1)} %convolution_convert_fusion), kind=kLoop, calls=%fused_computation.82 | loop fusion | bytes 4194304 | tf_op jit(solution)/shard_map/slice | solution.py:58
  11.4 0.9 %fusion.23 = s32[4]{0:T(128)S(1)} fusion(s32[4,4,128]{2,1,0:T(4,128)} %bitcast.25, s32[]{:T(128)S(6)} %select_n.77, s32[]{:T(128)S(6)} %axis_index.23), kind=kLoop, calls=%fused_computation.54 | loop fusion | flops 1532 | bytes 2072 | tf_op jit(solution)/shard_map/reduce_sum | solution.py:38
  13.2 1.2 %fusion.refs_5_ = bf16[128,4096]{1,0:T(8,128)(2,1)} fusion(bf16[1,128,4096]{2,1,0:T(8,128)(2,1)S(1)} %copy-done.5, f32[128]{0:T(128)S(1)} %select_reduce_fusion.2), kind=kLoop, calls=%fused_computation.2 | loop fusion | flops 1572864 | bytes 2097664 | tf_op jit(solution)/shard_map/convert_element_type | solution.py:214
  14.5 1.4 %collective-permute-start.2 = (bf16[64,4096]{1,0:T(8,128)(2,1)S(1)}, bf16[64,4096]{1,0:T(8,128)(2,1)S(1)}, u32[]{:S(2)}, u32[]{:S(2)}) collective-permute-start(bf16[64,4096]{1,0:T(8,128)(2,1)S(1)} %get-tuple-element.20), channel_id=1, source_target_pairs={{0,12},{4,0},{8,4},{12,8},{1,13},{5,1},{9,5},{13,9},{2,14},{6,2},{... | collective-permute-start | bytes 1572872 | tf_op jit(solution)/shard_map/ppermute | solution.py:57
  15.9 1.3 %convolution_convert_fusion.2 = bf16[128,1024]{1,0:T(8,128)(2,1)S(1)} fusion(bf16[64,1024]{1,0:T(8,128)(2,1)} %collective-permute-done.5, bf16[64,1024]{1,0:T(8,128)(2,1)} %collective-permute-done.4, bf16[64,1024]{1,0:T(8,128)(2,1)} %collective-permute-done.3, bf16[64,1024]{1,0:T(8,128)(2,1)S(1)} %copy-done.9, s32[128]{0:T(128)S(1)} %fusion.30), kind=kOutput, calls=%fused_computation.4 | convolution fusion | flops 69369856 | bytes 786944 | tf_op jit(solution)/shard_map/dot_general | solution.py:70
  17.3 3.8 %collective-permute-start.6 = (bf16[128,1152]{1,0:T(8,128)(2,1)S(1)}, bf16[128,1152]{1,0:T(8,128)(2,1)S(1)}, u32[]{:S(2)}, u32[]{:S(2)}) collective-permute-start(bf16[128,1152]{1,0:T(8,128)(2,1)S(1)} %pad_maximum_fusion.1), channel_id=1, source_target_pairs={{0,1},{1,2},{2,3},{4,5},{5,6},{6,7},{8,9},{9,10},{10,11},{12,13},{... | collective-permute-start | bytes 884744 | tf_op jit(solution)/shard_map/ppermute | solution.py:200
  21.1 4.5 %collective-permute-start.7 = (bf16[128,1152]{1,0:T(8,128)(2,1)S(1)}, bf16[128,1152]{1,0:T(8,128)(2,1)S(1)}, u32[]{:S(2)}, u32[]{:S(2)}) collective-permute-start(bf16[128,1152]{1,0:T(8,128)(2,1)S(1)} %pad_maximum_fusion.1), channel_id=1, source_target_pairs={{0,2},{1,3},{4,6},{5,7},{8,10},{9,11},{12,14},{13,15},{16,18},{17,... | collective-permute-start | bytes 884744 | tf_op jit(solution)/shard_map/ppermute | solution.py:200
  26.3 2.1 %collective-permute-done.6 = bf16[128,1152]{1,0:T(8,128)(2,1)S(1)} collective-permute-done((bf16[128,1152]{1,0:T(8,128)(2,1)S(1)}, bf16[128,1152]{1,0:T(8,128)(2,1)S(1)}, u32[]{:S(2)}, u32[]{:S(2)}) %collective-permute-start.6) | collective-permute-done | bytes 294944 | tf_op jit(solution)/shard_map/ppermute | solution.py:200
  28.4 5.3 %collective-permute-done.7 = bf16[128,1152]{1,0:T(8,128)(2,1)S(1)} collective-permute-done((bf16[128,1152]{1,0:T(8,128)(2,1)S(1)}, bf16[128,1152]{1,0:T(8,128)(2,1)S(1)}, u32[]{:S(2)}, u32[]{:S(2)}) %collective-permute-start.7) | collective-permute-done | bytes 294944 | tf_op jit(solution)/shard_map/ppermute | solution.py:200
  34.0 0.9 %and_select_fusion.refs_7_ = f32[384,128]{1,0:T(8,128)} fusion(s32[128]{0:T(128)S(1)} %iota_add_fusion, s32[128]{0:T(128)S(1)} %bitcast.27, s32[384]{0:T(512)S(1)} %fusion.21, s32[384]{0:T(512)S(1)} %convert_reduce_fusion, pred[384]{0:T(512)(128)(4,1)S(1)} %broadcast_compare_fusion), kind=kLoop, calls=%fused_computation.21 | loop fusion | flops 245760 | bytes 201088 | tf_op jit(solution)/shard_map/jit(_where)/select_n | solution.py:224
  34.9 1.5 %collective-permute-done.2.refs_3_ = bf16[64,4096]{1,0:T(8,128)(2,1)S(1)} collective-permute-done((bf16[64,4096]{1,0:T(8,128)(2,1)S(1)}, bf16[64,4096]{1,0:T(8,128)(2,1)S(1)}, u32[]{:S(2)}, u32[]{:S(2)}) %collective-permute-start.2) | collective-permute-done | bytes 524320 | tf_op jit(solution)/shard_map/ppermute | solution.py:57
  37.2 10.6 %shard_map.77 = (bf16[128,2048]{1,0:T(8,128)(2,1)}, f32[128,512]{1,0:T(8,128)}, bf16[128,512]{1,0:T(8,128)(2,1)}, bf16[128,512]{1,0:T(8,128)(2,1)}) custom-call(bf16[64,4096]{1,0:T(8,128)(2,1)} %get-tuple-element.23.refs_0_, bf16[64,4096]{1,0:T(8,128)(2,1)} %copy-done.1, bf16[64,4096]{1,0:T(8,128)(2,1)} %copy-done.2, bf16[64,4096]{1,0:T(8,128)(2,1)} %copy-done.3, ...), custom_call_target="tpu_custom_call" | custom-call | flops 1006632960 | bytes 2654208 | tf_op jit(solution)/shard_map/pallas_call | solution.py:158
  47.8 1.3 %collective-permute-start.8 = (bf16[128,512]{1,0:T(8,128)(2,1)}, bf16[128,512]{1,0:T(8,128)(2,1)S(1)}, u32[]{:S(2)}, u32[]{:S(2)}) collective-permute-start(bf16[128,512]{1,0:T(8,128)(2,1)} %get-tuple-element.13), channel_id=1, source_target_pairs={{1,0},{2,1},{3,2},{5,4},{6,5},{7,6},{9,8},{10,9},{11,10},{13,12},{... | collective-permute-start | bytes 393224 | tf_op jit(solution)/shard_map/ppermute | solution.py:232
  49.1 1.6 %collective-permute-start.9 = (bf16[128,512]{1,0:T(8,128)(2,1)}, bf16[128,512]{1,0:T(8,128)(2,1)S(1)}, u32[]{:S(2)}, u32[]{:S(2)}) collective-permute-start(bf16[128,512]{1,0:T(8,128)(2,1)} %get-tuple-element.14), channel_id=1, source_target_pairs={{2,0},{3,1},{6,4},{7,5},{10,8},{11,9},{14,12},{15,13},{18,16},{19,... | collective-permute-start | bytes 393224 | tf_op jit(solution)/shard_map/ppermute | solution.py:232
  50.7 10.6 %shard_map.78 = (bf16[128,2048]{1,0:T(8,128)(2,1)}, f32[128,512]{1,0:T(8,128)}, bf16[128,512]{1,0:T(8,128)(2,1)}, bf16[128,512]{1,0:T(8,128)(2,1)}) custom-call(bf16[64,4096]{1,0:T(8,128)(2,1)} %get-tuple-element.23.refs_0_, bf16[64,4096]{1,0:T(8,128)(2,1)} %copy-done.1, bf16[64,4096]{1,0:T(8,128)(2,1)} %copy-done.2, bf16[64,4096]{1,0:T(8,128)(2,1)} %copy-done.3, ...), custom_call_target="tpu_custom_call" | custom-call | flops 1006632960 | bytes 2654208 | tf_op jit(solution)/shard_map/pallas_call | solution.py:158
  61.4 1.4 %collective-permute-start.10 = (bf16[128,512]{1,0:T(8,128)(2,1)}, bf16[128,512]{1,0:T(8,128)(2,1)S(1)}, u32[]{:S(2)}, u32[]{:S(2)}) collective-permute-start(bf16[128,512]{1,0:T(8,128)(2,1)} %get-tuple-element.16), channel_id=1, source_target_pairs={{1,0},{2,1},{3,2},{5,4},{6,5},{7,6},{9,8},{10,9},{11,10},{13,12},{... | collective-permute-start | bytes 393224 | tf_op jit(solution)/shard_map/ppermute | solution.py:232
  62.8 1.3 %collective-permute-start.11 = (bf16[128,512]{1,0:T(8,128)(2,1)}, bf16[128,512]{1,0:T(8,128)(2,1)S(1)}, u32[]{:S(2)}, u32[]{:S(2)}) collective-permute-start(bf16[128,512]{1,0:T(8,128)(2,1)} %get-tuple-element.17), channel_id=1, source_target_pairs={{2,0},{3,1},{6,4},{7,5},{10,8},{11,9},{14,12},{15,13},{18,16},{19,... | collective-permute-start | bytes 393224 | tf_op jit(solution)/shard_map/ppermute | solution.py:232
  64.1 2.1 %maximum_bitcast_fusion = bf16[1,128,4096]{2,1,0:T(8,128)(2,1)} fusion(bf16[128,2048]{1,0:T(8,128)(2,1)} %get-tuple-element.11, bf16[128,2048]{1,0:T(8,128)(2,1)S(1)} %copy-done.6), kind=kLoop, calls=%fused_computation.5 | loop fusion | flops 2097152 | bytes 2097152 | tf_op jit(solution)/shard_map/reshape | solution.py:239
  66.3 8.6 %collective-permute-done.10 = bf16[128,512]{1,0:T(8,128)(2,1)S(1)} collective-permute-done((bf16[128,512]{1,0:T(8,128)(2,1)}, bf16[128,512]{1,0:T(8,128)(2,1)S(1)}, u32[]{:S(2)}, u32[]{:S(2)}) %collective-permute-start.10) | collective-permute-done | bytes 131104 | tf_op jit(solution)/shard_map/ppermute | solution.py:232
  74.8 5.5 %collective-permute-done.11 = bf16[128,512]{1,0:T(8,128)(2,1)S(1)} collective-permute-done((bf16[128,512]{1,0:T(8,128)(2,1)}, bf16[128,512]{1,0:T(8,128)(2,1)S(1)}, u32[]{:S(2)}, u32[]{:S(2)}) %collective-permute-start.11) | collective-permute-done | bytes 131104 | tf_op jit(solution)/shard_map/ppermute | solution.py:232
  (68 shorter events, 7.2 us)
Async XLA Ops:
  0.6 8.4 %copy-start.4 = (bf16[128,5120]{1,0:T(8,128)(2,1)S(1)}, bf16[128,5120]{1,0:T(8,128)(2,1)}, u32[]{:S(2)}) copy-start(bf16[128,5120]{1,0:T(8,128)(2,1)} %param.6) | copy-start | bytes 3932164
  4.6 9.8 %collective-permute-start.3 = (bf16[64,1024]{1,0:T(8,128)(2,1)}, bf16[64,1024]{1,0:T(8,128)(2,1)}, u32[]{:S(2)}, u32[]{:S(2)}) collective-permute-start(bf16[64,1024]{1,0:T(8,128)(2,1)} %get-tuple-element.27), channel_id=1, source_target_pairs={{0,4},{4,8},{8,12},{12,0},{1,5},{5,9},{9,13},{13,1},{2,6},{6,10},{... | collective-permute-start | bytes 393224 | tf_op jit(solution)/shard_map/ppermute | solution.py:57
  5.1 10.8 %collective-permute-start.4 = (bf16[64,1024]{1,0:T(8,128)(2,1)}, bf16[64,1024]{1,0:T(8,128)(2,1)}, u32[]{:S(2)}, u32[]{:S(2)}) collective-permute-start(bf16[64,1024]{1,0:T(8,128)(2,1)} %get-tuple-element.26), channel_id=1, source_target_pairs={{0,8},{4,12},{8,0},{12,4},{1,9},{5,13},{9,1},{13,5},{2,10},{6,14},... | collective-permute-start | bytes 393224 | tf_op jit(solution)/shard_map/ppermute | solution.py:57
  7.6 8.3 %collective-permute-start.5 = (bf16[64,1024]{1,0:T(8,128)(2,1)}, bf16[64,1024]{1,0:T(8,128)(2,1)}, u32[]{:S(2)}, u32[]{:S(2)}) collective-permute-start(bf16[64,1024]{1,0:T(8,128)(2,1)} %get-tuple-element.25), channel_id=1, source_target_pairs={{0,12},{4,0},{8,4},{12,8},{1,13},{5,1},{9,5},{13,9},{2,14},{6,2},{... | collective-permute-start | bytes 393224 | tf_op jit(solution)/shard_map/ppermute | solution.py:57
  9.8 3.0 %copy-start.10 = (s32[1,128]{1,0:T(1,128)S(1)}, s32[1,128]{1,0:T(1,128)}, u32[]{:S(2)}) copy-start(s32[1,128]{1,0:T(1,128)} %param.8) | copy-start | bytes 1540
  9.8 3.0 %copy-start.12 = (s32[16]{0:T(128)S(1)}, s32[16]{0:T(128)}, u32[]{:S(2)}) copy-start(s32[16]{0:T(128)} %param.10) | copy-start | bytes 196
  9.8 3.0 %copy-start.11 = (s32[16]{0:T(128)S(1)}, s32[16]{0:T(128)}, u32[]{:S(2)}) copy-start(s32[16]{0:T(128)} %param.11) | copy-start | bytes 196
  9.8 3.4 %copy-start.5 = (bf16[1,128,4096]{2,1,0:T(8,128)(2,1)S(1)}, bf16[1,128,4096]{2,1,0:T(8,128)(2,1)}, u32[]{:S(2)}) copy-start(bf16[1,128,4096]{2,1,0:T(8,128)(2,1)} %param.9) | copy-start | bytes 3145732
  11.0 4.9 %copy-start.9 = (bf16[64,1024]{1,0:T(8,128)(2,1)S(1)}, bf16[64,1024]{1,0:T(8,128)(2,1)}, u32[]{:S(2)}) copy-start(bf16[64,1024]{1,0:T(8,128)(2,1)} %get-tuple-element.24) | copy-start | bytes 393220
  11.0 23.9 %collective-permute-start = (bf16[64,4096]{1,0:T(8,128)(2,1)}, bf16[64,4096]{1,0:T(8,128)(2,1)S(1)}, u32[]{:S(2)}, u32[]{:S(2)}) collective-permute-start(bf16[64,4096]{1,0:T(8,128)(2,1)} %get-tuple-element.22), channel_id=1, source_target_pairs={{0,4},{4,8},{8,12},{12,0},{1,5},{5,9},{9,13},{13,1},{2,6},{6,10},{... | collective-permute-start | bytes 1572872 | tf_op jit(solution)/shard_map/ppermute | solution.py:57
  11.0 23.9 %collective-permute-start.1 = (bf16[64,4096]{1,0:T(8,128)(2,1)}, bf16[64,4096]{1,0:T(8,128)(2,1)S(1)}, u32[]{:S(2)}, u32[]{:S(2)}) collective-permute-start(bf16[64,4096]{1,0:T(8,128)(2,1)} %get-tuple-element.21), channel_id=1, source_target_pairs={{0,8},{4,12},{8,0},{12,4},{1,9},{5,13},{9,1},{13,5},{2,10},{6,14},... | collective-permute-start | bytes 1572872 | tf_op jit(solution)/shard_map/ppermute | solution.py:57
  14.5 21.9 %collective-permute-start.2 = (bf16[64,4096]{1,0:T(8,128)(2,1)S(1)}, bf16[64,4096]{1,0:T(8,128)(2,1)S(1)}, u32[]{:S(2)}, u32[]{:S(2)}) collective-permute-start(bf16[64,4096]{1,0:T(8,128)(2,1)S(1)} %get-tuple-element.20), channel_id=1, source_target_pairs={{0,12},{4,0},{8,4},{12,8},{1,13},{5,1},{9,5},{13,9},{2,14},{6,2},{... | collective-permute-start | bytes 1572872 | tf_op jit(solution)/shard_map/ppermute | solution.py:57
  17.3 11.1 %collective-permute-start.6 = (bf16[128,1152]{1,0:T(8,128)(2,1)S(1)}, bf16[128,1152]{1,0:T(8,128)(2,1)S(1)}, u32[]{:S(2)}, u32[]{:S(2)}) collective-permute-start(bf16[128,1152]{1,0:T(8,128)(2,1)S(1)} %pad_maximum_fusion.1), channel_id=1, source_target_pairs={{0,1},{1,2},{2,3},{4,5},{5,6},{6,7},{8,9},{9,10},{10,11},{12,13},{... | collective-permute-start | bytes 884744 | tf_op jit(solution)/shard_map/ppermute | solution.py:200
  21.1 12.7 %collective-permute-start.7 = (bf16[128,1152]{1,0:T(8,128)(2,1)S(1)}, bf16[128,1152]{1,0:T(8,128)(2,1)S(1)}, u32[]{:S(2)}, u32[]{:S(2)}) collective-permute-start(bf16[128,1152]{1,0:T(8,128)(2,1)S(1)} %pad_maximum_fusion.1), channel_id=1, source_target_pairs={{0,2},{1,3},{4,6},{5,7},{8,10},{9,11},{12,14},{13,15},{16,18},{17,... | collective-permute-start | bytes 884744 | tf_op jit(solution)/shard_map/ppermute | solution.py:200
  33.8 2.6 %copy-start = (bf16[384,1152]{1,0:T(8,128)(2,1)}, bf16[384,1152]{1,0:T(8,128)(2,1)S(1)}, u32[]{:S(2)}) copy-start(bf16[384,1152]{1,0:T(8,128)(2,1)S(1)} %pad_maximum_fusion.refs_6_) | copy-start | bytes 2654212
  34.9 1.5 %copy-start.1 = (bf16[64,4096]{1,0:T(8,128)(2,1)}, bf16[64,4096]{1,0:T(8,128)(2,1)S(1)}, u32[]{:S(2)}) copy-start(bf16[64,4096]{1,0:T(8,128)(2,1)S(1)} %collective-permute-done.refs_1_) | copy-start | bytes 1572868
  34.9 1.5 %copy-start.2 = (bf16[64,4096]{1,0:T(8,128)(2,1)}, bf16[64,4096]{1,0:T(8,128)(2,1)S(1)}, u32[]{:S(2)}) copy-start(bf16[64,4096]{1,0:T(8,128)(2,1)S(1)} %collective-permute-done.1.refs_2_) | copy-start | bytes 1572868
  47.8 18.4 %collective-permute-start.8 = (bf16[128,512]{1,0:T(8,128)(2,1)}, bf16[128,512]{1,0:T(8,128)(2,1)S(1)}, u32[]{:S(2)}, u32[]{:S(2)}) collective-permute-start(bf16[128,512]{1,0:T(8,128)(2,1)} %get-tuple-element.13), channel_id=1, source_target_pairs={{1,0},{2,1},{3,2},{5,4},{6,5},{7,6},{9,8},{10,9},{11,10},{13,12},{... | collective-permute-start | bytes 393224 | tf_op jit(solution)/shard_map/ppermute | solution.py:232
  49.1 15.0 %copy-start.6 = (bf16[128,2048]{1,0:T(8,128)(2,1)S(1)}, bf16[128,2048]{1,0:T(8,128)(2,1)}, u32[]{:S(2)}) copy-start(bf16[128,2048]{1,0:T(8,128)(2,1)} %get-tuple-element.10) | copy-start | bytes 1572868
  49.1 17.1 %collective-permute-start.9 = (bf16[128,512]{1,0:T(8,128)(2,1)}, bf16[128,512]{1,0:T(8,128)(2,1)S(1)}, u32[]{:S(2)}, u32[]{:S(2)}) collective-permute-start(bf16[128,512]{1,0:T(8,128)(2,1)} %get-tuple-element.14), channel_id=1, source_target_pairs={{2,0},{3,1},{6,4},{7,5},{10,8},{11,9},{14,12},{15,13},{18,16},{19,... | collective-permute-start | bytes 393224 | tf_op jit(solution)/shard_map/ppermute | solution.py:232
  61.4 4.8 %copy-start.8 = (f32[128,512]{1,0:T(8,128)S(1)}, f32[128,512]{1,0:T(8,128)}, u32[]{:S(2)}) copy-start(f32[128,512]{1,0:T(8,128)} %get-tuple-element.12) | copy-start | bytes 786436
  61.4 19.0 %copy-start.7 = (f32[128,512]{1,0:T(8,128)S(1)}, f32[128,512]{1,0:T(8,128)}, u32[]{:S(2)}) copy-start(f32[128,512]{1,0:T(8,128)} %get-tuple-element.15) | copy-start | bytes 786436
  61.4 13.5 %collective-permute-start.10 = (bf16[128,512]{1,0:T(8,128)(2,1)}, bf16[128,512]{1,0:T(8,128)(2,1)S(1)}, u32[]{:S(2)}, u32[]{:S(2)}) collective-permute-start(bf16[128,512]{1,0:T(8,128)(2,1)} %get-tuple-element.16), channel_id=1, source_target_pairs={{1,0},{2,1},{3,2},{5,4},{6,5},{7,6},{9,8},{10,9},{11,10},{13,12},{... | collective-permute-start | bytes 393224 | tf_op jit(solution)/shard_map/ppermute | solution.py:232
  62.8 17.6 %collective-permute-start.11 = (bf16[128,512]{1,0:T(8,128)(2,1)}, bf16[128,512]{1,0:T(8,128)(2,1)S(1)}, u32[]{:S(2)}, u32[]{:S(2)}) collective-permute-start(bf16[128,512]{1,0:T(8,128)(2,1)} %get-tuple-element.17), channel_id=1, source_target_pairs={{2,0},{3,1},{6,4},{7,5},{10,8},{11,9},{14,12},{15,13},{18,16},{19,... | collective-permute-start | bytes 393224 | tf_op jit(solution)/shard_map/ppermute | solution.py:232
  (1 other events, 0.8 us)

commit v16 on v15

--- a/solution.py
+++ b/solution.py
@@ -15,6 +15,7 @@
 SEGS = 4
 GROUP = 8
 TESTS = 10
+PIPELINE_PARTS = 4
 
 
 def group_advantage(passes, group_ids):
@@ -222,9 +223,9 @@
         & (key_pos[None, :] >= 0)
     )
     bias = jnp.where(allowed.T, 0.0, -1e30).astype(jnp.float32)
-    groups = KEY_VALUE_HEADS // 2
+    groups = KEY_VALUE_HEADS // PIPELINE_PARTS
     query_parts, key_parts, value_parts = [], [], []
-    for part in range(2):
+    for part in range(PIPELINE_PARTS):
         query_grad, total, *outgoing = attend_pallas(
             *packed_q, weighted, kv_all, bias, part, groups
         )

time: 81.6 us -> 93.4 us (1.14)
  starting transfers between devices: 20.1 us -> 25.1 us
  Pallas kernels: 21.2 us -> 25.9 us
  waiting for transfers between devices: 23.1 us -> 24.8 us
    ppermute x4 -> x8, starting transfers between devices: 5.6 us -> 10.6 us  [step(): lax.ppermute(outgoing[shift - 1], 'sp', [(k, k - shift) for k in range(sh...]
    pallas_call x2 -> x4, Pallas kernels: 21.2 us -> 25.9 us  [attend_pallas(): pl.pallas_call(functools.partial(attend_kernel, first_group=part * groups...]
    ppermute x4 -> x8, waiting for transfers between devices: 14.1 us -> 15.9 us  [step(): lax.ppermute(outgoing[shift - 1], 'sp', [(k, k - shift) for k in range(sh...]
  transfers between devices with their start and end apart: 12 -> 16, of which waited for: 5 -> 8; matrix products, arithmetic and copies ran while one was open for 13% -> 11% of each run, Pallas kernels for 13% -> 21%
where the time goes in v16:
time: 93.4 us; the launch traced here: 92.9 us
  Pallas kernels  25.9 us (28%)
  starting transfers between devices  25.1 us (27%)
  waiting for transfers between devices  24.8 us (27%)
  other arithmetic  8.15 us (9%)
  local copies, waits for them, and re-layouts  4.65 us (5%)
  matrix products  3.23 us (3%)
  between operations  1.13 us (1%)
    pallas_call x4, Pallas kernels, attend_pallas(): pl.pallas_call(functools.partial(attend_kernel, first_group=part * groups...  25.9 us
    ppermute x8, waiting for transfers between devices, step(): lax.ppermute(outgoing[shift - 1], 'sp', [(k, k - shift) for k in range(sh...  15.9 us
    ppermute x8, starting transfers between devices, step(): lax.ppermute(outgoing[shift - 1], 'sp', [(k, k - shift) for k in range(sh...  10.6 us
    ppermute x2, starting transfers between devices, step(): lax.ppermute(kv_local, 'sp', [(k, k + shift) for k in range(sp_size - shi...  8.25 us
    ppermute x2, waiting for transfers between devices, step(): lax.ppermute(kv_local, 'sp', [(k, k + shift) for k in range(sp_size - shi...  7.42 us
    ppermute x6, starting transfers between devices, send(): lax.ppermute(outgoing[shift], 'dp', [(k, (k + shift) % dp_size) for k in...  6.23 us
    reshape x1, other arithmetic, step(): jnp.concatenate(query_parts, axis=1)  2.11 us
    dot_general x2, matrix products, send(): jnp.dot(send_pick, columns, preferred_element_type=jnp.float32)  1.93 us
  transfers between devices with their start and end apart: 16, of which 8 were waited for; matrix products, arithmetic and copies ran while one was open for 11% of the time, Pallas kernels for 21%

profile of v16, /device:TPU:0, one launch (start us, length us, event | category | flops | bytes accessed | tf_op | source)
XLA Modules:
  0.0 92.9 jit_solution(12629792885405331951)
XLA Ops:
  5.1 2.5 %collective-permute-start.4 = (bf16[64,1024]{1,0:T(8,128)(2,1)}, bf16[64,1024]{1,0:T(8,128)(2,1)}, u32[]{:S(2)}, u32[]{:S(2)}) collective-permute-start(bf16[64,1024]{1,0:T(8,128)(2,1)} %get-tuple-element.42), channel_id=1, source_target_pairs={{0,8},{4,12},{8,0},{12,4},{1,9},{5,13},{9,1},{13,5},{2,10},{6,14},... | collective-permute-start | bytes 393224 | tf_op jit(solution)/shard_map/ppermute | solution.py:58
  7.6 1.5 %collective-permute-start.5 = (bf16[64,1024]{1,0:T(8,128)(2,1)}, bf16[64,1024]{1,0:T(8,128)(2,1)}, u32[]{:S(2)}, u32[]{:S(2)}) collective-permute-start(bf16[64,1024]{1,0:T(8,128)(2,1)} %get-tuple-element.41), channel_id=1, source_target_pairs={{0,12},{4,0},{8,4},{12,8},{1,13},{5,1},{9,5},{13,9},{2,14},{6,2},{... | collective-permute-start | bytes 393224 | tf_op jit(solution)/shard_map/ppermute | solution.py:58
  14.5 1.4 %collective-permute-start.2 = (bf16[64,4096]{1,0:T(8,128)(2,1)S(1)}, bf16[64,4096]{1,0:T(8,128)(2,1)S(1)}, u32[]{:S(2)}, u32[]{:S(2)}) collective-permute-start(bf16[64,4096]{1,0:T(8,128)(2,1)S(1)} %get-tuple-element.36), channel_id=1, source_target_pairs={{0,12},{4,0},{8,4},{12,8},{1,13},{5,1},{9,5},{13,9},{2,14},{6,2},{... | collective-permute-start | bytes 1572872 | tf_op jit(solution)/shard_map/ppermute | solution.py:58
  15.9 1.3 %convolution_convert_fusion.2 = bf16[128,1024]{1,0:T(8,128)(2,1)S(1)} fusion(bf16[64,1024]{1,0:T(8,128)(2,1)} %collective-permute-done.5, bf16[64,1024]{1,0:T(8,128)(2,1)} %collective-permute-done.4, bf16[64,1024]{1,0:T(8,128)(2,1)} %collective-permute-done.3, bf16[64,1024]{1,0:T(8,128)(2,1)S(1)} %copy-done.13, s32[128]{0:T(128)S(1)} %fusion.38), kind=kOutput, calls=%fused_computation.4 | convolution fusion | flops 69369856 | bytes 786944 | tf_op jit(solution)/shard_map/dot_general | solution.py:71
  17.4 3.7 %collective-permute-start.6 = (bf16[128,1152]{1,0:T(8,128)(2,1)S(1)}, bf16[128,1152]{1,0:T(8,128)(2,1)S(1)}, u32[]{:S(2)}, u32[]{:S(2)}) collective-permute-start(bf16[128,1152]{1,0:T(8,128)(2,1)S(1)} %pad_maximum_fusion.1), channel_id=1, source_target_pairs={{0,1},{1,2},{2,3},{4,5},{5,6},{6,7},{8,9},{9,10},{10,11},{12,13},{... | collective-permute-start | bytes 884744 | tf_op jit(solution)/shard_map/ppermute | solution.py:201
  21.1 4.5 %collective-permute-start.7 = (bf16[128,1152]{1,0:T(8,128)(2,1)S(1)}, bf16[128,1152]{1,0:T(8,128)(2,1)S(1)}, u32[]{:S(2)}, u32[]{:S(2)}) collective-permute-start(bf16[128,1152]{1,0:T(8,128)(2,1)S(1)} %pad_maximum_fusion.1), channel_id=1, source_target_pairs={{0,2},{1,3},{4,6},{5,7},{8,10},{9,11},{12,14},{13,15},{16,18},{17,... | collective-permute-start | bytes 884744 | tf_op jit(solution)/shard_map/ppermute | solution.py:201
  26.3 2.1 %collective-permute-done.6 = bf16[128,1152]{1,0:T(8,128)(2,1)S(1)} collective-permute-done((bf16[128,1152]{1,0:T(8,128)(2,1)S(1)}, bf16[128,1152]{1,0:T(8,128)(2,1)S(1)}, u32[]{:S(2)}, u32[]{:S(2)}) %collective-permute-start.6) | collective-permute-done | bytes 294944 | tf_op jit(solution)/shard_map/ppermute | solution.py:201
  28.5 5.3 %collective-permute-done.7 = bf16[128,1152]{1,0:T(8,128)(2,1)S(1)} collective-permute-done((bf16[128,1152]{1,0:T(8,128)(2,1)S(1)}, bf16[128,1152]{1,0:T(8,128)(2,1)S(1)}, u32[]{:S(2)}, u32[]{:S(2)}) %collective-permute-start.7) | collective-permute-done | bytes 294944 | tf_op jit(solution)/shard_map/ppermute | solution.py:201
  34.9 1.5 %collective-permute-done.2.refs_3_ = bf16[64,4096]{1,0:T(8,128)(2,1)S(1)} collective-permute-done((bf16[64,4096]{1,0:T(8,128)(2,1)S(1)}, bf16[64,4096]{1,0:T(8,128)(2,1)S(1)}, u32[]{:S(2)}, u32[]{:S(2)}) %collective-permute-start.2) | collective-permute-done | bytes 524320 | tf_op jit(solution)/shard_map/ppermute | solution.py:58
  37.2 6.4 %shard_map.80 = (bf16[128,1024]{1,0:T(8,128)(2,1)}, f32[128,256]{1,0:T(8,128)}, bf16[128,256]{1,0:T(8,128)(2,1)}, bf16[128,256]{1,0:T(8,128)(2,1)}) custom-call(bf16[64,4096]{1,0:T(8,128)(2,1)} %get-tuple-element.39.refs_0_, bf16[64,4096]{1,0:T(8,128)(2,1)} %copy-done.1, bf16[64,4096]{1,0:T(8,128)(2,1)} %copy-done.2, bf16[64,4096]{1,0:T(8,128)(2,1)} %copy-done.3, ...), custom_call_target="tpu_custom_call" | custom-call | flops 503316480 | bytes 1867776 | tf_op jit(solution)/shard_map/pallas_call | solution.py:159
  44.9 1.3 %collective-permute-start.15 = (bf16[128,256]{1,0:T(8,128)(2,1)}, bf16[128,256]{1,0:T(8,128)(2,1)S(1)}, u32[]{:S(2)}, u32[]{:S(2)}) collective-permute-start(bf16[128,256]{1,0:T(8,128)(2,1)} %get-tuple-element.33), channel_id=1, source_target_pairs={{2,0},{3,1},{6,4},{7,5},{10,8},{11,9},{14,12},{15,13},{18,16},{19,... | collective-permute-start | bytes 196616 | tf_op jit(solution)/shard_map/ppermute | solution.py:233
  46.2 6.5 %shard_map.79 = (bf16[128,1024]{1,0:T(8,128)(2,1)}, f32[128,256]{1,0:T(8,128)}, bf16[128,256]{1,0:T(8,128)(2,1)}, bf16[128,256]{1,0:T(8,128)(2,1)}) custom-call(bf16[64,4096]{1,0:T(8,128)(2,1)} %get-tuple-element.39.refs_0_, bf16[64,4096]{1,0:T(8,128)(2,1)} %copy-done.1, bf16[64,4096]{1,0:T(8,128)(2,1)} %copy-done.2, bf16[64,4096]{1,0:T(8,128)(2,1)} %copy-done.3, ...), custom_call_target="tpu_custom_call" | custom-call | flops 503316480 | bytes 1867776 | tf_op jit(solution)/shard_map/pallas_call | solution.py:159
  52.7 1.5 %collective-permute-start.12 = (bf16[128,256]{1,0:T(8,128)(2,1)}, bf16[128,256]{1,0:T(8,128)(2,1)S(1)}, u32[]{:S(2)}, u32[]{:S(2)}) collective-permute-start(bf16[128,256]{1,0:T(8,128)(2,1)} %get-tuple-element.29), channel_id=1, source_target_pairs={{1,0},{2,1},{3,2},{5,4},{6,5},{7,6},{9,8},{10,9},{11,10},{13,12},{... | collective-permute-start | bytes 196616 | tf_op jit(solution)/shard_map/ppermute | solution.py:233
  54.2 6.5 %shard_map.77 = (bf16[128,1024]{1,0:T(8,128)(2,1)}, f32[128,256]{1,0:T(8,128)}, bf16[128,256]{1,0:T(8,128)(2,1)}, bf16[128,256]{1,0:T(8,128)(2,1)}) custom-call(bf16[64,4096]{1,0:T(8,128)(2,1)} %get-tuple-element.39.refs_0_, bf16[64,4096]{1,0:T(8,128)(2,1)} %copy-done.1, bf16[64,4096]{1,0:T(8,128)(2,1)} %copy-done.2, bf16[64,4096]{1,0:T(8,128)(2,1)} %copy-done.3, ...), custom_call_target="tpu_custom_call" | custom-call | flops 503316480 | bytes 1867776 | tf_op jit(solution)/shard_map/pallas_call | solution.py:159
  62.0 1.4 %collective-permute-start.9 = (bf16[128,256]{1,0:T(8,128)(2,1)}, bf16[128,256]{1,0:T(8,128)(2,1)S(1)}, u32[]{:S(2)}, u32[]{:S(2)}) collective-permute-start(bf16[128,256]{1,0:T(8,128)(2,1)} %get-tuple-element.24), channel_id=1, source_target_pairs={{2,0},{3,1},{6,4},{7,5},{10,8},{11,9},{14,12},{15,13},{18,16},{19,... | collective-permute-start | bytes 196616 | tf_op jit(solution)/shard_map/ppermute | solution.py:233
  63.4 6.5 %shard_map.78 = (bf16[128,1024]{1,0:T(8,128)(2,1)}, f32[128,256]{1,0:T(8,128)}, bf16[128,256]{1,0:T(8,128)(2,1)}, bf16[128,256]{1,0:T(8,128)(2,1)}) custom-call(bf16[64,4096]{1,0:T(8,128)(2,1)} %get-tuple-element.39.refs_0_, bf16[64,4096]{1,0:T(8,128)(2,1)} %copy-done.1, bf16[64,4096]{1,0:T(8,128)(2,1)} %copy-done.2, bf16[64,4096]{1,0:T(8,128)(2,1)} %copy-done.3, ...), custom_call_target="tpu_custom_call" | custom-call | flops 503316480 | bytes 1867776 | tf_op jit(solution)/shard_map/pallas_call | solution.py:159
  69.9 2.1 %maximum_bitcast_fusion = bf16[1,128,4096]{2,1,0:T(8,128)(2,1)} fusion(bf16[128,1024]{1,0:T(8,128)(2,1)S(1)} %copy-done.6, bf16[128,1024]{1,0:T(8,128)(2,1)S(1)} %copy-done.7, bf16[128,1024]{1,0:T(8,128)(2,1)} %get-tuple-element.19, bf16[128,1024]{1,0:T(8,128)(2,1)S(1)} %copy-done.8), kind=kLoop, calls=%fused_computation.5 | loop fusion | flops 4194304 | bytes 2097152 | tf_op jit(solution)/shard_map/reshape | solution.py:240
  73.0 1.3 %collective-permute-start.10 = (bf16[128,256]{1,0:T(8,128)(2,1)S(1)}, bf16[128,256]{1,0:T(8,128)(2,1)S(1)}, u32[]{:S(2)}, u32[]{:S(2)}) collective-permute-start(bf16[128,256]{1,0:T(8,128)(2,1)S(1)} %copy-done.19), channel_id=1, source_target_pairs={{1,0},{2,1},{3,2},{5,4},{6,5},{7,6},{9,8},{10,9},{11,10},{13,12},{... | collective-permute-start | bytes 196616 | tf_op jit(solution)/shard_map/ppermute | solution.py:233
  74.3 1.9 %collective-permute-done.9 = bf16[128,256]{1,0:T(8,128)(2,1)S(1)} collective-permute-done((bf16[128,256]{1,0:T(8,128)(2,1)}, bf16[128,256]{1,0:T(8,128)(2,1)S(1)}, u32[]{:S(2)}, u32[]{:S(2)}) %collective-permute-start.9) | collective-permute-done | bytes 65568 | tf_op jit(solution)/shard_map/ppermute | solution.py:233
  76.2 1.3 %collective-permute-start.11 = (bf16[128,256]{1,0:T(8,128)(2,1)S(1)}, bf16[128,256]{1,0:T(8,128)(2,1)S(1)}, u32[]{:S(2)}, u32[]{:S(2)}) collective-permute-start(bf16[128,256]{1,0:T(8,128)(2,1)S(1)} %copy-done.18), channel_id=1, source_target_pairs={{2,0},{3,1},{6,4},{7,5},{10,8},{11,9},{14,12},{15,13},{18,16},{19,... | collective-permute-start | bytes 196616 | tf_op jit(solution)/shard_map/ppermute | solution.py:233
  77.5 7.3 %collective-permute-done.10 = bf16[128,256]{1,0:T(8,128)(2,1)S(1)} collective-permute-done((bf16[128,256]{1,0:T(8,128)(2,1)S(1)}, bf16[128,256]{1,0:T(8,128)(2,1)S(1)}, u32[]{:S(2)}, u32[]{:S(2)}) %collective-permute-start.10) | collective-permute-done | bytes 65568 | tf_op jit(solution)/shard_map/ppermute | solution.py:233
  84.8 1.3 %collective-permute-start.13 = (bf16[128,256]{1,0:T(8,128)(2,1)S(1)}, bf16[128,256]{1,0:T(8,128)(2,1)S(1)}, u32[]{:S(2)}, u32[]{:S(2)}) collective-permute-start(bf16[128,256]{1,0:T(8,128)(2,1)S(1)} %copy-done.17), channel_id=1, source_target_pairs={{2,0},{3,1},{6,4},{7,5},{10,8},{11,9},{14,12},{15,13},{18,16},{19,... | collective-permute-start | bytes 196616 | tf_op jit(solution)/shard_map/ppermute | solution.py:233
  86.1 1.8 %collective-permute-done.11 = bf16[128,256]{1,0:T(8,128)(2,1)S(1)} collective-permute-done((bf16[128,256]{1,0:T(8,128)(2,1)S(1)}, bf16[128,256]{1,0:T(8,128)(2,1)S(1)}, u32[]{:S(2)}, u32[]{:S(2)}) %collective-permute-start.11) | collective-permute-done | bytes 65568 | tf_op jit(solution)/shard_map/ppermute | solution.py:233
  87.9 4.0 %collective-permute-done.13 = bf16[128,256]{1,0:T(8,128)(2,1)S(1)} collective-permute-done((bf16[128,256]{1,0:T(8,128)(2,1)S(1)}, bf16[128,256]{1,0:T(8,128)(2,1)S(1)}, u32[]{:S(2)}, u32[]{:S(2)}) %collective-permute-start.13) | collective-permute-done | bytes 65568 | tf_op jit(solution)/shard_map/ppermute | solution.py:233
  (101 shorter events, 17.0 us)
Async XLA Ops:
  0.6 8.4 %copy-start.4 = (bf16[128,5120]{1,0:T(8,128)(2,1)S(1)}, bf16[128,5120]{1,0:T(8,128)(2,1)}, u32[]{:S(2)}) copy-start(bf16[128,5120]{1,0:T(8,128)(2,1)} %param.6) | copy-start | bytes 3932164
  4.6 9.9 %collective-permute-start.3 = (bf16[64,1024]{1,0:T(8,128)(2,1)}, bf16[64,1024]{1,0:T(8,128)(2,1)}, u32[]{:S(2)}, u32[]{:S(2)}) collective-permute-start(bf16[64,1024]{1,0:T(8,128)(2,1)} %get-tuple-element.43), channel_id=1, source_target_pairs={{0,4},{4,8},{8,12},{12,0},{1,5},{5,9},{9,13},{13,1},{2,6},{6,10},{... | collective-permute-start | bytes 393224 | tf_op jit(solution)/shard_map/ppermute | solution.py:58
  5.1 10.8 %collective-permute-start.4 = (bf16[64,1024]{1,0:T(8,128)(2,1)}, bf16[64,1024]{1,0:T(8,128)(2,1)}, u32[]{:S(2)}, u32[]{:S(2)}) collective-permute-start(bf16[64,1024]{1,0:T(8,128)(2,1)} %get-tuple-element.42), channel_id=1, source_target_pairs={{0,8},{4,12},{8,0},{12,4},{1,9},{5,13},{9,1},{13,5},{2,10},{6,14},... | collective-permute-start | bytes 393224 | tf_op jit(solution)/shard_map/ppermute | solution.py:58
  7.6 8.3 %collective-permute-start.5 = (bf16[64,1024]{1,0:T(8,128)(2,1)}, bf16[64,1024]{1,0:T(8,128)(2,1)}, u32[]{:S(2)}, u32[]{:S(2)}) collective-permute-start(bf16[64,1024]{1,0:T(8,128)(2,1)} %get-tuple-element.41), channel_id=1, source_target_pairs={{0,12},{4,0},{8,4},{12,8},{1,13},{5,1},{9,5},{13,9},{2,14},{6,2},{... | collective-permute-start | bytes 393224 | tf_op jit(solution)/shard_map/ppermute | solution.py:58
  11.0 23.9 %collective-permute-start = (bf16[64,4096]{1,0:T(8,128)(2,1)}, bf16[64,4096]{1,0:T(8,128)(2,1)S(1)}, u32[]{:S(2)}, u32[]{:S(2)}) collective-permute-start(bf16[64,4096]{1,0:T(8,128)(2,1)} %get-tuple-element.38), channel_id=1, source_target_pairs={{0,4},{4,8},{8,12},{12,0},{1,5},{5,9},{9,13},{13,1},{2,6},{6,10},{... | collective-permute-start | bytes 1572872 | tf_op jit(solution)/shard_map/ppermute | solution.py:58
  11.0 23.9 %collective-permute-start.1 = (bf16[64,4096]{1,0:T(8,128)(2,1)}, bf16[64,4096]{1,0:T(8,128)(2,1)S(1)}, u32[]{:S(2)}, u32[]{:S(2)}) collective-permute-start(bf16[64,4096]{1,0:T(8,128)(2,1)} %get-tuple-element.37), channel_id=1, source_target_pairs={{0,8},{4,12},{8,0},{12,4},{1,9},{5,13},{9,1},{13,5},{2,10},{6,14},... | collective-permute-start | bytes 1572872 | tf_op jit(solution)/shard_map/ppermute | solution.py:58
  14.5 21.9 %collective-permute-start.2 = (bf16[64,4096]{1,0:T(8,128)(2,1)S(1)}, bf16[64,4096]{1,0:T(8,128)(2,1)S(1)}, u32[]{:S(2)}, u32[]{:S(2)}) collective-permute-start(bf16[64,4096]{1,0:T(8,128)(2,1)S(1)} %get-tuple-element.36), channel_id=1, source_target_pairs={{0,12},{4,0},{8,4},{12,8},{1,13},{5,1},{9,5},{13,9},{2,14},{6,2},{... | collective-permute-start | bytes 1572872 | tf_op jit(solution)/shard_map/ppermute | solution.py:58
  17.4 11.1 %collective-permute-start.6 = (bf16[128,1152]{1,0:T(8,128)(2,1)S(1)}, bf16[128,1152]{1,0:T(8,128)(2,1)S(1)}, u32[]{:S(2)}, u32[]{:S(2)}) collective-permute-start(bf16[128,1152]{1,0:T(8,128)(2,1)S(1)} %pad_maximum_fusion.1), channel_id=1, source_target_pairs={{0,1},{1,2},{2,3},{4,5},{5,6},{6,7},{8,9},{9,10},{10,11},{12,13},{... | collective-permute-start | bytes 884744 | tf_op jit(solution)/shard_map/ppermute | solution.py:201
  21.1 12.6 %collective-permute-start.7 = (bf16[128,1152]{1,0:T(8,128)(2,1)S(1)}, bf16[128,1152]{1,0:T(8,128)(2,1)S(1)}, u32[]{:S(2)}, u32[]{:S(2)}) collective-permute-start(bf16[128,1152]{1,0:T(8,128)(2,1)S(1)} %pad_maximum_fusion.1), channel_id=1, source_target_pairs={{0,2},{1,3},{4,6},{5,7},{8,10},{9,11},{12,14},{13,15},{16,18},{17,... | collective-permute-start | bytes 884744 | tf_op jit(solution)/shard_map/ppermute | solution.py:201
  43.6 48.4 %collective-permute-start.14 = (bf16[128,256]{1,0:T(8,128)(2,1)}, bf16[128,256]{1,0:T(8,128)(2,1)S(1)}, u32[]{:S(2)}, u32[]{:S(2)}) collective-permute-start(bf16[128,256]{1,0:T(8,128)(2,1)} %get-tuple-element.32), channel_id=1, source_target_pairs={{1,0},{2,1},{3,2},{5,4},{6,5},{7,6},{9,8},{10,9},{11,10},{13,12},{... | collective-permute-start | bytes 196616 | tf_op jit(solution)/shard_map/ppermute | solution.py:233
  44.9 47.1 %collective-permute-start.15 = (bf16[128,256]{1,0:T(8,128)(2,1)}, bf16[128,256]{1,0:T(8,128)(2,1)S(1)}, u32[]{:S(2)}, u32[]{:S(2)}) collective-permute-start(bf16[128,256]{1,0:T(8,128)(2,1)} %get-tuple-element.33), channel_id=1, source_target_pairs={{2,0},{3,1},{6,4},{7,5},{10,8},{11,9},{14,12},{15,13},{18,16},{19,... | collective-permute-start | bytes 196616 | tf_op jit(solution)/shard_map/ppermute | solution.py:233
  52.7 35.2 %collective-permute-start.12 = (bf16[128,256]{1,0:T(8,128)(2,1)}, bf16[128,256]{1,0:T(8,128)(2,1)S(1)}, u32[]{:S(2)}, u32[]{:S(2)}) collective-permute-start(bf16[128,256]{1,0:T(8,128)(2,1)} %get-tuple-element.29), channel_id=1, source_target_pairs={{1,0},{2,1},{3,2},{5,4},{6,5},{7,6},{9,8},{10,9},{11,10},{13,12},{... | collective-permute-start | bytes 196616 | tf_op jit(solution)/shard_map/ppermute | solution.py:233
  60.7 12.3 %collective-permute-start.8 = (bf16[128,256]{1,0:T(8,128)(2,1)}, bf16[128,256]{1,0:T(8,128)(2,1)S(1)}, u32[]{:S(2)}, u32[]{:S(2)}) collective-permute-start(bf16[128,256]{1,0:T(8,128)(2,1)} %get-tuple-element.23), channel_id=1, source_target_pairs={{1,0},{2,1},{3,2},{5,4},{6,5},{7,6},{9,8},{10,9},{11,10},{13,12},{... | collective-permute-start | bytes 196616 | tf_op jit(solution)/shard_map/ppermute | solution.py:233
  61.9 8.0 %copy-start.6 = (bf16[128,1024]{1,0:T(8,128)(2,1)S(1)}, bf16[128,1024]{1,0:T(8,128)(2,1)}, u32[]{:S(2)}) copy-start(bf16[128,1024]{1,0:T(8,128)(2,1)} %get-tuple-element.21) | copy-start | bytes 786436
  62.0 8.0 %copy-start.7 = (bf16[128,1024]{1,0:T(8,128)(2,1)S(1)}, bf16[128,1024]{1,0:T(8,128)(2,1)}, u32[]{:S(2)}) copy-start(bf16[128,1024]{1,0:T(8,128)(2,1)} %get-tuple-element.20) | copy-start | bytes 786436
  62.0 8.0 %copy-start.8 = (bf16[128,1024]{1,0:T(8,128)(2,1)S(1)}, bf16[128,1024]{1,0:T(8,128)(2,1)}, u32[]{:S(2)}) copy-start(bf16[128,1024]{1,0:T(8,128)(2,1)} %get-tuple-element.18) | copy-start | bytes 786436
  62.0 14.2 %collective-permute-start.9 = (bf16[128,256]{1,0:T(8,128)(2,1)}, bf16[128,256]{1,0:T(8,128)(2,1)S(1)}, u32[]{:S(2)}, u32[]{:S(2)}) collective-permute-start(bf16[128,256]{1,0:T(8,128)(2,1)} %get-tuple-element.24), channel_id=1, source_target_pairs={{2,0},{3,1},{6,4},{7,5},{10,8},{11,9},{14,12},{15,13},{18,16},{19,... | collective-permute-start | bytes 196616 | tf_op jit(solution)/shard_map/ppermute | solution.py:233
  69.9 14.9 %copy-start.17 = (bf16[128,256]{1,0:T(8,128)(2,1)S(1)}, bf16[128,256]{1,0:T(8,128)(2,1)}, u32[]{:S(2)}) copy-start(bf16[128,256]{1,0:T(8,128)(2,1)} %get-tuple-element.30) | copy-start | bytes 196612
  69.9 18.0 %copy-start.11 = (f32[128,256]{1,0:T(8,128)S(1)}, f32[128,256]{1,0:T(8,128)}, u32[]{:S(2)}) copy-start(f32[128,256]{1,0:T(8,128)} %get-tuple-element.25) | copy-start | bytes 393220
  69.9 22.1 %copy-start.10 = (f32[128,256]{1,0:T(8,128)S(1)}, f32[128,256]{1,0:T(8,128)}, u32[]{:S(2)}) copy-start(f32[128,256]{1,0:T(8,128)} %get-tuple-element.28) | copy-start | bytes 393220
  69.9 22.1 %copy-start.9 = (f32[128,256]{1,0:T(8,128)S(1)}, f32[128,256]{1,0:T(8,128)}, u32[]{:S(2)}) copy-start(f32[128,256]{1,0:T(8,128)} %get-tuple-element.31) | copy-start | bytes 393220
  73.0 11.8 %collective-permute-start.10 = (bf16[128,256]{1,0:T(8,128)(2,1)S(1)}, bf16[128,256]{1,0:T(8,128)(2,1)S(1)}, u32[]{:S(2)}, u32[]{:S(2)}) collective-permute-start(bf16[128,256]{1,0:T(8,128)(2,1)S(1)} %copy-done.19), channel_id=1, source_target_pairs={{1,0},{2,1},{3,2},{5,4},{6,5},{7,6},{9,8},{10,9},{11,10},{13,12},{... | collective-permute-start | bytes 196616 | tf_op jit(solution)/shard_map/ppermute | solution.py:233
  76.2 11.7 %collective-permute-start.11 = (bf16[128,256]{1,0:T(8,128)(2,1)S(1)}, bf16[128,256]{1,0:T(8,128)(2,1)S(1)}, u32[]{:S(2)}, u32[]{:S(2)}) collective-permute-start(bf16[128,256]{1,0:T(8,128)(2,1)S(1)} %copy-done.18), channel_id=1, source_target_pairs={{2,0},{3,1},{6,4},{7,5},{10,8},{11,9},{14,12},{15,13},{18,16},{19,... | collective-permute-start | bytes 196616 | tf_op jit(solution)/shard_map/ppermute | solution.py:233
  84.8 7.1 %collective-permute-start.13 = (bf16[128,256]{1,0:T(8,128)(2,1)S(1)}, bf16[128,256]{1,0:T(8,128)(2,1)S(1)}, u32[]{:S(2)}, u32[]{:S(2)}) collective-permute-start(bf16[128,256]{1,0:T(8,128)(2,1)S(1)} %copy-done.17), channel_id=1, source_target_pairs={{2,0},{3,1},{6,4},{7,5},{10,8},{11,9},{14,12},{15,13},{18,16},{19,... | collective-permute-start | bytes 196616 | tf_op jit(solution)/shard_map/ppermute | solution.py:233
  (13 other events, 41.5 us)

commit v17 on v15

--- a/solution.py
+++ b/solution.py
@@ -97,6 +97,33 @@
     groups = local_ref.shape[1] // (2 * HEAD_SIZE)
     query_group = QUERY_HEADS // KEY_VALUE_HEADS
     bias = m_ref[...]
+    fold = len(send_refs) > 0 and bias.shape[0] == (len(send_refs) + 1) * token_rows
+    if fold:
+        far = len(send_refs) * token_rows
+        lower = (
+            lax.broadcasted_iota(jnp.int32, (token_rows, token_rows), 0)
+            <= lax.broadcasted_iota(jnp.int32, (token_rows, token_rows), 1)
+        )
+
+        def folded(full):
+            return jnp.concatenate(
+                [jnp.where(lower, full[:token_rows], full[far:]), full[token_rows:far]], axis=0
+            )
+
+        def unfolded(part):
+            zero = jnp.zeros_like(part[:token_rows])
+            return jnp.concatenate(
+                [
+                    jnp.where(lower, part[:token_rows], zero),
+                    part[token_rows:],
+                    jnp.where(lower, zero, part[:token_rows]),
+                ],
+                axis=0,
+            )
+
+        bias = folded(bias)
+    else:
+        folded = unfolded = lambda x: x
     for local_group in range(groups):
         group = first_group + local_group
         key_mat = kv_ref[:, group * HEAD_SIZE : (group + 1) * HEAD_SIZE]
@@ -113,8 +140,10 @@
             query_head = q_ref[:, cols]
             grad_head = g_ref[:, cols]
             scores = (
-                lax.dot_general(
-                    key_mat, query_head, (((1,), (1,)), ((), ())), preferred_element_type=jnp.float32
+                folded(
+                    lax.dot_general(
+                        key_mat, query_head, (((1,), (1,)), ((), ())), preferred_element_type=jnp.float32
+                    )
                 )
                 * inv_root
                 + bias
@@ -122,18 +151,21 @@
             row_top = jnp.max(scores, axis=0, keepdims=True)
             scaled_exp = jnp.exp(scores - row_top)
             weights = scaled_exp * (1.0 / jnp.sum(scaled_exp, axis=0, keepdims=True))
-            weight_grads = lax.dot_general(
-                value_mat, grad_head, (((1,), (1,)), ((), ())), preferred_element_type=jnp.float32
+            weight_grads = folded(
+                lax.dot_general(
+                    value_mat, grad_head, (((1,), (1,)), ((), ())), preferred_element_type=jnp.float32
+                )
             )
             row_dot = jnp.sum(weights * weight_grads, axis=0, keepdims=True)
-            score_grads = (weights * (weight_grads - row_dot) * inv_root).astype(jnp.bfloat16)
+            score_grads = unfolded(
+                (weights * (weight_grads - row_dot) * inv_root).astype(jnp.bfloat16)
+            )
+            weights_low = unfolded(weights.astype(jnp.bfloat16))
             dq_ref[:, cols] = lax.dot_general(
                 score_grads, key_mat, (((0,), (0,)), ((), ())), preferred_element_type=jnp.float32
             ).astype(dq_ref.dtype)
             key_sum = key_sum + jnp.dot(score_grads, query_head, preferred_element_type=jnp.float32)
-            value_sum = value_sum + jnp.dot(
-                weights.astype(jnp.bfloat16), grad_head, preferred_element_type=jnp.float32
-            )
+            value_sum = value_sum + jnp.dot(weights_low, grad_head, preferred_element_type=jnp.float32)
         key_cols = slice(local_group * HEAD_SIZE, (local_group + 1) * HEAD_SIZE)
         value_cols = slice((groups + local_group) * HEAD_SIZE, (groups + local_group + 1) * HEAD_SIZE)
         local_ref[:, key_cols] = key_sum[:token_rows]

time: 81.6 us -> 80.6 us (0.988)
  Pallas kernels: 21.2 us -> 20.2 us
    pallas_call x2, Pallas kernels: 21.2 us -> 20.2 us  [attend_pallas(): pl.pallas_call(functools.partial(attend_kernel, first_group=part * groups...]
  transfers between devices with their start and end apart: 12 -> 12, of which waited for: 5 -> 6; matrix products, arithmetic and copies ran while one was open for 13% -> 13% of each run, Pallas kernels for 13% -> 13%
where the time goes in v17:
time: 80.6 us; the launch traced here: 80.1 us
  waiting for transfers between devices  23.1 us (29%)
  Pallas kernels  20.2 us (25%)
  starting transfers between devices  20.1 us (25%)
  other arithmetic  8.83 us (11%)
  local copies, waits for them, and re-layouts  3.79 us (5%)
  matrix products  3.23 us (4%)
  between operations  0.94 us (1%)
    pallas_call x2, Pallas kernels, attend_pallas(): pl.pallas_call(functools.partial(attend_kernel, first_group=part * groups...  20.2 us
    ppermute x4, waiting for transfers between devices, step(): lax.ppermute(outgoing[shift - 1], 'sp', [(k, k - shift) for k in range(sh...  14.1 us
    ppermute x2, starting transfers between devices, step(): lax.ppermute(kv_local, 'sp', [(k, k + shift) for k in range(sp_size - shi...  8.25 us
    ppermute x2, waiting for transfers between devices, step(): lax.ppermute(kv_local, 'sp', [(k, k + shift) for k in range(sp_size - shi...  7.43 us
    ppermute x6, starting transfers between devices, send(): lax.ppermute(outgoing[shift], 'dp', [(k, (k + shift) % dp_size) for k in...  6.24 us
    ppermute x4, starting transfers between devices, step(): lax.ppermute(outgoing[shift - 1], 'sp', [(k, k - shift) for k in range(sh...  5.6 us
    reshape x1, other arithmetic, step(): jnp.concatenate(query_parts, axis=1)  2.09 us
    dot_general x2, matrix products, send(): jnp.dot(send_pick, columns, preferred_element_type=jnp.float32)  1.93 us
  transfers between devices with their start and end apart: 12, of which 6 were waited for; matrix products, arithmetic and copies ran while one was open for 13% of the time, Pallas kernels for 13%

profile of v17, /device:TPU:0, one launch (start us, length us, event | category | flops | bytes accessed | tf_op | source)
XLA Modules:
  0.0 80.1 jit_solution(11968943377840757435)
XLA Ops:
  2.6 1.2 %convolution_convert_fusion.1 = bf16[256,1024]{1,0:T(8,128)(2,1)S(1)} fusion(bf16[128,5120]{1,0:T(8,128)(2,1)} %param.6, s32[128]{0:T(128)S(1)} %fusion.27), kind=kOutput, calls=%fused_computation.3 | convolution fusion | flops 67403776 | bytes 786944 | tf_op jit(solution)/shard_map/dot_general | solution.py:52
  3.8 0.8 fusion.36
  5.1 2.5 %collective-permute-start.4 = (bf16[64,1024]{1,0:T(8,128)(2,1)}, bf16[64,1024]{1,0:T(8,128)(2,1)}, u32[]{:S(2)}, u32[]{:S(2)}) collective-permute-start(bf16[64,1024]{1,0:T(8,128)(2,1)} %get-tuple-element.26), channel_id=1, source_target_pairs={{0,8},{4,12},{8,0},{12,4},{1,9},{5,13},{9,1},{13,5},{2,10},{6,14},... | collective-permute-start | bytes 393224 | tf_op jit(solution)/shard_map/ppermute | solution.py:57
  7.6 1.5 %collective-permute-start.5 = (bf16[64,1024]{1,0:T(8,128)(2,1)}, bf16[64,1024]{1,0:T(8,128)(2,1)}, u32[]{:S(2)}, u32[]{:S(2)}) collective-permute-start(bf16[64,1024]{1,0:T(8,128)(2,1)} %get-tuple-element.25), channel_id=1, source_target_pairs={{0,12},{4,0},{8,4},{12,8},{1,13},{5,1},{9,5},{13,9},{2,14},{6,2},{... | collective-permute-start | bytes 393224 | tf_op jit(solution)/shard_map/ppermute | solution.py:57
  9.8 1.2 %fusion.35 = (bf16[64,4096]{1,0:T(8,128)(2,1)S(1)}, bf16[64,4096]{1,0:T(8,128)(2,1)}, bf16[64,4096]{1,0:T(8,128)(2,1)}, bf16[64,4096]{1,0:T(8,128)(2,1)}) fusion(bf16[256,4096]{1,0:T(8,128)(2,1)S(1)} %convolution_convert_fusion), kind=kLoop, calls=%fused_computation.82 | loop fusion | bytes 4194304 | tf_op jit(solution)/shard_map/slice | solution.py:58
  11.4 0.9 %fusion.23 = s32[4]{0:T(128)S(1)} fusion(s32[4,4,128]{2,1,0:T(4,128)} %bitcast.25, s32[]{:T(128)S(6)} %select_n.77, s32[]{:T(128)S(6)} %axis_index.23), kind=kLoop, calls=%fused_computation.54 | loop fusion | flops 1532 | bytes 2072 | tf_op jit(solution)/shard_map/reduce_sum | solution.py:38
  13.2 1.2 %fusion.refs_5_ = bf16[128,4096]{1,0:T(8,128)(2,1)} fusion(bf16[1,128,4096]{2,1,0:T(8,128)(2,1)S(1)} %copy-done.5, f32[128]{0:T(128)S(1)} %select_reduce_fusion.2), kind=kLoop, calls=%fused_computation.2 | loop fusion | flops 1572864 | bytes 2097664 | tf_op jit(solution)/shard_map/convert_element_type | solution.py:246
  14.5 1.4 %collective-permute-start.2 = (bf16[64,4096]{1,0:T(8,128)(2,1)S(1)}, bf16[64,4096]{1,0:T(8,128)(2,1)S(1)}, u32[]{:S(2)}, u32[]{:S(2)}) collective-permute-start(bf16[64,4096]{1,0:T(8,128)(2,1)S(1)} %get-tuple-element.20), channel_id=1, source_target_pairs={{0,12},{4,0},{8,4},{12,8},{1,13},{5,1},{9,5},{13,9},{2,14},{6,2},{... | collective-permute-start | bytes 1572872 | tf_op jit(solution)/shard_map/ppermute | solution.py:57
  15.9 1.3 %convolution_convert_fusion.2 = bf16[128,1024]{1,0:T(8,128)(2,1)S(1)} fusion(bf16[64,1024]{1,0:T(8,128)(2,1)} %collective-permute-done.5, bf16[64,1024]{1,0:T(8,128)(2,1)} %collective-permute-done.4, bf16[64,1024]{1,0:T(8,128)(2,1)} %collective-permute-done.3, bf16[64,1024]{1,0:T(8,128)(2,1)S(1)} %copy-done.9, s32[128]{0:T(128)S(1)} %fusion.30), kind=kOutput, calls=%fused_computation.4 | convolution fusion | flops 69369856 | bytes 786944 | tf_op jit(solution)/shard_map/dot_general | solution.py:70
  17.3 3.8 %collective-permute-start.6 = (bf16[128,1152]{1,0:T(8,128)(2,1)S(1)}, bf16[128,1152]{1,0:T(8,128)(2,1)S(1)}, u32[]{:S(2)}, u32[]{:S(2)}) collective-permute-start(bf16[128,1152]{1,0:T(8,128)(2,1)S(1)} %pad_maximum_fusion.1), channel_id=1, source_target_pairs={{0,1},{1,2},{2,3},{4,5},{5,6},{6,7},{8,9},{9,10},{10,11},{12,13},{... | collective-permute-start | bytes 884744 | tf_op jit(solution)/shard_map/ppermute | solution.py:232
  21.1 4.5 %collective-permute-start.7 = (bf16[128,1152]{1,0:T(8,128)(2,1)S(1)}, bf16[128,1152]{1,0:T(8,128)(2,1)S(1)}, u32[]{:S(2)}, u32[]{:S(2)}) collective-permute-start(bf16[128,1152]{1,0:T(8,128)(2,1)S(1)} %pad_maximum_fusion.1), channel_id=1, source_target_pairs={{0,2},{1,3},{4,6},{5,7},{8,10},{9,11},{12,14},{13,15},{16,18},{17,... | collective-permute-start | bytes 884744 | tf_op jit(solution)/shard_map/ppermute | solution.py:232
  26.3 2.1 %collective-permute-done.6 = bf16[128,1152]{1,0:T(8,128)(2,1)S(1)} collective-permute-done((bf16[128,1152]{1,0:T(8,128)(2,1)S(1)}, bf16[128,1152]{1,0:T(8,128)(2,1)S(1)}, u32[]{:S(2)}, u32[]{:S(2)}) %collective-permute-start.6) | collective-permute-done | bytes 294944 | tf_op jit(solution)/shard_map/ppermute | solution.py:232
  28.4 5.3 %collective-permute-done.7 = bf16[128,1152]{1,0:T(8,128)(2,1)S(1)} collective-permute-done((bf16[128,1152]{1,0:T(8,128)(2,1)S(1)}, bf16[128,1152]{1,0:T(8,128)(2,1)S(1)}, u32[]{:S(2)}, u32[]{:S(2)}) %collective-permute-start.7) | collective-permute-done | bytes 294944 | tf_op jit(solution)/shard_map/ppermute | solution.py:232
  34.0 0.9 %and_select_fusion.refs_7_ = f32[384,128]{1,0:T(8,128)} fusion(s32[128]{0:T(128)S(1)} %iota_add_fusion, s32[128]{0:T(128)S(1)} %bitcast.27, s32[384]{0:T(512)S(1)} %fusion.21, s32[384]{0:T(512)S(1)} %convert_reduce_fusion, pred[384]{0:T(512)(128)(4,1)S(1)} %broadcast_compare_fusion), kind=kLoop, calls=%fused_computation.21 | loop fusion | flops 245760 | bytes 201088 | tf_op jit(solution)/shard_map/jit(_where)/select_n | solution.py:256
  34.9 1.5 %collective-permute-done.2.refs_3_ = bf16[64,4096]{1,0:T(8,128)(2,1)S(1)} collective-permute-done((bf16[64,4096]{1,0:T(8,128)(2,1)S(1)}, bf16[64,4096]{1,0:T(8,128)(2,1)S(1)}, u32[]{:S(2)}, u32[]{:S(2)}) %collective-permute-start.2) | collective-permute-done | bytes 524320 | tf_op jit(solution)/shard_map/ppermute | solution.py:57
  37.2 10.1 %shard_map.77 = (bf16[128,2048]{1,0:T(8,128)(2,1)}, f32[128,512]{1,0:T(8,128)}, bf16[128,512]{1,0:T(8,128)(2,1)}, bf16[128,512]{1,0:T(8,128)(2,1)}) custom-call(bf16[64,4096]{1,0:T(8,128)(2,1)} %get-tuple-element.23.refs_0_, bf16[64,4096]{1,0:T(8,128)(2,1)} %copy-done.1, bf16[64,4096]{1,0:T(8,128)(2,1)} %copy-done.2, bf16[64,4096]{1,0:T(8,128)(2,1)} %copy-done.3, ...), custom_call_target="tpu_custom_call" | custom-call | flops 1006632960 | bytes 2654208 | tf_op jit(solution)/shard_map/pallas_call | solution.py:190
  47.3 1.3 %collective-permute-start.8 = (bf16[128,512]{1,0:T(8,128)(2,1)}, bf16[128,512]{1,0:T(8,128)(2,1)S(1)}, u32[]{:S(2)}, u32[]{:S(2)}) collective-permute-start(bf16[128,512]{1,0:T(8,128)(2,1)} %get-tuple-element.13), channel_id=1, source_target_pairs={{1,0},{2,1},{3,2},{5,4},{6,5},{7,6},{9,8},{10,9},{11,10},{13,12},{... | collective-permute-start | bytes 393224 | tf_op jit(solution)/shard_map/ppermute | solution.py:264
  48.6 1.6 %collective-permute-start.9 = (bf16[128,512]{1,0:T(8,128)(2,1)}, bf16[128,512]{1,0:T(8,128)(2,1)S(1)}, u32[]{:S(2)}, u32[]{:S(2)}) collective-permute-start(bf16[128,512]{1,0:T(8,128)(2,1)} %get-tuple-element.14), channel_id=1, source_target_pairs={{2,0},{3,1},{6,4},{7,5},{10,8},{11,9},{14,12},{15,13},{18,16},{19,... | collective-permute-start | bytes 393224 | tf_op jit(solution)/shard_map/ppermute | solution.py:264
  50.2 10.1 %shard_map.78 = (bf16[128,2048]{1,0:T(8,128)(2,1)}, f32[128,512]{1,0:T(8,128)}, bf16[128,512]{1,0:T(8,128)(2,1)}, bf16[128,512]{1,0:T(8,128)(2,1)}) custom-call(bf16[64,4096]{1,0:T(8,128)(2,1)} %get-tuple-element.23.refs_0_, bf16[64,4096]{1,0:T(8,128)(2,1)} %copy-done.1, bf16[64,4096]{1,0:T(8,128)(2,1)} %copy-done.2, bf16[64,4096]{1,0:T(8,128)(2,1)} %copy-done.3, ...), custom_call_target="tpu_custom_call" | custom-call | flops 1006632960 | bytes 2654208 | tf_op jit(solution)/shard_map/pallas_call | solution.py:190
  60.3 1.4 %collective-permute-start.10 = (bf16[128,512]{1,0:T(8,128)(2,1)}, bf16[128,512]{1,0:T(8,128)(2,1)S(1)}, u32[]{:S(2)}, u32[]{:S(2)}) collective-permute-start(bf16[128,512]{1,0:T(8,128)(2,1)} %get-tuple-element.16), channel_id=1, source_target_pairs={{1,0},{2,1},{3,2},{5,4},{6,5},{7,6},{9,8},{10,9},{11,10},{13,12},{... | collective-permute-start | bytes 393224 | tf_op jit(solution)/shard_map/ppermute | solution.py:264
  61.7 1.3 %collective-permute-start.11 = (bf16[128,512]{1,0:T(8,128)(2,1)}, bf16[128,512]{1,0:T(8,128)(2,1)S(1)}, u32[]{:S(2)}, u32[]{:S(2)}) collective-permute-start(bf16[128,512]{1,0:T(8,128)(2,1)} %get-tuple-element.17), channel_id=1, source_target_pairs={{2,0},{3,1},{6,4},{7,5},{10,8},{11,9},{14,12},{15,13},{18,16},{19,... | collective-permute-start | bytes 393224 | tf_op jit(solution)/shard_map/ppermute | solution.py:264
  63.0 2.1 %maximum_bitcast_fusion = bf16[1,128,4096]{2,1,0:T(8,128)(2,1)} fusion(bf16[128,2048]{1,0:T(8,128)(2,1)} %get-tuple-element.11, bf16[128,2048]{1,0:T(8,128)(2,1)S(1)} %copy-done.6), kind=kLoop, calls=%fused_computation.5 | loop fusion | flops 2097152 | bytes 2097152 | tf_op jit(solution)/shard_map/reshape | solution.py:271
  65.7 8.1 %collective-permute-done.10 = bf16[128,512]{1,0:T(8,128)(2,1)S(1)} collective-permute-done((bf16[128,512]{1,0:T(8,128)(2,1)}, bf16[128,512]{1,0:T(8,128)(2,1)S(1)}, u32[]{:S(2)}, u32[]{:S(2)}) %collective-permute-start.10) | collective-permute-done | bytes 131104 | tf_op jit(solution)/shard_map/ppermute | solution.py:264
  73.8 5.5 %collective-permute-done.11 = bf16[128,512]{1,0:T(8,128)(2,1)S(1)} collective-permute-done((bf16[128,512]{1,0:T(8,128)(2,1)}, bf16[128,512]{1,0:T(8,128)(2,1)S(1)}, u32[]{:S(2)}, u32[]{:S(2)}) %collective-permute-start.11) | collective-permute-done | bytes 131104 | tf_op jit(solution)/shard_map/ppermute | solution.py:264
  (68 shorter events, 7.6 us)
Async XLA Ops:
  0.6 8.4 %copy-start.4 = (bf16[128,5120]{1,0:T(8,128)(2,1)S(1)}, bf16[128,5120]{1,0:T(8,128)(2,1)}, u32[]{:S(2)}) copy-start(bf16[128,5120]{1,0:T(8,128)(2,1)} %param.6) | copy-start | bytes 3932164
  4.6 9.8 %collective-permute-start.3 = (bf16[64,1024]{1,0:T(8,128)(2,1)}, bf16[64,1024]{1,0:T(8,128)(2,1)}, u32[]{:S(2)}, u32[]{:S(2)}) collective-permute-start(bf16[64,1024]{1,0:T(8,128)(2,1)} %get-tuple-element.27), channel_id=1, source_target_pairs={{0,4},{4,8},{8,12},{12,0},{1,5},{5,9},{9,13},{13,1},{2,6},{6,10},{... | collective-permute-start | bytes 393224 | tf_op jit(solution)/shard_map/ppermute | solution.py:57
  5.1 10.8 %collective-permute-start.4 = (bf16[64,1024]{1,0:T(8,128)(2,1)}, bf16[64,1024]{1,0:T(8,128)(2,1)}, u32[]{:S(2)}, u32[]{:S(2)}) collective-permute-start(bf16[64,1024]{1,0:T(8,128)(2,1)} %get-tuple-element.26), channel_id=1, source_target_pairs={{0,8},{4,12},{8,0},{12,4},{1,9},{5,13},{9,1},{13,5},{2,10},{6,14},... | collective-permute-start | bytes 393224 | tf_op jit(solution)/shard_map/ppermute | solution.py:57
  7.6 8.3 %collective-permute-start.5 = (bf16[64,1024]{1,0:T(8,128)(2,1)}, bf16[64,1024]{1,0:T(8,128)(2,1)}, u32[]{:S(2)}, u32[]{:S(2)}) collective-permute-start(bf16[64,1024]{1,0:T(8,128)(2,1)} %get-tuple-element.25), channel_id=1, source_target_pairs={{0,12},{4,0},{8,4},{12,8},{1,13},{5,1},{9,5},{13,9},{2,14},{6,2},{... | collective-permute-start | bytes 393224 | tf_op jit(solution)/shard_map/ppermute | solution.py:57
  9.8 3.0 %copy-start.10 = (s32[1,128]{1,0:T(1,128)S(1)}, s32[1,128]{1,0:T(1,128)}, u32[]{:S(2)}) copy-start(s32[1,128]{1,0:T(1,128)} %param.8) | copy-start | bytes 1540
  9.8 3.0 %copy-start.12 = (s32[16]{0:T(128)S(1)}, s32[16]{0:T(128)}, u32[]{:S(2)}) copy-start(s32[16]{0:T(128)} %param.10) | copy-start | bytes 196
  9.8 3.0 %copy-start.11 = (s32[16]{0:T(128)S(1)}, s32[16]{0:T(128)}, u32[]{:S(2)}) copy-start(s32[16]{0:T(128)} %param.11) | copy-start | bytes 196
  9.8 3.4 %copy-start.5 = (bf16[1,128,4096]{2,1,0:T(8,128)(2,1)S(1)}, bf16[1,128,4096]{2,1,0:T(8,128)(2,1)}, u32[]{:S(2)}) copy-start(bf16[1,128,4096]{2,1,0:T(8,128)(2,1)} %param.9) | copy-start | bytes 3145732
  11.0 4.9 %copy-start.9 = (bf16[64,1024]{1,0:T(8,128)(2,1)S(1)}, bf16[64,1024]{1,0:T(8,128)(2,1)}, u32[]{:S(2)}) copy-start(bf16[64,1024]{1,0:T(8,128)(2,1)} %get-tuple-element.24) | copy-start | bytes 393220
  11.0 23.9 %collective-permute-start = (bf16[64,4096]{1,0:T(8,128)(2,1)}, bf16[64,4096]{1,0:T(8,128)(2,1)S(1)}, u32[]{:S(2)}, u32[]{:S(2)}) collective-permute-start(bf16[64,4096]{1,0:T(8,128)(2,1)} %get-tuple-element.22), channel_id=1, source_target_pairs={{0,4},{4,8},{8,12},{12,0},{1,5},{5,9},{9,13},{13,1},{2,6},{6,10},{... | collective-permute-start | bytes 1572872 | tf_op jit(solution)/shard_map/ppermute | solution.py:57
  11.0 23.9 %collective-permute-start.1 = (bf16[64,4096]{1,0:T(8,128)(2,1)}, bf16[64,4096]{1,0:T(8,128)(2,1)S(1)}, u32[]{:S(2)}, u32[]{:S(2)}) collective-permute-start(bf16[64,4096]{1,0:T(8,128)(2,1)} %get-tuple-element.21), channel_id=1, source_target_pairs={{0,8},{4,12},{8,0},{12,4},{1,9},{5,13},{9,1},{13,5},{2,10},{6,14},... | collective-permute-start | bytes 1572872 | tf_op jit(solution)/shard_map/ppermute | solution.py:57
  14.5 21.9 %collective-permute-start.2 = (bf16[64,4096]{1,0:T(8,128)(2,1)S(1)}, bf16[64,4096]{1,0:T(8,128)(2,1)S(1)}, u32[]{:S(2)}, u32[]{:S(2)}) collective-permute-start(bf16[64,4096]{1,0:T(8,128)(2,1)S(1)} %get-tuple-element.20), channel_id=1, source_target_pairs={{0,12},{4,0},{8,4},{12,8},{1,13},{5,1},{9,5},{13,9},{2,14},{6,2},{... | collective-permute-start | bytes 1572872 | tf_op jit(solution)/shard_map/ppermute | solution.py:57
  17.3 11.1 %collective-permute-start.6 = (bf16[128,1152]{1,0:T(8,128)(2,1)S(1)}, bf16[128,1152]{1,0:T(8,128)(2,1)S(1)}, u32[]{:S(2)}, u32[]{:S(2)}) collective-permute-start(bf16[128,1152]{1,0:T(8,128)(2,1)S(1)} %pad_maximum_fusion.1), channel_id=1, source_target_pairs={{0,1},{1,2},{2,3},{4,5},{5,6},{6,7},{8,9},{9,10},{10,11},{12,13},{... | collective-permute-start | bytes 884744 | tf_op jit(solution)/shard_map/ppermute | solution.py:232
  21.1 12.7 %collective-permute-start.7 = (bf16[128,1152]{1,0:T(8,128)(2,1)S(1)}, bf16[128,1152]{1,0:T(8,128)(2,1)S(1)}, u32[]{:S(2)}, u32[]{:S(2)}) collective-permute-start(bf16[128,1152]{1,0:T(8,128)(2,1)S(1)} %pad_maximum_fusion.1), channel_id=1, source_target_pairs={{0,2},{1,3},{4,6},{5,7},{8,10},{9,11},{12,14},{13,15},{16,18},{17,... | collective-permute-start | bytes 884744 | tf_op jit(solution)/shard_map/ppermute | solution.py:232
  33.8 2.6 %copy-start = (bf16[384,1152]{1,0:T(8,128)(2,1)}, bf16[384,1152]{1,0:T(8,128)(2,1)S(1)}, u32[]{:S(2)}) copy-start(bf16[384,1152]{1,0:T(8,128)(2,1)S(1)} %pad_maximum_fusion.refs_6_) | copy-start | bytes 2654212
  34.9 1.5 %copy-start.1 = (bf16[64,4096]{1,0:T(8,128)(2,1)}, bf16[64,4096]{1,0:T(8,128)(2,1)S(1)}, u32[]{:S(2)}) copy-start(bf16[64,4096]{1,0:T(8,128)(2,1)S(1)} %collective-permute-done.refs_1_) | copy-start | bytes 1572868
  34.9 1.5 %copy-start.2 = (bf16[64,4096]{1,0:T(8,128)(2,1)}, bf16[64,4096]{1,0:T(8,128)(2,1)S(1)}, u32[]{:S(2)}) copy-start(bf16[64,4096]{1,0:T(8,128)(2,1)S(1)} %collective-permute-done.1.refs_2_) | copy-start | bytes 1572868
  47.3 17.8 %collective-permute-start.8 = (bf16[128,512]{1,0:T(8,128)(2,1)}, bf16[128,512]{1,0:T(8,128)(2,1)S(1)}, u32[]{:S(2)}, u32[]{:S(2)}) collective-permute-start(bf16[128,512]{1,0:T(8,128)(2,1)} %get-tuple-element.13), channel_id=1, source_target_pairs={{1,0},{2,1},{3,2},{5,4},{6,5},{7,6},{9,8},{10,9},{11,10},{13,12},{... | collective-permute-start | bytes 393224 | tf_op jit(solution)/shard_map/ppermute | solution.py:264
  48.6 14.4 %copy-start.6 = (bf16[128,2048]{1,0:T(8,128)(2,1)S(1)}, bf16[128,2048]{1,0:T(8,128)(2,1)}, u32[]{:S(2)}) copy-start(bf16[128,2048]{1,0:T(8,128)(2,1)} %get-tuple-element.10) | copy-start | bytes 1572868
  48.6 17.0 %collective-permute-start.9 = (bf16[128,512]{1,0:T(8,128)(2,1)}, bf16[128,512]{1,0:T(8,128)(2,1)S(1)}, u32[]{:S(2)}, u32[]{:S(2)}) collective-permute-start(bf16[128,512]{1,0:T(8,128)(2,1)} %get-tuple-element.14), channel_id=1, source_target_pairs={{2,0},{3,1},{6,4},{7,5},{10,8},{11,9},{14,12},{15,13},{18,16},{19,... | collective-permute-start | bytes 393224 | tf_op jit(solution)/shard_map/ppermute | solution.py:264
  60.3 5.3 %copy-start.8 = (f32[128,512]{1,0:T(8,128)S(1)}, f32[128,512]{1,0:T(8,128)}, u32[]{:S(2)}) copy-start(f32[128,512]{1,0:T(8,128)} %get-tuple-element.12) | copy-start | bytes 786436
  60.3 19.0 %copy-start.7 = (f32[128,512]{1,0:T(8,128)S(1)}, f32[128,512]{1,0:T(8,128)}, u32[]{:S(2)}) copy-start(f32[128,512]{1,0:T(8,128)} %get-tuple-element.15) | copy-start | bytes 786436
  60.3 13.5 %collective-permute-start.10 = (bf16[128,512]{1,0:T(8,128)(2,1)}, bf16[128,512]{1,0:T(8,128)(2,1)S(1)}, u32[]{:S(2)}, u32[]{:S(2)}) collective-permute-start(bf16[128,512]{1,0:T(8,128)(2,1)} %get-tuple-element.16), channel_id=1, source_target_pairs={{1,0},{2,1},{3,2},{5,4},{6,5},{7,6},{9,8},{10,9},{11,10},{13,12},{... | collective-permute-start | bytes 393224 | tf_op jit(solution)/shard_map/ppermute | solution.py:264
  61.7 17.6 %collective-permute-start.11 = (bf16[128,512]{1,0:T(8,128)(2,1)}, bf16[128,512]{1,0:T(8,128)(2,1)S(1)}, u32[]{:S(2)}, u32[]{:S(2)}) collective-permute-start(bf16[128,512]{1,0:T(8,128)(2,1)} %get-tuple-element.17), channel_id=1, source_target_pairs={{2,0},{3,1},{6,4},{7,5},{10,8},{11,9},{14,12},{15,13},{18,16},{19,... | collective-permute-start | bytes 393224 | tf_op jit(solution)/shard_map/ppermute | solution.py:264
  (1 other events, 0.8 us)

commit v18 on v17

--- a/solution.py
+++ b/solution.py
@@ -76,11 +76,11 @@
     return packed_q, packed_kv
 
 
-def attend_kernel(*refs, first_group, chunks, reach):
+def attend_kernel(*refs, first_group, chunks, reach, fold):
     chunk_refs = refs[:chunks]
-    pick_ref, g_ref, kv_ref, m_ref, dq_ref, local_ref = refs[chunks : chunks + 6]
-    send_refs = refs[chunks + 6 : chunks + 6 + reach]
-    q_ref = refs[chunks + 6 + reach]
+    pick_ref, g_ref, kv_ref, key_info, query_info, dq_ref, local_ref = refs[chunks : chunks + 7]
+    send_refs = refs[chunks + 7 : chunks + 7 + reach]
+    q_ref = refs[chunks + 7 + reach]
     capacity = chunk_refs[0].shape[0]
     picked = jnp.dot(
         pick_ref[:, :capacity], chunk_refs[0][...], preferred_element_type=jnp.float32
@@ -96,8 +96,12 @@
     token_rows = q_ref.shape[0]
     groups = local_ref.shape[1] // (2 * HEAD_SIZE)
     query_group = QUERY_HEADS // KEY_VALUE_HEADS
-    bias = m_ref[...]
-    fold = len(send_refs) > 0 and bias.shape[0] == (len(send_refs) + 1) * token_rows
+    key_seg = key_info[:, 0:1]
+    key_pos = key_info[:, 1:2]
+    allowed = (
+        (key_seg == query_info[0:1, :]) & (key_pos <= query_info[1:2, :]) & (key_pos >= 0.0)
+    )
+    bias = jnp.where(allowed, 0.0, -1e30).astype(jnp.float32)
     if fold:
         far = len(send_refs) * token_rows
         lower = (
@@ -176,7 +180,7 @@
             send_ref[:, value_cols] = value_sum[rows].astype(send_ref.dtype)
 
 
-def attend_pallas(q_chunks, q_pick, weighted, kv_all, bias, part, groups):
+def attend_pallas(q_chunks, q_pick, weighted, kv_all, key_info, query_info, part, groups, fold):
     token_rows = weighted.shape[0]
     capacity = q_chunks[0].shape[0]
     key_rows = kv_all.shape[0]
@@ -185,17 +189,20 @@
     kv_width = 2 * groups * HEAD_SIZE
     heads = groups * (QUERY_HEADS // KEY_VALUE_HEADS)
     flops = 10 * token_rows * key_rows * HEAD_SIZE * heads
-    bytes_accessed = 6 * token_rows * part_width + 2 * key_rows * kv_all.shape[1] + 4 * token_rows * key_rows
+    bytes_accessed = 6 * token_rows * part_width + 2 * key_rows * kv_all.shape[1] + 8 * (token_rows + key_rows)
     whole = lambda i: (0, 0)
     return pl.pallas_call(
-        functools.partial(attend_kernel, first_group=part * groups, chunks=len(q_chunks), reach=reach),
+        functools.partial(
+            attend_kernel, first_group=part * groups, chunks=len(q_chunks), reach=reach, fold=fold
+        ),
         grid=(1,),
         in_specs=[pl.BlockSpec((capacity, part_width), lambda i: (0, part)) for _ in q_chunks]
         + [
             pl.BlockSpec(q_pick.shape, whole),
             pl.BlockSpec((token_rows, part_width), lambda i: (0, part)),
             pl.BlockSpec(kv_all.shape, whole),
-            pl.BlockSpec(bias.shape, whole),
+            pl.BlockSpec(key_info.shape, whole),
+            pl.BlockSpec(query_info.shape, whole),
         ],
         out_specs=[
             pl.BlockSpec((token_rows, part_width), whole)
@@ -210,7 +217,7 @@
             flops=flops, transcendentals=token_rows * key_rows * heads, bytes_accessed=bytes_accessed
         ),
         scratch_shapes=[pltpu.VMEM((token_rows, part_width), jnp.bfloat16)],
-    )(*q_chunks, q_pick, weighted, kv_all, bias)
+    )(*q_chunks, q_pick, weighted, kv_all, key_info, query_info)
 
 
 def step(rollout_rows, routing, segment_labels, upstream, passes, group_ids):
@@ -223,6 +230,7 @@
     longest_segment = sp_size * token_rows // 2
     reach = min(sp_size - 1, (longest_segment + token_rows - 2) // token_rows)
     seq_len = (reach + 1) * token_rows
+    fold = reach > 0 and longest_segment == reach * token_rows
 
     packed_q, packed_kv = exchange_rows(rollout_rows, routing, dp_size, sp_size, dp_index, sp_index)
     own_seg = segment_labels[0]
@@ -248,17 +256,13 @@
     query_pos = sp_index * token_rows + jnp.arange(token_rows, dtype=jnp.int32)
     rel_block = jnp.arange(seq_len, dtype=jnp.int32) // token_rows
     key_pos = (sp_index - rel_block) * token_rows + jnp.arange(seq_len, dtype=jnp.int32) % token_rows
-    allowed = (
-        (own_seg[:, None] == key_seg[None, :])
-        & (key_pos[None, :] <= query_pos[:, None])
-        & (key_pos[None, :] >= 0)
-    )
-    bias = jnp.where(allowed.T, 0.0, -1e30).astype(jnp.float32)
+    key_info = jnp.stack([key_seg, key_pos], axis=1).astype(jnp.float32)
+    query_info = jnp.stack([own_seg, query_pos], axis=0).astype(jnp.float32)
     groups = KEY_VALUE_HEADS // 2
     query_parts, key_parts, value_parts = [], [], []
     for part in range(2):
         query_grad, total, *outgoing = attend_pallas(
-            *packed_q, weighted, kv_all, bias, part, groups
+            *packed_q, weighted, kv_all, key_info, query_info, part, groups, fold
         )
         for shift in range(1, reach + 1):
             arrived = lax.ppermute(

time: 80.6 us -> 81.3 us (level)
    convert_element_type x0 -> x2, other arithmetic: none -> 1.29 us  [the longest x1 0.7 us: step(): key_info = jnp.stack([key_seg, key_pos], axis=1).astype(jnp.float32)]
    select_n x1 -> x0, other arithmetic: 0.9 us -> none  [step(): bias = jnp.where(allowed.T, 0.0, -1e+30).astype(jnp.float32)]
where the time goes in v18:
time: 81.3 us; the launch traced here: 80.9 us
  waiting for transfers between devices  23.2 us (29%)
  Pallas kernels  20.3 us (25%)
  starting transfers between devices  20 us (25%)
  other arithmetic  9.1 us (11%)
  local copies, waits for them, and re-layouts  4.07 us (5%)
  matrix products  3.23 us (4%)
  between operations  0.93 us (1%)
    pallas_call x2, Pallas kernels, attend_pallas(): pl.pallas_call(functools.partial(attend_kernel, first_group=part * groups...  20.3 us
    ppermute x4, waiting for transfers between devices, step(): lax.ppermute(outgoing[shift - 1], 'sp', [(k, k - shift) for k in range(sh...  14.7 us
    ppermute x2, starting transfers between devices, step(): lax.ppermute(kv_local, 'sp', [(k, k + shift) for k in range(sp_size - shi...  8.25 us
    ppermute x2, waiting for transfers between devices, step(): lax.ppermute(kv_local, 'sp', [(k, k + shift) for k in range(sp_size - shi...  7.53 us
    ppermute x6, starting transfers between devices, send(): lax.ppermute(outgoing[shift], 'dp', [(k, (k + shift) % dp_size) for k in...  6.18 us
    ppermute x4, starting transfers between devices, step(): lax.ppermute(outgoing[shift - 1], 'sp', [(k, k - shift) for k in range(sh...  5.6 us
    reshape x1, other arithmetic, step(): jnp.concatenate(query_parts, axis=1)  2.09 us
    dot_general x2, matrix products, send(): jnp.dot(send_pick, columns, preferred_element_type=jnp.float32)  1.93 us
  transfers between devices with their start and end apart: 12, of which 6 were waited for; matrix products, arithmetic and copies ran while one was open for 13% of the time, Pallas kernels for 13%

profile of v18, /device:TPU:0, one launch (start us, length us, event | category | flops | bytes accessed | tf_op | source)
XLA Modules:
  0.0 80.9 jit_solution(6644091665563391788)
XLA Ops:
  2.6 1.2 %convolution_convert_fusion.1 = bf16[256,1024]{1,0:T(8,128)(2,1)S(1)} fusion(bf16[128,5120]{1,0:T(8,128)(2,1)} %param.6, s32[128]{0:T(128)S(1)} %fusion.20), kind=kOutput, calls=%fused_computation.3 | convolution fusion | flops 67403776 | bytes 786944 | tf_op jit(solution)/shard_map/dot_general | solution.py:52
  3.8 0.8 %fusion.29 = (bf16[64,1024]{1,0:T(8,128)(2,1)}, bf16[64,1024]{1,0:T(8,128)(2,1)}, bf16[64,1024]{1,0:T(8,128)(2,1)}, bf16[64,1024]{1,0:T(8,128)(2,1)}) fusion(bf16[256,1024]{1,0:T(8,128)(2,1)S(1)} %convolution_convert_fusion.1), kind=kLoop, calls=%fused_computation.76 | loop fusion | bytes 1048576 | tf_op jit(solution)/shard_map/slice | solution.py:56
  5.1 2.5 %collective-permute-start.4 = (bf16[64,1024]{1,0:T(8,128)(2,1)}, bf16[64,1024]{1,0:T(8,128)(2,1)}, u32[]{:S(2)}, u32[]{:S(2)}) collective-permute-start(bf16[64,1024]{1,0:T(8,128)(2,1)} %get-tuple-element.26), channel_id=1, source_target_pairs={{0,8},{4,12},{8,0},{12,4},{1,9},{5,13},{9,1},{13,5},{2,10},{6,14},... | collective-permute-start | bytes 393224 | tf_op jit(solution)/shard_map/ppermute | solution.py:57
  7.6 1.5 %collective-permute-start.5 = (bf16[64,1024]{1,0:T(8,128)(2,1)}, bf16[64,1024]{1,0:T(8,128)(2,1)}, u32[]{:S(2)}, u32[]{:S(2)}) collective-permute-start(bf16[64,1024]{1,0:T(8,128)(2,1)} %get-tuple-element.25), channel_id=1, source_target_pairs={{0,12},{4,0},{8,4},{12,8},{1,13},{5,1},{9,5},{13,9},{2,14},{6,2},{... | collective-permute-start | bytes 393224 | tf_op jit(solution)/shard_map/ppermute | solution.py:57
  9.8 1.2 %fusion.28 = (bf16[64,4096]{1,0:T(8,128)(2,1)S(1)}, bf16[64,4096]{1,0:T(8,128)(2,1)}, bf16[64,4096]{1,0:T(8,128)(2,1)}, bf16[64,4096]{1,0:T(8,128)(2,1)}) fusion(bf16[256,4096]{1,0:T(8,128)(2,1)S(1)} %convolution_convert_fusion), kind=kLoop, calls=%fused_computation.75 | loop fusion | bytes 4194304 | tf_op jit(solution)/shard_map/slice | solution.py:58
  11.4 0.9 %fusion.15 = s32[4]{0:T(128)S(1)} fusion(s32[4,4,128]{2,1,0:T(4,128)} %bitcast.25, s32[]{:T(128)S(6)} %select_n.73, s32[]{:T(128)S(6)} %axis_index.23), kind=kLoop, calls=%fused_computation.46 | loop fusion | flops 1532 | bytes 2072 | tf_op jit(solution)/shard_map/reduce_sum | solution.py:38
  13.9 1.2 %fusion.refs_5_ = bf16[128,4096]{1,0:T(8,128)(2,1)} fusion(bf16[1,128,4096]{2,1,0:T(8,128)(2,1)S(1)} %copy-done.5, f32[128]{0:T(128)S(1)} %select_reduce_fusion.2), kind=kLoop, calls=%fused_computation.2 | loop fusion | flops 1572864 | bytes 2097664 | tf_op jit(solution)/shard_map/convert_element_type | solution.py:254
  15.2 1.4 %collective-permute-start.2 = (bf16[64,4096]{1,0:T(8,128)(2,1)S(1)}, bf16[64,4096]{1,0:T(8,128)(2,1)S(1)}, u32[]{:S(2)}, u32[]{:S(2)}) collective-permute-start(bf16[64,4096]{1,0:T(8,128)(2,1)S(1)} %get-tuple-element.20), channel_id=1, source_target_pairs={{0,12},{4,0},{8,4},{12,8},{1,13},{5,1},{9,5},{13,9},{2,14},{6,2},{... | collective-permute-start | bytes 1572872 | tf_op jit(solution)/shard_map/ppermute | solution.py:57
  16.5 1.3 %convolution_convert_fusion.2 = bf16[128,1024]{1,0:T(8,128)(2,1)S(1)} fusion(bf16[64,1024]{1,0:T(8,128)(2,1)} %collective-permute-done.5, bf16[64,1024]{1,0:T(8,128)(2,1)} %collective-permute-done.4, bf16[64,1024]{1,0:T(8,128)(2,1)} %collective-permute-done.3, bf16[64,1024]{1,0:T(8,128)(2,1)S(1)} %copy-done.9, s32[128]{0:T(128)S(1)} %fusion.23), kind=kOutput, calls=%fused_computation.4 | convolution fusion | flops 69369856 | bytes 786944 | tf_op jit(solution)/shard_map/dot_general | solution.py:70
  18.0 3.7 %collective-permute-start.6 = (bf16[128,1152]{1,0:T(8,128)(2,1)S(1)}, bf16[128,1152]{1,0:T(8,128)(2,1)S(1)}, u32[]{:S(2)}, u32[]{:S(2)}) collective-permute-start(bf16[128,1152]{1,0:T(8,128)(2,1)S(1)} %pad_maximum_fusion.1), channel_id=1, source_target_pairs={{0,1},{1,2},{2,3},{4,5},{5,6},{6,7},{8,9},{9,10},{10,11},{12,13},{... | collective-permute-start | bytes 884744 | tf_op jit(solution)/shard_map/ppermute | solution.py:240
  21.7 4.5 %collective-permute-start.7 = (bf16[128,1152]{1,0:T(8,128)(2,1)S(1)}, bf16[128,1152]{1,0:T(8,128)(2,1)S(1)}, u32[]{:S(2)}, u32[]{:S(2)}) collective-permute-start(bf16[128,1152]{1,0:T(8,128)(2,1)S(1)} %pad_maximum_fusion.1), channel_id=1, source_target_pairs={{0,2},{1,3},{4,6},{5,7},{8,10},{9,11},{12,14},{13,15},{16,18},{17,... | collective-permute-start | bytes 884744 | tf_op jit(solution)/shard_map/ppermute | solution.py:240
  26.8 2.2 %collective-permute-done.6 = bf16[128,1152]{1,0:T(8,128)(2,1)S(1)} collective-permute-done((bf16[128,1152]{1,0:T(8,128)(2,1)S(1)}, bf16[128,1152]{1,0:T(8,128)(2,1)S(1)}, u32[]{:S(2)}, u32[]{:S(2)}) %collective-permute-start.6) | collective-permute-done | bytes 294944 | tf_op jit(solution)/shard_map/ppermute | solution.py:240
  29.1 5.3 %collective-permute-done.7 = bf16[128,1152]{1,0:T(8,128)(2,1)S(1)} collective-permute-done((bf16[128,1152]{1,0:T(8,128)(2,1)S(1)}, bf16[128,1152]{1,0:T(8,128)(2,1)S(1)}, u32[]{:S(2)}, u32[]{:S(2)}) %collective-permute-start.7) | collective-permute-done | bytes 294944 | tf_op jit(solution)/shard_map/ppermute | solution.py:240
  35.5 1.0 %collective-permute-done.2.refs_3_ = bf16[64,4096]{1,0:T(8,128)(2,1)S(1)} collective-permute-done((bf16[64,4096]{1,0:T(8,128)(2,1)S(1)}, bf16[64,4096]{1,0:T(8,128)(2,1)S(1)}, u32[]{:S(2)}, u32[]{:S(2)}) %collective-permute-start.2) | collective-permute-done | bytes 524320 | tf_op jit(solution)/shard_map/ppermute | solution.py:57
  37.2 10.2 %shard_map.77 = (bf16[128,2048]{1,0:T(8,128)(2,1)}, f32[128,512]{1,0:T(8,128)}, bf16[128,512]{1,0:T(8,128)(2,1)}, bf16[128,512]{1,0:T(8,128)(2,1)}) custom-call(bf16[64,4096]{1,0:T(8,128)(2,1)} %get-tuple-element.23.refs_0_, bf16[64,4096]{1,0:T(8,128)(2,1)} %copy-done.1, bf16[64,4096]{1,0:T(8,128)(2,1)} %copy-done.2, bf16[64,4096]{1,0:T(8,128)(2,1)} %copy-done.3, ...), custom_call_target="tpu_custom_call" | custom-call | flops 1006632960 | bytes 2461696 | tf_op jit(solution)/shard_map/pallas_call | solution.py:194
  47.4 1.3 %collective-permute-start.8 = (bf16[128,512]{1,0:T(8,128)(2,1)}, bf16[128,512]{1,0:T(8,128)(2,1)S(1)}, u32[]{:S(2)}, u32[]{:S(2)}) collective-permute-start(bf16[128,512]{1,0:T(8,128)(2,1)} %get-tuple-element.13), channel_id=1, source_target_pairs={{1,0},{2,1},{3,2},{5,4},{6,5},{7,6},{9,8},{10,9},{11,10},{13,12},{... | collective-permute-start | bytes 393224 | tf_op jit(solution)/shard_map/ppermute | solution.py:268
  48.7 1.6 %collective-permute-start.9 = (bf16[128,512]{1,0:T(8,128)(2,1)}, bf16[128,512]{1,0:T(8,128)(2,1)S(1)}, u32[]{:S(2)}, u32[]{:S(2)}) collective-permute-start(bf16[128,512]{1,0:T(8,128)(2,1)} %get-tuple-element.14), channel_id=1, source_target_pairs={{2,0},{3,1},{6,4},{7,5},{10,8},{11,9},{14,12},{15,13},{18,16},{19,... | collective-permute-start | bytes 393224 | tf_op jit(solution)/shard_map/ppermute | solution.py:268
  50.3 10.2 %shard_map.78 = (bf16[128,2048]{1,0:T(8,128)(2,1)}, f32[128,512]{1,0:T(8,128)}, bf16[128,512]{1,0:T(8,128)(2,1)}, bf16[128,512]{1,0:T(8,128)(2,1)}) custom-call(bf16[64,4096]{1,0:T(8,128)(2,1)} %get-tuple-element.23.refs_0_, bf16[64,4096]{1,0:T(8,128)(2,1)} %copy-done.1, bf16[64,4096]{1,0:T(8,128)(2,1)} %copy-done.2, bf16[64,4096]{1,0:T(8,128)(2,1)} %copy-done.3, ...), custom_call_target="tpu_custom_call" | custom-call | flops 1006632960 | bytes 2461696 | tf_op jit(solution)/shard_map/pallas_call | solution.py:194
  60.5 1.4 %collective-permute-start.10 = (bf16[128,512]{1,0:T(8,128)(2,1)}, bf16[128,512]{1,0:T(8,128)(2,1)S(1)}, u32[]{:S(2)}, u32[]{:S(2)}) collective-permute-start(bf16[128,512]{1,0:T(8,128)(2,1)} %get-tuple-element.16), channel_id=1, source_target_pairs={{1,0},{2,1},{3,2},{5,4},{6,5},{7,6},{9,8},{10,9},{11,10},{13,12},{... | collective-permute-start | bytes 393224 | tf_op jit(solution)/shard_map/ppermute | solution.py:268
  61.9 1.3 %collective-permute-start.11 = (bf16[128,512]{1,0:T(8,128)(2,1)}, bf16[128,512]{1,0:T(8,128)(2,1)S(1)}, u32[]{:S(2)}, u32[]{:S(2)}) collective-permute-start(bf16[128,512]{1,0:T(8,128)(2,1)} %get-tuple-element.17), channel_id=1, source_target_pairs={{2,0},{3,1},{6,4},{7,5},{10,8},{11,9},{14,12},{15,13},{18,16},{19,... | collective-permute-start | bytes 393224 | tf_op jit(solution)/shard_map/ppermute | solution.py:268
  63.2 2.1 %maximum_bitcast_fusion = bf16[1,128,4096]{2,1,0:T(8,128)(2,1)} fusion(bf16[128,2048]{1,0:T(8,128)(2,1)} %get-tuple-element.11, bf16[128,2048]{1,0:T(8,128)(2,1)S(1)} %copy-done.6), kind=kLoop, calls=%fused_computation.5 | loop fusion | flops 2097152 | bytes 2097152 | tf_op jit(solution)/shard_map/reshape | solution.py:275
  65.3 0.9 %collective-permute-done.9 = bf16[128,512]{1,0:T(8,128)(2,1)S(1)} collective-permute-done((bf16[128,512]{1,0:T(8,128)(2,1)}, bf16[128,512]{1,0:T(8,128)(2,1)S(1)}, u32[]{:S(2)}, u32[]{:S(2)}) %collective-permute-start.9) | collective-permute-done | bytes 131104 | tf_op jit(solution)/shard_map/ppermute | solution.py:268
  66.3 8.2 %collective-permute-done.10 = bf16[128,512]{1,0:T(8,128)(2,1)S(1)} collective-permute-done((bf16[128,512]{1,0:T(8,128)(2,1)}, bf16[128,512]{1,0:T(8,128)(2,1)S(1)}, u32[]{:S(2)}, u32[]{:S(2)}) %collective-permute-start.10) | collective-permute-done | bytes 131104 | tf_op jit(solution)/shard_map/ppermute | solution.py:268
  74.5 5.5 %collective-permute-done.11 = bf16[128,512]{1,0:T(8,128)(2,1)S(1)} collective-permute-done((bf16[128,512]{1,0:T(8,128)(2,1)}, bf16[128,512]{1,0:T(8,128)(2,1)S(1)}, u32[]{:S(2)}, u32[]{:S(2)}) %collective-permute-start.11) | collective-permute-done | bytes 131104 | tf_op jit(solution)/shard_map/ppermute | solution.py:268
  (72 shorter events, 8.6 us)
Async XLA Ops:
  0.6 8.5 %copy-start.4 = (bf16[128,5120]{1,0:T(8,128)(2,1)S(1)}, bf16[128,5120]{1,0:T(8,128)(2,1)}, u32[]{:S(2)}) copy-start(bf16[128,5120]{1,0:T(8,128)(2,1)} %param.6) | copy-start | bytes 3932164
  4.6 10.5 %collective-permute-start.3 = (bf16[64,1024]{1,0:T(8,128)(2,1)}, bf16[64,1024]{1,0:T(8,128)(2,1)}, u32[]{:S(2)}, u32[]{:S(2)}) collective-permute-start(bf16[64,1024]{1,0:T(8,128)(2,1)} %get-tuple-element.27), channel_id=1, source_target_pairs={{0,4},{4,8},{8,12},{12,0},{1,5},{5,9},{9,13},{13,1},{2,6},{6,10},{... | collective-permute-start | bytes 393224 | tf_op jit(solution)/shard_map/ppermute | solution.py:57
  5.1 11.4 %collective-permute-start.4 = (bf16[64,1024]{1,0:T(8,128)(2,1)}, bf16[64,1024]{1,0:T(8,128)(2,1)}, u32[]{:S(2)}, u32[]{:S(2)}) collective-permute-start(bf16[64,1024]{1,0:T(8,128)(2,1)} %get-tuple-element.26), channel_id=1, source_target_pairs={{0,8},{4,12},{8,0},{12,4},{1,9},{5,13},{9,1},{13,5},{2,10},{6,14},... | collective-permute-start | bytes 393224 | tf_op jit(solution)/shard_map/ppermute | solution.py:57
  7.6 8.9 %collective-permute-start.5 = (bf16[64,1024]{1,0:T(8,128)(2,1)}, bf16[64,1024]{1,0:T(8,128)(2,1)}, u32[]{:S(2)}, u32[]{:S(2)}) collective-permute-start(bf16[64,1024]{1,0:T(8,128)(2,1)} %get-tuple-element.25), channel_id=1, source_target_pairs={{0,12},{4,0},{8,4},{12,8},{1,13},{5,1},{9,5},{13,9},{2,14},{6,2},{... | collective-permute-start | bytes 393224 | tf_op jit(solution)/shard_map/ppermute | solution.py:57
  9.8 3.7 %copy-start.12 = (s32[16]{0:T(128)S(1)}, s32[16]{0:T(128)}, u32[]{:S(2)}) copy-start(s32[16]{0:T(128)} %param.10) | copy-start | bytes 196
  9.8 3.7 %copy-start.10 = (s32[16]{0:T(128)S(1)}, s32[16]{0:T(128)}, u32[]{:S(2)}) copy-start(s32[16]{0:T(128)} %param.11) | copy-start | bytes 196
  9.8 4.0 %copy-start.11 = (s32[1,128]{1,0:T(1,128)S(1)}, s32[1,128]{1,0:T(1,128)}, u32[]{:S(2)}) copy-start(s32[1,128]{1,0:T(1,128)} %param.8) | copy-start | bytes 1540
  9.8 4.1 %copy-start.5 = (bf16[1,128,4096]{2,1,0:T(8,128)(2,1)S(1)}, bf16[1,128,4096]{2,1,0:T(8,128)(2,1)}, u32[]{:S(2)}) copy-start(bf16[1,128,4096]{2,1,0:T(8,128)(2,1)} %param.9) | copy-start | bytes 3145732
  11.0 5.5 %copy-start.9 = (bf16[64,1024]{1,0:T(8,128)(2,1)S(1)}, bf16[64,1024]{1,0:T(8,128)(2,1)}, u32[]{:S(2)}) copy-start(bf16[64,1024]{1,0:T(8,128)(2,1)} %get-tuple-element.24) | copy-start | bytes 393220
  11.0 24.4 %collective-permute-start = (bf16[64,4096]{1,0:T(8,128)(2,1)}, bf16[64,4096]{1,0:T(8,128)(2,1)S(1)}, u32[]{:S(2)}, u32[]{:S(2)}) collective-permute-start(bf16[64,4096]{1,0:T(8,128)(2,1)} %get-tuple-element.22), channel_id=1, source_target_pairs={{0,4},{4,8},{8,12},{12,0},{1,5},{5,9},{9,13},{13,1},{2,6},{6,10},{... | collective-permute-start | bytes 1572872 | tf_op jit(solution)/shard_map/ppermute | solution.py:57
  11.0 24.4 %collective-permute-start.1 = (bf16[64,4096]{1,0:T(8,128)(2,1)}, bf16[64,4096]{1,0:T(8,128)(2,1)S(1)}, u32[]{:S(2)}, u32[]{:S(2)}) collective-permute-start(bf16[64,4096]{1,0:T(8,128)(2,1)} %get-tuple-element.21), channel_id=1, source_target_pairs={{0,8},{4,12},{8,0},{12,4},{1,9},{5,13},{9,1},{13,5},{2,10},{6,14},... | collective-permute-start | bytes 1572872 | tf_op jit(solution)/shard_map/ppermute | solution.py:57
  15.2 21.3 %collective-permute-start.2 = (bf16[64,4096]{1,0:T(8,128)(2,1)S(1)}, bf16[64,4096]{1,0:T(8,128)(2,1)S(1)}, u32[]{:S(2)}, u32[]{:S(2)}) collective-permute-start(bf16[64,4096]{1,0:T(8,128)(2,1)S(1)} %get-tuple-element.20), channel_id=1, source_target_pairs={{0,12},{4,0},{8,4},{12,8},{1,13},{5,1},{9,5},{13,9},{2,14},{6,2},{... | collective-permute-start | bytes 1572872 | tf_op jit(solution)/shard_map/ppermute | solution.py:57
  18.0 11.1 %collective-permute-start.6 = (bf16[128,1152]{1,0:T(8,128)(2,1)S(1)}, bf16[128,1152]{1,0:T(8,128)(2,1)S(1)}, u32[]{:S(2)}, u32[]{:S(2)}) collective-permute-start(bf16[128,1152]{1,0:T(8,128)(2,1)S(1)} %pad_maximum_fusion.1), channel_id=1, source_target_pairs={{0,1},{1,2},{2,3},{4,5},{5,6},{6,7},{8,9},{9,10},{10,11},{12,13},{... | collective-permute-start | bytes 884744 | tf_op jit(solution)/shard_map/ppermute | solution.py:240
  21.7 12.6 %collective-permute-start.7 = (bf16[128,1152]{1,0:T(8,128)(2,1)S(1)}, bf16[128,1152]{1,0:T(8,128)(2,1)S(1)}, u32[]{:S(2)}, u32[]{:S(2)}) collective-permute-start(bf16[128,1152]{1,0:T(8,128)(2,1)S(1)} %pad_maximum_fusion.1), channel_id=1, source_target_pairs={{0,2},{1,3},{4,6},{5,7},{8,10},{9,11},{12,14},{13,15},{16,18},{17,... | collective-permute-start | bytes 884744 | tf_op jit(solution)/shard_map/ppermute | solution.py:240
  34.4 2.0 %copy-start = (bf16[384,1152]{1,0:T(8,128)(2,1)}, bf16[384,1152]{1,0:T(8,128)(2,1)S(1)}, u32[]{:S(2)}) copy-start(bf16[384,1152]{1,0:T(8,128)(2,1)S(1)} %pad_maximum_fusion.refs_6_) | copy-start | bytes 2654212
  35.5 1.0 %copy-start.1 = (bf16[64,4096]{1,0:T(8,128)(2,1)}, bf16[64,4096]{1,0:T(8,128)(2,1)S(1)}, u32[]{:S(2)}) copy-start(bf16[64,4096]{1,0:T(8,128)(2,1)S(1)} %collective-permute-done.refs_1_) | copy-start | bytes 1572868
  35.5 1.0 %copy-start.2 = (bf16[64,4096]{1,0:T(8,128)(2,1)}, bf16[64,4096]{1,0:T(8,128)(2,1)S(1)}, u32[]{:S(2)}) copy-start(bf16[64,4096]{1,0:T(8,128)(2,1)S(1)} %collective-permute-done.1.refs_2_) | copy-start | bytes 1572868
  47.4 17.9 %collective-permute-start.8 = (bf16[128,512]{1,0:T(8,128)(2,1)}, bf16[128,512]{1,0:T(8,128)(2,1)S(1)}, u32[]{:S(2)}, u32[]{:S(2)}) collective-permute-start(bf16[128,512]{1,0:T(8,128)(2,1)} %get-tuple-element.13), channel_id=1, source_target_pairs={{1,0},{2,1},{3,2},{5,4},{6,5},{7,6},{9,8},{10,9},{11,10},{13,12},{... | collective-permute-start | bytes 393224 | tf_op jit(solution)/shard_map/ppermute | solution.py:268
  48.7 14.5 %copy-start.6 = (bf16[128,2048]{1,0:T(8,128)(2,1)S(1)}, bf16[128,2048]{1,0:T(8,128)(2,1)}, u32[]{:S(2)}) copy-start(bf16[128,2048]{1,0:T(8,128)(2,1)} %get-tuple-element.10) | copy-start | bytes 1572868
  48.7 17.6 %collective-permute-start.9 = (bf16[128,512]{1,0:T(8,128)(2,1)}, bf16[128,512]{1,0:T(8,128)(2,1)S(1)}, u32[]{:S(2)}, u32[]{:S(2)}) collective-permute-start(bf16[128,512]{1,0:T(8,128)(2,1)} %get-tuple-element.14), channel_id=1, source_target_pairs={{2,0},{3,1},{6,4},{7,5},{10,8},{11,9},{14,12},{15,13},{18,16},{19,... | collective-permute-start | bytes 393224 | tf_op jit(solution)/shard_map/ppermute | solution.py:268
  60.5 5.8 %copy-start.8 = (f32[128,512]{1,0:T(8,128)S(1)}, f32[128,512]{1,0:T(8,128)}, u32[]{:S(2)}) copy-start(f32[128,512]{1,0:T(8,128)} %get-tuple-element.12) | copy-start | bytes 786436
  60.5 19.6 %copy-start.7 = (f32[128,512]{1,0:T(8,128)S(1)}, f32[128,512]{1,0:T(8,128)}, u32[]{:S(2)}) copy-start(f32[128,512]{1,0:T(8,128)} %get-tuple-element.15) | copy-start | bytes 786436
  60.5 14.1 %collective-permute-start.10 = (bf16[128,512]{1,0:T(8,128)(2,1)}, bf16[128,512]{1,0:T(8,128)(2,1)S(1)}, u32[]{:S(2)}, u32[]{:S(2)}) collective-permute-start(bf16[128,512]{1,0:T(8,128)(2,1)} %get-tuple-element.16), channel_id=1, source_target_pairs={{1,0},{2,1},{3,2},{5,4},{6,5},{7,6},{9,8},{10,9},{11,10},{13,12},{... | collective-permute-start | bytes 393224 | tf_op jit(solution)/shard_map/ppermute | solution.py:268
  61.9 18.2 %collective-permute-start.11 = (bf16[128,512]{1,0:T(8,128)(2,1)}, bf16[128,512]{1,0:T(8,128)(2,1)S(1)}, u32[]{:S(2)}, u32[]{:S(2)}) collective-permute-start(bf16[128,512]{1,0:T(8,128)(2,1)} %get-tuple-element.17), channel_id=1, source_target_pairs={{2,0},{3,1},{6,4},{7,5},{10,8},{11,9},{14,12},{15,13},{18,16},{19,... | collective-permute-start | bytes 393224 | tf_op jit(solution)/shard_map/ppermute | solution.py:268
  (1 other events, 0.8 us)

commit v19 on v17

--- a/solution.py
+++ b/solution.py
@@ -76,7 +76,7 @@
     return packed_q, packed_kv
 
 
-def attend_kernel(*refs, first_group, chunks, reach):
+def attend_kernel(*refs, first_group, chunks, reach, fold):
     chunk_refs = refs[:chunks]
     pick_ref, g_ref, kv_ref, m_ref, dq_ref, local_ref = refs[chunks : chunks + 6]
     send_refs = refs[chunks + 6 : chunks + 6 + reach]
@@ -97,7 +97,6 @@
     groups = local_ref.shape[1] // (2 * HEAD_SIZE)
     query_group = QUERY_HEADS // KEY_VALUE_HEADS
     bias = m_ref[...]
-    fold = len(send_refs) > 0 and bias.shape[0] == (len(send_refs) + 1) * token_rows
     if fold:
         far = len(send_refs) * token_rows
         lower = (
@@ -176,7 +175,7 @@
             send_ref[:, value_cols] = value_sum[rows].astype(send_ref.dtype)
 
 
-def attend_pallas(q_chunks, q_pick, weighted, kv_all, bias, part, groups):
+def attend_pallas(q_chunks, q_pick, weighted, kv_all, bias, part, groups, fold):
     token_rows = weighted.shape[0]
     capacity = q_chunks[0].shape[0]
     key_rows = kv_all.shape[0]
@@ -188,7 +187,9 @@
     bytes_accessed = 6 * token_rows * part_width + 2 * key_rows * kv_all.shape[1] + 4 * token_rows * key_rows
     whole = lambda i: (0, 0)
     return pl.pallas_call(
-        functools.partial(attend_kernel, first_group=part * groups, chunks=len(q_chunks), reach=reach),
+        functools.partial(
+            attend_kernel, first_group=part * groups, chunks=len(q_chunks), reach=reach, fold=fold
+        ),
         grid=(1,),
         in_specs=[pl.BlockSpec((capacity, part_width), lambda i: (0, part)) for _ in q_chunks]
         + [
@@ -223,6 +224,7 @@
     longest_segment = sp_size * token_rows // 2
     reach = min(sp_size - 1, (longest_segment + token_rows - 2) // token_rows)
     seq_len = (reach + 1) * token_rows
+    fold = reach > 0 and longest_segment == reach * token_rows
 
     packed_q, packed_kv = exchange_rows(rollout_rows, routing, dp_size, sp_size, dp_index, sp_index)
     own_seg = segment_labels[0]
@@ -258,9 +260,9 @@
     query_parts, key_parts, value_parts = [], [], []
     for part in range(2):
         query_grad, total, *outgoing = attend_pallas(
-            *packed_q, weighted, kv_all, bias, part, groups
-        )
-        for shift in range(1, reach + 1):
+            *packed_q, weighted, kv_all, bias, part, groups, fold
+        )
+        for shift in range(reach, 0, -1):
             arrived = lax.ppermute(
                 outgoing[shift - 1], "sp", [(k, k - shift) for k in range(shift, sp_size)]
             )

time: 80.6 us -> 78.7 us (0.976)
  waiting for transfers between devices: 23.1 us -> 21.2 us
    ppermute x4, waiting for transfers between devices: 14.1 us -> 12.2 us  [step(): lax.ppermute(outgoing[shift - 1], 'sp', [(k, k - shift) for k in range(sh...]
  transfers between devices with their start and end apart: 12 -> 12, of which waited for: 6 -> 4; matrix products, arithmetic and copies ran while one was open for 13% -> 13% of each run, Pallas kernels for 13% -> 13%
where the time goes in v19:
time: 78.7 us; the launch traced here: 78.2 us
  waiting for transfers between devices  21.2 us (27%)
  Pallas kernels  20.2 us (26%)
  starting transfers between devices  20.1 us (26%)
  other arithmetic  8.84 us (11%)
  local copies, waits for them, and re-layouts  3.79 us (5%)
  matrix products  3.23 us (4%)
  between operations  0.95 us (1%)
    pallas_call x2, Pallas kernels, attend_pallas(): pl.pallas_call(functools.partial(attend_kernel, first_group=part * groups...  20.2 us
    ppermute x4, waiting for transfers between devices, step(): lax.ppermute(outgoing[shift - 1], 'sp', [(k, k - shift) for k in range(sh...  12.2 us
    ppermute x2, starting transfers between devices, step(): lax.ppermute(kv_local, 'sp', [(k, k + shift) for k in range(sp_size - shi...  8.25 us
    ppermute x2, waiting for transfers between devices, step(): lax.ppermute(kv_local, 'sp', [(k, k + shift) for k in range(sp_size - shi...  7.43 us
    ppermute x6, starting transfers between devices, send(): lax.ppermute(outgoing[shift], 'dp', [(k, (k + shift) % dp_size) for k in...  6.24 us
    ppermute x4, starting transfers between devices, step(): lax.ppermute(outgoing[shift - 1], 'sp', [(k, k - shift) for k in range(sh...  5.6 us
    reshape x1, other arithmetic, step(): jnp.concatenate(query_parts, axis=1)  2.09 us
    dot_general x2, matrix products, send(): jnp.dot(send_pick, columns, preferred_element_type=jnp.float32)  1.93 us
  transfers between devices with their start and end apart: 12, of which 4 were waited for; matrix products, arithmetic and copies ran while one was open for 13% of the time, Pallas kernels for 13%

profile of v19, /device:TPU:0, one launch (start us, length us, event | category | flops | bytes accessed | tf_op | source)
XLA Modules:
  0.0 78.2 jit_solution(13705680327215819611)
XLA Ops:
  0.7 0.8 %dynamic-slice_bitcast_fusion = s32[128]{0:T(128)S(1)} fusion(s32[4,4,128]{2,1,0:T(4,128)} %bitcast.23, s32[]{:T(128)S(6)} %select_n.76, s32[]{:T(128)S(6)} %select_n.78), kind=kLoop, calls=%fused_computation.77 | loop fusion | bytes 1032 | tf_op jit(solution)/shard_map/jit(dynamic_index_in_dim)/squeeze | solution.py:33
  2.6 1.2 %convolution_convert_fusion.1 = bf16[256,1024]{1,0:T(8,128)(2,1)S(1)} fusion(bf16[128,5120]{1,0:T(8,128)(2,1)} %param.6, s32[128]{0:T(128)S(1)} %fusion.27), kind=kOutput, calls=%fused_computation.3 | convolution fusion | flops 67403776 | bytes 786944 | tf_op jit(solution)/shard_map/dot_general | solution.py:52
  3.8 0.8 %fusion.36 = (bf16[64,1024]{1,0:T(8,128)(2,1)}, bf16[64,1024]{1,0:T(8,128)(2,1)}, bf16[64,1024]{1,0:T(8,128)(2,1)}, bf16[64,1024]{1,0:T(8,128)(2,1)}) fusion(bf16[256,1024]{1,0:T(8,128)(2,1)S(1)} %convolution_convert_fusion.1), kind=kLoop, calls=%fused_computation.83 | loop fusion | bytes 1048576 | tf_op jit(solution)/shard_map/slice | solution.py:56
  5.1 2.5 %collective-permute-start.4 = (bf16[64,1024]{1,0:T(8,128)(2,1)}, bf16[64,1024]{1,0:T(8,128)(2,1)}, u32[]{:S(2)}, u32[]{:S(2)}) collective-permute-start(bf16[64,1024]{1,0:T(8,128)(2,1)} %get-tuple-element.26), channel_id=1, source_target_pairs={{0,8},{4,12},{8,0},{12,4},{1,9},{5,13},{9,1},{13,5},{2,10},{6,14},... | collective-permute-start | bytes 393224 | tf_op jit(solution)/shard_map/ppermute | solution.py:57
  7.6 1.5 %collective-permute-start.5 = (bf16[64,1024]{1,0:T(8,128)(2,1)}, bf16[64,1024]{1,0:T(8,128)(2,1)}, u32[]{:S(2)}, u32[]{:S(2)}) collective-permute-start(bf16[64,1024]{1,0:T(8,128)(2,1)} %get-tuple-element.25), channel_id=1, source_target_pairs={{0,12},{4,0},{8,4},{12,8},{1,13},{5,1},{9,5},{13,9},{2,14},{6,2},{... | collective-permute-start | bytes 393224 | tf_op jit(solution)/shard_map/ppermute | solution.py:57
  9.8 1.2 %fusion.35 = (bf16[64,4096]{1,0:T(8,128)(2,1)S(1)}, bf16[64,4096]{1,0:T(8,128)(2,1)}, bf16[64,4096]{1,0:T(8,128)(2,1)}, bf16[64,4096]{1,0:T(8,128)(2,1)}) fusion(bf16[256,4096]{1,0:T(8,128)(2,1)S(1)} %convolution_convert_fusion), kind=kLoop, calls=%fused_computation.82 | loop fusion | bytes 4194304 | tf_op jit(solution)/shard_map/slice | solution.py:58
  11.4 0.9 %fusion.23 = s32[4]{0:T(128)S(1)} fusion(s32[4,4,128]{2,1,0:T(4,128)} %bitcast.25, s32[]{:T(128)S(6)} %select_n.77, s32[]{:T(128)S(6)} %axis_index.23), kind=kLoop, calls=%fused_computation.54 | loop fusion | flops 1532 | bytes 2072 | tf_op jit(solution)/shard_map/reduce_sum | solution.py:38
  13.2 1.2 %fusion.refs_5_ = bf16[128,4096]{1,0:T(8,128)(2,1)} fusion(bf16[1,128,4096]{2,1,0:T(8,128)(2,1)S(1)} %copy-done.5, f32[128]{0:T(128)S(1)} %select_reduce_fusion.2), kind=kLoop, calls=%fused_computation.2 | loop fusion | flops 1572864 | bytes 2097664 | tf_op jit(solution)/shard_map/convert_element_type | solution.py:248
  14.5 1.4 %collective-permute-start.2 = (bf16[64,4096]{1,0:T(8,128)(2,1)S(1)}, bf16[64,4096]{1,0:T(8,128)(2,1)S(1)}, u32[]{:S(2)}, u32[]{:S(2)}) collective-permute-start(bf16[64,4096]{1,0:T(8,128)(2,1)S(1)} %get-tuple-element.20), channel_id=1, source_target_pairs={{0,12},{4,0},{8,4},{12,8},{1,13},{5,1},{9,5},{13,9},{2,14},{6,2},{... | collective-permute-start | bytes 1572872 | tf_op jit(solution)/shard_map/ppermute | solution.py:57
  15.9 1.3 %convolution_convert_fusion.2 = bf16[128,1024]{1,0:T(8,128)(2,1)S(1)} fusion(bf16[64,1024]{1,0:T(8,128)(2,1)} %collective-permute-done.5, bf16[64,1024]{1,0:T(8,128)(2,1)} %collective-permute-done.4, bf16[64,1024]{1,0:T(8,128)(2,1)} %collective-permute-done.3, bf16[64,1024]{1,0:T(8,128)(2,1)S(1)} %copy-done.9, s32[128]{0:T(128)S(1)} %fusion.30), kind=kOutput, calls=%fused_computation.4 | convolution fusion | flops 69369856 | bytes 786944 | tf_op jit(solution)/shard_map/dot_general | solution.py:70
  17.3 3.8 %collective-permute-start.6 = (bf16[128,1152]{1,0:T(8,128)(2,1)S(1)}, bf16[128,1152]{1,0:T(8,128)(2,1)S(1)}, u32[]{:S(2)}, u32[]{:S(2)}) collective-permute-start(bf16[128,1152]{1,0:T(8,128)(2,1)S(1)} %pad_maximum_fusion.1), channel_id=1, source_target_pairs={{0,1},{1,2},{2,3},{4,5},{5,6},{6,7},{8,9},{9,10},{10,11},{12,13},{... | collective-permute-start | bytes 884744 | tf_op jit(solution)/shard_map/ppermute | solution.py:234
  21.1 4.5 %collective-permute-start.7 = (bf16[128,1152]{1,0:T(8,128)(2,1)S(1)}, bf16[128,1152]{1,0:T(8,128)(2,1)S(1)}, u32[]{:S(2)}, u32[]{:S(2)}) collective-permute-start(bf16[128,1152]{1,0:T(8,128)(2,1)S(1)} %pad_maximum_fusion.1), channel_id=1, source_target_pairs={{0,2},{1,3},{4,6},{5,7},{8,10},{9,11},{12,14},{13,15},{16,18},{17,... | collective-permute-start | bytes 884744 | tf_op jit(solution)/shard_map/ppermute | solution.py:234
  26.3 2.1 %collective-permute-done.6 = bf16[128,1152]{1,0:T(8,128)(2,1)S(1)} collective-permute-done((bf16[128,1152]{1,0:T(8,128)(2,1)S(1)}, bf16[128,1152]{1,0:T(8,128)(2,1)S(1)}, u32[]{:S(2)}, u32[]{:S(2)}) %collective-permute-start.6) | collective-permute-done | bytes 294944 | tf_op jit(solution)/shard_map/ppermute | solution.py:234
  28.4 5.3 %collective-permute-done.7 = bf16[128,1152]{1,0:T(8,128)(2,1)S(1)} collective-permute-done((bf16[128,1152]{1,0:T(8,128)(2,1)S(1)}, bf16[128,1152]{1,0:T(8,128)(2,1)S(1)}, u32[]{:S(2)}, u32[]{:S(2)}) %collective-permute-start.7) | collective-permute-done | bytes 294944 | tf_op jit(solution)/shard_map/ppermute | solution.py:234
  34.0 0.9 %and_select_fusion.refs_7_ = f32[384,128]{1,0:T(8,128)} fusion(s32[128]{0:T(128)S(1)} %iota_add_fusion, s32[128]{0:T(128)S(1)} %bitcast.27, s32[384]{0:T(512)S(1)} %fusion.21, s32[384]{0:T(512)S(1)} %convert_reduce_fusion, pred[384]{0:T(512)(128)(4,1)S(1)} %broadcast_compare_fusion), kind=kLoop, calls=%fused_computation.21 | loop fusion | flops 245760 | bytes 201088 | tf_op jit(solution)/shard_map/jit(_where)/select_n | solution.py:258
  34.9 1.5 %collective-permute-done.2.refs_3_ = bf16[64,4096]{1,0:T(8,128)(2,1)S(1)} collective-permute-done((bf16[64,4096]{1,0:T(8,128)(2,1)S(1)}, bf16[64,4096]{1,0:T(8,128)(2,1)S(1)}, u32[]{:S(2)}, u32[]{:S(2)}) %collective-permute-start.2) | collective-permute-done | bytes 524320 | tf_op jit(solution)/shard_map/ppermute | solution.py:57
  37.2 10.1 %shard_map.77 = (bf16[128,2048]{1,0:T(8,128)(2,1)}, f32[128,512]{1,0:T(8,128)}, bf16[128,512]{1,0:T(8,128)(2,1)}, bf16[128,512]{1,0:T(8,128)(2,1)}) custom-call(bf16[64,4096]{1,0:T(8,128)(2,1)} %get-tuple-element.23.refs_0_, bf16[64,4096]{1,0:T(8,128)(2,1)} %copy-done.1, bf16[64,4096]{1,0:T(8,128)(2,1)} %copy-done.2, bf16[64,4096]{1,0:T(8,128)(2,1)} %copy-done.3, ...), custom_call_target="tpu_custom_call" | custom-call | flops 1006632960 | bytes 2654208 | tf_op jit(solution)/shard_map/pallas_call | solution.py:189
  47.3 1.3 %collective-permute-start.8 = (bf16[128,512]{1,0:T(8,128)(2,1)}, bf16[128,512]{1,0:T(8,128)(2,1)S(1)}, u32[]{:S(2)}, u32[]{:S(2)}) collective-permute-start(bf16[128,512]{1,0:T(8,128)(2,1)} %get-tuple-element.13), channel_id=1, source_target_pairs={{2,0},{3,1},{6,4},{7,5},{10,8},{11,9},{14,12},{15,13},{18,16},{19,... | collective-permute-start | bytes 393224 | tf_op jit(solution)/shard_map/ppermute | solution.py:266
  48.6 1.6 %collective-permute-start.9 = (bf16[128,512]{1,0:T(8,128)(2,1)}, bf16[128,512]{1,0:T(8,128)(2,1)S(1)}, u32[]{:S(2)}, u32[]{:S(2)}) collective-permute-start(bf16[128,512]{1,0:T(8,128)(2,1)} %get-tuple-element.14), channel_id=1, source_target_pairs={{1,0},{2,1},{3,2},{5,4},{6,5},{7,6},{9,8},{10,9},{11,10},{13,12},{... | collective-permute-start | bytes 393224 | tf_op jit(solution)/shard_map/ppermute | solution.py:266
  50.2 10.1 %shard_map.78 = (bf16[128,2048]{1,0:T(8,128)(2,1)}, f32[128,512]{1,0:T(8,128)}, bf16[128,512]{1,0:T(8,128)(2,1)}, bf16[128,512]{1,0:T(8,128)(2,1)}) custom-call(bf16[64,4096]{1,0:T(8,128)(2,1)} %get-tuple-element.23.refs_0_, bf16[64,4096]{1,0:T(8,128)(2,1)} %copy-done.1, bf16[64,4096]{1,0:T(8,128)(2,1)} %copy-done.2, bf16[64,4096]{1,0:T(8,128)(2,1)} %copy-done.3, ...), custom_call_target="tpu_custom_call" | custom-call | flops 1006632960 | bytes 2654208 | tf_op jit(solution)/shard_map/pallas_call | solution.py:189
  60.3 1.4 %collective-permute-start.10 = (bf16[128,512]{1,0:T(8,128)(2,1)}, bf16[128,512]{1,0:T(8,128)(2,1)S(1)}, u32[]{:S(2)}, u32[]{:S(2)}) collective-permute-start(bf16[128,512]{1,0:T(8,128)(2,1)} %get-tuple-element.16), channel_id=1, source_target_pairs={{2,0},{3,1},{6,4},{7,5},{10,8},{11,9},{14,12},{15,13},{18,16},{19,... | collective-permute-start | bytes 393224 | tf_op jit(solution)/shard_map/ppermute | solution.py:266
  61.7 1.3 %collective-permute-start.11 = (bf16[128,512]{1,0:T(8,128)(2,1)}, bf16[128,512]{1,0:T(8,128)(2,1)S(1)}, u32[]{:S(2)}, u32[]{:S(2)}) collective-permute-start(bf16[128,512]{1,0:T(8,128)(2,1)} %get-tuple-element.17), channel_id=1, source_target_pairs={{1,0},{2,1},{3,2},{5,4},{6,5},{7,6},{9,8},{10,9},{11,10},{13,12},{... | collective-permute-start | bytes 393224 | tf_op jit(solution)/shard_map/ppermute | solution.py:266
  63.0 2.1 %maximum_bitcast_fusion = bf16[1,128,4096]{2,1,0:T(8,128)(2,1)} fusion(bf16[128,2048]{1,0:T(8,128)(2,1)} %get-tuple-element.11, bf16[128,2048]{1,0:T(8,128)(2,1)S(1)} %copy-done.6), kind=kLoop, calls=%fused_computation.5 | loop fusion | flops 2097152 | bytes 2097152 | tf_op jit(solution)/shard_map/reshape | solution.py:273
  65.2 12.2 %collective-permute-done.10 = bf16[128,512]{1,0:T(8,128)(2,1)S(1)} collective-permute-done((bf16[128,512]{1,0:T(8,128)(2,1)}, bf16[128,512]{1,0:T(8,128)(2,1)S(1)}, u32[]{:S(2)}, u32[]{:S(2)}) %collective-permute-start.10) | collective-permute-done | bytes 131104 | tf_op jit(solution)/shard_map/ppermute | solution.py:266
  (68 shorter events, 6.4 us)
Async XLA Ops:
  0.6 8.4 %copy-start.4 = (bf16[128,5120]{1,0:T(8,128)(2,1)S(1)}, bf16[128,5120]{1,0:T(8,128)(2,1)}, u32[]{:S(2)}) copy-start(bf16[128,5120]{1,0:T(8,128)(2,1)} %param.6) | copy-start | bytes 3932164
  4.6 9.8 %collective-permute-start.3 = (bf16[64,1024]{1,0:T(8,128)(2,1)}, bf16[64,1024]{1,0:T(8,128)(2,1)}, u32[]{:S(2)}, u32[]{:S(2)}) collective-permute-start(bf16[64,1024]{1,0:T(8,128)(2,1)} %get-tuple-element.27), channel_id=1, source_target_pairs={{0,4},{4,8},{8,12},{12,0},{1,5},{5,9},{9,13},{13,1},{2,6},{6,10},{... | collective-permute-start | bytes 393224 | tf_op jit(solution)/shard_map/ppermute | solution.py:57
  5.1 10.8 %collective-permute-start.4 = (bf16[64,1024]{1,0:T(8,128)(2,1)}, bf16[64,1024]{1,0:T(8,128)(2,1)}, u32[]{:S(2)}, u32[]{:S(2)}) collective-permute-start(bf16[64,1024]{1,0:T(8,128)(2,1)} %get-tuple-element.26), channel_id=1, source_target_pairs={{0,8},{4,12},{8,0},{12,4},{1,9},{5,13},{9,1},{13,5},{2,10},{6,14},... | collective-permute-start | bytes 393224 | tf_op jit(solution)/shard_map/ppermute | solution.py:57
  7.6 8.3 %collective-permute-start.5 = (bf16[64,1024]{1,0:T(8,128)(2,1)}, bf16[64,1024]{1,0:T(8,128)(2,1)}, u32[]{:S(2)}, u32[]{:S(2)}) collective-permute-start(bf16[64,1024]{1,0:T(8,128)(2,1)} %get-tuple-element.25), channel_id=1, source_target_pairs={{0,12},{4,0},{8,4},{12,8},{1,13},{5,1},{9,5},{13,9},{2,14},{6,2},{... | collective-permute-start | bytes 393224 | tf_op jit(solution)/shard_map/ppermute | solution.py:57
  9.8 3.0 %copy-start.10 = (s32[1,128]{1,0:T(1,128)S(1)}, s32[1,128]{1,0:T(1,128)}, u32[]{:S(2)}) copy-start(s32[1,128]{1,0:T(1,128)} %param.8) | copy-start | bytes 1540
  9.8 3.0 %copy-start.12 = (s32[16]{0:T(128)S(1)}, s32[16]{0:T(128)}, u32[]{:S(2)}) copy-start(s32[16]{0:T(128)} %param.10) | copy-start | bytes 196
  9.8 3.0 %copy-start.11 = (s32[16]{0:T(128)S(1)}, s32[16]{0:T(128)}, u32[]{:S(2)}) copy-start(s32[16]{0:T(128)} %param.11) | copy-start | bytes 196
  9.8 3.4 %copy-start.5 = (bf16[1,128,4096]{2,1,0:T(8,128)(2,1)S(1)}, bf16[1,128,4096]{2,1,0:T(8,128)(2,1)}, u32[]{:S(2)}) copy-start(bf16[1,128,4096]{2,1,0:T(8,128)(2,1)} %param.9) | copy-start | bytes 3145732
  11.0 4.9 %copy-start.9 = (bf16[64,1024]{1,0:T(8,128)(2,1)S(1)}, bf16[64,1024]{1,0:T(8,128)(2,1)}, u32[]{:S(2)}) copy-start(bf16[64,1024]{1,0:T(8,128)(2,1)} %get-tuple-element.24) | copy-start | bytes 393220
  11.0 23.9 %collective-permute-start = (bf16[64,4096]{1,0:T(8,128)(2,1)}, bf16[64,4096]{1,0:T(8,128)(2,1)S(1)}, u32[]{:S(2)}, u32[]{:S(2)}) collective-permute-start(bf16[64,4096]{1,0:T(8,128)(2,1)} %get-tuple-element.22), channel_id=1, source_target_pairs={{0,4},{4,8},{8,12},{12,0},{1,5},{5,9},{9,13},{13,1},{2,6},{6,10},{... | collective-permute-start | bytes 1572872 | tf_op jit(solution)/shard_map/ppermute | solution.py:57
  11.0 23.9 %collective-permute-start.1 = (bf16[64,4096]{1,0:T(8,128)(2,1)}, bf16[64,4096]{1,0:T(8,128)(2,1)S(1)}, u32[]{:S(2)}, u32[]{:S(2)}) collective-permute-start(bf16[64,4096]{1,0:T(8,128)(2,1)} %get-tuple-element.21), channel_id=1, source_target_pairs={{0,8},{4,12},{8,0},{12,4},{1,9},{5,13},{9,1},{13,5},{2,10},{6,14},... | collective-permute-start | bytes 1572872 | tf_op jit(solution)/shard_map/ppermute | solution.py:57
  14.5 21.9 %collective-permute-start.2 = (bf16[64,4096]{1,0:T(8,128)(2,1)S(1)}, bf16[64,4096]{1,0:T(8,128)(2,1)S(1)}, u32[]{:S(2)}, u32[]{:S(2)}) collective-permute-start(bf16[64,4096]{1,0:T(8,128)(2,1)S(1)} %get-tuple-element.20), channel_id=1, source_target_pairs={{0,12},{4,0},{8,4},{12,8},{1,13},{5,1},{9,5},{13,9},{2,14},{6,2},{... | collective-permute-start | bytes 1572872 | tf_op jit(solution)/shard_map/ppermute | solution.py:57
  17.3 11.1 %collective-permute-start.6 = (bf16[128,1152]{1,0:T(8,128)(2,1)S(1)}, bf16[128,1152]{1,0:T(8,128)(2,1)S(1)}, u32[]{:S(2)}, u32[]{:S(2)}) collective-permute-start(bf16[128,1152]{1,0:T(8,128)(2,1)S(1)} %pad_maximum_fusion.1), channel_id=1, source_target_pairs={{0,1},{1,2},{2,3},{4,5},{5,6},{6,7},{8,9},{9,10},{10,11},{12,13},{... | collective-permute-start | bytes 884744 | tf_op jit(solution)/shard_map/ppermute | solution.py:234
  21.1 12.7 %collective-permute-start.7 = (bf16[128,1152]{1,0:T(8,128)(2,1)S(1)}, bf16[128,1152]{1,0:T(8,128)(2,1)S(1)}, u32[]{:S(2)}, u32[]{:S(2)}) collective-permute-start(bf16[128,1152]{1,0:T(8,128)(2,1)S(1)} %pad_maximum_fusion.1), channel_id=1, source_target_pairs={{0,2},{1,3},{4,6},{5,7},{8,10},{9,11},{12,14},{13,15},{16,18},{17,... | collective-permute-start | bytes 884744 | tf_op jit(solution)/shard_map/ppermute | solution.py:234
  33.8 2.6 %copy-start = (bf16[384,1152]{1,0:T(8,128)(2,1)}, bf16[384,1152]{1,0:T(8,128)(2,1)S(1)}, u32[]{:S(2)}) copy-start(bf16[384,1152]{1,0:T(8,128)(2,1)S(1)} %pad_maximum_fusion.refs_6_) | copy-start | bytes 2654212
  34.9 1.5 %copy-start.1 = (bf16[64,4096]{1,0:T(8,128)(2,1)}, bf16[64,4096]{1,0:T(8,128)(2,1)S(1)}, u32[]{:S(2)}) copy-start(bf16[64,4096]{1,0:T(8,128)(2,1)S(1)} %collective-permute-done.refs_1_) | copy-start | bytes 1572868
  34.9 1.5 %copy-start.2 = (bf16[64,4096]{1,0:T(8,128)(2,1)}, bf16[64,4096]{1,0:T(8,128)(2,1)S(1)}, u32[]{:S(2)}) copy-start(bf16[64,4096]{1,0:T(8,128)(2,1)S(1)} %collective-permute-done.1.refs_2_) | copy-start | bytes 1572868
  47.3 17.8 %collective-permute-start.8 = (bf16[128,512]{1,0:T(8,128)(2,1)}, bf16[128,512]{1,0:T(8,128)(2,1)S(1)}, u32[]{:S(2)}, u32[]{:S(2)}) collective-permute-start(bf16[128,512]{1,0:T(8,128)(2,1)} %get-tuple-element.13), channel_id=1, source_target_pairs={{2,0},{3,1},{6,4},{7,5},{10,8},{11,9},{14,12},{15,13},{18,16},{19,... | collective-permute-start | bytes 393224 | tf_op jit(solution)/shard_map/ppermute | solution.py:266
  48.6 14.4 %copy-start.6 = (bf16[128,2048]{1,0:T(8,128)(2,1)S(1)}, bf16[128,2048]{1,0:T(8,128)(2,1)}, u32[]{:S(2)}) copy-start(bf16[128,2048]{1,0:T(8,128)(2,1)} %get-tuple-element.10) | copy-start | bytes 1572868
  48.6 16.5 %collective-permute-start.9 = (bf16[128,512]{1,0:T(8,128)(2,1)}, bf16[128,512]{1,0:T(8,128)(2,1)S(1)}, u32[]{:S(2)}, u32[]{:S(2)}) collective-permute-start(bf16[128,512]{1,0:T(8,128)(2,1)} %get-tuple-element.14), channel_id=1, source_target_pairs={{1,0},{2,1},{3,2},{5,4},{6,5},{7,6},{9,8},{10,9},{11,10},{13,12},{... | collective-permute-start | bytes 393224 | tf_op jit(solution)/shard_map/ppermute | solution.py:266
  60.3 4.8 %copy-start.8 = (f32[128,512]{1,0:T(8,128)S(1)}, f32[128,512]{1,0:T(8,128)}, u32[]{:S(2)}) copy-start(f32[128,512]{1,0:T(8,128)} %get-tuple-element.12) | copy-start | bytes 786436
  60.3 17.1 %copy-start.7 = (f32[128,512]{1,0:T(8,128)S(1)}, f32[128,512]{1,0:T(8,128)}, u32[]{:S(2)}) copy-start(f32[128,512]{1,0:T(8,128)} %get-tuple-element.15) | copy-start | bytes 786436
  60.3 17.1 %collective-permute-start.10 = (bf16[128,512]{1,0:T(8,128)(2,1)}, bf16[128,512]{1,0:T(8,128)(2,1)S(1)}, u32[]{:S(2)}, u32[]{:S(2)}) collective-permute-start(bf16[128,512]{1,0:T(8,128)(2,1)} %get-tuple-element.16), channel_id=1, source_target_pairs={{2,0},{3,1},{6,4},{7,5},{10,8},{11,9},{14,12},{15,13},{18,16},{19,... | collective-permute-start | bytes 393224 | tf_op jit(solution)/shard_map/ppermute | solution.py:266
  61.7 15.7 %collective-permute-start.11 = (bf16[128,512]{1,0:T(8,128)(2,1)}, bf16[128,512]{1,0:T(8,128)(2,1)S(1)}, u32[]{:S(2)}, u32[]{:S(2)}) collective-permute-start(bf16[128,512]{1,0:T(8,128)(2,1)} %get-tuple-element.17), channel_id=1, source_target_pairs={{1,0},{2,1},{3,2},{5,4},{6,5},{7,6},{9,8},{10,9},{11,10},{13,12},{... | collective-permute-start | bytes 393224 | tf_op jit(solution)/shard_map/ppermute | solution.py:266
  (1 other events, 0.8 us)
